TPU v7x, 32 devices: a whole 2x2x4 slice. The times are simulated.
32 devices in a mesh: gx: 8 (over z, x), gy: 4 (over y, core).
Axes of the slice: x: 2, y: 2, z: 4, core: 2. Of those that a mesh axis runs over, the one named last changes fastest.
Arguments:
- inputs: bfloat16 [3, 256, 8192], P(None, 'gy', 'gx'), may hold values from -600 to 600
- norm_gain: bfloat16 [8192], P('gx'), may hold values from 0.099609375 to 1.8984375
- query_weight: bfloat16 [8192, 8192], P('gx', 'gy'), may hold values from -0.0625 to 0.0625
- key_weight: bfloat16 [8192, 1024], P('gx', 'gy'), may hold values from -0.0625 to 0.0625
- value_weight: bfloat16 [8192, 1024], P('gx', 'gy'), may hold values from -0.0625 to 0.0625
- output_weight: bfloat16 [8192, 8192], P('gy', 'gx'), may hold values from -0.0625 to 0.0625
- query_down: bfloat16 [256, 8192, 64], P('gy', 'gx'), may hold values from -0.0625 to 0.0625
- query_up: bfloat16 [256, 64, 8192], P('gx', None, 'gy'), may hold values from -0.75 to 0.75
- output_down: bfloat16 [256, 8192, 64], P('gx', 'gy'), may hold values from -0.0625 to 0.0625
- output_up: bfloat16 [256, 64, 8192], P('gy', None, 'gx'), may hold values from -0.75 to 0.75
- block_adapter: int32 [2], replicated, may hold values from 0 to 255
- cache_lengths: int32 [256], P(('gx', 'gy')), may hold values from 1 to 256, as said below
- cache_keys: bfloat16 [256, 256, 1024], P(('gx', 'gy')), may hold values from -160 to 160
- cache_values: bfloat16 [256, 256, 1024], P(('gx', 'gy')), may hold values from -6 to 6
Outputs:
- block_output: bfloat16 [3, 256, 8192], P(None, 'gy', 'gx')
Inputs may be any that keep to these rules, and one draw needn't show every extreme that they name: `cache_lengths`: some request has exactly 256 cached positions.
All inputs are finite; a program needn't handle non-finite values.
Results may differ from a plain program's by a relative error of at most 0.012.
The roundings to bfloat16 on the way count: a program that leaves them out, or rounds other values in their place, can miss the bound.
Values may be sent and summed in bfloat16 or wider, within the bound.
No kernel may reach another device: no remote copies, remote signals or barrier semaphores. Data moves between devices by JAX's collectives and lax.ppermute only.
A program may use at most 192 MiB of HBM per device.

v0:
```python
import jax
import jax.numpy as jnp
from jax import lax
from jax.sharding import PartitionSpec as P

D = 8192
QUERY_HEADS = 64
KEY_VALUE_HEADS = 8
HEAD_FEATURES = 128
BLOCK = 128
STEPS = 3


EPS = 1e-05
THETA = 500000.0


def rotary_embedding(values_in, token_positions):
    half_size = values_in.shape[-1] // 2
    exponent = jnp.arange(half_size, dtype=jnp.float32) * 2.0 / values_in.shape[-1]
    frequency = THETA ** (-exponent)
    angles = token_positions.astype(jnp.float32)[:, None] * frequency[None, :]
    cosine = jnp.cos(angles)[:, None, :]
    sine_part = jnp.sin(angles)[:, None, :]
    lower = values_in[..., :half_size]
    upper = values_in[..., half_size:]
    return jnp.concatenate(
        [lower * cosine - upper * sine_part, upper * cosine + lower * sine_part], axis=-1
    )


def pick_adapters(table, adapter_ids, first_id):
    table_count = table.shape[0]
    wanted = first_id + jnp.arange(table_count, dtype=jnp.int32)
    onehot = (adapter_ids[:, None] == wanted[None, :]).astype(table.dtype)
    flat_table = table.reshape(table_count, -1)
    picked = jnp.dot(onehot, flat_table, preferred_element_type=jnp.float32).astype(table.dtype)
    return picked.reshape((adapter_ids.shape[0],) + table.shape[1:])


def attend(
    query_rows, previous_keys, previous_values, incoming_keys, incoming_values, lengths, step_index
):
    count_of_rows = query_rows.shape[0]
    context_window = previous_keys.shape[1]
    grouped_heads = query_rows.reshape(
        count_of_rows, KEY_VALUE_HEADS, QUERY_HEADS // KEY_VALUE_HEADS, HEAD_FEATURES
    )
    keys_previous = previous_keys.reshape(
        count_of_rows, context_window, KEY_VALUE_HEADS, HEAD_FEATURES
    )
    values_previous = previous_values.reshape(
        count_of_rows, context_window, KEY_VALUE_HEADS, HEAD_FEATURES
    )
    keys_incoming = incoming_keys.reshape(count_of_rows, -1, KEY_VALUE_HEADS, HEAD_FEATURES)
    values_incoming = incoming_values.reshape(count_of_rows, -1, KEY_VALUE_HEADS, HEAD_FEATURES)
    factor = HEAD_FEATURES ** (-0.5)
    score_old = (
        jnp.einsum(
            "rhgd,rchd->rhgc", grouped_heads, keys_previous, preferred_element_type=jnp.float32
        )
        * factor
    )
    score_new = (
        jnp.einsum(
            "rhgd,rshd->rhgs", grouped_heads, keys_incoming, preferred_element_type=jnp.float32
        )
        * factor
    )
    live_old = (jnp.arange(context_window, dtype=jnp.int32)[None, :] < lengths[:, None])[
        :, None, None, :
    ]
    live_new = (jnp.arange(keys_incoming.shape[1], dtype=jnp.int32) <= step_index)[
        None, None, None, :
    ]
    score_old = jnp.where(live_old, score_old, -1e30)
    score_new = jnp.where(live_new, score_new, -1e30)
    peak_score = jnp.maximum(jnp.max(score_old, axis=-1), jnp.max(score_new, axis=-1))
    weight_old = jnp.where(live_old, jnp.exp(score_old - peak_score[..., None]), 0.0)
    weight_new = jnp.where(live_new, jnp.exp(score_new - peak_score[..., None]), 0.0)
    weight_sum = jnp.sum(weight_old, axis=-1) + jnp.sum(weight_new, axis=-1)
    mixed_out = jnp.einsum(
        "rhgc,rchd->rhgd",
        weight_old.astype(jnp.bfloat16),
        values_previous,
        preferred_element_type=jnp.float32,
    )
    mixed_out = mixed_out + jnp.einsum(
        "rhgs,rshd->rhgd",
        weight_new.astype(jnp.bfloat16),
        values_incoming,
        preferred_element_type=jnp.float32,
    )
    return (mixed_out / weight_sum[..., None]).reshape(count_of_rows, -1).astype(jnp.bfloat16)


def normalize(rows_in, squares, norm_scale):
    factor_rows = lax.rsqrt(squares / D + EPS)
    return (rows_in.astype(jnp.float32) * factor_rows[:, None] * norm_scale[None, :]).astype(
        jnp.bfloat16
    )


def local(
    inputs,
    norm_gain,
    query_weight,
    key_weight,
    value_weight,
    output_weight,
    query_down,
    query_up,
    output_down,
    output_up,
    block_adapter,
    cache_lengths,
    cache_keys,
    cache_values,
):
    across_second = lax.axis_size("gy")
    index_first = lax.axis_index("gx")
    index_second = lax.axis_index("gy")
    request_count = inputs.shape[1] * across_second
    local_rows = cache_keys.shape[0]
    block_count = block_adapter.shape[0]
    norm_scale = norm_gain.astype(jnp.float32)
    query_first = pick_adapters(query_down, block_adapter, index_second * query_down.shape[0])
    query_second = pick_adapters(query_up, block_adapter, index_first * query_up.shape[0])
    output_first = pick_adapters(output_down, block_adapter, index_first * output_down.shape[0])
    output_second = pick_adapters(output_up, block_adapter, index_second * output_up.shape[0])
    incoming_keys = jnp.zeros((local_rows, STEPS, cache_keys.shape[2]), jnp.bfloat16)
    incoming_values = jnp.zeros((local_rows, STEPS, cache_values.shape[2]), jnp.bfloat16)
    results = []
    for step_index in range(STEPS):
        own_inputs = inputs[step_index]
        rows_all = lax.all_gather(own_inputs, "gy", axis=0, tiled=True)
        squares = lax.psum(jnp.sum(jnp.square(rows_all.astype(jnp.float32)), axis=1), "gx")
        normed = normalize(rows_all, squares, norm_scale)
        blocked = normed.reshape(block_count, BLOCK, -1)
        rank_part = jnp.einsum(
            "bnd,bdr->bnr", blocked, query_first, preferred_element_type=jnp.float32
        )
        rank_query = lax.psum(rank_part, ("gx", "gy")).astype(jnp.bfloat16)
        delta_query = jnp.einsum(
            "bnr,bre->bne", rank_query, query_second, preferred_element_type=jnp.float32
        ).reshape(request_count, -1)
        part_query = jnp.dot(normed, query_weight, preferred_element_type=jnp.float32) + delta_query
        part_key = jnp.dot(normed, key_weight, preferred_element_type=jnp.float32)
        part_value = jnp.dot(normed, value_weight, preferred_element_type=jnp.float32)
        summed = (
            lax.psum_scatter(part_query, "gx", scatter_dimension=0, tiled=True),
            lax.psum_scatter(part_key, "gx", scatter_dimension=0, tiled=True),
            lax.psum_scatter(part_value, "gx", scatter_dimension=0, tiled=True),
        )
        query_full, key_complete, value_full = (
            lax.all_to_all(
                summed[0].astype(jnp.bfloat16), "gy", split_axis=0, concat_axis=1, tiled=True
            ),
            lax.all_to_all(
                summed[1].astype(jnp.bfloat16), "gy", split_axis=0, concat_axis=1, tiled=True
            ),
            lax.all_to_all(
                summed[2].astype(jnp.bfloat16), "gy", split_axis=0, concat_axis=1, tiled=True
            ),
        )
        token_positions = cache_lengths + step_index
        query_rot = rotary_embedding(
            query_full.astype(jnp.float32).reshape(local_rows, QUERY_HEADS, HEAD_FEATURES),
            token_positions,
        ).astype(jnp.bfloat16)
        key_rotated = rotary_embedding(
            key_complete.astype(jnp.float32).reshape(local_rows, KEY_VALUE_HEADS, HEAD_FEATURES),
            token_positions,
        ).astype(jnp.bfloat16)
        incoming_keys = incoming_keys.at[:, step_index].set(key_rotated.reshape(local_rows, -1))
        incoming_values = incoming_values.at[:, step_index].set(value_full)
        mixed_local = attend(
            query_rot.reshape(local_rows, -1),
            cache_keys,
            cache_values,
            incoming_keys,
            incoming_values,
            cache_lengths,
            step_index,
        )
        head_group = lax.all_to_all(mixed_local, "gy", split_axis=1, concat_axis=0, tiled=True)
        mixed_all = lax.all_gather(head_group, "gx", axis=0, tiled=True)
        rank_part_out = jnp.einsum(
            "bnq,bqr->bnr",
            mixed_all.reshape(block_count, BLOCK, -1),
            output_first,
            preferred_element_type=jnp.float32,
        )
        rank_output = lax.psum(rank_part_out, ("gx", "gy")).astype(jnp.bfloat16)
        delta_output = jnp.einsum(
            "bnr,bre->bne", rank_output, output_second, preferred_element_type=jnp.float32
        ).reshape(request_count, -1)
        partial_out = (
            jnp.dot(mixed_all, output_weight, preferred_element_type=jnp.float32) + delta_output
        )
        results.append(
            lax.psum_scatter(partial_out, "gy", scatter_dimension=0, tiled=True).astype(
                jnp.bfloat16
            )
        )
    return jnp.stack(results)


def solution(mesh):
    in_specs = (
        P(None, "gy", "gx"),
        P("gx"),
        P("gx", "gy"),
        P("gx", "gy"),
        P("gx", "gy"),
        P("gy", "gx"),
        P("gy", "gx", None),
        P("gx", None, "gy"),
        P("gx", "gy", None),
        P("gy", None, "gx"),
        P(),
        P(("gx", "gy")),
        P(("gx", "gy"), None, None),
        P(("gx", "gy"), None, None),
    )
    out_specs = P(None, "gy", "gx")
    return jax.shard_map(local, mesh=mesh, in_specs=in_specs, out_specs=out_specs, check_vma=False)
```

profile of v0, /device:TPU:0, one launch (start us, length us, event | category | flops | bytes accessed | tf_op | source)
XLA Modules:
  0.0 940.9 jit_solution(17731421883246101163)
XLA Ops:
  7.7 8.6 all-gather.2
  16.3 7.3 all-gather
  23.8 7.3 all-gather.1
  32.3 21.7 %all-reduce.4 = (f32[256]{0:T(256)S(1)}, f32[256]{0:T(256)S(1)}, f32[256]{0:T(256)S(1)}) all-reduce(f32[256]{0:T(256)S(1)} %fusion.66, f32[256]{0:T(256)S(1)} %fusion.69, f32[256]{0:T(256)S(1)} %fusion.72), channel_id=1, replica_groups=mesh['gx'=8,'gy'=4] {'gx'}, use_global_device_ids=true, to_apply=%region_1.0 | all-reduce | flops 768 | bytes 6144 | tf_op jit(solution)/shard_map/psum | solution.py:137
  64.2 11.4 %copy.109 = bf16[4,8,64,2048]{3,1,2,0:T(8,128)(2,1)} copy(bf16[4,8,64,2048]{3,2,1,0:T(8,128)(2,1)} %bitcast.289) | data formatting | bytes 16777216
  75.6 15.6 %copy.74 = bf16[64,1024,64]{2,1,0:T(8,128)(2,1)} copy(bf16[64,1024,64]{1,2,0:T(8,128)(2,1)} %param.32) | data formatting | bytes 16777216 | tf_op args[6]
  91.3 16.5 %reshape.597 = bf16[64,65536]{1,0:T(8,128)(2,1)} reshape(bf16[64,1024,64]{2,1,0:T(8,128)(2,1)} %copy.74) | data formatting | bytes 16777216 | tf_op jit(solution)/shard_map/reshape | solution.py:36
  113.8 4.7 convolution_convert_fusion.1
  118.5 40.4 %all-reduce.7 = (bf16[2,128,64]{1,2,0:T(8,128)(2,1)S(1)}, bf16[2,128,64]{1,2,0:T(8,128)(2,1)S(1)}, bf16[2,128,64]{1,2,0:T(8,128)(2,1)S(1)}) all-reduce(f32[2,128,64]{1,2,0:T(8,128)S(1)} %fusion.191, f32[2,128,64]{1,2,0:T(8,128)S(1)} %fusion.183, f32[2,128,64]{1,2,0:T(8,128)S(1)} %fusion.187), channel_id=1, replica_groups=mesh['gx'=8,'gy'=4] {'gx','gy'}, use_global_device_ids=true, to_apply=%region_26.27 | all-reduce | flops 49152 | bytes 294912 | tf_op jit(solution)/shard_map/psum | solution.py:143
  159.4 4.8 convolution_add_fusion.1
  164.8 4.9 convolution_add_fusion
  170.2 4.8 convolution_add_fusion.2
  181.4 61.1 %reduce-scatter.17.cloned.1.call-done = f32[32,256]{1,0:T(8,128)} async-done(((f32[256,256]{1,0:T(8,128)}), f32[32,256]{1,0:T(8,128)}) %reduce-scatter.17.cloned.1.call-update) | async-done | bytes 32784 | tf_op jit(solution)/shard_map/reduce_scatter | solution.py:153
  243.9 62.1 %reduce-scatter.25.cloned.1.call-done = f32[32,256]{1,0:T(8,128)} async-done(((f32[256,256]{1,0:T(8,128)}), f32[32,256]{1,0:T(8,128)}) %reduce-scatter.25.cloned.1.call-update) | async-done | bytes 32784 | tf_op jit(solution)/shard_map/reduce_scatter | solution.py:153
  307.4 62.1 %reduce-scatter.31.cloned.1.call-done = f32[32,256]{1,0:T(8,128)} async-done(((f32[256,256]{1,0:T(8,128)}), f32[32,256]{1,0:T(8,128)}) %reduce-scatter.31.cloned.1.call-update) | async-done | bytes 32784 | tf_op jit(solution)/shard_map/reduce_scatter | solution.py:152
  370.8 62.1 %reduce-scatter.33.cloned.1.call-done = f32[32,256]{1,0:T(8,128)} async-done(((f32[256,256]{1,0:T(8,128)}), f32[32,256]{1,0:T(8,128)}) %reduce-scatter.33.cloned.1.call-update) | async-done | bytes 32784 | tf_op jit(solution)/shard_map/reduce_scatter | solution.py:153
  462.6 40.5 %reduce-scatter.21.cloned.1.call-done = f32[32,2048]{1,0:T(8,128)} async-done(((f32[256,2048]{1,0:T(8,128)}), f32[32,2048]{1,0:T(8,128)}) %reduce-scatter.21.cloned.1.call-update) | async-done | bytes 262160 | tf_op jit(solution)/shard_map/reduce_scatter | solution.py:151
  508.1 65.3 %reduce-scatter.29.cloned.1.call-done = f32[32,2048]{1,0:T(8,128)} async-done(((f32[256,2048]{1,0:T(8,128)}), f32[32,2048]{1,0:T(8,128)}) %reduce-scatter.29.cloned.1.call-update) | async-done | bytes 262160 | tf_op jit(solution)/shard_map/reduce_scatter | solution.py:151
  575.0 68.7 %reduce-scatter.13.cloned.1.call-done = f32[32,2048]{1,0:T(8,128)} async-done(((f32[256,2048]{1,0:T(8,128)}), f32[32,2048]{1,0:T(8,128)}) %reduce-scatter.13.cloned.1.call-update) | async-done | bytes 262160 | tf_op jit(solution)/shard_map/reduce_scatter | solution.py:151
  677.1 7.7 all_to_all.174
  688.1 7.7 all_to_all.175
  699.5 7.7 all_to_all.176
  707.2 12.0 %copy.113 = bf16[8,8,64,1024]{3,1,2,0:T(8,128)(2,1)} copy(bf16[8,8,64,1024]{3,2,1,0:T(8,128)(2,1)} %bitcast.290) | data formatting | bytes 16777216
  719.2 15.7 %copy.83 = bf16[32,2048,64]{2,1,0:T(8,128)(2,1)} copy(bf16[32,2048,64]{1,2,0:T(8,128)(2,1)} %param.34) | data formatting | bytes 16777216 | tf_op args[8]
  735.0 15.9 %reshape.608 = bf16[32,131072]{1,0:T(8,128)(2,1)} reshape(bf16[32,2048,64]{2,1,0:T(8,128)(2,1)} %copy.83) | data formatting | bytes 16777216 | tf_op jit(solution)/shard_map/reshape | solution.py:36
  756.2 4.7 convolution_convert_fusion.2
  766.0 39.2 %all-gather.7.cloned.1.call-done = bf16[256,2048]{1,0:T(8,128)(2,1)} async-done(((bf16[32,2048]{1,0:T(8,128)(2,1)}), bf16[256,2048]{1,0:T(8,128)(2,1)}) %all-gather.7.cloned.1.call-update) | async-done | bytes 1048592 | tf_op jit(solution)/shard_map/all_gather | solution.py:187
  807.0 41.8 %all-reduce.8 = (bf16[2,128,64]{1,2,0:T(8,128)(2,1)S(1)}, bf16[2,128,64]{1,2,0:T(8,128)(2,1)S(1)}, bf16[2,128,64]{1,2,0:T(8,128)(2,1)S(1)}) all-reduce(f32[2,128,64]{1,2,0:T(8,128)S(1)} %fusion.194, f32[2,128,64]{1,2,0:T(8,128)S(1)} %fusion.190, f32[2,128,64]{1,2,0:T(8,128)S(1)} %fusion.186), channel_id=1, replica_groups=mesh['gx'=8,'gy'=4] {'gx','gy'}, use_global_device_ids=true, to_apply=%region_34.35 | all-reduce | flops 49152 | bytes 294912 | tf_op jit(solution)/shard_map/psum | solution.py:194
  859.1 4.7 convolution_add_fusion.5
  863.9 13.7 %reduce-scatter.35.cloned.1.call-done = f32[64,1024]{1,0:T(8,128)} async-done(((f32[256,1024]{1,0:T(8,128)}), f32[64,1024]{1,0:T(8,128)}) %reduce-scatter.35.cloned.1.call-update) | async-done | bytes 262160 | tf_op jit(solution)/shard_map/reduce_scatter | solution.py:202
  878.5 26.5 %reduce-scatter.27.cloned.1.call-done = f32[64,1024]{1,0:T(8,128)} async-done(((f32[256,1024]{1,0:T(8,128)}), f32[64,1024]{1,0:T(8,128)}) %reduce-scatter.27.cloned.1.call-update) | async-done | bytes 262160 | tf_op jit(solution)/shard_map/reduce_scatter | solution.py:202
  906.0 26.4 %reduce-scatter.19.cloned.1.call-done = f32[64,1024]{1,0:T(8,128)} async-done(((f32[256,1024]{1,0:T(8,128)}), f32[64,1024]{1,0:T(8,128)}) %reduce-scatter.19.cloned.1.call-update) | async-done | bytes 262160 | tf_op jit(solution)/shard_map/reduce_scatter | solution.py:202
  (190 shorter events, 132.9 us)
Async XLA Ops:
  6.5 48.9 %copy-start = (bf16[1024,256]{1,0:T(8,128)(2,1)S(1)}, bf16[1024,256]{1,0:T(8,128)(2,1)}, u32[]{:S(2)}) copy-start(bf16[1024,256]{1,0:T(8,128)(2,1)} %param.29) | copy-start | bytes 1572868
  6.5 25.7 %copy-start.9 = (bf16[1024]{0:T(1024)(128)(2,1)S(1)}, bf16[1024]{0:T(1024)(128)(2,1)}, u32[]{:S(2)}) copy-start(bf16[1024]{0:T(1024)(128)(2,1)} %param.27) | copy-start | bytes 6148
  6.5 168.8 %reduce-scatter.15.cloned.1.call-start = ((), (), s32[]{:S(2)}) async-start(), calls=%async_computation.25 | async-start | bytes 294912 | tf_op jit(solution)/shard_map/reduce_scatter | solution.py:152
  55.4 7.5 copy-start.4
  56.5 123.6 %reduce-scatter.23.cloned.1.call-start = ((), (), s32[]{:S(2)}) async-start(), calls=%async_computation.30 | async-start | bytes 294912 | tf_op jit(solution)/shard_map/reduce_scatter | solution.py:152
  57.5 185.0 %reduce-scatter.17.cloned.1.call-start = ((), (), s32[]{:S(2)}) async-start(), calls=%async_computation.26 | async-start | bytes 294912 | tf_op jit(solution)/shard_map/reduce_scatter | solution.py:153
  59.7 246.4 %reduce-scatter.25.cloned.1.call-start = ((), (), s32[]{:S(2)}) async-start(), calls=%async_computation.31 | async-start | bytes 294912 | tf_op jit(solution)/shard_map/reduce_scatter | solution.py:153
  61.8 307.7 %reduce-scatter.31.cloned.1.call-start = ((), (), s32[]{:S(2)}) async-start(), calls=%async_computation.35 | async-start | bytes 294912 | tf_op jit(solution)/shard_map/reduce_scatter | solution.py:152
  62.9 370.1 %reduce-scatter.33.cloned.1.call-start = ((), (), s32[]{:S(2)}) async-start(), calls=%async_computation.36 | async-start | bytes 294912 | tf_op jit(solution)/shard_map/reduce_scatter | solution.py:153
  63.9 439.2 %reduce-scatter.21.cloned.1.call-start = ((), (), s32[]{:S(2)}) async-start(), calls=%async_computation.29 | async-start | bytes 2359296 | tf_op jit(solution)/shard_map/reduce_scatter | solution.py:151
  91.3 16.5 %copy-start.8 = (s32[2]{0:T(128)S(1)}, s32[2]{0:T(128)}, u32[]{:S(2)}) copy-start(s32[2]{0:T(128)} %param.36) | copy-start | bytes 28
  164.3 409.1 %reduce-scatter.29.cloned.1.call-start = ((), (), s32[]{:S(2)}) async-start(), calls=%async_computation.34 | async-start | bytes 2359296 | tf_op jit(solution)/shard_map/reduce_scatter | solution.py:151
  169.7 474.1 %reduce-scatter.13.cloned.1.call-start = ((), (), s32[]{:S(2)}) async-start(), calls=%async_computation.24 | async-start | bytes 2359296 | tf_op jit(solution)/shard_map/reduce_scatter | solution.py:151
  176.8 257.6 %all-to-all-start.1 = ((bf16[4,8,256]{2,1,0:T(8,128)(2,1)}), bf16[4,8,256]{2,1,0:T(8,128)(2,1)S(1)}, u32[]{:S(2)}, u32[]{:S(2)}) async-start(bf16[4,8,256]{2,1,0:T(8,128)(2,1)} %convert_bitcast_fusion.15), calls=%async_computation.3 | async-start | bytes 32768 | tf_op jit(solution)/shard_map/all_to_all | solution.py:159
  434.3 7.1 all-to-all-start.5
  441.4 7.1 all-to-all-start.9
  448.5 7.1 all-to-all-start.2
  455.5 7.1 all-to-all-start.6
  504.8 140.6 %all-to-all-start.4 = ((bf16[4,8,2048]{2,1,0:T(8,128)(2,1)}), bf16[4,8,2048]{2,1,0:T(8,128)(2,1)S(1)}, u32[]{:S(2)}, u32[]{:S(2)}) async-start(bf16[4,8,2048]{2,1,0:T(8,128)(2,1)} %convert_bitcast_fusion.6), calls=%async_computation.9 | async-start | bytes 262144 | tf_op jit(solution)/shard_map/all_to_all | solution.py:156
  645.4 7.9 all-to-all-start.8
  653.3 9.9 %all-to-all-start.10 = ((bf16[4,8,256]{2,1,0:T(8,128)(2,1)}), bf16[4,8,256]{2,1,0:T(8,128)(2,1)S(1)}, u32[]{:S(2)}, u32[]{:S(2)}) async-start(bf16[4,8,256]{2,1,0:T(8,128)(2,1)} %convert_bitcast_fusion.10), calls=%async_computation.21 | async-start | bytes 32768 | tf_op jit(solution)/shard_map/all_to_all | solution.py:162
  663.2 7.9 all-to-all-start
  666.5 94.3 %all-gather.11.cloned.1.call-start = ((), (), s32[]{:S(2)}) async-start(), calls=%async_computation.37 | async-start | bytes 1179648 | tf_op jit(solution)/shard_map/all_gather | solution.py:187
  684.8 79.5 %all-gather.9.cloned.1.call-start = ((), (), s32[]{:S(2)}) async-start(), calls=%async_computation.32 | async-start | bytes 1179648 | tf_op jit(solution)/shard_map/all_gather | solution.py:187
  695.8 109.4 %all-gather.7.cloned.1.call-start = ((), (), s32[]{:S(2)}) async-start(), calls=%async_computation.27 | async-start | bytes 1179648 | tf_op jit(solution)/shard_map/all_gather | solution.py:187
  707.2 170.4 %reduce-scatter.35.cloned.1.call-start = ((), (), s32[]{:S(2)}) async-start(), calls=%async_computation.38 | async-start | bytes 1310720 | tf_op jit(solution)/shard_map/reduce_scatter | solution.py:202
  760.9 88.2 %copy-start.5 = (bf16[256,2048]{1,0:T(8,128)(2,1)S(1)}, bf16[256,2048]{1,0:T(8,128)(2,1)}, u32[]{:S(2)}) copy-start(bf16[256,2048]{1,0:T(8,128)(2,1)} %all-gather.11.cloned.1.call-done) | copy-start | bytes 3145732
  849.1 4.9 copy-start.6
  853.7 51.4 %reduce-scatter.27.cloned.1.call-start = ((), (), s32[]{:S(2)}) async-start(), calls=%async_computation.33 | async-start | bytes 1310720 | tf_op jit(solution)/shard_map/reduce_scatter | solution.py:202
  854.1 5.0 copy-start.7
  858.7 73.7 %reduce-scatter.19.cloned.1.call-start = ((), (), s32[]{:S(2)}) async-start(), calls=%async_computation.28 | async-start | bytes 1310720 | tf_op jit(solution)/shard_map/reduce_scatter | solution.py:202
  859.1 75.0 %copy-start.1 = (bf16[1024,256]{1,0:T(8,128)(2,1)S(1)}, bf16[1024,256]{1,0:T(8,128)(2,1)}, u32[]{:S(2)}) copy-start(bf16[1024,256]{1,0:T(8,128)(2,1)} %param.29) | copy-start | bytes 1572868
  (4 other events, 14.7 us)
Sparse Core Ops, SparseCore 0:
  56.6 58.6 reduce-scatter.14
  118.6 60.2 reduce-scatter.22
  182.2 60.2 reduce-scatter.16
  245.7 60.2 reduce-scatter.24
  309.2 60.2 reduce-scatter.30
  372.7 60.2 reduce-scatter.32
  436.5 66.6 reduce-scatter.20
  506.7 66.6 reduce-scatter.28
  576.9 66.7 reduce-scatter.12
  685.0 38.2 all-gather.10
  725.4 38.8 all-gather.8
  766.3 38.8 all-gather.6
  853.8 23.7 reduce-scatter.34
  880.1 24.8 reduce-scatter.26
  907.4 24.9 reduce-scatter.18
where the time goes:
time: 947 us; the launch traced here: 941 us
  waiting for transfers between devices  552 us (58%)
  blocking collectives  150 us (16%)
  local copies, waits for them, and re-layouts  91.6 us (10%)
  matrix products  81.2 us (9%)
  starting transfers between devices  30.7 us (3%)
  other arithmetic  21.1 us (2%)
  between operations  14.2 us (1%)
    reduce_scatter x3, waiting for transfers between devices, local(): lax.psum_scatter(part_value, 'gx', scatter_dimension=0, tiled=True)  185 us
    reduce_scatter x3, waiting for transfers between devices, local(): lax.psum_scatter(part_query, 'gx', scatter_dimension=0, tiled=True)  175 us
    reduce_scatter x3, waiting for transfers between devices, local(): lax.psum_scatter(partial_out, 'gy', scatter_dimension=0, tiled=True)  66.6 us
    reduce_scatter x3, waiting for transfers between devices, local(): lax.psum_scatter(part_key, 'gx', scatter_dimension=0, tiled=True)  62.1 us
    unnamed x34, local copies, waits for them, and re-layouts  55.7 us
    psum x1, blocking collectives, local(): rank_output = lax.psum(rank_part_out, ('gx', 'gy')).astype(jnp.bfloat16)  41.8 us
    all_gather x3, waiting for transfers between devices, local(): mixed_all = lax.all_gather(head_group, 'gx', axis=0, tiled=True)  40.7 us
    psum x1, blocking collectives, local(): rank_query = lax.psum(rank_part, ('gx', 'gy')).astype(jnp.bfloat16)  40.4 us
  transfers between devices with their start and end apart: 24, of which 18 were waited for; matrix products, arithmetic and copies ran while one was open for 19% of the time, Pallas kernels for 0%

commit v1 on v0

v1 whole, which is shorter than its diff:
```python
import jax
import jax.numpy as jnp
from jax import lax
from jax.sharding import PartitionSpec as P

QUERY_HEADS = 64
KEY_VALUE_HEADS = 8
HEAD_FEATURES = 128
BLOCK = 128


EPS = 1e-05
THETA = 500000.0


def rotary_embedding(values_in, token_positions):
    half_size = values_in.shape[-1] // 2
    exponent = jnp.arange(half_size, dtype=jnp.float32) * 2.0 / values_in.shape[-1]
    frequency = THETA ** (-exponent)
    angles = token_positions.astype(jnp.float32)[:, None] * frequency[None, :]
    cosine = jnp.cos(angles)[:, None, :]
    sine_part = jnp.sin(angles)[:, None, :]
    lower = values_in[..., :half_size]
    upper = values_in[..., half_size:]
    return jnp.concatenate(
        [lower * cosine - upper * sine_part, upper * cosine + lower * sine_part], axis=-1
    )


def pick_adapters(table, adapter_ids, owner_index):
    table_count = table.shape[0]
    picked = []
    for block in range(adapter_ids.shape[0]):
        wanted = adapter_ids[block]
        owned = (wanted // table_count) == owner_index
        entry = lax.dynamic_index_in_dim(table, wanted % table_count, axis=0, keepdims=False)
        picked.append(jnp.where(owned, entry, jnp.zeros_like(entry)))
    return jnp.stack(picked)


def attend(query_rows, previous_keys, previous_values, incoming_keys, incoming_values, lengths):
    steps, count_of_rows = query_rows.shape[0], query_rows.shape[1]
    groups = QUERY_HEADS // KEY_VALUE_HEADS
    context_window = previous_keys.shape[1]
    grouped_heads = query_rows.reshape(
        steps, count_of_rows, KEY_VALUE_HEADS, groups, HEAD_FEATURES
    ).transpose(1, 2, 0, 3, 4).reshape(count_of_rows, KEY_VALUE_HEADS, steps * groups, HEAD_FEATURES)
    keys_previous = previous_keys.reshape(
        count_of_rows, context_window, KEY_VALUE_HEADS, HEAD_FEATURES
    )
    values_previous = previous_values.reshape(
        count_of_rows, context_window, KEY_VALUE_HEADS, HEAD_FEATURES
    )
    keys_incoming = incoming_keys.reshape(
        steps, count_of_rows, KEY_VALUE_HEADS, HEAD_FEATURES
    ).transpose(1, 0, 2, 3)
    values_incoming = incoming_values.reshape(
        steps, count_of_rows, KEY_VALUE_HEADS, HEAD_FEATURES
    ).transpose(1, 0, 2, 3)
    factor = HEAD_FEATURES ** (-0.5)
    score_old = (
        jnp.einsum(
            "rhqd,rchd->rhqc", grouped_heads, keys_previous, preferred_element_type=jnp.float32
        )
        * factor
    )
    score_new = (
        jnp.einsum(
            "rhqd,rshd->rhqs", grouped_heads, keys_incoming, preferred_element_type=jnp.float32
        )
        * factor
    )
    live_old = (jnp.arange(context_window, dtype=jnp.int32)[None, :] < lengths[:, None])[
        :, None, None, :
    ]
    query_step = jnp.arange(steps * groups, dtype=jnp.int32) // groups
    live_new = (jnp.arange(steps, dtype=jnp.int32)[None, :] <= query_step[:, None])[
        None, None, :, :
    ]
    score_old = jnp.where(live_old, score_old, -1e30)
    score_new = jnp.where(live_new, score_new, -1e30)
    peak_score = jnp.maximum(jnp.max(score_old, axis=-1), jnp.max(score_new, axis=-1))
    weight_old = jnp.where(live_old, jnp.exp(score_old - peak_score[..., None]), 0.0)
    weight_new = jnp.where(live_new, jnp.exp(score_new - peak_score[..., None]), 0.0)
    weight_sum = jnp.sum(weight_old, axis=-1) + jnp.sum(weight_new, axis=-1)
    mixed_out = jnp.einsum(
        "rhqc,rchd->rhqd",
        weight_old.astype(jnp.bfloat16),
        values_previous,
        preferred_element_type=jnp.float32,
    )
    mixed_out = mixed_out + jnp.einsum(
        "rhqs,rshd->rhqd",
        weight_new.astype(jnp.bfloat16),
        values_incoming,
        preferred_element_type=jnp.float32,
    )
    mixed_out = (mixed_out / weight_sum[..., None]).astype(jnp.bfloat16)
    return mixed_out.reshape(
        count_of_rows, KEY_VALUE_HEADS, steps, groups, HEAD_FEATURES
    ).transpose(2, 0, 1, 3, 4).reshape(steps, count_of_rows, -1)


def local(
    inputs,
    norm_gain,
    query_weight,
    key_weight,
    value_weight,
    output_weight,
    query_down,
    query_up,
    output_down,
    output_up,
    block_adapter,
    cache_lengths,
    cache_keys,
    cache_values,
):
    across_first = lax.axis_size("gx")
    across_second = lax.axis_size("gy")
    index_first = lax.axis_index("gx")
    index_second = lax.axis_index("gy")
    steps = inputs.shape[0]
    request_count = inputs.shape[1] * across_second
    width = inputs.shape[2] * across_first
    local_rows = cache_keys.shape[0]
    block_count = block_adapter.shape[0]
    block_rows = request_count // block_count
    query_width = query_weight.shape[1]
    key_width = key_weight.shape[1]
    norm_scale = norm_gain.astype(jnp.float32)
    query_first = pick_adapters(query_down, block_adapter, index_second)
    query_second = pick_adapters(query_up, block_adapter, index_first)
    output_first = pick_adapters(output_down, block_adapter, index_first)
    output_second = pick_adapters(output_up, block_adapter, index_second)

    rows_all = lax.all_gather(inputs, "gy", axis=1, tiled=True)
    rows_wide = rows_all.astype(jnp.float32)
    squares = lax.psum(jnp.sum(rows_wide * rows_wide, axis=2), "gx")
    factor_rows = lax.rsqrt(squares / width + EPS)
    normed = (rows_wide * factor_rows[..., None] * norm_scale).astype(jnp.bfloat16)

    blocked = normed.reshape(steps, block_count, block_rows, -1)
    rank_part = jnp.einsum(
        "tbnd,bdr->tbnr", blocked, query_first, preferred_element_type=jnp.float32
    )
    rank_query = lax.psum(rank_part, ("gx", "gy")).astype(jnp.bfloat16)
    delta_query = jnp.einsum(
        "tbnr,bre->tbne", rank_query, query_second, preferred_element_type=jnp.float32
    ).reshape(steps, request_count, -1)
    part_query = (
        jnp.einsum("tnd,de->tne", normed, query_weight, preferred_element_type=jnp.float32)
        + delta_query
    )
    part_key = jnp.einsum("tnd,de->tne", normed, key_weight, preferred_element_type=jnp.float32)
    part_value = jnp.einsum(
        "tnd,de->tne", normed, value_weight, preferred_element_type=jnp.float32
    )
    joined = jnp.concatenate([part_query, part_key, part_value], axis=-1)
    summed = lax.psum_scatter(joined, "gx", scatter_dimension=1, tiled=True).astype(jnp.bfloat16)
    chunk_rows = summed.shape[1] // across_second
    spread = lax.all_to_all(
        summed.reshape(steps, across_second, chunk_rows, -1), "gy", 1, 2, tiled=False
    )
    query_full = spread[..., :query_width].reshape(steps, local_rows, -1)
    key_full = spread[..., query_width : query_width + key_width].reshape(steps, local_rows, -1)
    value_full = spread[..., query_width + key_width :].reshape(steps, local_rows, -1)

    token_positions = (
        cache_lengths[None, :] + jnp.arange(steps, dtype=jnp.int32)[:, None]
    ).reshape(-1)
    query_rot = rotary_embedding(
        query_full.astype(jnp.float32).reshape(steps * local_rows, QUERY_HEADS, HEAD_FEATURES),
        token_positions,
    ).astype(jnp.bfloat16)
    key_rot = rotary_embedding(
        key_full.astype(jnp.float32).reshape(steps * local_rows, KEY_VALUE_HEADS, HEAD_FEATURES),
        token_positions,
    ).astype(jnp.bfloat16)
    mixed_local = attend(
        query_rot.reshape(steps, local_rows, -1),
        cache_keys,
        cache_values,
        key_rot.reshape(steps, local_rows, -1),
        value_full,
        cache_lengths,
    )
    head_group = lax.all_to_all(
        mixed_local.reshape(steps, local_rows, across_second, -1), "gy", 2, 1, tiled=False
    ).reshape(steps, across_second * local_rows, -1)
    mixed_all = lax.all_gather(head_group, "gx", axis=1, tiled=True)
    rank_part_out = jnp.einsum(
        "tbnq,bqr->tbnr",
        mixed_all.reshape(steps, block_count, block_rows, -1),
        output_first,
        preferred_element_type=jnp.float32,
    )
    rank_output = lax.psum(rank_part_out, ("gx", "gy")).astype(jnp.bfloat16)
    delta_output = jnp.einsum(
        "tbnr,bre->tbne", rank_output, output_second, preferred_element_type=jnp.float32
    ).reshape(steps, request_count, -1)
    partial_out = (
        jnp.einsum("tnq,qe->tne", mixed_all, output_weight, preferred_element_type=jnp.float32)
        + delta_output
    )
    return lax.psum_scatter(partial_out, "gy", scatter_dimension=1, tiled=True).astype(
        jnp.bfloat16
    )


def solution(mesh):
    in_specs = (
        P(None, "gy", "gx"),
        P("gx"),
        P("gx", "gy"),
        P("gx", "gy"),
        P("gx", "gy"),
        P("gy", "gx"),
        P("gy", "gx", None),
        P("gx", None, "gy"),
        P("gx", "gy", None),
        P("gy", None, "gx"),
        P(),
        P(("gx", "gy")),
        P(("gx", "gy"), None, None),
        P(("gx", "gy"), None, None),
    )
    out_specs = P(None, "gy", "gx")
    return jax.shard_map(local, mesh=mesh, in_specs=in_specs, out_specs=out_specs, check_vma=False)
```

time: 947 us -> 442 us (0.47)
  waiting for transfers between devices: 552 us -> 256 us
  local copies, waits for them, and re-layouts: 91.6 us -> 9.71 us
  matrix products: 81.2 us -> 23.5 us
  blocking collectives: 150 us -> 113 us
  starting transfers between devices: 30.7 us -> 3.77 us
    reduce_scatter x12 -> x2, waiting for transfers between devices: 489 us -> 176 us  [the longest x1 139 us: local(): lax.psum_scatter(joined, 'gx', scatter_dimension=1, tiled=True)]
    dot_general x40 -> x12, matrix products: 81.2 us -> 23.5 us  [the longest x1 5.09 us: local(): jnp.einsum('tnq,qe->tne', mixed_all, output_weight, preferred_element_typ...]
    unnamed x34 -> x14, local copies, waits for them, and re-layouts: 55.7 us -> 3.97 us
    reshape x4 -> x1, local copies, waits for them, and re-layouts: 33.5 us -> 0.1 us  [attend(): mixed_out.reshape(count_of_rows, KEY_VALUE_HEADS, steps, groups, HEAD_FEA...]
    all_gather x3 -> x2, waiting for transfers between devices: 40.7 us -> 71.4 us  [the longest x1 56.7 us: local(): mixed_all = lax.all_gather(head_group, 'gx', axis=1, tiled=True)]
    all_to_all x9 -> x1, starting transfers between devices: 29.5 us -> 3.47 us  [local(): lax.all_to_all(summed.reshape(steps, across_second, chunk_rows, -1), 'gy'...]
    all_gather x3 -> x0, blocking collectives: 23.2 us -> none  [local(): rows_all = lax.all_gather(own_inputs, 'gy', axis=0, tiled=True)]
    all_to_all x9 -> x1, waiting for transfers between devices: 22.2 us -> 7.99 us  [local(): lax.all_to_all(summed.reshape(steps, across_second, chunk_rows, -1), 'gy'...]
  transfers between devices with their start and end apart: 24 -> 5, of which waited for: 18 -> 5; matrix products, arithmetic and copies ran while one was open for 19% -> 1% of each run, Pallas kernels for 0% -> 0%
where the time goes in v1:
time: 442 us; the launch traced here: 441 us
  waiting for transfers between devices  256 us (58%)
  blocking collectives  113 us (26%)
  matrix products  23.5 us (5%)
  between operations  18.7 us (4%)
  other arithmetic  16.6 us (4%)
  local copies, waits for them, and re-layouts  9.71 us (2%)
    reduce_scatter x1, waiting for transfers between devices, local(): lax.psum_scatter(joined, 'gx', scatter_dimension=1, tiled=True)  139 us
    all_gather x1, waiting for transfers between devices, local(): mixed_all = lax.all_gather(head_group, 'gx', axis=1, tiled=True)  56.7 us
    psum x1, blocking collectives, local(): rank_output = lax.psum(rank_part_out, ('gx', 'gy')).astype(jnp.bfloat16)  42.6 us
    psum x1, blocking collectives, local(): rank_query = lax.psum(rank_part, ('gx', 'gy')).astype(jnp.bfloat16)  39.3 us
    reduce_scatter x1, waiting for transfers between devices, local(): lax.psum_scatter(partial_out, 'gy', scatter_dimension=1, tiled=True)  36.8 us
    psum x1, blocking collectives, local(): squares = lax.psum(jnp.sum(rows_wide * rows_wide, axis=2), 'gx')  21.4 us
    all_gather x1, waiting for transfers between devices, local(): rows_all = lax.all_gather(inputs, 'gy', axis=1, tiled=True)  14.6 us
    all_to_all x1, blocking collectives, local(): lax.all_to_all(mixed_local.reshape(steps, local_rows, across_second, -1),...  9.84 us
  transfers between devices with their start and end apart: 5, of which 5 were waited for; matrix products, arithmetic and copies ran while one was open for 1% of the time, Pallas kernels for 0%

profile of v1, /device:TPU:0, one launch (start us, length us, event | category | flops | bytes accessed | tf_op | source)
XLA Modules:
  0.0 441.3 jit_solution(3828490205044012605)
XLA Ops:
  7.3 1.4 fusion.85
  14.6 1.0 dynamic-slice_select_fusion.7
  15.6 1.1 dynamic-slice_select_fusion.3
  16.7 14.6 %all-gather.3.cloned.1.call-done = bf16[3,256,1024]{2,1,0:T(8,128)(2,1)} async-done(((bf16[3,64,1024]{2,1,0:T(8,128)(2,1)}), bf16[3,256,1024]{2,1,0:T(8,128)(2,1)}) %all-gather.3.cloned.1.call-update) | async-done | bytes 1572880 | tf_op jit(solution)/shard_map/all_gather | solution.py:138
  31.3 1.8 fusion.12
  33.1 21.4 %psum.21 = f32[3,256]{1,0:T(4,128)S(1)} all-reduce(f32[3,256]{1,0:T(4,128)S(1)} %fusion.12), channel_id=1, replica_groups=mesh['gx'=8,'gy'=4] {'gx'}, use_global_device_ids=true, to_apply=%region_1.2 | all-reduce | flops 768 | bytes 6144 | tf_op jit(solution)/shard_map/psum | solution.py:140
  54.5 1.8 fusion.14
  56.9 39.3 %all-reduce.2 = bf16[3,2,128,64]{2,3,0,1:T(8,128)(2,1)S(1)} all-reduce(f32[3,2,128,64]{2,3,0,1:T(8,128)S(1)} %fusion.28), channel_id=1, replica_groups=mesh['gx'=8,'gy'=4] {'gx','gy'}, use_global_device_ids=true, to_apply=%region_2.3 | all-reduce | flops 49152 | bytes 294912 | tf_op jit(solution)/shard_map/psum | solution.py:148
  96.2 1.0 convolution_bitcast_fusion
  97.3 0.8 copy.39
  99.3 1.0 copy-done.4
  100.3 3.5 bitcast_add_fusion
  103.8 3.5 pad_maximum_fusion
  108.1 139.1 %reduce-scatter.3.cloned.1.call-done = f32[3,32,2560]{2,1,0:T(8,128)} async-done(((f32[3,256,2560]{2,1,0:T(8,128)}), f32[3,32,2560]{2,1,0:T(8,128)}) %reduce-scatter.3.cloned.1.call-update) | async-done | bytes 983056 | tf_op jit(solution)/shard_map/reduce_scatter | solution.py:161
  247.1 1.3 convert_bitcast_fusion
  248.4 0.8 copy.44
  249.2 3.5 all-to-all-start
  253.1 8.0 %all-to-all-done = bf16[3,4,8,1,2560]{4,2,0,3,1:T(8,128)(2,1)S(1)} async-done(((bf16[3,4,8,1,2560]{4,2,0,3,1:T(8,128)(2,1)}), bf16[3,4,8,1,2560]{4,2,0,3,1:T(8,128)(2,1)S(1)}, u32[]{:S(2)}, u32[]{:S(2)}) %all-to-all-start) | async-done | bytes 491552 | tf_op jit(solution)/shard_map/all_to_all | solution.py:163
  262.8 4.6 %fusion.86 = (f32[8,8,24]{2,1,0:T(8,128)S(1)}, f32[8,8,24,256]{3,2,1,0:T(8,128)S(1)}) fusion(pred[8,256]{1,0:T(8,128)(4,1)S(1)} %iota_compare_fusion, bf16[8,256,1024]{2,1,0:T(8,128)(2,1)} %param.26, bf16[3,8,8,8,64]{4,3,2,1,0:T(8,128)(2,1)S(1)} %bitcast.137, bf16[3,8,8,8,64]{4,3,2,1,0:T(8,128)(2,1)S(1)} %bitcast.135), kind=kOutput, calls=%fused_computation.111 | convolution fusion | flops 102627840 | bytes 6168576 | tf_op jit(solution)/shard_map/rhqd,rchd->rhqc/dot_general | solution.py:62
  269.1 3.1 fusion.41
  272.6 9.8 %all_to_all.30 = bf16[3,1,8,4,2048]{4,2,0,1,3:T(8,128)(2,1)S(1)} all-to-all(bf16[3,1,8,4,2048]{4,2,0,1,3:T(8,128)(2,1)S(1)} %copy.55), channel_id=1, replica_groups=mesh['gx'=8,'gy'=4] {'gy'}, dimensions={3} | all-to-all | bytes 786432 | tf_op jit(solution)/shard_map/all_to_all | solution.py:189
  282.4 0.8 copy_bitcast_fusion
  283.3 1.0 dynamic-slice_select_fusion.5
  284.3 1.1 dynamic-slice_select_fusion.1
  285.4 56.7 %all-gather.5.cloned.1.call-done = bf16[3,256,2048]{2,1,0:T(8,128)(2,1)} async-done(((bf16[3,32,2048]{2,1,0:T(8,128)(2,1)}), bf16[3,256,2048]{2,1,0:T(8,128)(2,1)}) %all-gather.5.cloned.1.call-update) | async-done | bytes 3145744 | tf_op jit(solution)/shard_map/all_gather | solution.py:192
  342.1 3.0 fusion.31
  345.1 42.6 %all-reduce.3 = bf16[3,2,128,64]{2,3,0,1:T(8,128)(2,1)S(1)} all-reduce(f32[3,2,128,64]{2,3,0,1:T(8,128)S(1)} %fusion.31), channel_id=1, replica_groups=mesh['gx'=8,'gy'=4] {'gx','gy'}, use_global_device_ids=true, to_apply=%region_8.9 | all-reduce | flops 49152 | bytes 294912 | tf_op jit(solution)/shard_map/psum | solution.py:199
  388.7 0.9 copy-done.6
  389.5 1.4 copy-done.5
  390.9 5.1 %bitcast_add_fusion.1 = f32[3,256,1024]{2,1,0:T(8,128)} fusion(f32[3,2,128,1024]{3,2,1,0:T(8,128)S(1)} %copy.58, bf16[3,256,2048]{2,1,0:T(8,128)(2,1)S(1)} %copy-done.6, bf16[2048,1024]{1,0:T(8,128)(2,1)S(1)} %copy-done.5), kind=kOutput, calls=%fused_computation.18 | convolution fusion | flops 3222011904 | bytes 13631488 | tf_op jit(solution)/shard_map/tnq,qe->tne/dot_general | solution.py:204
  396.1 36.8 %reduce-scatter.5.cloned.1.call-done = f32[3,64,1024]{2,1,0:T(8,128)} async-done(((f32[3,256,1024]{2,1,0:T(8,128)}), f32[3,64,1024]{2,1,0:T(8,128)}) %reduce-scatter.5.cloned.1.call-update) | async-done | bytes 786448 | tf_op jit(solution)/shard_map/reduce_scatter | solution.py:207
  432.8 1.9 convert_element_type.74
  (54 shorter events, 9.1 us)
Async XLA Ops:
  6.5 91.5 %copy-start = (bf16[1024,256]{1,0:T(8,128)(2,1)S(1)}, bf16[1024,256]{1,0:T(8,128)(2,1)}, u32[]{:S(2)}) copy-start(bf16[1024,256]{1,0:T(8,128)(2,1)} %param.18) | copy-start | bytes 1572868
  6.5 24.8 %all-gather.3.cloned.1.call-start = ((), (), s32[]{:S(2)}) async-start(), calls=%async_computation.4 | async-start | bytes 1966080 | tf_op jit(solution)/shard_map/all_gather | solution.py:138
  7.3 239.9 %reduce-scatter.3.cloned.1.call-start = ((), (), s32[]{:S(2)}) async-start(), calls=%async_computation.5 | async-start | bytes 8847360 | tf_op jit(solution)/shard_map/reduce_scatter | solution.py:161
  97.3 1.4 copy-start.2
  98.1 2.2 copy-start.4
  107.3 0.7 copy-start.3
  249.2 11.9 %all-to-all-start = ((bf16[3,4,8,1,2560]{4,2,0,3,1:T(8,128)(2,1)}), bf16[3,4,8,1,2560]{4,2,0,3,1:T(8,128)(2,1)S(1)}, u32[]{:S(2)}, u32[]{:S(2)}) async-start(bf16[3,4,8,1,2560]{4,2,0,3,1:T(8,128)(2,1)} %copy.44), calls=%async_computation.1 | async-start | bytes 983040 | tf_op jit(solution)/shard_map/all_to_all | solution.py:163
  252.7 89.4 %all-gather.5.cloned.1.call-start = ((), (), s32[]{:S(2)}) async-start(), calls=%async_computation.6 | async-start | bytes 3538944 | tf_op jit(solution)/shard_map/all_gather | solution.py:192
  283.2 149.6 %reduce-scatter.5.cloned.1.call-start = ((), (), s32[]{:S(2)}) async-start(), calls=%async_computation.7 | async-start | bytes 3932160 | tf_op jit(solution)/shard_map/reduce_scatter | solution.py:207
  387.6 1.9 copy-start.6
  388.3 2.7 copy-start.5
  390.9 43.8 %copy-start.1 = (bf16[1024,256]{1,0:T(8,128)(2,1)S(1)}, bf16[1024,256]{1,0:T(8,128)(2,1)}, u32[]{:S(2)}) copy-start(bf16[1024,256]{1,0:T(8,128)(2,1)} %param.18) | copy-start | bytes 1572868
Sparse Core Ops, SparseCore 0:
  8.9 22.3 all-gather.2
  107.5 139.6 reduce-scatter.2
  283.4 58.6 all-gather.4
  396.2 36.6 reduce-scatter.4

commit v2 on v1

--- a/solution.py
+++ b/solution.py
@@ -36,6 +36,13 @@
         entry = lax.dynamic_index_in_dim(table, wanted % table_count, axis=0, keepdims=False)
         picked.append(jnp.where(owned, entry, jnp.zeros_like(entry)))
     return jnp.stack(picked)
+
+
+def reduce_scatter_rows(partial, axis_name, axis_size):
+    steps, rows, columns = partial.shape
+    pieces = partial.astype(jnp.bfloat16).reshape(steps, axis_size, rows // axis_size, columns)
+    received = lax.all_to_all(pieces, axis_name, 1, 1, tiled=False)
+    return jnp.sum(received.astype(jnp.float32), axis=1)
 
 
 def attend(query_rows, previous_keys, previous_values, incoming_keys, incoming_values, lengths):
@@ -158,7 +165,7 @@
         "tnd,de->tne", normed, value_weight, preferred_element_type=jnp.float32
     )
     joined = jnp.concatenate([part_query, part_key, part_value], axis=-1)
-    summed = lax.psum_scatter(joined, "gx", scatter_dimension=1, tiled=True).astype(jnp.bfloat16)
+    summed = reduce_scatter_rows(joined, "gx", across_first).astype(jnp.bfloat16)
     chunk_rows = summed.shape[1] // across_second
     spread = lax.all_to_all(
         summed.reshape(steps, across_second, chunk_rows, -1), "gy", 1, 2, tiled=False
@@ -204,9 +211,7 @@
         jnp.einsum("tnq,qe->tne", mixed_all, output_weight, preferred_element_type=jnp.float32)
         + delta_output
     )
-    return lax.psum_scatter(partial_out, "gy", scatter_dimension=1, tiled=True).astype(
-        jnp.bfloat16
-    )
+    return reduce_scatter_rows(partial_out, "gy", across_second).astype(jnp.bfloat16)
 
 
 def solution(mesh):

time: 442 us -> 379 us (0.86)
  waiting for transfers between devices: 256 us -> 167 us
  blocking collectives: 113 us -> 136 us
  starting transfers between devices: 3.77 us -> 8.96 us
    reduce_scatter x2 -> x0, waiting for transfers between devices: 176 us -> none  [the longest x1 139 us: local(): lax.psum_scatter(joined, 'gx', scatter_dimension=1, tiled=True)]
    all_to_all x0 -> x1, waiting for transfers between devices: none -> 87 us  [reduce_scatter_rows(): received = lax.all_to_all(pieces, axis_name, 1, 1, tiled=False)]
    all_to_all x0 -> x1, blocking collectives: none -> 22.5 us  [reduce_scatter_rows(): received = lax.all_to_all(pieces, axis_name, 1, 1, tiled=False)]
    all_to_all x0 -> x1, starting transfers between devices: none -> 5.26 us  [reduce_scatter_rows(): received = lax.all_to_all(pieces, axis_name, 1, 1, tiled=False)]
  transfers between devices with their start and end apart: 5 -> 4, of which waited for: 5 -> 4; matrix products, arithmetic and copies ran while one was open for 1% -> 2% of each run, Pallas kernels for 0% -> 0%
where the time goes in v2:
time: 379 us; the launch traced here: 378 us
  waiting for transfers between devices  167 us (44%)
  blocking collectives  136 us (36%)
  matrix products  22.4 us (6%)
  between operations  18.9 us (5%)
  other arithmetic  14.1 us (4%)
  local copies, waits for them, and re-layouts  11.5 us (3%)
  starting transfers between devices  8.96 us (2%)
    all_to_all x1, waiting for transfers between devices, reduce_scatter_rows(): received = lax.all_to_all(pieces, axis_name, 1, 1, tiled=False)  87 us
    all_gather x1, waiting for transfers between devices, local(): mixed_all = lax.all_gather(head_group, 'gx', axis=1, tiled=True)  56.1 us
    psum x1, blocking collectives, local(): rank_output = lax.psum(rank_part_out, ('gx', 'gy')).astype(jnp.bfloat16)  42.6 us
    psum x1, blocking collectives, local(): rank_query = lax.psum(rank_part, ('gx', 'gy')).astype(jnp.bfloat16)  39.3 us
    all_to_all x1, blocking collectives, reduce_scatter_rows(): received = lax.all_to_all(pieces, axis_name, 1, 1, tiled=False)  22.5 us
    psum x1, blocking collectives, local(): squares = lax.psum(jnp.sum(rows_wide * rows_wide, axis=2), 'gx')  21.4 us
    all_gather x1, waiting for transfers between devices, local(): rows_all = lax.all_gather(inputs, 'gy', axis=1, tiled=True)  14.8 us
    all_to_all x1, blocking collectives, local(): lax.all_to_all(mixed_local.reshape(steps, local_rows, across_second, -1),...  9.84 us
  transfers between devices with their start and end apart: 4, of which 4 were waited for; matrix products, arithmetic and copies ran while one was open for 2% of the time, Pallas kernels for 0%

profile of v2, /device:TPU:0, one launch (start us, length us, event | category | flops | bytes accessed | tf_op | source)
XLA Modules:
  0.0 378.2 jit_solution(7142531335100699540)
XLA Ops:
  7.3 1.3 fusion.85
  14.4 1.0 dynamic-slice_select_fusion.7
  15.4 1.1 dynamic-slice_select_fusion.3
  16.5 14.8 %all-gather.3.cloned.1.call-done = bf16[3,256,1024]{2,1,0:T(8,128)(2,1)} async-done(((bf16[3,64,1024]{2,1,0:T(8,128)(2,1)}), bf16[3,256,1024]{2,1,0:T(8,128)(2,1)}) %all-gather.3.cloned.1.call-update) | async-done | bytes 1572880 | tf_op jit(solution)/shard_map/all_gather | solution.py:145
  31.3 1.8 fusion.11
  33.1 21.4 %psum.21 = f32[3,256]{1,0:T(4,128)S(1)} all-reduce(f32[3,256]{1,0:T(4,128)S(1)} %fusion.11), channel_id=1, replica_groups=mesh['gx'=8,'gy'=4] {'gx'}, use_global_device_ids=true, to_apply=%region_1.2 | all-reduce | flops 768 | bytes 6144 | tf_op jit(solution)/shard_map/psum | solution.py:147
  54.5 1.8 fusion.13
  56.9 39.3 %all-reduce.2 = bf16[3,2,128,64]{2,3,0,1:T(8,128)(2,1)S(1)} all-reduce(f32[3,2,128,64]{2,3,0,1:T(8,128)S(1)} %fusion.30), channel_id=1, replica_groups=mesh['gx'=8,'gy'=4] {'gx','gy'}, use_global_device_ids=true, to_apply=%region_2.3 | all-reduce | flops 49152 | bytes 294912 | tf_op jit(solution)/shard_map/psum | solution.py:155
  96.3 1.0 convolution_bitcast_fusion
  97.3 0.8 copy.45
  99.3 1.0 copy-done.3
  100.3 4.1 %fusion = bf16[3,256,2048]{2,1,0:T(8,128)(2,1)S(1)} fusion(f32[3,2,128,2048]{3,2,1,0:T(8,128)S(1)} %copy.45, bf16[3,256,1024]{2,1,0:T(8,128)(2,1)S(1)} %fusion.13, bf16[1024,2048]{1,0:T(8,128)(2,1)S(1)} %copy-done.3), kind=kOutput, calls=%fused_computation.1 | convolution fusion | flops 3224371200 | bytes 15204352 | tf_op jit(solution)/shard_map/tnd,de->tne/dot_general | solution.py:160
  104.8 2.3 copy.69
  107.1 5.3 %all-to-all-start = ((bf16[3,8,32,2560]{3,2,0,1:T(8,128)(2,1)}), bf16[3,8,32,2560]{3,2,0,1:T(8,128)(2,1)}, u32[]{:S(2)}, u32[]{:S(2)}) async-start(bf16[3,8,32,2560]{3,2,0,1:T(8,128)(2,1)} %copy.69), calls=%async_computation | async-start | bytes 7864320 | tf_op jit(solution)/shard_map/all_to_all | solution.py:44
  112.5 87.0 %all-to-all-done = bf16[3,8,32,2560]{3,2,0,1:T(8,128)(2,1)} async-done(((bf16[3,8,32,2560]{3,2,0,1:T(8,128)(2,1)}), bf16[3,8,32,2560]{3,2,0,1:T(8,128)(2,1)}, u32[]{:S(2)}, u32[]{:S(2)}) %all-to-all-start) | async-done | bytes 3932192 | tf_op jit(solution)/shard_map/all_to_all | solution.py:44
  199.4 2.7 reduce_sum.52
  202.2 0.8 copy.49
  203.0 3.5 all-to-all-start.1
  206.9 8.0 %all-to-all-done.1 = bf16[3,4,8,1,2560]{4,2,0,3,1:T(8,128)(2,1)S(1)} async-done(((bf16[3,4,8,1,2560]{4,2,0,3,1:T(8,128)(2,1)}), bf16[3,4,8,1,2560]{4,2,0,3,1:T(8,128)(2,1)S(1)}, u32[]{:S(2)}, u32[]{:S(2)}) %all-to-all-start.1) | async-done | bytes 491552 | tf_op jit(solution)/shard_map/all_to_all | solution.py:170
  216.6 4.6 %fusion.86 = (f32[8,8,24]{2,1,0:T(8,128)S(1)}, f32[8,8,24,256]{3,2,1,0:T(8,128)S(1)}) fusion(pred[8,256]{1,0:T(8,128)(4,1)S(1)} %iota_compare_fusion, bf16[8,256,1024]{2,1,0:T(8,128)(2,1)} %param.26, bf16[3,8,8,8,64]{4,3,2,1,0:T(8,128)(2,1)S(1)} %bitcast.145, bf16[3,8,8,8,64]{4,3,2,1,0:T(8,128)(2,1)S(1)} %bitcast.143), kind=kOutput, calls=%fused_computation.112 | convolution fusion | flops 102627840 | bytes 6168576 | tf_op jit(solution)/shard_map/rhqd,rchd->rhqc/dot_general | solution.py:69
  222.9 3.1 fusion.43
  226.4 9.8 %all_to_all.40 = bf16[3,1,8,4,2048]{4,2,0,1,3:T(8,128)(2,1)S(1)} all-to-all(bf16[3,1,8,4,2048]{4,2,0,1,3:T(8,128)(2,1)S(1)} %copy.60), channel_id=1, replica_groups=mesh['gx'=8,'gy'=4] {'gy'}, dimensions={3} | all-to-all | bytes 786432 | tf_op jit(solution)/shard_map/all_to_all | solution.py:196
  237.0 1.0 dynamic-slice_select_fusion.5
  238.0 1.1 dynamic-slice_select_fusion.1
  239.1 56.1 %all-gather.5.cloned.1.call-done = bf16[3,256,2048]{2,1,0:T(8,128)(2,1)} async-done(((bf16[3,32,2048]{2,1,0:T(8,128)(2,1)}), bf16[3,256,2048]{2,1,0:T(8,128)(2,1)}) %all-gather.5.cloned.1.call-update) | async-done | bytes 3145744 | tf_op jit(solution)/shard_map/all_gather | solution.py:199
  295.2 3.0 fusion.33
  298.2 42.6 %all-reduce.3 = bf16[3,2,128,64]{2,3,0,1:T(8,128)(2,1)S(1)} all-reduce(f32[3,2,128,64]{2,3,0,1:T(8,128)S(1)} %fusion.33), channel_id=1, replica_groups=mesh['gx'=8,'gy'=4] {'gx','gy'}, use_global_device_ids=true, to_apply=%region_8.9 | all-reduce | flops 49152 | bytes 294912 | tf_op jit(solution)/shard_map/psum | solution.py:206
  341.7 1.0 copy-done.5
  342.7 1.4 copy-done.4
  344.1 3.4 fusion.14
  347.7 22.5 %all_to_all.41 = bf16[3,4,64,1024]{3,2,0,1:T(8,128)(2,1)S(1)} all-to-all(bf16[3,4,64,1024]{3,2,0,1:T(8,128)(2,1)S(1)} %copy.64), channel_id=1, replica_groups=mesh['gx'=8,'gy'=4] {'gy'}, dimensions={1} | all-to-all | bytes 3145728 | tf_op jit(solution)/shard_map/all_to_all | solution.py:44
  370.2 1.1 reduce_sum.55
  (53 shorter events, 9.5 us)
Async XLA Ops:
  6.5 91.5 %copy-start = (bf16[1024,256]{1,0:T(8,128)(2,1)S(1)}, bf16[1024,256]{1,0:T(8,128)(2,1)}, u32[]{:S(2)}) copy-start(bf16[1024,256]{1,0:T(8,128)(2,1)} %param.17) | copy-start | bytes 1572868
  6.5 24.8 %all-gather.3.cloned.1.call-start = ((), (), s32[]{:S(2)}) async-start(), calls=%async_computation.4 | async-start | bytes 1966080 | tf_op jit(solution)/shard_map/all_gather | solution.py:145
  97.3 1.4 copy-start.6
  98.1 2.2 copy-start.3
  107.1 5.3 %copy-start.2 = (s32[8]{0:T(128)S(1)}, s32[8]{0:T(128)}, u32[]{:S(2)}) copy-start(s32[8]{0:T(128)} %param.25) | copy-start | bytes 100
  107.1 92.3 %all-to-all-start = ((bf16[3,8,32,2560]{3,2,0,1:T(8,128)(2,1)}), bf16[3,8,32,2560]{3,2,0,1:T(8,128)(2,1)}, u32[]{:S(2)}, u32[]{:S(2)}) async-start(bf16[3,8,32,2560]{3,2,0,1:T(8,128)(2,1)} %copy.69), calls=%async_computation | async-start | bytes 7864320 | tf_op jit(solution)/shard_map/all_to_all | solution.py:44
  203.0 11.9 %all-to-all-start.1 = ((bf16[3,4,8,1,2560]{4,2,0,3,1:T(8,128)(2,1)}), bf16[3,4,8,1,2560]{4,2,0,3,1:T(8,128)(2,1)S(1)}, u32[]{:S(2)}, u32[]{:S(2)}) async-start(bf16[3,4,8,1,2560]{4,2,0,3,1:T(8,128)(2,1)} %copy.49), calls=%async_computation.1 | async-start | bytes 983040 | tf_op jit(solution)/shard_map/all_to_all | solution.py:170
  206.5 88.8 %all-gather.5.cloned.1.call-start = ((), (), s32[]{:S(2)}) async-start(), calls=%async_computation.5 | async-start | bytes 3538944 | tf_op jit(solution)/shard_map/all_gather | solution.py:199
  340.8 1.9 copy-start.5
  341.4 2.7 copy-start.4
  347.5 23.8 %copy-start.1 = (bf16[1024,256]{1,0:T(8,128)(2,1)S(1)}, bf16[1024,256]{1,0:T(8,128)(2,1)}, u32[]{:S(2)}) copy-start(bf16[1024,256]{1,0:T(8,128)(2,1)} %param.17) | copy-start | bytes 1572868
Sparse Core Ops, SparseCore 0:
  8.9 22.3 all-gather.2
  237.2 58.0 all-gather.4

commit v3 on v2

--- a/solution.py
+++ b/solution.py
@@ -43,6 +43,39 @@
     pieces = partial.astype(jnp.bfloat16).reshape(steps, axis_size, rows // axis_size, columns)
     received = lax.all_to_all(pieces, axis_name, 1, 1, tiled=False)
     return jnp.sum(received.astype(jnp.float32), axis=1)
+
+
+def tree_sum(value, axes):
+    for axis_name in axes:
+        size = lax.axis_size(axis_name)
+        if size & (size - 1):
+            value = lax.psum(value, axis_name)
+            continue
+        distance = 1
+        while distance < size:
+            pairs = [(i, i ^ distance) for i in range(size)]
+            value = value + lax.ppermute(value, axis_name, pairs)
+            distance *= 2
+    return value
+
+
+def halving_scatter(partial, axis_name, axis_size):
+    steps, rows, columns = partial.shape
+    if axis_size & (axis_size - 1):
+        return lax.psum_scatter(partial, axis_name, scatter_dimension=1, tiled=True)
+    me = lax.axis_index(axis_name)
+    held = partial.reshape(steps, axis_size, rows // axis_size, columns)
+    distance = 1
+    while distance < axis_size:
+        count = held.shape[1]
+        pairs = held.reshape(steps, count // 2, 2, rows // axis_size, columns)
+        mine = (me // distance) % 2
+        keep = lax.dynamic_index_in_dim(pairs, mine, axis=2, keepdims=False)
+        give = lax.dynamic_index_in_dim(pairs, 1 - mine, axis=2, keepdims=False)
+        swap = [(i, i ^ distance) for i in range(axis_size)]
+        held = keep + lax.ppermute(give, axis_name, swap)
+        distance *= 2
+    return held.reshape(steps, rows // axis_size, columns)
 
 
 def attend(query_rows, previous_keys, previous_values, incoming_keys, incoming_values, lengths):
@@ -144,7 +177,7 @@
 
     rows_all = lax.all_gather(inputs, "gy", axis=1, tiled=True)
     rows_wide = rows_all.astype(jnp.float32)
-    squares = lax.psum(jnp.sum(rows_wide * rows_wide, axis=2), "gx")
+    squares = tree_sum(jnp.sum(rows_wide * rows_wide, axis=2), ("gx",))
     factor_rows = lax.rsqrt(squares / width + EPS)
     normed = (rows_wide * factor_rows[..., None] * norm_scale).astype(jnp.bfloat16)
 
@@ -152,7 +185,7 @@
     rank_part = jnp.einsum(
         "tbnd,bdr->tbnr", blocked, query_first, preferred_element_type=jnp.float32
     )
-    rank_query = lax.psum(rank_part, ("gx", "gy")).astype(jnp.bfloat16)
+    rank_query = tree_sum(rank_part, ("gy", "gx")).astype(jnp.bfloat16)
     delta_query = jnp.einsum(
         "tbnr,bre->tbne", rank_query, query_second, preferred_element_type=jnp.float32
     ).reshape(steps, request_count, -1)
@@ -203,7 +236,7 @@
         output_first,
         preferred_element_type=jnp.float32,
     )
-    rank_output = lax.psum(rank_part_out, ("gx", "gy")).astype(jnp.bfloat16)
+    rank_output = tree_sum(rank_part_out, ("gy", "gx")).astype(jnp.bfloat16)
     delta_output = jnp.einsum(
         "tbnr,bre->tbne", rank_output, output_second, preferred_element_type=jnp.float32
     ).reshape(steps, request_count, -1)
@@ -211,7 +244,7 @@
         jnp.einsum("tnq,qe->tne", mixed_all, output_weight, preferred_element_type=jnp.float32)
         + delta_output
     )
-    return reduce_scatter_rows(partial_out, "gy", across_second).astype(jnp.bfloat16)
+    return halving_scatter(partial_out, "gy", across_second).astype(jnp.bfloat16)
 
 
 def solution(mesh):

time: 379 us -> 355 us (0.937)
  blocking collectives: 136 us -> 9.84 us
  waiting for transfers between devices: 167 us -> 244 us
  starting transfers between devices: 8.96 us -> 27.5 us
  local copies, waits for them, and re-layouts: 11.5 us -> 15.5 us
    psum x3 -> x0, blocking collectives: 103 us -> none  [the longest x1 42.6 us: local(): rank_output = lax.psum(rank_part_out, ('gx', 'gy')).astype(jnp.bfloat16)]
    ppermute x0 -> x15, waiting for transfers between devices: none -> 67 us  [the longest x13 45.2 us: tree_sum(): value = value + lax.ppermute(value, axis_name, pairs)]
    all_to_all x1 -> x0, blocking collectives: 22.5 us -> none  [reduce_scatter_rows(): received = lax.all_to_all(pieces, axis_name, 1, 1, tiled=False)]
    ppermute x0 -> x15, starting transfers between devices: none -> 19.1 us  [the longest x13 17.5 us: tree_sum(): value = value + lax.ppermute(value, axis_name, pairs)]
    all_gather x1, waiting for transfers between devices: 14.8 us -> 24.1 us  [local(): rows_all = lax.all_gather(inputs, 'gy', axis=1, tiled=True)]
  transfers between devices with their start and end apart: 4 -> 19, of which waited for: 4 -> 18; matrix products, arithmetic and copies ran while one was open for 2% -> 3% of each run, Pallas kernels for 0% -> 0%
where the time goes in v3:
time: 355 us
  waiting for transfers between devices  244 us (69%)
  starting transfers between devices  27.5 us (8%)
  matrix products  23.8 us (7%)
  between operations  19.3 us (5%)
  local copies, waits for them, and re-layouts  15.5 us (4%)
  other arithmetic  15 us (4%)
  blocking collectives  9.84 us (3%)
    all_to_all x1, waiting for transfers between devices, reduce_scatter_rows(): received = lax.all_to_all(pieces, axis_name, 1, 1, tiled=False)  86.2 us
    all_gather x1, waiting for transfers between devices, local(): mixed_all = lax.all_gather(head_group, 'gx', axis=1, tiled=True)  57.7 us
    ppermute x13, waiting for transfers between devices, tree_sum(): value = value + lax.ppermute(value, axis_name, pairs)  45.2 us
    all_gather x1, waiting for transfers between devices, local(): rows_all = lax.all_gather(inputs, 'gy', axis=1, tiled=True)  24.1 us
    ppermute x2, waiting for transfers between devices, halving_scatter(): held = keep + lax.ppermute(give, axis_name, swap)  21.8 us
    ppermute x13, starting transfers between devices, tree_sum(): value = value + lax.ppermute(value, axis_name, pairs)  17.5 us
    all_to_all x1, blocking collectives, local(): lax.all_to_all(mixed_local.reshape(steps, local_rows, across_second, -1),...  9.84 us
    all_to_all x1, waiting for transfers between devices, local(): lax.all_to_all(summed.reshape(steps, across_second, chunk_rows, -1), 'gy'...  7.99 us
  transfers between devices with their start and end apart: 19, of which 18 were waited for; matrix products, arithmetic and copies ran while one was open for 3% of the time, Pallas kernels for 0%

profile of v3, /device:TPU:0, one launch (start us, length us, event | category | flops | bytes accessed | tf_op | source)
XLA Modules:
  0.0 354.5 jit_solution(13272453895214916598)
XLA Ops:
  7.3 24.1 %all-gather.3.cloned.1.call-done = bf16[3,256,1024]{2,1,0:T(8,128)(2,1)} async-done(((bf16[3,64,1024]{2,1,0:T(8,128)(2,1)}), bf16[3,256,1024]{2,1,0:T(8,128)(2,1)}) %all-gather.3.cloned.1.call-update) | async-done | bytes 1572880 | tf_op jit(solution)/shard_map/all_gather | solution.py:178
  31.3 1.9 fusion.11
  34.8 2.1 collective-permute-done
  45.2 2.5 collective-permute-start.2
  54.2 6.4 %collective-permute-done.4 = f32[3,2,128,64]{2,3,0,1:T(8,128)S(1)} collective-permute-done((f32[3,2,128,64]{2,3,0,1:T(8,128)S(1)}, f32[3,2,128,64]{2,3,0,1:T(8,128)S(1)}, u32[]{:S(2)}, u32[]{:S(2)}) %collective-permute-start.4) | collective-permute-done | bytes 196640 | tf_op jit(solution)/shard_map/ppermute | solution.py:57
  63.2 3.6 %collective-permute-done.5 = f32[3,2,128,64]{2,3,0,1:T(8,128)S(1)} collective-permute-done((f32[3,2,128,64]{2,3,0,1:T(8,128)S(1)}, f32[3,2,128,64]{2,3,0,1:T(8,128)S(1)}, u32[]{:S(2)}, u32[]{:S(2)}) %collective-permute-start.5) | collective-permute-done | bytes 196640 | tf_op jit(solution)/shard_map/ppermute | solution.py:57
  67.4 2.0 convolution_convert_fusion.1
  69.4 3.2 collective-permute-done.6
  72.6 3.5 collective-permute-start.7
  76.7 5.1 %collective-permute-done.7 = f32[3,2,128,64]{2,3,0,1:T(8,128)S(1)} collective-permute-done((f32[3,2,128,64]{2,3,0,1:T(8,128)S(1)}, f32[3,2,128,64]{2,3,0,1:T(8,128)S(1)}, u32[]{:S(2)}, u32[]{:S(2)}) %collective-permute-start.7) | collective-permute-done | bytes 196640 | tf_op jit(solution)/shard_map/ppermute | solution.py:57
  85.0 4.1 %fusion = bf16[3,256,2048]{2,1,0:T(8,128)(2,1)S(1)} fusion(f32[3,2,128,2048]{3,2,1,0:T(8,128)S(1)} %copy.55, bf16[3,256,1024]{2,1,0:T(8,128)(2,1)S(1)} %copy-done.4, bf16[1024,2048]{1,0:T(8,128)(2,1)S(1)} %copy-done.6), kind=kOutput, calls=%fused_computation.1 | convolution fusion | flops 3224371200 | bytes 15204352 | tf_op jit(solution)/shard_map/tnd,de->tne/dot_general | solution.py:193
  89.5 2.3 copy.80
  91.8 4.7 %all-to-all-start = ((bf16[3,8,32,2560]{3,2,0,1:T(8,128)(2,1)}), bf16[3,8,32,2560]{3,2,0,1:T(8,128)(2,1)}, u32[]{:S(2)}, u32[]{:S(2)}) async-start(bf16[3,8,32,2560]{3,2,0,1:T(8,128)(2,1)} %copy.80), calls=%async_computation | async-start | bytes 7864320 | tf_op jit(solution)/shard_map/all_to_all | solution.py:44
  96.6 86.2 %all-to-all-done = bf16[3,8,32,2560]{3,2,0,1:T(8,128)(2,1)} async-done(((bf16[3,8,32,2560]{3,2,0,1:T(8,128)(2,1)}), bf16[3,8,32,2560]{3,2,0,1:T(8,128)(2,1)}, u32[]{:S(2)}, u32[]{:S(2)}) %all-to-all-start) | async-done | bytes 3932192 | tf_op jit(solution)/shard_map/all_to_all | solution.py:44
  182.8 2.7 reduce_sum.40
  186.4 3.5 all-to-all-start.1
  190.3 8.0 %all-to-all-done.1 = bf16[3,4,8,1,2560]{4,2,0,3,1:T(8,128)(2,1)S(1)} async-done(((bf16[3,4,8,1,2560]{4,2,0,3,1:T(8,128)(2,1)}), bf16[3,4,8,1,2560]{4,2,0,3,1:T(8,128)(2,1)S(1)}, u32[]{:S(2)}, u32[]{:S(2)}) %all-to-all-start.1) | async-done | bytes 491552 | tf_op jit(solution)/shard_map/all_to_all | solution.py:203
  200.0 4.6 %fusion.84 = (f32[8,8,24]{2,1,0:T(8,128)S(1)}, f32[8,8,24,256]{3,2,1,0:T(8,128)S(1)}) fusion(pred[8,256]{1,0:T(8,128)(4,1)S(1)} %iota_compare_fusion, bf16[8,256,1024]{2,1,0:T(8,128)(2,1)} %param.26, bf16[3,8,8,8,64]{4,3,2,1,0:T(8,128)(2,1)S(1)} %bitcast.149, bf16[3,8,8,8,64]{4,3,2,1,0:T(8,128)(2,1)S(1)} %bitcast.147), kind=kOutput, calls=%fused_computation.118 | convolution fusion | flops 102627840 | bytes 6168576 | tf_op jit(solution)/shard_map/rhqd,rchd->rhqc/dot_general | solution.py:102
  206.3 3.1 fusion.42
  209.8 9.8 %all_to_all.35 = bf16[3,1,8,4,2048]{4,2,0,1,3:T(8,128)(2,1)S(1)} all-to-all(bf16[3,1,8,4,2048]{4,2,0,1,3:T(8,128)(2,1)S(1)} %copy.70), channel_id=1, replica_groups=mesh['gx'=8,'gy'=4] {'gy'}, dimensions={3} | all-to-all | bytes 786432 | tf_op jit(solution)/shard_map/all_to_all | solution.py:229
  221.5 57.7 %all-gather.5.cloned.1.call-done = bf16[3,256,2048]{2,1,0:T(8,128)(2,1)} async-done(((bf16[3,32,2048]{2,1,0:T(8,128)(2,1)}), bf16[3,256,2048]{2,1,0:T(8,128)(2,1)}) %all-gather.5.cloned.1.call-update) | async-done | bytes 3145744 | tf_op jit(solution)/shard_map/all_gather | solution.py:232
  279.2 3.0 fusion.32
  283.7 1.5 collective-permute-start.9
  285.3 5.5 %collective-permute-done.9 = f32[3,2,128,64]{2,3,0,1:T(8,128)S(1)} collective-permute-done((f32[3,2,128,64]{2,3,0,1:T(8,128)S(1)}, f32[3,2,128,64]{2,3,0,1:T(8,128)S(1)}, u32[]{:S(2)}, u32[]{:S(2)}) %collective-permute-start.9) | collective-permute-done | bytes 196640 | tf_op jit(solution)/shard_map/ppermute | solution.py:57
  291.4 5.6 %collective-permute-done.10 = f32[3,2,128,64]{2,3,0,1:T(8,128)S(1)} collective-permute-done((f32[3,2,128,64]{2,3,0,1:T(8,128)S(1)}, f32[3,2,128,64]{2,3,0,1:T(8,128)S(1)}, u32[]{:S(2)}, u32[]{:S(2)}) %collective-permute-start.10) | collective-permute-done | bytes 196640 | tf_op jit(solution)/shard_map/ppermute | solution.py:57
  298.5 4.2 %collective-permute-done.11 = f32[3,2,128,64]{2,3,0,1:T(8,128)S(1)} collective-permute-done((f32[3,2,128,64]{2,3,0,1:T(8,128)S(1)}, f32[3,2,128,64]{2,3,0,1:T(8,128)S(1)}, u32[]{:S(2)}, u32[]{:S(2)}) %collective-permute-start.11) | collective-permute-done | bytes 196640 | tf_op jit(solution)/shard_map/ppermute | solution.py:57
  302.7 2.0 collective-permute-start.12
  305.7 6.2 %collective-permute-done.12 = f32[3,2,128,64]{2,3,0,1:T(8,128)S(1)} collective-permute-done((f32[3,2,128,64]{2,3,0,1:T(8,128)S(1)}, f32[3,2,128,64]{2,3,0,1:T(8,128)S(1)}, u32[]{:S(2)}, u32[]{:S(2)}) %collective-permute-start.12) | collective-permute-done | bytes 196640 | tf_op jit(solution)/shard_map/ppermute | solution.py:57
  315.2 3.4 bitcast_add_fusion.1
  320.4 3.5 collective-permute-done.13
  323.9 2.2 bitcast_add_fusion.2
  328.5 18.3 %collective-permute-done.14 = f32[3,1,64,1024]{3,2,0,1:T(8,128)S(1)} collective-permute-done((f32[3,1,64,1024]{3,2,0,1:T(8,128)}, f32[3,1,64,1024]{3,2,0,1:T(8,128)S(1)}, u32[]{:S(2)}, u32[]{:S(2)}) %collective-permute-start.14) | collective-permute-done | bytes 786464 | tf_op jit(solution)/shard_map/ppermute | solution.py:76
  (98 shorter events, 38.8 us)
Async XLA Ops:
  6.5 60.9 %copy-start = (bf16[1024,256]{1,0:T(8,128)(2,1)S(1)}, bf16[1024,256]{1,0:T(8,128)(2,1)}, u32[]{:S(2)}) copy-start(bf16[1024,256]{1,0:T(8,128)(2,1)} %param.17) | copy-start | bytes 1572868
  6.5 24.8 %all-gather.3.cloned.1.call-start = ((), (), s32[]{:S(2)}) async-start(), calls=%async_computation.3 | async-start | bytes 1966080 | tf_op jit(solution)/shard_map/all_gather | solution.py:178
  31.3 18.5 %copy-start.2 = (bf16[3,256,1024]{2,1,0:T(8,128)(2,1)S(1)}, bf16[3,256,1024]{2,1,0:T(8,128)(2,1)}, u32[]{:S(2)}) copy-start(bf16[3,256,1024]{2,1,0:T(8,128)(2,1)} %all-gather.3.cloned.1.call-done) | copy-start | bytes 4718596
  33.2 3.7 %collective-permute-start = (f32[3,256]{1,0:T(4,128)S(1)}, f32[3,256]{1,0:T(4,128)S(1)}, u32[]{:S(2)}, u32[]{:S(2)}) collective-permute-start(f32[3,256]{1,0:T(4,128)S(1)} %fusion.11), channel_id=1, source_target_pairs={{0,4},{4,0},{8,12},{12,8},{16,20},{20,16},{24,28},{28,24},{1,5},{5... | collective-permute-start | bytes 9224 | tf_op jit(solution)/shard_map/ppermute | solution.py:57
  36.9 8.3 %collective-permute-start.1 = (f32[3,256]{1,0:T(4,128)S(1)}, f32[3,256]{1,0:T(4,128)S(1)}, u32[]{:S(2)}, u32[]{:S(2)}) collective-permute-start(f32[3,256]{1,0:T(4,128)S(1)} %add.162), channel_id=1, source_target_pairs={{0,8},{4,12},{8,0},{12,4},{16,24},{20,28},{24,16},{28,20},{1,9},{5... | collective-permute-start | bytes 9224 | tf_op jit(solution)/shard_map/ppermute | solution.py:57
  45.2 4.6 %collective-permute-start.2 = (f32[3,256]{1,0:T(4,128)S(1)}, f32[3,256]{1,0:T(4,128)S(1)}, u32[]{:S(2)}, u32[]{:S(2)}) collective-permute-start(f32[3,256]{1,0:T(4,128)S(1)} %add.163), channel_id=1, source_target_pairs={{0,16},{4,20},{8,24},{12,28},{16,0},{20,4},{24,8},{28,12},{1,17},{... | collective-permute-start | bytes 9224 | tf_op jit(solution)/shard_map/ppermute | solution.py:57
  50.3 1.2 copy-start.3
  52.0 24.1 %copy-start.4 = (bf16[3,256,1024]{2,1,0:T(8,128)(2,1)S(1)}, bf16[3,256,1024]{2,1,0:T(8,128)(2,1)}, u32[]{:S(2)}) copy-start(bf16[3,256,1024]{2,1,0:T(8,128)(2,1)} %copy-done.3) | copy-start | bytes 4718596
  52.1 24.1 %copy-start.9 = (bf16[1024,256]{1,0:T(8,128)(2,1)S(1)}, bf16[1024,256]{1,0:T(8,128)(2,1)}, u32[]{:S(2)}) copy-start(bf16[1024,256]{1,0:T(8,128)(2,1)} %param.18) | copy-start | bytes 1572868
  52.1 1.5 collective-permute-start.3
  53.6 7.0 %collective-permute-start.4 = (f32[3,2,128,64]{2,3,0,1:T(8,128)S(1)}, f32[3,2,128,64]{2,3,0,1:T(8,128)S(1)}, u32[]{:S(2)}, u32[]{:S(2)}) collective-permute-start(f32[3,2,128,64]{2,3,0,1:T(8,128)S(1)} %add.175), channel_id=1, source_target_pairs={{0,2},{1,3},{2,0},{3,1},{4,6},{5,7},{6,4},{7,5},{8,10},{9,11},{10,... | collective-permute-start | bytes 589832 | tf_op jit(solution)/shard_map/ppermute | solution.py:57
  60.6 6.2 %collective-permute-start.5 = (f32[3,2,128,64]{2,3,0,1:T(8,128)S(1)}, f32[3,2,128,64]{2,3,0,1:T(8,128)S(1)}, u32[]{:S(2)}, u32[]{:S(2)}) collective-permute-start(f32[3,2,128,64]{2,3,0,1:T(8,128)S(1)} %add.176), channel_id=1, source_target_pairs={{0,4},{4,0},{8,12},{12,8},{16,20},{20,16},{24,28},{28,24},{1,5},{5... | collective-permute-start | bytes 589832 | tf_op jit(solution)/shard_map/ppermute | solution.py:57
  66.8 5.7 %collective-permute-start.6 = (f32[3,2,128,64]{2,3,0,1:T(8,128)S(1)}, f32[3,2,128,64]{2,3,0,1:T(8,128)S(1)}, u32[]{:S(2)}, u32[]{:S(2)}) collective-permute-start(f32[3,2,128,64]{2,3,0,1:T(8,128)S(1)} %add.177), channel_id=1, source_target_pairs={{0,8},{4,12},{8,0},{12,4},{16,24},{20,28},{24,16},{28,20},{1,9},{5... | collective-permute-start | bytes 589832 | tf_op jit(solution)/shard_map/ppermute | solution.py:57
  72.6 9.2 %collective-permute-start.7 = (f32[3,2,128,64]{2,3,0,1:T(8,128)S(1)}, f32[3,2,128,64]{2,3,0,1:T(8,128)S(1)}, u32[]{:S(2)}, u32[]{:S(2)}) collective-permute-start(f32[3,2,128,64]{2,3,0,1:T(8,128)S(1)} %add.178), channel_id=1, source_target_pairs={{0,16},{4,20},{8,24},{12,28},{16,0},{20,4},{24,8},{28,12},{1,17},{... | collective-permute-start | bytes 589832 | tf_op jit(solution)/shard_map/ppermute | solution.py:57
  82.8 2.2 copy-start.6
  91.8 4.7 %copy-start.5 = (s32[8]{0:T(128)S(1)}, s32[8]{0:T(128)}, u32[]{:S(2)}) copy-start(s32[8]{0:T(128)} %param.25) | copy-start | bytes 100
  91.8 91.0 %all-to-all-start = ((bf16[3,8,32,2560]{3,2,0,1:T(8,128)(2,1)}), bf16[3,8,32,2560]{3,2,0,1:T(8,128)(2,1)}, u32[]{:S(2)}, u32[]{:S(2)}) async-start(bf16[3,8,32,2560]{3,2,0,1:T(8,128)(2,1)} %copy.80), calls=%async_computation | async-start | bytes 7864320 | tf_op jit(solution)/shard_map/all_to_all | solution.py:44
  186.4 11.9 %all-to-all-start.1 = ((bf16[3,4,8,1,2560]{4,2,0,3,1:T(8,128)(2,1)}), bf16[3,4,8,1,2560]{4,2,0,3,1:T(8,128)(2,1)S(1)}, u32[]{:S(2)}, u32[]{:S(2)}) async-start(bf16[3,4,8,1,2560]{4,2,0,3,1:T(8,128)(2,1)} %copy.59), calls=%async_computation.1 | async-start | bytes 983040 | tf_op jit(solution)/shard_map/all_to_all | solution.py:203
  189.8 89.3 %all-gather.5.cloned.1.call-start = ((), (), s32[]{:S(2)}) async-start(), calls=%async_computation.4 | async-start | bytes 3538944 | tf_op jit(solution)/shard_map/all_gather | solution.py:232
  282.2 1.5 collective-permute-start.8
  283.7 7.0 %collective-permute-start.9 = (f32[3,2,128,64]{2,3,0,1:T(8,128)S(1)}, f32[3,2,128,64]{2,3,0,1:T(8,128)S(1)}, u32[]{:S(2)}, u32[]{:S(2)}) collective-permute-start(f32[3,2,128,64]{2,3,0,1:T(8,128)S(1)} %add.188), channel_id=1, source_target_pairs={{0,2},{1,3},{2,0},{3,1},{4,6},{5,7},{6,4},{7,5},{8,10},{9,11},{10,... | collective-permute-start | bytes 589832 | tf_op jit(solution)/shard_map/ppermute | solution.py:57
  290.8 6.2 %collective-permute-start.10 = (f32[3,2,128,64]{2,3,0,1:T(8,128)S(1)}, f32[3,2,128,64]{2,3,0,1:T(8,128)S(1)}, u32[]{:S(2)}, u32[]{:S(2)}) collective-permute-start(f32[3,2,128,64]{2,3,0,1:T(8,128)S(1)} %add.189), channel_id=1, source_target_pairs={{0,4},{4,0},{8,12},{12,8},{16,20},{20,16},{24,28},{28,24},{1,5},{5... | collective-permute-start | bytes 589832 | tf_op jit(solution)/shard_map/ppermute | solution.py:57
  297.0 5.7 %collective-permute-start.11 = (f32[3,2,128,64]{2,3,0,1:T(8,128)S(1)}, f32[3,2,128,64]{2,3,0,1:T(8,128)S(1)}, u32[]{:S(2)}, u32[]{:S(2)}) collective-permute-start(f32[3,2,128,64]{2,3,0,1:T(8,128)S(1)} %add.190), channel_id=1, source_target_pairs={{0,8},{4,12},{8,0},{12,4},{16,24},{20,28},{24,16},{28,20},{1,9},{5... | collective-permute-start | bytes 589832 | tf_op jit(solution)/shard_map/ppermute | solution.py:57
  302.7 9.2 %collective-permute-start.12 = (f32[3,2,128,64]{2,3,0,1:T(8,128)S(1)}, f32[3,2,128,64]{2,3,0,1:T(8,128)S(1)}, u32[]{:S(2)}, u32[]{:S(2)}) collective-permute-start(f32[3,2,128,64]{2,3,0,1:T(8,128)S(1)} %add.191), channel_id=1, source_target_pairs={{0,16},{4,20},{8,24},{12,28},{16,0},{20,4},{24,8},{28,12},{1,17},{... | collective-permute-start | bytes 589832 | tf_op jit(solution)/shard_map/ppermute | solution.py:57
  311.9 1.9 copy-start.8
  312.6 2.7 copy-start.7
  320.3 3.6 %collective-permute-start.13 = (f32[3,2,64,1024]{3,2,0,1:T(8,128)S(1)}, f32[3,2,64,1024]{3,2,0,1:T(8,128)}, u32[]{:S(2)}, u32[]{:S(2)}) collective-permute-start(f32[3,2,64,1024]{3,2,0,1:T(8,128)S(1)} %bitcast.152), channel_id=1, source_target_pairs={{0,1},{1,0},{2,3},{3,2},{4,5},{5,4},{6,7},{7,6},{8,9},{9,8},{10,11... | collective-permute-start | bytes 4718600 | tf_op jit(solution)/shard_map/ppermute | solution.py:76
  323.9 23.8 %copy-start.1 = (bf16[1024,256]{1,0:T(8,128)(2,1)S(1)}, bf16[1024,256]{1,0:T(8,128)(2,1)}, u32[]{:S(2)}) copy-start(bf16[1024,256]{1,0:T(8,128)(2,1)} %param.17) | copy-start | bytes 1572868
  327.1 19.8 %collective-permute-start.14 = (f32[3,1,64,1024]{3,2,0,1:T(8,128)}, f32[3,1,64,1024]{3,2,0,1:T(8,128)S(1)}, u32[]{:S(2)}, u32[]{:S(2)}) collective-permute-start(f32[3,1,64,1024]{3,2,0,1:T(8,128)} %constant_dynamic-slice_fusion), channel_id=1, source_target_pairs={{0,2},{1,3},{2,0},{3,1},{4,6},{5,7},{6,4},{7,5},{8,10},{9,11},{10,... | collective-permute-start | bytes 2359304 | tf_op jit(solution)/shard_map/ppermute | solution.py:76
Sparse Core Ops, SparseCore 0:
  8.9 22.3 all-gather.2
  220.5 58.6 all-gather.4

commit v4 on v3

--- a/solution.py
+++ b/solution.py
@@ -43,6 +43,35 @@
     pieces = partial.astype(jnp.bfloat16).reshape(steps, axis_size, rows // axis_size, columns)
     received = lax.all_to_all(pieces, axis_name, 1, 1, tiled=False)
     return jnp.sum(received.astype(jnp.float32), axis=1)
+
+
+def split_half_scatter(partial, axis_name, axis_size):
+    steps, rows, columns = partial.shape
+    if axis_size < 4 or axis_size & (axis_size - 1):
+        return reduce_scatter_rows(partial, axis_name, axis_size)
+    half = axis_size // 2
+    me = lax.axis_index(axis_name)
+    chunks = partial.reshape(steps, axis_size, rows // axis_size, columns)
+    narrow = chunks.astype(jnp.bfloat16)
+    own = lax.dynamic_index_in_dim(chunks, me, axis=1, keepdims=False)
+    mirror = lax.dynamic_index_in_dim(chunks, me ^ half, axis=1, keepdims=False)
+    for offset in range(1, half):
+        peer = me ^ offset
+        outgoing = jnp.stack(
+            [
+                lax.dynamic_index_in_dim(narrow, peer, axis=1, keepdims=False),
+                lax.dynamic_index_in_dim(narrow, peer ^ half, axis=1, keepdims=False),
+            ]
+        )
+        incoming = lax.ppermute(
+            outgoing, axis_name, [(i, i ^ offset) for i in range(axis_size)]
+        ).astype(jnp.float32)
+        own = own + incoming[0]
+        mirror = mirror + incoming[1]
+    across = lax.ppermute(
+        mirror.astype(jnp.bfloat16), axis_name, [(i, i ^ half) for i in range(axis_size)]
+    )
+    return own + across.astype(jnp.float32)
 
 
 def tree_sum(value, axes):
@@ -73,7 +102,9 @@
         keep = lax.dynamic_index_in_dim(pairs, mine, axis=2, keepdims=False)
         give = lax.dynamic_index_in_dim(pairs, 1 - mine, axis=2, keepdims=False)
         swap = [(i, i ^ distance) for i in range(axis_size)]
-        held = keep + lax.ppermute(give, axis_name, swap)
+        if distance > 1:
+            give = give.astype(jnp.bfloat16)
+        held = keep + lax.ppermute(give, axis_name, swap).astype(jnp.float32)
         distance *= 2
     return held.reshape(steps, rows // axis_size, columns)
 
@@ -198,7 +229,7 @@
         "tnd,de->tne", normed, value_weight, preferred_element_type=jnp.float32
     )
     joined = jnp.concatenate([part_query, part_key, part_value], axis=-1)
-    summed = reduce_scatter_rows(joined, "gx", across_first).astype(jnp.bfloat16)
+    summed = split_half_scatter(joined, "gx", across_first).astype(jnp.bfloat16)
     chunk_rows = summed.shape[1] // across_second
     spread = lax.all_to_all(
         summed.reshape(steps, across_second, chunk_rows, -1), "gy", 1, 2, tiled=False

time: 355 us -> 327 us (0.921)
  waiting for transfers between devices: 244 us -> 210 us
  other arithmetic: 15 us -> 24.7 us
    all_to_all x1 -> x0, waiting for transfers between devices: 86.2 us -> none  [reduce_scatter_rows(): received = lax.all_to_all(pieces, axis_name, 1, 1, tiled=False)]
    ppermute x2 -> x6, waiting for transfers between devices: 21.8 us -> 73.4 us  [the longest x3 38.4 us: split_half_scatter(): lax.ppermute(outgoing, axis_name, [(i, i ^ offset) for i in range(axis_si...]
    convert_element_type x0 -> x5, other arithmetic: none -> 5.79 us  [the longest x3 3.04 us: split_half_scatter(): incoming = lax.ppermute(outgoing, axis_name, [(i, i ^ offset) for i in ra...]
    all_to_all x1 -> x0, starting transfers between devices: 4.7 us -> none  [reduce_scatter_rows(): received = lax.all_to_all(pieces, axis_name, 1, 1, tiled=False)]
    another operation x2 -> x6, other arithmetic: 0.47 us -> 4.79 us  [the longest x3 2.23 us: split_half_scatter(): jnp.stack([lax.dynamic_index_in_dim(narrow, peer, axis=1, keepdims=False)...]
    ppermute x2 -> x6, starting transfers between devices: 1.55 us -> 5.17 us  [the longest x3 3.55 us: split_half_scatter(): lax.ppermute(outgoing, axis_name, [(i, i ^ offset) for i in range(axis_si...]
    unnamed x20 -> x22, local copies, waits for them, and re-layouts: 4.9 us -> 7.37 us
  transfers between devices with their start and end apart: 19 -> 22, of which waited for: 18 -> 21; matrix products, arithmetic and copies ran while one was open for 3% -> 3% of each run, Pallas kernels for 0% -> 0%
where the time goes in v4:
time: 327 us; the launch traced here: 326 us
  waiting for transfers between devices  210 us (64%)
  starting transfers between devices  26.4 us (8%)
  other arithmetic  24.7 us (8%)
  matrix products  21.8 us (7%)
  between operations  19.1 us (6%)
  local copies, waits for them, and re-layouts  14.9 us (5%)
  blocking collectives  9.84 us (3%)
    all_gather x1, waiting for transfers between devices, local(): mixed_all = lax.all_gather(head_group, 'gx', axis=1, tiled=True)  56.8 us
    ppermute x13, waiting for transfers between devices, tree_sum(): value = value + lax.ppermute(value, axis_name, pairs)  46.6 us
    ppermute x3, waiting for transfers between devices, split_half_scatter(): lax.ppermute(outgoing, axis_name, [(i, i ^ offset) for i in range(axis_si...  38.4 us
    all_gather x1, waiting for transfers between devices, local(): rows_all = lax.all_gather(inputs, 'gy', axis=1, tiled=True)  24.1 us
    ppermute x1, waiting for transfers between devices, split_half_scatter(): lax.ppermute(mirror.astype(jnp.bfloat16), axis_name, [(i, i ^ half) for i...  21.6 us
    ppermute x13, starting transfers between devices, tree_sum(): value = value + lax.ppermute(value, axis_name, pairs)  17.5 us
    ppermute x2, waiting for transfers between devices, halving_scatter(): held = keep + lax.ppermute(give, axis_name, swap).astype(jnp.float32)  13.4 us
    all_to_all x1, blocking collectives, local(): lax.all_to_all(mixed_local.reshape(steps, local_rows, across_second, -1),...  9.84 us
  transfers between devices with their start and end apart: 22, of which 21 were waited for; matrix products, arithmetic and copies ran while one was open for 3% of the time, Pallas kernels for 0%

profile of v4, /device:TPU:0, one launch (start us, length us, event | category | flops | bytes accessed | tf_op | source)
XLA Modules:
  0.0 326.3 jit_solution(10089933715577238836)
XLA Ops:
  7.3 24.1 %all-gather.3.cloned.1.call-done = bf16[3,256,1024]{2,1,0:T(8,128)(2,1)} async-done(((bf16[3,64,1024]{2,1,0:T(8,128)(2,1)}), bf16[3,256,1024]{2,1,0:T(8,128)(2,1)}) %all-gather.3.cloned.1.call-update) | async-done | bytes 1572880 | tf_op jit(solution)/shard_map/all_gather | solution.py:209
  34.6 2.1 collective-permute-done
  44.8 2.5 collective-permute-start.2
  54.0 6.4 %collective-permute-done.4 = f32[3,2,128,64]{2,3,0,1:T(8,128)S(1)} collective-permute-done((f32[3,2,128,64]{2,3,0,1:T(8,128)S(1)}, f32[3,2,128,64]{2,3,0,1:T(8,128)S(1)}, u32[]{:S(2)}, u32[]{:S(2)}) %collective-permute-start.4) | collective-permute-done | bytes 196640 | tf_op jit(solution)/shard_map/ppermute | solution.py:86
  63.0 3.6 %collective-permute-done.5 = f32[3,2,128,64]{2,3,0,1:T(8,128)S(1)} collective-permute-done((f32[3,2,128,64]{2,3,0,1:T(8,128)S(1)}, f32[3,2,128,64]{2,3,0,1:T(8,128)S(1)}, u32[]{:S(2)}, u32[]{:S(2)}) %collective-permute-start.5) | collective-permute-done | bytes 196640 | tf_op jit(solution)/shard_map/ppermute | solution.py:86
  67.8 4.6 %collective-permute-done.6 = f32[3,2,128,64]{2,3,0,1:T(8,128)S(1)} collective-permute-done((f32[3,2,128,64]{2,3,0,1:T(8,128)S(1)}, f32[3,2,128,64]{2,3,0,1:T(8,128)S(1)}, u32[]{:S(2)}, u32[]{:S(2)}) %collective-permute-start.6) | collective-permute-done | bytes 196640 | tf_op jit(solution)/shard_map/ppermute | solution.py:86
  72.4 3.5 %collective-permute-start.7 = (f32[3,2,128,64]{2,3,0,1:T(8,128)S(1)}, f32[3,2,128,64]{2,3,0,1:T(8,128)S(1)}, u32[]{:S(2)}, u32[]{:S(2)}) collective-permute-start(f32[3,2,128,64]{2,3,0,1:T(8,128)S(1)} %add.225), channel_id=1, source_target_pairs={{0,16},{4,20},{8,24},{12,28},{16,0},{20,4},{24,8},{28,12},{1,17},{... | collective-permute-start | bytes 589832 | tf_op jit(solution)/shard_map/ppermute | solution.py:86
  76.5 5.1 %collective-permute-done.7 = f32[3,2,128,64]{2,3,0,1:T(8,128)S(1)} collective-permute-done((f32[3,2,128,64]{2,3,0,1:T(8,128)S(1)}, f32[3,2,128,64]{2,3,0,1:T(8,128)S(1)}, u32[]{:S(2)}, u32[]{:S(2)}) %collective-permute-start.7) | collective-permute-done | bytes 196640 | tf_op jit(solution)/shard_map/ppermute | solution.py:86
  84.8 3.5 %bitcast_add_fusion = f32[3,256,2048]{2,1,0:T(8,128)S(1)} fusion(f32[3,2,128,2048]{3,2,1,0:T(8,128)S(1)} %copy.67, bf16[3,256,1024]{2,1,0:T(8,128)(2,1)S(1)} %fusion.14, bf16[1024,2048]{1,0:T(8,128)(2,1)S(1)} %copy-done.8), kind=kOutput, calls=%fused_computation.1 | convolution fusion | flops 3222798336 | bytes 18350080 | tf_op jit(solution)/shard_map/tnd,de->tne/dot_general | solution.py:224
  89.7 2.5 copy-done.2
  96.1 2.0 collective-permute-start.10
  98.1 16.8 %collective-permute-done.8 = bf16[2,3,32,2560]{3,2,1,0:T(8,128)(2,1)S(1)} collective-permute-done((bf16[2,3,32,2560]{3,2,1,0:T(8,128)(2,1)S(1)}, bf16[2,3,32,2560]{3,2,1,0:T(8,128)(2,1)S(1)}, u32[]{:S(2)}, u32[]{:S(2)}) %collective-permute-start.8) | collective-permute-done | bytes 983072 | tf_op jit(solution)/shard_map/ppermute | solution.py:66
  115.2 4.9 %collective-permute-done.9 = bf16[2,3,32,2560]{3,2,1,0:T(8,128)(2,1)} collective-permute-done((bf16[2,3,32,2560]{3,2,1,0:T(8,128)(2,1)}, bf16[2,3,32,2560]{3,2,1,0:T(8,128)(2,1)}, u32[]{:S(2)}, u32[]{:S(2)}) %collective-permute-start.9) | collective-permute-done | bytes 983072 | tf_op jit(solution)/shard_map/ppermute | solution.py:66
  121.5 16.7 %collective-permute-done.10 = bf16[2,3,32,2560]{3,2,1,0:T(8,128)(2,1)} collective-permute-done((bf16[2,3,32,2560]{3,2,1,0:T(8,128)(2,1)}, bf16[2,3,32,2560]{3,2,1,0:T(8,128)(2,1)}, u32[]{:S(2)}, u32[]{:S(2)}) %collective-permute-start.10) | collective-permute-done | bytes 983072 | tf_op jit(solution)/shard_map/ppermute | solution.py:66
  139.6 2.2 fusion.45
  142.0 21.6 %collective-permute-done.11 = bf16[3,32,2560]{2,1,0:T(8,128)(2,1)S(1)} collective-permute-done((bf16[3,32,2560]{2,1,0:T(8,128)(2,1)S(1)}, bf16[3,32,2560]{2,1,0:T(8,128)(2,1)S(1)}, u32[]{:S(2)}, u32[]{:S(2)}) %collective-permute-start.11) | collective-permute-done | bytes 491552 | tf_op jit(solution)/shard_map/ppermute | solution.py:71
  163.6 2.1 fusion.65
  166.5 3.5 %all-to-all-start = ((bf16[3,4,8,1,2560]{4,2,0,3,1:T(8,128)(2,1)}), bf16[3,4,8,1,2560]{4,2,0,3,1:T(8,128)(2,1)S(1)}, u32[]{:S(2)}, u32[]{:S(2)}) async-start(bf16[3,4,8,1,2560]{4,2,0,3,1:T(8,128)(2,1)} %copy.72), calls=%async_computation | async-start | bytes 983040 | tf_op jit(solution)/shard_map/all_to_all | solution.py:234
  170.4 8.0 %all-to-all-done = bf16[3,4,8,1,2560]{4,2,0,3,1:T(8,128)(2,1)S(1)} async-done(((bf16[3,4,8,1,2560]{4,2,0,3,1:T(8,128)(2,1)}), bf16[3,4,8,1,2560]{4,2,0,3,1:T(8,128)(2,1)S(1)}, u32[]{:S(2)}, u32[]{:S(2)}) %all-to-all-start) | async-done | bytes 491552 | tf_op jit(solution)/shard_map/all_to_all | solution.py:234
  180.1 4.6 %fusion.95 = (f32[8,8,24]{2,1,0:T(8,128)S(1)}, f32[8,8,24,256]{3,2,1,0:T(8,128)S(1)}) fusion(pred[8,256]{1,0:T(8,128)(4,1)S(1)} %iota_compare_fusion, bf16[8,256,1024]{2,1,0:T(8,128)(2,1)} %param.26, bf16[3,8,8,8,64]{4,3,2,1,0:T(8,128)(2,1)S(1)} %bitcast.210, bf16[3,8,8,8,64]{4,3,2,1,0:T(8,128)(2,1)S(1)} %bitcast.208), kind=kOutput, calls=%fused_computation.142 | convolution fusion | flops 102627840 | bytes 6168576 | tf_op jit(solution)/shard_map/rhqd,rchd->rhqc/dot_general | solution.py:133
  186.4 3.1 fusion.41
  189.9 9.8 %all_to_all.30 = bf16[3,1,8,4,2048]{4,2,0,1,3:T(8,128)(2,1)S(1)} all-to-all(bf16[3,1,8,4,2048]{4,2,0,1,3:T(8,128)(2,1)S(1)} %copy.83), channel_id=1, replica_groups=mesh['gx'=8,'gy'=4] {'gy'}, dimensions={3} | all-to-all | bytes 786432 | tf_op jit(solution)/shard_map/all_to_all | solution.py:260
  201.6 56.8 %all-gather.5.cloned.1.call-done = bf16[3,256,2048]{2,1,0:T(8,128)(2,1)} async-done(((bf16[3,32,2048]{2,1,0:T(8,128)(2,1)}), bf16[3,256,2048]{2,1,0:T(8,128)(2,1)}) %all-gather.5.cloned.1.call-update) | async-done | bytes 3145744 | tf_op jit(solution)/shard_map/all_gather | solution.py:263
  258.4 3.0 fusion.31
  264.5 5.5 %collective-permute-done.13 = f32[3,2,128,64]{2,3,0,1:T(8,128)S(1)} collective-permute-done((f32[3,2,128,64]{2,3,0,1:T(8,128)S(1)}, f32[3,2,128,64]{2,3,0,1:T(8,128)S(1)}, u32[]{:S(2)}, u32[]{:S(2)}) %collective-permute-start.13) | collective-permute-done | bytes 196640 | tf_op jit(solution)/shard_map/ppermute | solution.py:86
  270.6 5.6 %collective-permute-done.14 = f32[3,2,128,64]{2,3,0,1:T(8,128)S(1)} collective-permute-done((f32[3,2,128,64]{2,3,0,1:T(8,128)S(1)}, f32[3,2,128,64]{2,3,0,1:T(8,128)S(1)}, u32[]{:S(2)}, u32[]{:S(2)}) %collective-permute-start.14) | collective-permute-done | bytes 196640 | tf_op jit(solution)/shard_map/ppermute | solution.py:86
  277.7 4.2 %collective-permute-done.15 = f32[3,2,128,64]{2,3,0,1:T(8,128)S(1)} collective-permute-done((f32[3,2,128,64]{2,3,0,1:T(8,128)S(1)}, f32[3,2,128,64]{2,3,0,1:T(8,128)S(1)}, u32[]{:S(2)}, u32[]{:S(2)}) %collective-permute-start.15) | collective-permute-done | bytes 196640 | tf_op jit(solution)/shard_map/ppermute | solution.py:86
  282.0 2.0 collective-permute-start.16
  285.0 6.2 %collective-permute-done.16 = f32[3,2,128,64]{2,3,0,1:T(8,128)S(1)} collective-permute-done((f32[3,2,128,64]{2,3,0,1:T(8,128)S(1)}, f32[3,2,128,64]{2,3,0,1:T(8,128)S(1)}, u32[]{:S(2)}, u32[]{:S(2)}) %collective-permute-start.16) | collective-permute-done | bytes 196640 | tf_op jit(solution)/shard_map/ppermute | solution.py:86
  294.5 3.4 %bitcast_add_fusion.1 = f32[3,256,1024]{2,1,0:T(8,128)S(1)} fusion(f32[3,2,128,1024]{3,2,1,0:T(8,128)S(1)} %copy.86, bf16[3,256,2048]{2,1,0:T(8,128)(2,1)S(1)} %copy-done.10, bf16[2048,1024]{1,0:T(8,128)(2,1)S(1)} %copy-done.9), kind=kOutput, calls=%fused_computation.18 | convolution fusion | flops 3222011904 | bytes 13631488 | tf_op jit(solution)/shard_map/tnq,qe->tne/dot_general | solution.py:275
  299.5 3.7 %collective-permute-done.17 = f32[3,2,64,1024]{3,2,0,1:T(8,128)} collective-permute-done((f32[3,2,64,1024]{3,2,0,1:T(8,128)}, f32[3,2,64,1024]{3,2,0,1:T(8,128)}, u32[]{:S(2)}, u32[]{:S(2)}) %collective-permute-start.17) | collective-permute-done | bytes 1572896 | tf_op jit(solution)/shard_map/ppermute | solution.py:107
  307.8 9.7 %collective-permute-done.18 = bf16[3,1,64,1024]{3,2,0,1:T(8,128)(2,1)S(1)} collective-permute-done((bf16[3,1,64,1024]{3,2,0,1:T(8,128)(2,1)S(1)}, bf16[3,1,64,1024]{3,2,0,1:T(8,128)(2,1)S(1)}, u32[]{:S(2)}, u32[]{:S(2)}) %collective-permute-start.18) | collective-permute-done | bytes 393248 | tf_op jit(solution)/shard_map/ppermute | solution.py:107
  (114 shorter events, 54.0 us)
Async XLA Ops:
  6.5 60.7 %copy-start = (bf16[1024,256]{1,0:T(8,128)(2,1)S(1)}, bf16[1024,256]{1,0:T(8,128)(2,1)}, u32[]{:S(2)}) copy-start(bf16[1024,256]{1,0:T(8,128)(2,1)} %param.18) | copy-start | bytes 1572868
  6.5 24.8 %all-gather.3.cloned.1.call-start = ((), (), s32[]{:S(2)}) async-start(), calls=%async_computation.2 | async-start | bytes 1966080 | tf_op jit(solution)/shard_map/all_gather | solution.py:209
  33.1 3.7 %collective-permute-start = (f32[3,256]{1,0:T(4,128)S(1)}, f32[3,256]{1,0:T(4,128)S(1)}, u32[]{:S(2)}, u32[]{:S(2)}) collective-permute-start(f32[3,256]{1,0:T(4,128)S(1)} %fusion.12), channel_id=1, source_target_pairs={{0,4},{4,0},{8,12},{12,8},{16,20},{20,16},{24,28},{28,24},{1,5},{5... | collective-permute-start | bytes 9224 | tf_op jit(solution)/shard_map/ppermute | solution.py:86
  36.8 8.0 %collective-permute-start.1 = (f32[3,256]{1,0:T(4,128)S(1)}, f32[3,256]{1,0:T(4,128)S(1)}, u32[]{:S(2)}, u32[]{:S(2)}) collective-permute-start(f32[3,256]{1,0:T(4,128)S(1)} %add.209), channel_id=1, source_target_pairs={{0,8},{4,12},{8,0},{12,4},{16,24},{20,28},{24,16},{28,20},{1,9},{5... | collective-permute-start | bytes 9224 | tf_op jit(solution)/shard_map/ppermute | solution.py:86
  44.8 4.6 %collective-permute-start.2 = (f32[3,256]{1,0:T(4,128)S(1)}, f32[3,256]{1,0:T(4,128)S(1)}, u32[]{:S(2)}, u32[]{:S(2)}) collective-permute-start(f32[3,256]{1,0:T(4,128)S(1)} %add.210), channel_id=1, source_target_pairs={{0,16},{4,20},{8,24},{12,28},{16,0},{20,4},{24,8},{28,12},{1,17},{... | collective-permute-start | bytes 9224 | tf_op jit(solution)/shard_map/ppermute | solution.py:86
  51.8 24.0 %copy-start.6 = (bf16[1024,256]{1,0:T(8,128)(2,1)S(1)}, bf16[1024,256]{1,0:T(8,128)(2,1)}, u32[]{:S(2)}) copy-start(bf16[1024,256]{1,0:T(8,128)(2,1)} %param.17) | copy-start | bytes 1572868
  51.8 1.5 collective-permute-start.3
  53.4 7.0 %collective-permute-start.4 = (f32[3,2,128,64]{2,3,0,1:T(8,128)S(1)}, f32[3,2,128,64]{2,3,0,1:T(8,128)S(1)}, u32[]{:S(2)}, u32[]{:S(2)}) collective-permute-start(f32[3,2,128,64]{2,3,0,1:T(8,128)S(1)} %add.222), channel_id=1, source_target_pairs={{0,2},{1,3},{2,0},{3,1},{4,6},{5,7},{6,4},{7,5},{8,10},{9,11},{10,... | collective-permute-start | bytes 589832 | tf_op jit(solution)/shard_map/ppermute | solution.py:86
  60.4 6.2 %collective-permute-start.5 = (f32[3,2,128,64]{2,3,0,1:T(8,128)S(1)}, f32[3,2,128,64]{2,3,0,1:T(8,128)S(1)}, u32[]{:S(2)}, u32[]{:S(2)}) collective-permute-start(f32[3,2,128,64]{2,3,0,1:T(8,128)S(1)} %add.223), channel_id=1, source_target_pairs={{0,4},{4,0},{8,12},{12,8},{16,20},{20,16},{24,28},{28,24},{1,5},{5... | collective-permute-start | bytes 589832 | tf_op jit(solution)/shard_map/ppermute | solution.py:86
  66.6 5.7 %collective-permute-start.6 = (f32[3,2,128,64]{2,3,0,1:T(8,128)S(1)}, f32[3,2,128,64]{2,3,0,1:T(8,128)S(1)}, u32[]{:S(2)}, u32[]{:S(2)}) collective-permute-start(f32[3,2,128,64]{2,3,0,1:T(8,128)S(1)} %add.224), channel_id=1, source_target_pairs={{0,8},{4,12},{8,0},{12,4},{16,24},{20,28},{24,16},{28,20},{1,9},{5... | collective-permute-start | bytes 589832 | tf_op jit(solution)/shard_map/ppermute | solution.py:86
  72.4 9.2 %collective-permute-start.7 = (f32[3,2,128,64]{2,3,0,1:T(8,128)S(1)}, f32[3,2,128,64]{2,3,0,1:T(8,128)S(1)}, u32[]{:S(2)}, u32[]{:S(2)}) collective-permute-start(f32[3,2,128,64]{2,3,0,1:T(8,128)S(1)} %add.225), channel_id=1, source_target_pairs={{0,16},{4,20},{8,24},{12,28},{16,0},{20,4},{24,8},{28,12},{1,17},{... | collective-permute-start | bytes 589832 | tf_op jit(solution)/shard_map/ppermute | solution.py:86
  82.6 2.2 copy-start.8
  89.1 3.1 copy-start.2
  92.4 22.5 %collective-permute-start.8 = (bf16[2,3,32,2560]{3,2,1,0:T(8,128)(2,1)S(1)}, bf16[2,3,32,2560]{3,2,1,0:T(8,128)(2,1)S(1)}, u32[]{:S(2)}, u32[]{:S(2)}) collective-permute-start(bf16[2,3,32,2560]{3,2,1,0:T(8,128)(2,1)S(1)} %pad_maximum_fusion.1), channel_id=1, source_target_pairs={{0,4},{4,0},{8,12},{12,8},{16,20},{20,16},{24,28},{28,24},{1,5},{5... | collective-permute-start | bytes 2949128 | tf_op jit(solution)/shard_map/ppermute | solution.py:66
  95.1 25.0 %collective-permute-start.9 = (bf16[2,3,32,2560]{3,2,1,0:T(8,128)(2,1)}, bf16[2,3,32,2560]{3,2,1,0:T(8,128)(2,1)}, u32[]{:S(2)}, u32[]{:S(2)}) collective-permute-start(bf16[2,3,32,2560]{3,2,1,0:T(8,128)(2,1)} %pad_maximum_fusion.2), channel_id=1, source_target_pairs={{0,8},{4,12},{8,0},{12,4},{16,24},{20,28},{24,16},{28,20},{1,9},{5... | collective-permute-start | bytes 2949128 | tf_op jit(solution)/shard_map/ppermute | solution.py:66
  96.1 42.1 %collective-permute-start.10 = (bf16[2,3,32,2560]{3,2,1,0:T(8,128)(2,1)}, bf16[2,3,32,2560]{3,2,1,0:T(8,128)(2,1)}, u32[]{:S(2)}, u32[]{:S(2)}) collective-permute-start(bf16[2,3,32,2560]{3,2,1,0:T(8,128)(2,1)} %pad_maximum_fusion.3), channel_id=1, source_target_pairs={{0,12},{4,8},{8,4},{12,0},{16,28},{20,24},{24,20},{28,16},{1,13},{... | collective-permute-start | bytes 2949128 | tf_op jit(solution)/shard_map/ppermute | solution.py:66
  121.5 20.3 %copy-start.3 = (f32[2,3,32,2560]{3,2,1,0:T(8,128)}, f32[2,3,32,2560]{3,2,1,0:T(8,128)S(1)}, u32[]{:S(2)}) copy-start(f32[2,3,32,2560]{3,2,1,0:T(8,128)S(1)} %convert_element_type.94) | copy-start | bytes 5898244
  121.5 20.4 %copy-start.7 = (s32[8]{0:T(128)S(1)}, s32[8]{0:T(128)}, u32[]{:S(2)}) copy-start(s32[8]{0:T(128)} %param.25) | copy-start | bytes 100
  139.6 2.3 copy-start.4
  141.8 21.8 %collective-permute-start.11 = (bf16[3,32,2560]{2,1,0:T(8,128)(2,1)S(1)}, bf16[3,32,2560]{2,1,0:T(8,128)(2,1)S(1)}, u32[]{:S(2)}, u32[]{:S(2)}) collective-permute-start(bf16[3,32,2560]{2,1,0:T(8,128)(2,1)S(1)} %fusion.45), channel_id=1, source_target_pairs={{0,16},{4,20},{8,24},{12,28},{16,0},{20,4},{24,8},{28,12},{1,17},{... | collective-permute-start | bytes 1474568 | tf_op jit(solution)/shard_map/ppermute | solution.py:71
  166.5 11.9 %all-to-all-start = ((bf16[3,4,8,1,2560]{4,2,0,3,1:T(8,128)(2,1)}), bf16[3,4,8,1,2560]{4,2,0,3,1:T(8,128)(2,1)S(1)}, u32[]{:S(2)}, u32[]{:S(2)}) async-start(bf16[3,4,8,1,2560]{4,2,0,3,1:T(8,128)(2,1)} %copy.72), calls=%async_computation | async-start | bytes 983040 | tf_op jit(solution)/shard_map/all_to_all | solution.py:234
  170.0 88.5 %all-gather.5.cloned.1.call-start = ((), (), s32[]{:S(2)}) async-start(), calls=%async_computation.3 | async-start | bytes 3538944 | tf_op jit(solution)/shard_map/all_gather | solution.py:263
  261.4 1.5 collective-permute-start.12
  263.0 7.0 %collective-permute-start.13 = (f32[3,2,128,64]{2,3,0,1:T(8,128)S(1)}, f32[3,2,128,64]{2,3,0,1:T(8,128)S(1)}, u32[]{:S(2)}, u32[]{:S(2)}) collective-permute-start(f32[3,2,128,64]{2,3,0,1:T(8,128)S(1)} %add.250), channel_id=1, source_target_pairs={{0,2},{1,3},{2,0},{3,1},{4,6},{5,7},{6,4},{7,5},{8,10},{9,11},{10,... | collective-permute-start | bytes 589832 | tf_op jit(solution)/shard_map/ppermute | solution.py:86
  270.0 6.2 %collective-permute-start.14 = (f32[3,2,128,64]{2,3,0,1:T(8,128)S(1)}, f32[3,2,128,64]{2,3,0,1:T(8,128)S(1)}, u32[]{:S(2)}, u32[]{:S(2)}) collective-permute-start(f32[3,2,128,64]{2,3,0,1:T(8,128)S(1)} %add.251), channel_id=1, source_target_pairs={{0,4},{4,0},{8,12},{12,8},{16,20},{20,16},{24,28},{28,24},{1,5},{5... | collective-permute-start | bytes 589832 | tf_op jit(solution)/shard_map/ppermute | solution.py:86
  276.2 5.7 %collective-permute-start.15 = (f32[3,2,128,64]{2,3,0,1:T(8,128)S(1)}, f32[3,2,128,64]{2,3,0,1:T(8,128)S(1)}, u32[]{:S(2)}, u32[]{:S(2)}) collective-permute-start(f32[3,2,128,64]{2,3,0,1:T(8,128)S(1)} %add.252), channel_id=1, source_target_pairs={{0,8},{4,12},{8,0},{12,4},{16,24},{20,28},{24,16},{28,20},{1,9},{5... | collective-permute-start | bytes 589832 | tf_op jit(solution)/shard_map/ppermute | solution.py:86
  282.0 9.2 %collective-permute-start.16 = (f32[3,2,128,64]{2,3,0,1:T(8,128)S(1)}, f32[3,2,128,64]{2,3,0,1:T(8,128)S(1)}, u32[]{:S(2)}, u32[]{:S(2)}) collective-permute-start(f32[3,2,128,64]{2,3,0,1:T(8,128)S(1)} %add.253), channel_id=1, source_target_pairs={{0,16},{4,20},{8,24},{12,28},{16,0},{20,4},{24,8},{28,12},{1,17},{... | collective-permute-start | bytes 589832 | tf_op jit(solution)/shard_map/ppermute | solution.py:86
  291.2 1.9 copy-start.10
  291.8 2.7 copy-start.9
  299.5 3.8 %collective-permute-start.17 = (f32[3,2,64,1024]{3,2,0,1:T(8,128)}, f32[3,2,64,1024]{3,2,0,1:T(8,128)}, u32[]{:S(2)}, u32[]{:S(2)}) collective-permute-start(f32[3,2,64,1024]{3,2,0,1:T(8,128)} %bitcast.199), channel_id=1, source_target_pairs={{0,1},{1,0},{2,3},{3,2},{4,5},{5,4},{6,7},{7,6},{8,9},{9,8},{10,11... | collective-permute-start | bytes 4718600 | tf_op jit(solution)/shard_map/ppermute | solution.py:107
  303.3 16.1 %copy-start.1 = (bf16[1024,256]{1,0:T(8,128)(2,1)S(1)}, bf16[1024,256]{1,0:T(8,128)(2,1)}, u32[]{:S(2)}) copy-start(bf16[1024,256]{1,0:T(8,128)(2,1)} %param.18) | copy-start | bytes 1572868
  306.2 11.2 %collective-permute-start.18 = (bf16[3,1,64,1024]{3,2,0,1:T(8,128)(2,1)S(1)}, bf16[3,1,64,1024]{3,2,0,1:T(8,128)(2,1)S(1)}, u32[]{:S(2)}, u32[]{:S(2)}) collective-permute-start(bf16[3,1,64,1024]{3,2,0,1:T(8,128)(2,1)S(1)} %dynamic-slice_convert_fusion), channel_id=1, source_target_pairs={{0,2},{1,3},{2,0},{3,1},{4,6},{5,7},{6,4},{7,5},{8,10},{9,11},{10,... | collective-permute-start | bytes 1179656 | tf_op jit(solution)/shard_map/ppermute | solution.py:107
  (1 other events, 1.2 us)
Sparse Core Ops, SparseCore 0:
  8.9 22.3 all-gather.2
  200.7 57.7 all-gather.4

commit v5 on v4

--- a/solution.py
+++ b/solution.py
@@ -72,6 +72,41 @@
         mirror.astype(jnp.bfloat16), axis_name, [(i, i ^ half) for i in range(axis_size)]
     )
     return own + across.astype(jnp.float32)
+
+
+def doubling_gather(value, axis_name, axis_size, axis):
+    if axis_size & (axis_size - 1):
+        return lax.all_gather(value, axis_name, axis=axis, tiled=True)
+    me = lax.axis_index(axis_name)
+    held = value
+    distance = 1
+    while distance < axis_size:
+        other = lax.ppermute(held, axis_name, [(i, i ^ distance) for i in range(axis_size)])
+        upper = (me // distance) % 2 == 1
+        first = jnp.where(upper, other, held)
+        second = jnp.where(upper, held, other)
+        held = jnp.concatenate([first, second], axis=axis)
+        distance *= 2
+    return held
+
+
+def split_half_gather(value, axis_name, axis_size):
+    if axis_size < 4 or axis_size & (axis_size - 1):
+        return lax.all_gather(value, axis_name, axis=1, tiled=True)
+    half = axis_size // 2
+    me = lax.axis_index(axis_name)
+    mirror = lax.ppermute(value, axis_name, [(i, i ^ half) for i in range(axis_size)])
+    pair = jnp.stack([value, mirror])
+    slots = [None] * axis_size
+    slots[0], slots[half] = value, mirror
+    for offset in range(1, half):
+        incoming = lax.ppermute(pair, axis_name, [(i, i ^ offset) for i in range(axis_size)])
+        slots[offset], slots[offset + half] = incoming[0], incoming[1]
+    stacked = jnp.stack(slots)
+    order = jnp.arange(axis_size, dtype=jnp.int32) ^ me
+    gathered = jnp.take(stacked, order, axis=0)
+    steps, rows, columns = value.shape
+    return gathered.transpose(1, 0, 2, 3).reshape(steps, axis_size * rows, columns)
 
 
 def tree_sum(value, axes):
@@ -206,7 +241,7 @@
     output_first = pick_adapters(output_down, block_adapter, index_first)
     output_second = pick_adapters(output_up, block_adapter, index_second)
 
-    rows_all = lax.all_gather(inputs, "gy", axis=1, tiled=True)
+    rows_all = doubling_gather(inputs, "gy", across_second, 1)
     rows_wide = rows_all.astype(jnp.float32)
     squares = tree_sum(jnp.sum(rows_wide * rows_wide, axis=2), ("gx",))
     factor_rows = lax.rsqrt(squares / width + EPS)
@@ -260,7 +295,7 @@
     head_group = lax.all_to_all(
         mixed_local.reshape(steps, local_rows, across_second, -1), "gy", 2, 1, tiled=False
     ).reshape(steps, across_second * local_rows, -1)
-    mixed_all = lax.all_gather(head_group, "gx", axis=1, tiled=True)
+    mixed_all = split_half_gather(head_group, "gx", across_first)
     rank_part_out = jnp.einsum(
         "tbnq,bqr->tbnr",
         mixed_all.reshape(steps, block_count, block_rows, -1),

time: 327 us -> 319 us (0.976)
  between operations: 19.1 us -> 5.83 us
  waiting for transfers between devices: 210 us -> 198 us
  local copies, waits for them, and re-layouts: 14.9 us -> 24.5 us
  starting transfers between devices: 26.4 us -> 33.3 us
    all_gather x2 -> x0, waiting for transfers between devices: 80.9 us -> none  [the longest x1 56.8 us: local(): mixed_all = lax.all_gather(head_group, 'gx', axis=1, tiled=True)]
    ppermute x0 -> x6, waiting for transfers between devices: none -> 70 us  [the longest x3 30.7 us: split_half_gather(): lax.ppermute(pair, axis_name, [(i, i ^ offset) for i in range(axis_size)])]
    ppermute x0 -> x6, starting transfers between devices: none -> 7.09 us  [the longest x3 3.61 us: split_half_gather(): lax.ppermute(pair, axis_name, [(i, i ^ offset) for i in range(axis_size)])]
    unnamed x22 -> x35, local copies, waits for them, and re-layouts: 7.37 us -> 12.9 us
    select_n x0 -> x4, other arithmetic: none -> 4.85 us  [the longest x2 2.59 us: doubling_gather(): first = jnp.where(upper, other, held)]
    gather x0 -> x1, local copies, waits for them, and re-layouts: none -> 4.33 us  [split_half_gather(): gathered = jnp.take(stacked, order, axis=0)]
    ppermute x1, starting transfers between devices: 0.07 us -> 3.59 us  [split_half_scatter(): lax.ppermute(mirror.astype(jnp.bfloat16), axis_name, [(i, i ^ half) for i...]
  transfers between devices with their start and end apart: 22 -> 26, of which waited for: 21 -> 25; matrix products, arithmetic and copies ran while one was open for 3% -> 4% of each run, Pallas kernels for 0% -> 0%
where the time goes in v5:
time: 319 us; the launch traced here: 318 us
  waiting for transfers between devices  198 us (62%)
  starting transfers between devices  33.3 us (10%)
  other arithmetic  26.2 us (8%)
  local copies, waits for them, and re-layouts  24.5 us (8%)
  matrix products  20.1 us (6%)
  blocking collectives  9.84 us (3%)
  between operations  5.83 us (2%)
    ppermute x13, waiting for transfers between devices, tree_sum(): value = value + lax.ppermute(value, axis_name, pairs)  49.3 us
    ppermute x3, waiting for transfers between devices, split_half_scatter(): lax.ppermute(outgoing, axis_name, [(i, i ^ offset) for i in range(axis_si...  37.1 us
    ppermute x3, waiting for transfers between devices, split_half_gather(): lax.ppermute(pair, axis_name, [(i, i ^ offset) for i in range(axis_size)])  30.7 us
    ppermute x1, waiting for transfers between devices, split_half_gather(): lax.ppermute(value, axis_name, [(i, i ^ half) for i in range(axis_size)])  19.8 us
    ppermute x2, waiting for transfers between devices, doubling_gather(): lax.ppermute(held, axis_name, [(i, i ^ distance) for i in range(axis_size)])  19.5 us
    ppermute x1, waiting for transfers between devices, split_half_scatter(): lax.ppermute(mirror.astype(jnp.bfloat16), axis_name, [(i, i ^ half) for i...  19.2 us
    ppermute x13, starting transfers between devices, tree_sum(): value = value + lax.ppermute(value, axis_name, pairs)  15 us
    ppermute x2, waiting for transfers between devices, halving_scatter(): held = keep + lax.ppermute(give, axis_name, swap).astype(jnp.float32)  14.5 us
  transfers between devices with their start and end apart: 26, of which 25 were waited for; matrix products, arithmetic and copies ran while one was open for 4% of the time, Pallas kernels for 0%

profile of v5, /device:TPU:0, one launch (start us, length us, event | category | flops | bytes accessed | tf_op | source)
XLA Modules:
  0.0 317.9 jit_solution(6474549047284708089)
XLA Ops:
  3.2 3.0 collective-permute-start.1
  6.1 17.9 %collective-permute-done.1 = bf16[3,128,1024]{2,1,0:T(8,128)(2,1)} collective-permute-done((bf16[3,128,1024]{2,1,0:T(8,128)(2,1)S(1)}, bf16[3,128,1024]{2,1,0:T(8,128)(2,1)}, u32[]{:S(2)}, u32[]{:S(2)}) %collective-permute-start.1) | collective-permute-done | bytes 786464 | tf_op jit(solution)/shard_map/ppermute | solution.py:84
  37.3 2.6 collective-permute-start.4
  45.6 5.4 %collective-permute-done.6 = f32[3,2,128,64]{2,3,0,1:T(8,128)S(1)} collective-permute-done((f32[3,2,128,64]{2,3,0,1:T(8,128)S(1)}, f32[3,2,128,64]{2,3,0,1:T(8,128)S(1)}, u32[]{:S(2)}, u32[]{:S(2)}) %collective-permute-start.6) | collective-permute-done | bytes 196640 | tf_op jit(solution)/shard_map/ppermute | solution.py:121
  52.5 4.7 %collective-permute-done.7 = f32[3,2,128,64]{2,3,0,1:T(8,128)S(1)} collective-permute-done((f32[3,2,128,64]{2,3,0,1:T(8,128)S(1)}, f32[3,2,128,64]{2,3,0,1:T(8,128)S(1)}, u32[]{:S(2)}, u32[]{:S(2)}) %collective-permute-start.7) | collective-permute-done | bytes 196640 | tf_op jit(solution)/shard_map/ppermute | solution.py:121
  59.6 3.5 %collective-permute-done.8 = f32[3,2,128,64]{2,3,0,1:T(8,128)S(1)} collective-permute-done((f32[3,2,128,64]{2,3,0,1:T(8,128)S(1)}, f32[3,2,128,64]{2,3,0,1:T(8,128)S(1)}, u32[]{:S(2)}, u32[]{:S(2)}) %collective-permute-start.8) | collective-permute-done | bytes 196640 | tf_op jit(solution)/shard_map/ppermute | solution.py:121
  63.0 2.8 collective-permute-start.9
  66.5 5.8 %collective-permute-done.9 = f32[3,2,128,64]{2,3,0,1:T(8,128)S(1)} collective-permute-done((f32[3,2,128,64]{2,3,0,1:T(8,128)S(1)}, f32[3,2,128,64]{2,3,0,1:T(8,128)S(1)}, u32[]{:S(2)}, u32[]{:S(2)}) %collective-permute-start.9) | collective-permute-done | bytes 196640 | tf_op jit(solution)/shard_map/ppermute | solution.py:121
  75.5 3.5 %bitcast_add_fusion = f32[3,256,2048]{2,1,0:T(8,128)S(1)} fusion(f32[3,2,128,2048]{3,2,1,0:T(8,128)S(1)} %copy.75, bf16[1024,2048]{1,0:T(8,128)(2,1)S(1)} %copy-done.11, f32[1024]{0:T(1024)S(1)} %convert_element_type.98, f32[3,256]{1,0:T(4,128)S(1)} %add_rsqrt_fusion, bf16[3,128,1024]{2,1,0:T(8,128)(2,1)S(1)} %get-tuple-element.22, ...), kind=kOutput, calls=%fused_computation.2 | convolution fusion | flops 3228303360 | bytes 18357248 | tf_op jit(solution)/shard_map/tnd,de->tne/dot_general | solution.py:259
  88.9 15.3 %collective-permute-done.10 = bf16[2,3,32,2560]{3,2,1,0:T(8,128)(2,1)S(1)} collective-permute-done((bf16[2,3,32,2560]{3,2,1,0:T(8,128)(2,1)S(1)}, bf16[2,3,32,2560]{3,2,1,0:T(8,128)(2,1)S(1)}, u32[]{:S(2)}, u32[]{:S(2)}) %collective-permute-start.10) | collective-permute-done | bytes 983072 | tf_op jit(solution)/shard_map/ppermute | solution.py:66
  104.4 5.5 %collective-permute-done.11 = bf16[2,3,32,2560]{3,2,1,0:T(8,128)(2,1)} collective-permute-done((bf16[2,3,32,2560]{3,2,1,0:T(8,128)(2,1)}, bf16[2,3,32,2560]{3,2,1,0:T(8,128)(2,1)}, u32[]{:S(2)}, u32[]{:S(2)}) %collective-permute-start.11) | collective-permute-done | bytes 983072 | tf_op jit(solution)/shard_map/ppermute | solution.py:66
  111.3 16.4 %collective-permute-done.12 = bf16[2,3,32,2560]{3,2,1,0:T(8,128)(2,1)} collective-permute-done((bf16[2,3,32,2560]{3,2,1,0:T(8,128)(2,1)}, bf16[2,3,32,2560]{3,2,1,0:T(8,128)(2,1)}, u32[]{:S(2)}, u32[]{:S(2)}) %collective-permute-start.12) | collective-permute-done | bytes 983072 | tf_op jit(solution)/shard_map/ppermute | solution.py:66
  131.3 3.6 %collective-permute-start.13 = (bf16[3,32,2560]{2,1,0:T(8,128)(2,1)S(1)}, bf16[3,32,2560]{2,1,0:T(8,128)(2,1)S(1)}, u32[]{:S(2)}, u32[]{:S(2)}) collective-permute-start(bf16[3,32,2560]{2,1,0:T(8,128)(2,1)S(1)} %fusion.44), channel_id=1, source_target_pairs={{0,16},{4,20},{8,24},{12,28},{16,0},{20,4},{24,8},{28,12},{1,17},{... | collective-permute-start | bytes 1474568 | tf_op jit(solution)/shard_map/ppermute | solution.py:71
  135.0 19.2 %collective-permute-done.13 = bf16[3,32,2560]{2,1,0:T(8,128)(2,1)S(1)} collective-permute-done((bf16[3,32,2560]{2,1,0:T(8,128)(2,1)S(1)}, bf16[3,32,2560]{2,1,0:T(8,128)(2,1)S(1)}, u32[]{:S(2)}, u32[]{:S(2)}) %collective-permute-start.13) | collective-permute-done | bytes 491552 | tf_op jit(solution)/shard_map/ppermute | solution.py:71
  157.1 3.6 %all-to-all-start = ((bf16[3,4,8,1,2560]{4,2,0,3,1:T(8,128)(2,1)}), bf16[3,4,8,1,2560]{4,2,0,3,1:T(8,128)(2,1)S(1)}, u32[]{:S(2)}, u32[]{:S(2)}) async-start(bf16[3,4,8,1,2560]{4,2,0,3,1:T(8,128)(2,1)} %copy.80), calls=%async_computation | async-start | bytes 983040 | tf_op jit(solution)/shard_map/all_to_all | solution.py:269
  161.0 8.0 %all-to-all-done = bf16[3,4,8,1,2560]{4,2,0,3,1:T(8,128)(2,1)S(1)} async-done(((bf16[3,4,8,1,2560]{4,2,0,3,1:T(8,128)(2,1)}), bf16[3,4,8,1,2560]{4,2,0,3,1:T(8,128)(2,1)S(1)}, u32[]{:S(2)}, u32[]{:S(2)}) %all-to-all-start) | async-done | bytes 491552 | tf_op jit(solution)/shard_map/all_to_all | solution.py:269
  170.8 4.6 %fusion.95 = (f32[8,8,24]{2,1,0:T(8,128)S(1)}, f32[8,8,24,256]{3,2,1,0:T(8,128)S(1)}) fusion(pred[8,256]{1,0:T(8,128)(4,1)S(1)} %iota_compare_fusion, bf16[8,256,1024]{2,1,0:T(8,128)(2,1)} %param.26, bf16[3,8,8,8,64]{4,3,2,1,0:T(8,128)(2,1)S(1)} %bitcast.222, bf16[3,8,8,8,64]{4,3,2,1,0:T(8,128)(2,1)S(1)} %bitcast.220), kind=kOutput, calls=%fused_computation.164 | convolution fusion | flops 102627840 | bytes 6168576 | tf_op jit(solution)/shard_map/rhqd,rchd->rhqc/dot_general | solution.py:168
  177.0 3.1 fusion.40
  180.5 9.8 %all_to_all.30 = bf16[3,1,8,4,2048]{4,2,0,1,3:T(8,128)(2,1)S(1)} all-to-all(bf16[3,1,8,4,2048]{4,2,0,1,3:T(8,128)(2,1)S(1)} %copy.91), channel_id=1, replica_groups=mesh['gx'=8,'gy'=4] {'gy'}, dimensions={3} | all-to-all | bytes 786432 | tf_op jit(solution)/shard_map/all_to_all | solution.py:295
  190.5 19.8 %collective-permute-done.14 = bf16[3,32,2048]{2,1,0:T(8,128)(2,1)S(1)} collective-permute-done((bf16[3,32,2048]{2,1,0:T(8,128)(2,1)S(1)}, bf16[3,32,2048]{2,1,0:T(8,128)(2,1)S(1)}, u32[]{:S(2)}, u32[]{:S(2)}) %collective-permute-start.14) | collective-permute-done | bytes 393248 | tf_op jit(solution)/shard_map/ppermute | solution.py:98
  212.9 2.9 collective-permute-start.17
  215.8 13.1 %collective-permute-done.15 = bf16[2,3,32,2048]{3,2,1,0:T(8,128)(2,1)S(1)} collective-permute-done((bf16[2,3,32,2048]{3,2,1,0:T(8,128)(2,1)S(1)}, bf16[2,3,32,2048]{3,2,1,0:T(8,128)(2,1)S(1)}, u32[]{:S(2)}, u32[]{:S(2)}) %collective-permute-start.15) | collective-permute-done | bytes 786464 | tf_op jit(solution)/shard_map/ppermute | solution.py:103
  229.7 2.9 collective-permute-done.16
  233.4 14.7 %collective-permute-done.17 = bf16[2,3,32,2048]{3,2,1,0:T(8,128)(2,1)S(1)} collective-permute-done((bf16[2,3,32,2048]{3,2,1,0:T(8,128)(2,1)S(1)}, bf16[2,3,32,2048]{3,2,1,0:T(8,128)(2,1)S(1)}, u32[]{:S(2)}, u32[]{:S(2)}) %collective-permute-start.17) | collective-permute-done | bytes 786464 | tf_op jit(solution)/shard_map/ppermute | solution.py:103
  252.0 4.3 %gather_fusion = bf16[8,3,32,2048]{3,2,1,0:T(8,128)(2,1)} fusion(bf16[8,3,32,2048]{3,2,1,0:T(8,128)(2,1)} %slice_dynamic-update-slice_fusion, s32[1024]{0:T(1024)S(1)} %pad_clamp_fusion), kind=kCustom, calls=%fused_computation | custom fusion | bytes 6291488 | tf_op jit(solution)/shard_map/jit(_take)/gather | solution.py:107
  262.1 6.6 %collective-permute-done.19 = f32[3,2,128,64]{2,3,0,1:T(8,128)S(1)} collective-permute-done((f32[3,2,128,64]{2,3,0,1:T(8,128)S(1)}, f32[3,2,128,64]{2,3,0,1:T(8,128)S(1)}, u32[]{:S(2)}, u32[]{:S(2)}) %collective-permute-start.19) | collective-permute-done | bytes 196640 | tf_op jit(solution)/shard_map/ppermute | solution.py:121
  269.3 5.6 %collective-permute-done.20 = f32[3,2,128,64]{2,3,0,1:T(8,128)S(1)} collective-permute-done((f32[3,2,128,64]{2,3,0,1:T(8,128)S(1)}, f32[3,2,128,64]{2,3,0,1:T(8,128)S(1)}, u32[]{:S(2)}, u32[]{:S(2)}) %collective-permute-start.20) | collective-permute-done | bytes 196640 | tf_op jit(solution)/shard_map/ppermute | solution.py:121
  275.3 5.4 %collective-permute-done.21 = f32[3,2,128,64]{2,3,0,1:T(8,128)S(1)} collective-permute-done((f32[3,2,128,64]{2,3,0,1:T(8,128)S(1)}, f32[3,2,128,64]{2,3,0,1:T(8,128)S(1)}, u32[]{:S(2)}, u32[]{:S(2)}) %collective-permute-start.21) | collective-permute-done | bytes 196640 | tf_op jit(solution)/shard_map/ppermute | solution.py:121
  282.7 6.9 %collective-permute-done.22 = f32[3,2,128,64]{2,3,0,1:T(8,128)S(1)} collective-permute-done((f32[3,2,128,64]{2,3,0,1:T(8,128)S(1)}, f32[3,2,128,64]{2,3,0,1:T(8,128)S(1)}, u32[]{:S(2)}, u32[]{:S(2)}) %collective-permute-start.22) | collective-permute-done | bytes 196640 | tf_op jit(solution)/shard_map/ppermute | solution.py:121
  292.9 3.4 %bitcast_add_fusion.1 = f32[3,256,1024]{2,1,0:T(8,128)S(1)} fusion(f32[3,2,128,1024]{3,2,1,0:T(8,128)S(1)} %copy.96, bf16[3,256,2048]{2,1,0:T(8,128)(2,1)S(1)} %bitcast.216, bf16[2048,1024]{1,0:T(8,128)(2,1)S(1)} %copy-done.12), kind=kOutput, calls=%fused_computation.14 | convolution fusion | flops 3222011904 | bytes 13631488 | tf_op jit(solution)/shard_map/tnq,qe->tne/dot_general | solution.py:310
  298.0 3.7 %collective-permute-done.23 = f32[3,2,64,1024]{3,2,0,1:T(8,128)} collective-permute-done((f32[3,2,64,1024]{3,2,0,1:T(8,128)}, f32[3,2,64,1024]{3,2,0,1:T(8,128)}, u32[]{:S(2)}, u32[]{:S(2)}) %collective-permute-start.23) | collective-permute-done | bytes 1572896 | tf_op jit(solution)/shard_map/ppermute | solution.py:142
  305.1 10.8 %collective-permute-done.24 = bf16[3,1,64,1024]{3,2,0,1:T(8,128)(2,1)S(1)} collective-permute-done((bf16[3,1,64,1024]{3,2,0,1:T(8,128)(2,1)S(1)}, bf16[3,1,64,1024]{3,2,0,1:T(8,128)(2,1)S(1)}, u32[]{:S(2)}, u32[]{:S(2)}) %collective-permute-start.24) | collective-permute-done | bytes 393248 | tf_op jit(solution)/shard_map/ppermute | solution.py:142
  (144 shorter events, 73.6 us)
Async XLA Ops:
  0.0 58.9 %copy-start = (bf16[1024,256]{1,0:T(8,128)(2,1)S(1)}, bf16[1024,256]{1,0:T(8,128)(2,1)}, u32[]{:S(2)}) copy-start(bf16[1024,256]{1,0:T(8,128)(2,1)} %param.17) | copy-start | bytes 1572868
  0.0 2.0 collective-permute-start
  3.1 24.7 %copy-start.10 = (s32[2]{0:T(128)S(1)}, s32[2]{0:T(128)}, u32[]{:S(2)}) copy-start(s32[2]{0:T(128)} %param.24) | copy-start | bytes 28
  3.1 33.2 %copy-start.8 = (bf16[1024]{0:T(1024)(128)(2,1)S(1)}, bf16[1024]{0:T(1024)(128)(2,1)}, u32[]{:S(2)}) copy-start(bf16[1024]{0:T(1024)(128)(2,1)} %param.15) | copy-start | bytes 6148
  3.2 20.9 %collective-permute-start.1 = (bf16[3,128,1024]{2,1,0:T(8,128)(2,1)S(1)}, bf16[3,128,1024]{2,1,0:T(8,128)(2,1)}, u32[]{:S(2)}, u32[]{:S(2)}) collective-permute-start(bf16[3,128,1024]{2,1,0:T(8,128)(2,1)S(1)} %pad_maximum_fusion.4), channel_id=1, source_target_pairs={{0,2},{1,3},{2,0},{3,1},{4,6},{5,7},{6,4},{7,5},{8,10},{9,11},{10,... | collective-permute-start | bytes 2359304 | tf_op jit(solution)/shard_map/ppermute | solution.py:84
  26.0 7.6 %collective-permute-start.2 = (f32[3,256]{1,0:T(4,128)S(1)}, f32[3,256]{1,0:T(4,128)S(1)}, u32[]{:S(2)}, u32[]{:S(2)}) collective-permute-start(f32[3,256]{1,0:T(4,128)S(1)} %multiply_reduce_fusion), channel_id=1, source_target_pairs={{0,4},{4,0},{8,12},{12,8},{16,20},{20,16},{24,28},{28,24},{1,5},{5... | collective-permute-start | bytes 9224 | tf_op jit(solution)/shard_map/ppermute | solution.py:121
  33.6 3.7 %collective-permute-start.3 = (f32[3,256]{1,0:T(4,128)S(1)}, f32[3,256]{1,0:T(4,128)S(1)}, u32[]{:S(2)}, u32[]{:S(2)}) collective-permute-start(f32[3,256]{1,0:T(4,128)S(1)} %add.229), channel_id=1, source_target_pairs={{0,8},{4,12},{8,0},{12,4},{16,24},{20,28},{24,16},{28,20},{1,9},{5... | collective-permute-start | bytes 9224 | tf_op jit(solution)/shard_map/ppermute | solution.py:121
  37.3 4.5 %collective-permute-start.4 = (f32[3,256]{1,0:T(4,128)S(1)}, f32[3,256]{1,0:T(4,128)S(1)}, u32[]{:S(2)}, u32[]{:S(2)}) collective-permute-start(f32[3,256]{1,0:T(4,128)S(1)} %add.230), channel_id=1, source_target_pairs={{0,16},{4,20},{8,24},{12,28},{16,0},{20,4},{24,8},{28,12},{1,17},{... | collective-permute-start | bytes 9224 | tf_op jit(solution)/shard_map/ppermute | solution.py:121
  42.5 1.5 collective-permute-start.5
  44.0 7.0 %collective-permute-start.6 = (f32[3,2,128,64]{2,3,0,1:T(8,128)S(1)}, f32[3,2,128,64]{2,3,0,1:T(8,128)S(1)}, u32[]{:S(2)}, u32[]{:S(2)}) collective-permute-start(f32[3,2,128,64]{2,3,0,1:T(8,128)S(1)} %add.242), channel_id=1, source_target_pairs={{0,2},{1,3},{2,0},{3,1},{4,6},{5,7},{6,4},{7,5},{8,10},{9,11},{10,... | collective-permute-start | bytes 589832 | tf_op jit(solution)/shard_map/ppermute | solution.py:121
  51.1 6.2 %collective-permute-start.7 = (f32[3,2,128,64]{2,3,0,1:T(8,128)S(1)}, f32[3,2,128,64]{2,3,0,1:T(8,128)S(1)}, u32[]{:S(2)}, u32[]{:S(2)}) collective-permute-start(f32[3,2,128,64]{2,3,0,1:T(8,128)S(1)} %add.243), channel_id=1, source_target_pairs={{0,4},{4,0},{8,12},{12,8},{16,20},{20,16},{24,28},{28,24},{1,5},{5... | collective-permute-start | bytes 589832 | tf_op jit(solution)/shard_map/ppermute | solution.py:121
  57.3 5.7 %collective-permute-start.8 = (f32[3,2,128,64]{2,3,0,1:T(8,128)S(1)}, f32[3,2,128,64]{2,3,0,1:T(8,128)S(1)}, u32[]{:S(2)}, u32[]{:S(2)}) collective-permute-start(f32[3,2,128,64]{2,3,0,1:T(8,128)S(1)} %add.244), channel_id=1, source_target_pairs={{0,8},{4,12},{8,0},{12,4},{16,24},{20,28},{24,16},{28,20},{1,9},{5... | collective-permute-start | bytes 589832 | tf_op jit(solution)/shard_map/ppermute | solution.py:121
  63.0 9.2 %collective-permute-start.9 = (f32[3,2,128,64]{2,3,0,1:T(8,128)S(1)}, f32[3,2,128,64]{2,3,0,1:T(8,128)S(1)}, u32[]{:S(2)}, u32[]{:S(2)}) collective-permute-start(f32[3,2,128,64]{2,3,0,1:T(8,128)S(1)} %add.245), channel_id=1, source_target_pairs={{0,16},{4,20},{8,24},{12,28},{16,0},{20,4},{24,8},{28,12},{1,17},{... | collective-permute-start | bytes 589832 | tf_op jit(solution)/shard_map/ppermute | solution.py:121
  83.2 21.0 %collective-permute-start.10 = (bf16[2,3,32,2560]{3,2,1,0:T(8,128)(2,1)S(1)}, bf16[2,3,32,2560]{3,2,1,0:T(8,128)(2,1)S(1)}, u32[]{:S(2)}, u32[]{:S(2)}) collective-permute-start(bf16[2,3,32,2560]{3,2,1,0:T(8,128)(2,1)S(1)} %pad_maximum_fusion.1), channel_id=1, source_target_pairs={{0,4},{4,0},{8,12},{12,8},{16,20},{20,16},{24,28},{28,24},{1,5},{5... | collective-permute-start | bytes 2949128 | tf_op jit(solution)/shard_map/ppermute | solution.py:66
  84.9 25.0 %collective-permute-start.11 = (bf16[2,3,32,2560]{3,2,1,0:T(8,128)(2,1)}, bf16[2,3,32,2560]{3,2,1,0:T(8,128)(2,1)}, u32[]{:S(2)}, u32[]{:S(2)}) collective-permute-start(bf16[2,3,32,2560]{3,2,1,0:T(8,128)(2,1)} %pad_maximum_fusion.2), channel_id=1, source_target_pairs={{0,8},{4,12},{8,0},{12,4},{16,24},{20,28},{24,16},{28,20},{1,9},{5... | collective-permute-start | bytes 2949128 | tf_op jit(solution)/shard_map/ppermute | solution.py:66
  86.6 41.1 %collective-permute-start.12 = (bf16[2,3,32,2560]{3,2,1,0:T(8,128)(2,1)}, bf16[2,3,32,2560]{3,2,1,0:T(8,128)(2,1)}, u32[]{:S(2)}, u32[]{:S(2)}) collective-permute-start(bf16[2,3,32,2560]{3,2,1,0:T(8,128)(2,1)} %pad_maximum_fusion.3), channel_id=1, source_target_pairs={{0,12},{4,8},{8,4},{12,0},{16,28},{20,24},{24,20},{28,16},{1,13},{... | collective-permute-start | bytes 2949128 | tf_op jit(solution)/shard_map/ppermute | solution.py:66
  111.3 20.0 %copy-start.3 = (f32[2,3,32,2560]{3,2,1,0:T(8,128)}, f32[2,3,32,2560]{3,2,1,0:T(8,128)S(1)}, u32[]{:S(2)}) copy-start(f32[2,3,32,2560]{3,2,1,0:T(8,128)S(1)} %convert_element_type.106) | copy-start | bytes 5898244
  111.3 23.6 %copy-start.9 = (s32[8]{0:T(128)S(1)}, s32[8]{0:T(128)}, u32[]{:S(2)}) copy-start(s32[8]{0:T(128)} %param.25) | copy-start | bytes 100
  131.3 22.9 %collective-permute-start.13 = (bf16[3,32,2560]{2,1,0:T(8,128)(2,1)S(1)}, bf16[3,32,2560]{2,1,0:T(8,128)(2,1)S(1)}, u32[]{:S(2)}, u32[]{:S(2)}) collective-permute-start(bf16[3,32,2560]{2,1,0:T(8,128)(2,1)S(1)} %fusion.44), channel_id=1, source_target_pairs={{0,16},{4,20},{8,24},{12,28},{16,0},{20,4},{24,8},{28,12},{1,17},{... | collective-permute-start | bytes 1474568 | tf_op jit(solution)/shard_map/ppermute | solution.py:71
  157.1 11.9 %all-to-all-start = ((bf16[3,4,8,1,2560]{4,2,0,3,1:T(8,128)(2,1)}), bf16[3,4,8,1,2560]{4,2,0,3,1:T(8,128)(2,1)S(1)}, u32[]{:S(2)}, u32[]{:S(2)}) async-start(bf16[3,4,8,1,2560]{4,2,0,3,1:T(8,128)(2,1)} %copy.80), calls=%async_computation | async-start | bytes 983040 | tf_op jit(solution)/shard_map/all_to_all | solution.py:269
  190.4 19.9 %collective-permute-start.14 = (bf16[3,32,2048]{2,1,0:T(8,128)(2,1)S(1)}, bf16[3,32,2048]{2,1,0:T(8,128)(2,1)S(1)}, u32[]{:S(2)}, u32[]{:S(2)}) collective-permute-start(bf16[3,32,2048]{2,1,0:T(8,128)(2,1)S(1)} %bitcast.226), channel_id=1, source_target_pairs={{0,16},{4,20},{8,24},{12,28},{16,0},{20,4},{24,8},{28,12},{1,17},{... | collective-permute-start | bytes 1179656 | tf_op jit(solution)/shard_map/ppermute | solution.py:98
  210.4 18.6 %collective-permute-start.15 = (bf16[2,3,32,2048]{3,2,1,0:T(8,128)(2,1)S(1)}, bf16[2,3,32,2048]{3,2,1,0:T(8,128)(2,1)S(1)}, u32[]{:S(2)}, u32[]{:S(2)}) collective-permute-start(bf16[2,3,32,2048]{3,2,1,0:T(8,128)(2,1)S(1)} %pad_maximum_fusion.5), channel_id=1, source_target_pairs={{0,4},{4,0},{8,12},{12,8},{16,20},{20,16},{24,28},{28,24},{1,5},{5... | collective-permute-start | bytes 2359304 | tf_op jit(solution)/shard_map/ppermute | solution.py:103
  212.1 20.5 %collective-permute-start.16 = (bf16[2,3,32,2048]{3,2,1,0:T(8,128)(2,1)S(1)}, bf16[2,3,32,2048]{3,2,1,0:T(8,128)(2,1)S(1)}, u32[]{:S(2)}, u32[]{:S(2)}) collective-permute-start(bf16[2,3,32,2048]{3,2,1,0:T(8,128)(2,1)S(1)} %pad_maximum_fusion.5), channel_id=1, source_target_pairs={{0,8},{4,12},{8,0},{12,4},{16,24},{20,28},{24,16},{28,20},{1,9},{5... | collective-permute-start | bytes 2359304 | tf_op jit(solution)/shard_map/ppermute | solution.py:103
  212.9 35.2 %collective-permute-start.17 = (bf16[2,3,32,2048]{3,2,1,0:T(8,128)(2,1)S(1)}, bf16[2,3,32,2048]{3,2,1,0:T(8,128)(2,1)S(1)}, u32[]{:S(2)}, u32[]{:S(2)}) collective-permute-start(bf16[2,3,32,2048]{3,2,1,0:T(8,128)(2,1)S(1)} %pad_maximum_fusion.5), channel_id=1, source_target_pairs={{0,12},{4,8},{8,4},{12,0},{16,28},{20,24},{24,20},{28,16},{1,13},{... | collective-permute-start | bytes 2359304 | tf_op jit(solution)/shard_map/ppermute | solution.py:103
  260.1 1.5 collective-permute-start.18
  261.6 7.0 %collective-permute-start.19 = (f32[3,2,128,64]{2,3,0,1:T(8,128)S(1)}, f32[3,2,128,64]{2,3,0,1:T(8,128)S(1)}, u32[]{:S(2)}, u32[]{:S(2)}) collective-permute-start(f32[3,2,128,64]{2,3,0,1:T(8,128)S(1)} %add.271), channel_id=1, source_target_pairs={{0,2},{1,3},{2,0},{3,1},{4,6},{5,7},{6,4},{7,5},{8,10},{9,11},{10,... | collective-permute-start | bytes 589832 | tf_op jit(solution)/shard_map/ppermute | solution.py:121
  268.7 6.2 %collective-permute-start.20 = (f32[3,2,128,64]{2,3,0,1:T(8,128)S(1)}, f32[3,2,128,64]{2,3,0,1:T(8,128)S(1)}, u32[]{:S(2)}, u32[]{:S(2)}) collective-permute-start(f32[3,2,128,64]{2,3,0,1:T(8,128)S(1)} %add.272), channel_id=1, source_target_pairs={{0,4},{4,0},{8,12},{12,8},{16,20},{20,16},{24,28},{28,24},{1,5},{5... | collective-permute-start | bytes 589832 | tf_op jit(solution)/shard_map/ppermute | solution.py:121
  274.9 5.7 %collective-permute-start.21 = (f32[3,2,128,64]{2,3,0,1:T(8,128)S(1)}, f32[3,2,128,64]{2,3,0,1:T(8,128)S(1)}, u32[]{:S(2)}, u32[]{:S(2)}) collective-permute-start(f32[3,2,128,64]{2,3,0,1:T(8,128)S(1)} %add.273), channel_id=1, source_target_pairs={{0,8},{4,12},{8,0},{12,4},{16,24},{20,28},{24,16},{28,20},{1,9},{5... | collective-permute-start | bytes 589832 | tf_op jit(solution)/shard_map/ppermute | solution.py:121
  280.7 8.9 %collective-permute-start.22 = (f32[3,2,128,64]{2,3,0,1:T(8,128)S(1)}, f32[3,2,128,64]{2,3,0,1:T(8,128)S(1)}, u32[]{:S(2)}, u32[]{:S(2)}) collective-permute-start(f32[3,2,128,64]{2,3,0,1:T(8,128)S(1)} %add.274), channel_id=1, source_target_pairs={{0,16},{4,20},{8,24},{12,28},{16,0},{20,4},{24,8},{28,12},{1,17},{... | collective-permute-start | bytes 589832 | tf_op jit(solution)/shard_map/ppermute | solution.py:121
  298.0 3.8 %collective-permute-start.23 = (f32[3,2,64,1024]{3,2,0,1:T(8,128)}, f32[3,2,64,1024]{3,2,0,1:T(8,128)}, u32[]{:S(2)}, u32[]{:S(2)}) collective-permute-start(f32[3,2,64,1024]{3,2,0,1:T(8,128)} %bitcast.208), channel_id=1, source_target_pairs={{0,1},{1,0},{2,3},{3,2},{4,5},{5,4},{6,7},{7,6},{8,9},{9,8},{10,11... | collective-permute-start | bytes 4718600 | tf_op jit(solution)/shard_map/ppermute | solution.py:142
  301.7 16.2 %copy-start.1 = (bf16[1024,256]{1,0:T(8,128)(2,1)S(1)}, bf16[1024,256]{1,0:T(8,128)(2,1)}, u32[]{:S(2)}) copy-start(bf16[1024,256]{1,0:T(8,128)(2,1)} %param.17) | copy-start | bytes 1572868
  304.7 11.2 %collective-permute-start.24 = (bf16[3,1,64,1024]{3,2,0,1:T(8,128)(2,1)S(1)}, bf16[3,1,64,1024]{3,2,0,1:T(8,128)(2,1)S(1)}, u32[]{:S(2)}, u32[]{:S(2)}) collective-permute-start(bf16[3,1,64,1024]{3,2,0,1:T(8,128)(2,1)S(1)} %dynamic-slice_convert_fusion), channel_id=1, source_target_pairs={{0,2},{1,3},{2,0},{3,1},{4,6},{5,7},{6,4},{7,5},{8,10},{9,11},{10,... | collective-permute-start | bytes 1179656 | tf_op jit(solution)/shard_map/ppermute | solution.py:142
  (8 other events, 41.6 us)

commit v6 on v5

--- a/solution.py
+++ b/solution.py
@@ -43,6 +43,24 @@
     pieces = partial.astype(jnp.bfloat16).reshape(steps, axis_size, rows // axis_size, columns)
     received = lax.all_to_all(pieces, axis_name, 1, 1, tiled=False)
     return jnp.sum(received.astype(jnp.float32), axis=1)
+
+
+def split_half_scatter_steps(partial, axis_name, axis_size):
+    return jnp.concatenate(
+        [
+            split_half_scatter(partial[step : step + 1], axis_name, axis_size)
+            for step in range(partial.shape[0])
+        ]
+    )
+
+
+def split_half_gather_steps(value, axis_name, axis_size):
+    return jnp.concatenate(
+        [
+            split_half_gather(value[step : step + 1], axis_name, axis_size)
+            for step in range(value.shape[0])
+        ]
+    )
 
 
 def split_half_scatter(partial, axis_name, axis_size):
@@ -264,7 +282,7 @@
         "tnd,de->tne", normed, value_weight, preferred_element_type=jnp.float32
     )
     joined = jnp.concatenate([part_query, part_key, part_value], axis=-1)
-    summed = split_half_scatter(joined, "gx", across_first).astype(jnp.bfloat16)
+    summed = split_half_scatter_steps(joined, "gx", across_first).astype(jnp.bfloat16)
     chunk_rows = summed.shape[1] // across_second
     spread = lax.all_to_all(
         summed.reshape(steps, across_second, chunk_rows, -1), "gy", 1, 2, tiled=False
@@ -295,7 +313,7 @@
     head_group = lax.all_to_all(
         mixed_local.reshape(steps, local_rows, across_second, -1), "gy", 2, 1, tiled=False
     ).reshape(steps, across_second * local_rows, -1)
-    mixed_all = split_half_gather(head_group, "gx", across_first)
+    mixed_all = split_half_gather_steps(head_group, "gx", across_first)
     rank_part_out = jnp.einsum(
         "tbnq,bqr->tbnr",
         mixed_all.reshape(steps, block_count, block_rows, -1),

time: 319 us -> 296 us (0.928)
  waiting for transfers between devices: 198 us -> 160 us
  starting transfers between devices: 33.3 us -> 57.4 us
  blocking collectives: 9.84 us -> 0 us
  local copies, waits for them, and re-layouts: 24.5 us -> 32.3 us
  other arithmetic: 26.2 us -> 19.2 us
    ppermute x1 -> x3, waiting for transfers between devices: 19.2 us -> 6.84 us  [split_half_scatter(): lax.ppermute(mirror.astype(jnp.bfloat16), axis_name, [(i, i ^ half) for i...]
    ppermute x3 -> x9, waiting for transfers between devices: 30.7 us -> 20 us  [split_half_gather(): lax.ppermute(pair, axis_name, [(i, i ^ offset) for i in range(axis_size)])]
    all_to_all x1 -> x0, blocking collectives: 9.84 us -> none  [local(): lax.all_to_all(mixed_local.reshape(steps, local_rows, across_second, -1),...]
    ppermute x3 -> x9, starting transfers between devices: 3.55 us -> 13.3 us  [split_half_scatter(): lax.ppermute(outgoing, axis_name, [(i, i ^ offset) for i in range(axis_si...]
    ppermute x1 -> x3, waiting for transfers between devices: 19.8 us -> 10.6 us  [split_half_gather(): lax.ppermute(value, axis_name, [(i, i ^ half) for i in range(axis_size)])]
    ppermute x2, waiting for transfers between devices: 19.5 us -> 10.9 us  [doubling_gather(): lax.ppermute(held, axis_name, [(i, i ^ distance) for i in range(axis_size)])]
    all_to_all x0 -> x1, waiting for transfers between devices: none -> 5.3 us  [local(): lax.all_to_all(mixed_local.reshape(steps, local_rows, across_second, -1),...]
    ppermute x3 -> x9, waiting for transfers between devices: 37.1 us -> 33.4 us  [split_half_scatter(): lax.ppermute(outgoing, axis_name, [(i, i ^ offset) for i in range(axis_si...]
  transfers between devices with their start and end apart: 26 -> 43, of which waited for: 25 -> 34; matrix products, arithmetic and copies ran while one was open for 4% -> 7% of each run, Pallas kernels for 0% -> 0%
where the time goes in v6:
time: 296 us
  waiting for transfers between devices  160 us (54%)
  starting transfers between devices  57.4 us (19%)
  local copies, waits for them, and re-layouts  32.3 us (11%)
  matrix products  20.2 us (7%)
  other arithmetic  19.2 us (6%)
  between operations  6.15 us (2%)
    ppermute x13, waiting for transfers between devices, tree_sum(): value = value + lax.ppermute(value, axis_name, pairs)  50.9 us
    ppermute x9, waiting for transfers between devices, split_half_scatter(): lax.ppermute(outgoing, axis_name, [(i, i ^ offset) for i in range(axis_si...  33.4 us
    ppermute x9, waiting for transfers between devices, split_half_gather(): lax.ppermute(pair, axis_name, [(i, i ^ offset) for i in range(axis_size)])  20 us
    ppermute x13, starting transfers between devices, tree_sum(): value = value + lax.ppermute(value, axis_name, pairs)  17.3 us
    unnamed x59, local copies, waits for them, and re-layouts  16 us
    ppermute x2, waiting for transfers between devices, halving_scatter(): held = keep + lax.ppermute(give, axis_name, swap).astype(jnp.float32)  14.4 us
    ppermute x9, starting transfers between devices, split_half_scatter(): lax.ppermute(outgoing, axis_name, [(i, i ^ offset) for i in range(axis_si...  13.3 us
    ppermute x2, waiting for transfers between devices, doubling_gather(): lax.ppermute(held, axis_name, [(i, i ^ distance) for i in range(axis_size)])  10.9 us
  transfers between devices with their start and end apart: 43, of which 34 were waited for; matrix products, arithmetic and copies ran while one was open for 7% of the time, Pallas kernels for 0%

profile of v6, /device:TPU:0, one launch (start us, length us, event | category | flops | bytes accessed | tf_op | source)
XLA Modules:
  0.0 295.5 jit_solution(16287597609737254024)
XLA Ops:
  14.7 9.3 %collective-permute-done.1 = bf16[3,128,1024]{2,1,0:T(8,128)(2,1)} collective-permute-done((bf16[3,128,1024]{2,1,0:T(8,128)(2,1)S(1)}, bf16[3,128,1024]{2,1,0:T(8,128)(2,1)}, u32[]{:S(2)}, u32[]{:S(2)}) %collective-permute-start.1) | collective-permute-done | bytes 786464 | tf_op jit(solution)/shard_map/ppermute | solution.py:102
  41.9 5.1 %collective-permute-done.6 = f32[3,2,128,64]{2,3,0,1:T(8,128)S(1)} collective-permute-done((f32[3,2,128,64]{2,3,0,1:T(8,128)S(1)}, f32[3,2,128,64]{2,3,0,1:T(8,128)S(1)}, u32[]{:S(2)}, u32[]{:S(2)}) %collective-permute-start.6) | collective-permute-done | bytes 196640 | tf_op jit(solution)/shard_map/ppermute | solution.py:139
  48.8 4.4 %collective-permute-done.7 = f32[3,2,128,64]{2,3,0,1:T(8,128)S(1)} collective-permute-done((f32[3,2,128,64]{2,3,0,1:T(8,128)S(1)}, f32[3,2,128,64]{2,3,0,1:T(8,128)S(1)}, u32[]{:S(2)}, u32[]{:S(2)}) %collective-permute-start.7) | collective-permute-done | bytes 196640 | tf_op jit(solution)/shard_map/ppermute | solution.py:139
  55.8 3.2 %collective-permute-done.8 = f32[3,2,128,64]{2,3,0,1:T(8,128)S(1)} collective-permute-done((f32[3,2,128,64]{2,3,0,1:T(8,128)S(1)}, f32[3,2,128,64]{2,3,0,1:T(8,128)S(1)}, u32[]{:S(2)}, u32[]{:S(2)}) %collective-permute-start.8) | collective-permute-done | bytes 196640 | tf_op jit(solution)/shard_map/ppermute | solution.py:139
  59.0 3.0 %collective-permute-start.9 = (f32[3,2,128,64]{2,3,0,1:T(8,128)S(1)}, f32[3,2,128,64]{2,3,0,1:T(8,128)S(1)}, u32[]{:S(2)}, u32[]{:S(2)}) collective-permute-start(f32[3,2,128,64]{2,3,0,1:T(8,128)S(1)} %add.458), channel_id=1, source_target_pairs={{0,16},{4,20},{8,24},{12,28},{16,0},{20,4},{24,8},{28,12},{1,17},{... | collective-permute-start | bytes 589832 | tf_op jit(solution)/shard_map/ppermute | solution.py:139
  62.7 5.8 %collective-permute-done.9 = f32[3,2,128,64]{2,3,0,1:T(8,128)S(1)} collective-permute-done((f32[3,2,128,64]{2,3,0,1:T(8,128)S(1)}, f32[3,2,128,64]{2,3,0,1:T(8,128)S(1)}, u32[]{:S(2)}, u32[]{:S(2)}) %collective-permute-start.9) | collective-permute-done | bytes 196640 | tf_op jit(solution)/shard_map/ppermute | solution.py:139
  71.6 3.6 %bitcast_add_fusion = f32[3,256,2048]{2,1,0:T(8,128)S(1)} fusion(f32[3,2,128,2048]{3,2,1,0:T(8,128)S(1)} %copy.78, bf16[1024,2048]{1,0:T(8,128)(2,1)S(1)} %copy-done.17, f32[1024]{0:T(1024)S(1)} %convert_element_type.196, f32[3,256]{1,0:T(4,128)S(1)} %add_rsqrt_fusion, bf16[3,128,1024]{2,1,0:T(8,128)(2,1)S(1)} %get-tuple-element.20, ...), kind=kOutput, calls=%fused_computation.4 | convolution fusion | flops 3228303360 | bytes 18357248 | tf_op jit(solution)/shard_map/tnd,de->tne/dot_general | solution.py:277
  83.6 9.1 %collective-permute-done.10 = bf16[2,1,32,2560]{3,2,1,0:T(8,128)(2,1)S(1)} collective-permute-done((bf16[2,1,32,2560]{3,2,1,0:T(8,128)(2,1)S(1)}, bf16[2,1,32,2560]{3,2,1,0:T(8,128)(2,1)S(1)}, u32[]{:S(2)}, u32[]{:S(2)}) %collective-permute-start.10) | collective-permute-done | bytes 327712 | tf_op jit(solution)/shard_map/ppermute | solution.py:84
  97.0 7.7 %collective-permute-done.14 = bf16[2,1,32,2560]{3,2,1,0:T(8,128)(2,1)S(1)} collective-permute-done((bf16[2,1,32,2560]{3,2,1,0:T(8,128)(2,1)S(1)}, bf16[2,1,32,2560]{3,2,1,0:T(8,128)(2,1)S(1)}, u32[]{:S(2)}, u32[]{:S(2)}) %collective-permute-start.14) | collective-permute-done | bytes 327712 | tf_op jit(solution)/shard_map/ppermute | solution.py:84
  104.7 4.0 %collective-permute-start.20 = (bf16[2,1,32,2560]{3,2,1,0:T(8,128)(2,1)S(1)}, bf16[2,1,32,2560]{3,2,1,0:T(8,128)(2,1)S(1)}, u32[]{:S(2)}, u32[]{:S(2)}) collective-permute-start(bf16[2,1,32,2560]{3,2,1,0:T(8,128)(2,1)S(1)} %pad_maximum_fusion.11), channel_id=1, source_target_pairs={{0,12},{4,8},{8,4},{12,0},{16,28},{20,24},{24,20},{28,16},{1,13},{... | collective-permute-start | bytes 983048 | tf_op jit(solution)/shard_map/ppermute | solution.py:84
  109.5 6.1 %collective-permute-done.16 = bf16[2,1,32,2560]{3,2,1,0:T(8,128)(2,1)S(1)} collective-permute-done((bf16[2,1,32,2560]{3,2,1,0:T(8,128)(2,1)S(1)}, bf16[2,1,32,2560]{3,2,1,0:T(8,128)(2,1)S(1)}, u32[]{:S(2)}, u32[]{:S(2)}) %collective-permute-start.16) | collective-permute-done | bytes 327712 | tf_op jit(solution)/shard_map/ppermute | solution.py:84
  117.4 6.2 %collective-permute-done.19 = bf16[2,1,32,2560]{3,2,1,0:T(8,128)(2,1)S(1)} collective-permute-done((bf16[2,1,32,2560]{3,2,1,0:T(8,128)(2,1)S(1)}, bf16[2,1,32,2560]{3,2,1,0:T(8,128)(2,1)S(1)}, u32[]{:S(2)}, u32[]{:S(2)}) %collective-permute-start.19) | collective-permute-done | bytes 327712 | tf_op jit(solution)/shard_map/ppermute | solution.py:84
  123.7 3.4 %collective-permute-done.20 = bf16[2,1,32,2560]{3,2,1,0:T(8,128)(2,1)S(1)} collective-permute-done((bf16[2,1,32,2560]{3,2,1,0:T(8,128)(2,1)S(1)}, bf16[2,1,32,2560]{3,2,1,0:T(8,128)(2,1)S(1)}, u32[]{:S(2)}, u32[]{:S(2)}) %collective-permute-start.20) | collective-permute-done | bytes 327712 | tf_op jit(solution)/shard_map/ppermute | solution.py:84
  130.4 6.8 %collective-permute-done.21 = bf16[1,32,2560]{2,1,0:T(8,128)(2,1)S(1)} collective-permute-done((bf16[1,32,2560]{2,1,0:T(8,128)(2,1)S(1)}, bf16[1,32,2560]{2,1,0:T(8,128)(2,1)S(1)}, u32[]{:S(2)}, u32[]{:S(2)}) %collective-permute-start.21) | collective-permute-done | bytes 163872 | tf_op jit(solution)/shard_map/ppermute | solution.py:89
  138.2 3.6 %all-to-all-start = ((bf16[3,4,8,1,2560]{4,2,3,0,1:T(8,128)(2,1)}), bf16[3,4,8,1,2560]{4,2,3,0,1:T(8,128)(2,1)S(1)}, u32[]{:S(2)}, u32[]{:S(2)}) async-start(bf16[3,4,8,1,2560]{4,2,3,0,1:T(8,128)(2,1)} %copy.83), calls=%async_computation | async-start | bytes 983040 | tf_op jit(solution)/shard_map/all_to_all | solution.py:287
  142.1 8.0 %all-to-all-done = bf16[3,4,8,1,2560]{4,2,3,0,1:T(8,128)(2,1)S(1)} async-done(((bf16[3,4,8,1,2560]{4,2,3,0,1:T(8,128)(2,1)}), bf16[3,4,8,1,2560]{4,2,3,0,1:T(8,128)(2,1)S(1)}, u32[]{:S(2)}, u32[]{:S(2)}) %all-to-all-start) | async-done | bytes 491552 | tf_op jit(solution)/shard_map/all_to_all | solution.py:287
  151.8 4.6 %fusion.115 = (f32[8,8,24]{2,1,0:T(8,128)S(1)}, f32[8,8,24,256]{3,2,1,0:T(8,128)S(1)}) fusion(pred[8,256]{1,0:T(8,128)(4,1)S(1)} %iota_compare_fusion, bf16[8,256,1024]{2,1,0:T(8,128)(2,1)} %param.28, bf16[3,8,8,8,64]{4,3,2,1,0:T(8,128)(2,1)S(1)} %bitcast.225, bf16[3,8,8,8,64]{4,3,2,1,0:T(8,128)(2,1)S(1)} %bitcast.223), kind=kOutput, calls=%fused_computation.239 | convolution fusion | flops 102627840 | bytes 6168576 | tf_op jit(solution)/shard_map/rhqd,rchd->rhqc/dot_general | solution.py:186
  158.1 3.1 %fusion.51 = bf16[8,8,3,8,128]{4,3,2,1,0:T(8,128)(2,1)S(1)} fusion(f32[8,8,24,128]{3,2,1,0:T(8,128)S(1)} %fusion.95, f32[8,8,24,256]{3,2,1,0:T(8,128)S(1)} %get-tuple-element.64, f32[8,8,24]{2,1,0:T(8,128)S(1)} %max.7, pred[8,256]{1,0:T(8,128)(4,1)S(1)} %iota_compare_fusion, f32[8,8,24]{2,1,0:T(8,128)S(1)} %add.499, bf16[8,256,1024]{2,1,0:T(8,128)(2,1)} %param.29), kind=kOutput, calls=%fused_computation.52 | convolution fusion | flops 102432768 | bytes 6961152 | tf_op jit(solution)/shard_map/rhqc,rchd->rhqd/dot_general | solution.py:210
  162.3 3.7 %all-to-all-start.1 = ((bf16[3,1,8,4,2048]{4,2,0,1,3:T(8,128)(2,1)}), bf16[3,1,8,4,2048]{4,2,0,1,3:T(8,128)(2,1)S(1)}, u32[]{:S(2)}, u32[]{:S(2)}) async-start(bf16[3,1,8,4,2048]{4,2,0,1,3:T(8,128)(2,1)} %copy.94), calls=%async_computation.1 | async-start | bytes 786432 | tf_op jit(solution)/shard_map/all_to_all | solution.py:313
  167.9 5.3 %all-to-all-done.1 = bf16[3,1,8,4,2048]{4,2,0,1,3:T(8,128)(2,1)S(1)} async-done(((bf16[3,1,8,4,2048]{4,2,0,1,3:T(8,128)(2,1)}), bf16[3,1,8,4,2048]{4,2,0,1,3:T(8,128)(2,1)S(1)}, u32[]{:S(2)}, u32[]{:S(2)}) %all-to-all-start.1) | async-done | bytes 393248 | tf_op jit(solution)/shard_map/all_to_all | solution.py:313
  177.0 10.0 %collective-permute-done.30 = bf16[1,32,2048]{2,1,0:T(8,128)(2,1)S(1)} collective-permute-done((bf16[1,32,2048]{2,1,0:T(8,128)(2,1)S(1)}, bf16[1,32,2048]{2,1,0:T(8,128)(2,1)S(1)}, u32[]{:S(2)}, u32[]{:S(2)}) %collective-permute-start.30) | collective-permute-done | bytes 131104 | tf_op jit(solution)/shard_map/ppermute | solution.py:116
  192.7 3.6 %collective-permute-done.31 = bf16[2,1,32,2048]{3,2,1,0:T(8,128)(2,1)S(1)} collective-permute-done((bf16[2,1,32,2048]{3,2,1,0:T(8,128)(2,1)S(1)}, bf16[2,1,32,2048]{3,2,1,0:T(8,128)(2,1)S(1)}, u32[]{:S(2)}, u32[]{:S(2)}) %collective-permute-start.31) | collective-permute-done | bytes 262176 | tf_op jit(solution)/shard_map/ppermute | solution.py:121
  199.0 5.1 %collective-permute-done.33 = bf16[2,1,32,2048]{3,2,1,0:T(8,128)(2,1)S(1)} collective-permute-done((bf16[2,1,32,2048]{3,2,1,0:T(8,128)(2,1)S(1)}, bf16[2,1,32,2048]{3,2,1,0:T(8,128)(2,1)S(1)}, u32[]{:S(2)}, u32[]{:S(2)}) %collective-permute-start.33) | collective-permute-done | bytes 262176 | tf_op jit(solution)/shard_map/ppermute | solution.py:121
  210.8 4.7 %collective-permute-done.29 = bf16[2,1,32,2048]{3,2,1,0:T(8,128)(2,1)} collective-permute-done((bf16[2,1,32,2048]{3,2,1,0:T(8,128)(2,1)}, bf16[2,1,32,2048]{3,2,1,0:T(8,128)(2,1)}, u32[]{:S(2)}, u32[]{:S(2)}) %collective-permute-start.29) | collective-permute-done | bytes 262176 | tf_op jit(solution)/shard_map/ppermute | solution.py:121
  222.5 4.2 %collective-permute-done.25 = bf16[2,1,32,2048]{3,2,1,0:T(8,128)(2,1)} collective-permute-done((bf16[2,1,32,2048]{3,2,1,0:T(8,128)(2,1)S(1)}, bf16[2,1,32,2048]{3,2,1,0:T(8,128)(2,1)}, u32[]{:S(2)}, u32[]{:S(2)}) %collective-permute-start.25) | collective-permute-done | bytes 262176 | tf_op jit(solution)/shard_map/ppermute | solution.py:121
  240.0 6.5 %collective-permute-done.35 = f32[3,2,128,64]{2,3,0,1:T(8,128)S(1)} collective-permute-done((f32[3,2,128,64]{2,3,0,1:T(8,128)S(1)}, f32[3,2,128,64]{2,3,0,1:T(8,128)S(1)}, u32[]{:S(2)}, u32[]{:S(2)}) %collective-permute-start.35) | collective-permute-done | bytes 196640 | tf_op jit(solution)/shard_map/ppermute | solution.py:139
  247.8 4.8 %collective-permute-done.36 = f32[3,2,128,64]{2,3,0,1:T(8,128)S(1)} collective-permute-done((f32[3,2,128,64]{2,3,0,1:T(8,128)S(1)}, f32[3,2,128,64]{2,3,0,1:T(8,128)S(1)}, u32[]{:S(2)}, u32[]{:S(2)}) %collective-permute-start.36) | collective-permute-done | bytes 196640 | tf_op jit(solution)/shard_map/ppermute | solution.py:139
  252.8 5.7 %collective-permute-done.37 = f32[3,2,128,64]{2,3,0,1:T(8,128)S(1)} collective-permute-done((f32[3,2,128,64]{2,3,0,1:T(8,128)S(1)}, f32[3,2,128,64]{2,3,0,1:T(8,128)S(1)}, u32[]{:S(2)}, u32[]{:S(2)}) %collective-permute-start.37) | collective-permute-done | bytes 196640 | tf_op jit(solution)/shard_map/ppermute | solution.py:139
  259.8 7.6 %collective-permute-done.38 = f32[3,2,128,64]{2,3,0,1:T(8,128)S(1)} collective-permute-done((f32[3,2,128,64]{2,3,0,1:T(8,128)S(1)}, f32[3,2,128,64]{2,3,0,1:T(8,128)S(1)}, u32[]{:S(2)}, u32[]{:S(2)}) %collective-permute-start.38) | collective-permute-done | bytes 196640 | tf_op jit(solution)/shard_map/ppermute | solution.py:139
  270.6 3.4 %bitcast_add_fusion.1 = f32[3,256,1024]{2,1,0:T(8,128)S(1)} fusion(f32[3,2,128,1024]{3,2,1,0:T(8,128)S(1)} %copy.96, bf16[2048,1024]{1,0:T(8,128)(2,1)S(1)} %copy-done.18, bf16[1,256,2048]{2,1,0:T(8,128)(2,1)S(1)} %bitcast.236, bf16[1,256,2048]{2,1,0:T(8,128)(2,1)S(1)} %bitcast.234, bf16[1,256,2048]{2,1,0:T(8,128)(2,1)S(1)} %bitcast.232), kind=kOutput, calls=%fused_computation.27 | convolution fusion | flops 3225157632 | bytes 13631488 | tf_op jit(solution)/shard_map/tnq,qe->tne/dot_general | solution.py:328
  275.6 3.7 %collective-permute-done.39 = f32[3,2,64,1024]{3,2,0,1:T(8,128)} collective-permute-done((f32[3,2,64,1024]{3,2,0,1:T(8,128)}, f32[3,2,64,1024]{3,2,0,1:T(8,128)}, u32[]{:S(2)}, u32[]{:S(2)}) %collective-permute-start.39) | collective-permute-done | bytes 1572896 | tf_op jit(solution)/shard_map/ppermute | solution.py:160
  282.9 10.7 %collective-permute-done.40 = bf16[3,1,64,1024]{3,2,0,1:T(8,128)(2,1)S(1)} collective-permute-done((bf16[3,1,64,1024]{3,2,0,1:T(8,128)(2,1)S(1)}, bf16[3,1,64,1024]{3,2,0,1:T(8,128)(2,1)S(1)}, u32[]{:S(2)}, u32[]{:S(2)}) %collective-permute-start.40) | collective-permute-done | bytes 393248 | tf_op jit(solution)/shard_map/ppermute | solution.py:160
  (228 shorter events, 113.4 us)
Async XLA Ops:
  3.1 20.9 %collective-permute-start.1 = (bf16[3,128,1024]{2,1,0:T(8,128)(2,1)S(1)}, bf16[3,128,1024]{2,1,0:T(8,128)(2,1)}, u32[]{:S(2)}, u32[]{:S(2)}) collective-permute-start(bf16[3,128,1024]{2,1,0:T(8,128)(2,1)S(1)} %pad_maximum_fusion.1), channel_id=1, source_target_pairs={{0,2},{1,3},{2,0},{3,1},{4,6},{5,7},{6,4},{7,5},{8,10},{9,11},{10,... | collective-permute-start | bytes 2359304 | tf_op jit(solution)/shard_map/ppermute | solution.py:102
  40.0 7.0 %collective-permute-start.6 = (f32[3,2,128,64]{2,3,0,1:T(8,128)S(1)}, f32[3,2,128,64]{2,3,0,1:T(8,128)S(1)}, u32[]{:S(2)}, u32[]{:S(2)}) collective-permute-start(f32[3,2,128,64]{2,3,0,1:T(8,128)S(1)} %add.455), channel_id=1, source_target_pairs={{0,2},{1,3},{2,0},{3,1},{4,6},{5,7},{6,4},{7,5},{8,10},{9,11},{10,... | collective-permute-start | bytes 589832 | tf_op jit(solution)/shard_map/ppermute | solution.py:139
  59.0 9.4 %collective-permute-start.9 = (f32[3,2,128,64]{2,3,0,1:T(8,128)S(1)}, f32[3,2,128,64]{2,3,0,1:T(8,128)S(1)}, u32[]{:S(2)}, u32[]{:S(2)}) collective-permute-start(f32[3,2,128,64]{2,3,0,1:T(8,128)S(1)} %add.458), channel_id=1, source_target_pairs={{0,16},{4,20},{8,24},{12,28},{16,0},{20,4},{24,8},{28,12},{1,17},{... | collective-permute-start | bytes 589832 | tf_op jit(solution)/shard_map/ppermute | solution.py:139
  76.9 15.9 %collective-permute-start.10 = (bf16[2,1,32,2560]{3,2,1,0:T(8,128)(2,1)S(1)}, bf16[2,1,32,2560]{3,2,1,0:T(8,128)(2,1)S(1)}, u32[]{:S(2)}, u32[]{:S(2)}) collective-permute-start(bf16[2,1,32,2560]{3,2,1,0:T(8,128)(2,1)S(1)} %pad_maximum_fusion.3), channel_id=1, source_target_pairs={{0,4},{4,0},{8,12},{12,8},{16,20},{20,16},{24,28},{28,24},{1,5},{5... | collective-permute-start | bytes 983048 | tf_op jit(solution)/shard_map/ppermute | solution.py:84
  78.5 16.2 %collective-permute-start.11 = (bf16[2,1,32,2560]{3,2,1,0:T(8,128)(2,1)S(1)}, bf16[2,1,32,2560]{3,2,1,0:T(8,128)(2,1)S(1)}, u32[]{:S(2)}, u32[]{:S(2)}) collective-permute-start(bf16[2,1,32,2560]{3,2,1,0:T(8,128)(2,1)S(1)} %pad_maximum_fusion.4), channel_id=1, source_target_pairs={{0,8},{4,12},{8,0},{12,4},{16,24},{20,28},{24,16},{28,20},{1,9},{5... | collective-permute-start | bytes 983048 | tf_op jit(solution)/shard_map/ppermute | solution.py:84
  79.3 17.0 %collective-permute-start.12 = (bf16[2,1,32,2560]{3,2,1,0:T(8,128)(2,1)S(1)}, bf16[2,1,32,2560]{3,2,1,0:T(8,128)(2,1)S(1)}, u32[]{:S(2)}, u32[]{:S(2)}) collective-permute-start(bf16[2,1,32,2560]{3,2,1,0:T(8,128)(2,1)S(1)} %pad_maximum_fusion.5), channel_id=1, source_target_pairs={{0,12},{4,8},{8,4},{12,0},{16,28},{20,24},{24,20},{28,16},{1,13},{... | collective-permute-start | bytes 983048 | tf_op jit(solution)/shard_map/ppermute | solution.py:84
  81.1 23.6 %collective-permute-start.14 = (bf16[2,1,32,2560]{3,2,1,0:T(8,128)(2,1)S(1)}, bf16[2,1,32,2560]{3,2,1,0:T(8,128)(2,1)S(1)}, u32[]{:S(2)}, u32[]{:S(2)}) collective-permute-start(bf16[2,1,32,2560]{3,2,1,0:T(8,128)(2,1)S(1)} %pad_maximum_fusion.6), channel_id=1, source_target_pairs={{0,4},{4,0},{8,12},{12,8},{16,20},{20,16},{24,28},{28,24},{1,5},{5... | collective-permute-start | bytes 983048 | tf_op jit(solution)/shard_map/ppermute | solution.py:84
  82.7 26.0 %collective-permute-start.15 = (bf16[2,1,32,2560]{3,2,1,0:T(8,128)(2,1)S(1)}, bf16[2,1,32,2560]{3,2,1,0:T(8,128)(2,1)S(1)}, u32[]{:S(2)}, u32[]{:S(2)}) collective-permute-start(bf16[2,1,32,2560]{3,2,1,0:T(8,128)(2,1)S(1)} %pad_maximum_fusion.7), channel_id=1, source_target_pairs={{0,8},{4,12},{8,0},{12,4},{16,24},{20,28},{24,16},{28,20},{1,9},{5... | collective-permute-start | bytes 983048 | tf_op jit(solution)/shard_map/ppermute | solution.py:84
  92.7 22.8 %collective-permute-start.16 = (bf16[2,1,32,2560]{3,2,1,0:T(8,128)(2,1)S(1)}, bf16[2,1,32,2560]{3,2,1,0:T(8,128)(2,1)S(1)}, u32[]{:S(2)}, u32[]{:S(2)}) collective-permute-start(bf16[2,1,32,2560]{3,2,1,0:T(8,128)(2,1)S(1)} %pad_maximum_fusion.8), channel_id=1, source_target_pairs={{0,12},{4,8},{8,4},{12,0},{16,28},{20,24},{24,20},{28,16},{1,13},{... | collective-permute-start | bytes 983048 | tf_op jit(solution)/shard_map/ppermute | solution.py:84
  94.7 22.7 %collective-permute-start.18 = (bf16[2,1,32,2560]{3,2,1,0:T(8,128)(2,1)S(1)}, bf16[2,1,32,2560]{3,2,1,0:T(8,128)(2,1)S(1)}, u32[]{:S(2)}, u32[]{:S(2)}) collective-permute-start(bf16[2,1,32,2560]{3,2,1,0:T(8,128)(2,1)S(1)} %pad_maximum_fusion.9), channel_id=1, source_target_pairs={{0,4},{4,0},{8,12},{12,8},{16,20},{20,16},{24,28},{28,24},{1,5},{5... | collective-permute-start | bytes 983048 | tf_op jit(solution)/shard_map/ppermute | solution.py:84
  96.3 27.4 %collective-permute-start.19 = (bf16[2,1,32,2560]{3,2,1,0:T(8,128)(2,1)S(1)}, bf16[2,1,32,2560]{3,2,1,0:T(8,128)(2,1)S(1)}, u32[]{:S(2)}, u32[]{:S(2)}) collective-permute-start(bf16[2,1,32,2560]{3,2,1,0:T(8,128)(2,1)S(1)} %pad_maximum_fusion.10), channel_id=1, source_target_pairs={{0,8},{4,12},{8,0},{12,4},{16,24},{20,28},{24,16},{28,20},{1,9},{5... | collective-permute-start | bytes 983048 | tf_op jit(solution)/shard_map/ppermute | solution.py:84
  104.7 22.5 %collective-permute-start.20 = (bf16[2,1,32,2560]{3,2,1,0:T(8,128)(2,1)S(1)}, bf16[2,1,32,2560]{3,2,1,0:T(8,128)(2,1)S(1)}, u32[]{:S(2)}, u32[]{:S(2)}) collective-permute-start(bf16[2,1,32,2560]{3,2,1,0:T(8,128)(2,1)S(1)} %pad_maximum_fusion.11), channel_id=1, source_target_pairs={{0,12},{4,8},{8,4},{12,0},{16,28},{20,24},{24,20},{28,16},{1,13},{... | collective-permute-start | bytes 983048 | tf_op jit(solution)/shard_map/ppermute | solution.py:84
  108.8 21.4 %collective-permute-start.13 = (bf16[1,32,2560]{2,1,0:T(8,128)(2,1)S(1)}, bf16[1,32,2560]{2,1,0:T(8,128)(2,1)S(1)}, u32[]{:S(2)}, u32[]{:S(2)}) collective-permute-start(bf16[1,32,2560]{2,1,0:T(8,128)(2,1)S(1)} %fusion.88), channel_id=1, source_target_pairs={{0,16},{4,20},{8,24},{12,28},{16,0},{20,4},{24,8},{28,12},{1,17},{... | collective-permute-start | bytes 491528 | tf_op jit(solution)/shard_map/ppermute | solution.py:89
  115.6 14.6 %collective-permute-start.17 = (bf16[1,32,2560]{2,1,0:T(8,128)(2,1)S(1)}, bf16[1,32,2560]{2,1,0:T(8,128)(2,1)S(1)}, u32[]{:S(2)}, u32[]{:S(2)}) collective-permute-start(bf16[1,32,2560]{2,1,0:T(8,128)(2,1)S(1)} %fusion.90), channel_id=1, source_target_pairs={{0,16},{4,20},{8,24},{12,28},{16,0},{20,4},{24,8},{28,12},{1,17},{... | collective-permute-start | bytes 491528 | tf_op jit(solution)/shard_map/ppermute | solution.py:89
  127.3 9.9 %collective-permute-start.21 = (bf16[1,32,2560]{2,1,0:T(8,128)(2,1)S(1)}, bf16[1,32,2560]{2,1,0:T(8,128)(2,1)S(1)}, u32[]{:S(2)}, u32[]{:S(2)}) collective-permute-start(bf16[1,32,2560]{2,1,0:T(8,128)(2,1)S(1)} %fusion.92), channel_id=1, source_target_pairs={{0,16},{4,20},{8,24},{12,28},{16,0},{20,4},{24,8},{28,12},{1,17},{... | collective-permute-start | bytes 491528 | tf_op jit(solution)/shard_map/ppermute | solution.py:89
  138.2 11.9 %all-to-all-start = ((bf16[3,4,8,1,2560]{4,2,3,0,1:T(8,128)(2,1)}), bf16[3,4,8,1,2560]{4,2,3,0,1:T(8,128)(2,1)S(1)}, u32[]{:S(2)}, u32[]{:S(2)}) async-start(bf16[3,4,8,1,2560]{4,2,3,0,1:T(8,128)(2,1)} %copy.83), calls=%async_computation | async-start | bytes 983040 | tf_op jit(solution)/shard_map/all_to_all | solution.py:287
  162.3 10.9 %all-to-all-start.1 = ((bf16[3,1,8,4,2048]{4,2,0,1,3:T(8,128)(2,1)}), bf16[3,1,8,4,2048]{4,2,0,1,3:T(8,128)(2,1)S(1)}, u32[]{:S(2)}, u32[]{:S(2)}) async-start(bf16[3,1,8,4,2048]{4,2,0,1,3:T(8,128)(2,1)} %copy.94), calls=%async_computation.1 | async-start | bytes 786432 | tf_op jit(solution)/shard_map/all_to_all | solution.py:313
  173.3 13.7 %collective-permute-start.30 = (bf16[1,32,2048]{2,1,0:T(8,128)(2,1)S(1)}, bf16[1,32,2048]{2,1,0:T(8,128)(2,1)S(1)}, u32[]{:S(2)}, u32[]{:S(2)}) collective-permute-start(bf16[1,32,2048]{2,1,0:T(8,128)(2,1)S(1)} %get-tuple-element.48), channel_id=1, source_target_pairs={{0,16},{4,20},{8,24},{12,28},{16,0},{20,4},{24,8},{28,12},{1,17},{... | collective-permute-start | bytes 393224 | tf_op jit(solution)/shard_map/ppermute | solution.py:116
  174.1 16.6 %collective-permute-start.26 = (bf16[1,32,2048]{2,1,0:T(8,128)(2,1)S(1)}, bf16[1,32,2048]{2,1,0:T(8,128)(2,1)S(1)}, u32[]{:S(2)}, u32[]{:S(2)}) collective-permute-start(bf16[1,32,2048]{2,1,0:T(8,128)(2,1)S(1)} %get-tuple-element.47), channel_id=1, source_target_pairs={{0,16},{4,20},{8,24},{12,28},{16,0},{20,4},{24,8},{28,12},{1,17},{... | collective-permute-start | bytes 393224 | tf_op jit(solution)/shard_map/ppermute | solution.py:116
  177.0 15.7 %collective-permute-start.22 = (bf16[1,32,2048]{2,1,0:T(8,128)(2,1)S(1)}, bf16[1,32,2048]{2,1,0:T(8,128)(2,1)S(1)}, u32[]{:S(2)}, u32[]{:S(2)}) collective-permute-start(bf16[1,32,2048]{2,1,0:T(8,128)(2,1)S(1)} %get-tuple-element.46), channel_id=1, source_target_pairs={{0,16},{4,20},{8,24},{12,28},{16,0},{20,4},{24,8},{28,12},{1,17},{... | collective-permute-start | bytes 393224 | tf_op jit(solution)/shard_map/ppermute | solution.py:116
  187.1 9.2 %collective-permute-start.31 = (bf16[2,1,32,2048]{3,2,1,0:T(8,128)(2,1)S(1)}, bf16[2,1,32,2048]{3,2,1,0:T(8,128)(2,1)S(1)}, u32[]{:S(2)}, u32[]{:S(2)}) collective-permute-start(bf16[2,1,32,2048]{3,2,1,0:T(8,128)(2,1)S(1)} %pad_maximum_fusion.14), channel_id=1, source_target_pairs={{0,4},{4,0},{8,12},{12,8},{16,20},{20,16},{24,28},{28,24},{1,5},{5... | collective-permute-start | bytes 786440 | tf_op jit(solution)/shard_map/ppermute | solution.py:121
  187.9 10.4 %collective-permute-start.32 = (bf16[2,1,32,2048]{3,2,1,0:T(8,128)(2,1)S(1)}, bf16[2,1,32,2048]{3,2,1,0:T(8,128)(2,1)S(1)}, u32[]{:S(2)}, u32[]{:S(2)}) collective-permute-start(bf16[2,1,32,2048]{3,2,1,0:T(8,128)(2,1)S(1)} %pad_maximum_fusion.14), channel_id=1, source_target_pairs={{0,8},{4,12},{8,0},{12,4},{16,24},{20,28},{24,16},{28,20},{1,9},{5... | collective-permute-start | bytes 786440 | tf_op jit(solution)/shard_map/ppermute | solution.py:121
  187.9 16.2 %collective-permute-start.33 = (bf16[2,1,32,2048]{3,2,1,0:T(8,128)(2,1)S(1)}, bf16[2,1,32,2048]{3,2,1,0:T(8,128)(2,1)S(1)}, u32[]{:S(2)}, u32[]{:S(2)}) collective-permute-start(bf16[2,1,32,2048]{3,2,1,0:T(8,128)(2,1)S(1)} %pad_maximum_fusion.14), channel_id=1, source_target_pairs={{0,12},{4,8},{8,4},{12,0},{16,28},{20,24},{24,20},{28,16},{1,13},{... | collective-permute-start | bytes 786440 | tf_op jit(solution)/shard_map/ppermute | solution.py:121
  191.4 16.2 %collective-permute-start.27 = (bf16[2,1,32,2048]{3,2,1,0:T(8,128)(2,1)}, bf16[2,1,32,2048]{3,2,1,0:T(8,128)(2,1)S(1)}, u32[]{:S(2)}, u32[]{:S(2)}) collective-permute-start(bf16[2,1,32,2048]{3,2,1,0:T(8,128)(2,1)} %pad_maximum_fusion.13), channel_id=1, source_target_pairs={{0,4},{4,0},{8,12},{12,8},{16,20},{20,16},{24,28},{28,24},{1,5},{5... | collective-permute-start | bytes 786440 | tf_op jit(solution)/shard_map/ppermute | solution.py:121
  192.7 17.2 %collective-permute-start.28 = (bf16[2,1,32,2048]{3,2,1,0:T(8,128)(2,1)}, bf16[2,1,32,2048]{3,2,1,0:T(8,128)(2,1)}, u32[]{:S(2)}, u32[]{:S(2)}) collective-permute-start(bf16[2,1,32,2048]{3,2,1,0:T(8,128)(2,1)} %pad_maximum_fusion.13), channel_id=1, source_target_pairs={{0,8},{4,12},{8,0},{12,4},{16,24},{20,28},{24,16},{28,20},{1,9},{5... | collective-permute-start | bytes 786440 | tf_op jit(solution)/shard_map/ppermute | solution.py:121
  196.3 19.2 %collective-permute-start.29 = (bf16[2,1,32,2048]{3,2,1,0:T(8,128)(2,1)}, bf16[2,1,32,2048]{3,2,1,0:T(8,128)(2,1)}, u32[]{:S(2)}, u32[]{:S(2)}) collective-permute-start(bf16[2,1,32,2048]{3,2,1,0:T(8,128)(2,1)} %pad_maximum_fusion.13), channel_id=1, source_target_pairs={{0,12},{4,8},{8,4},{12,0},{16,28},{20,24},{24,20},{28,16},{1,13},{... | collective-permute-start | bytes 786440 | tf_op jit(solution)/shard_map/ppermute | solution.py:121
  198.3 22.9 %collective-permute-start.23 = (bf16[2,1,32,2048]{3,2,1,0:T(8,128)(2,1)S(1)}, bf16[2,1,32,2048]{3,2,1,0:T(8,128)(2,1)S(1)}, u32[]{:S(2)}, u32[]{:S(2)}) collective-permute-start(bf16[2,1,32,2048]{3,2,1,0:T(8,128)(2,1)S(1)} %pad_maximum_fusion.12), channel_id=1, source_target_pairs={{0,4},{4,0},{8,12},{12,8},{16,20},{20,16},{24,28},{28,24},{1,5},{5... | collective-permute-start | bytes 786440 | tf_op jit(solution)/shard_map/ppermute | solution.py:121
  204.1 17.7 %collective-permute-start.24 = (bf16[2,1,32,2048]{3,2,1,0:T(8,128)(2,1)S(1)}, bf16[2,1,32,2048]{3,2,1,0:T(8,128)(2,1)S(1)}, u32[]{:S(2)}, u32[]{:S(2)}) collective-permute-start(bf16[2,1,32,2048]{3,2,1,0:T(8,128)(2,1)S(1)} %pad_maximum_fusion.12), channel_id=1, source_target_pairs={{0,8},{4,12},{8,0},{12,4},{16,24},{20,28},{24,16},{28,20},{1,9},{5... | collective-permute-start | bytes 786440 | tf_op jit(solution)/shard_map/ppermute | solution.py:121
  207.6 19.1 %collective-permute-start.25 = (bf16[2,1,32,2048]{3,2,1,0:T(8,128)(2,1)S(1)}, bf16[2,1,32,2048]{3,2,1,0:T(8,128)(2,1)}, u32[]{:S(2)}, u32[]{:S(2)}) collective-permute-start(bf16[2,1,32,2048]{3,2,1,0:T(8,128)(2,1)S(1)} %pad_maximum_fusion.12), channel_id=1, source_target_pairs={{0,12},{4,8},{8,4},{12,0},{16,28},{20,24},{24,20},{28,16},{1,13},{... | collective-permute-start | bytes 786440 | tf_op jit(solution)/shard_map/ppermute | solution.py:121
  239.4 7.0 %collective-permute-start.35 = (f32[3,2,128,64]{2,3,0,1:T(8,128)S(1)}, f32[3,2,128,64]{2,3,0,1:T(8,128)S(1)}, u32[]{:S(2)}, u32[]{:S(2)}) collective-permute-start(f32[3,2,128,64]{2,3,0,1:T(8,128)S(1)} %add.500), channel_id=1, source_target_pairs={{0,2},{1,3},{2,0},{3,1},{4,6},{5,7},{6,4},{7,5},{8,10},{9,11},{10,... | collective-permute-start | bytes 589832 | tf_op jit(solution)/shard_map/ppermute | solution.py:139
  258.4 8.9 %collective-permute-start.38 = (f32[3,2,128,64]{2,3,0,1:T(8,128)S(1)}, f32[3,2,128,64]{2,3,0,1:T(8,128)S(1)}, u32[]{:S(2)}, u32[]{:S(2)}) collective-permute-start(f32[3,2,128,64]{2,3,0,1:T(8,128)S(1)} %add.503), channel_id=1, source_target_pairs={{0,16},{4,20},{8,24},{12,28},{16,0},{20,4},{24,8},{28,12},{1,17},{... | collective-permute-start | bytes 589832 | tf_op jit(solution)/shard_map/ppermute | solution.py:139
  282.3 11.2 %collective-permute-start.40 = (bf16[3,1,64,1024]{3,2,0,1:T(8,128)(2,1)S(1)}, bf16[3,1,64,1024]{3,2,0,1:T(8,128)(2,1)S(1)}, u32[]{:S(2)}, u32[]{:S(2)}) collective-permute-start(bf16[3,1,64,1024]{3,2,0,1:T(8,128)(2,1)S(1)} %dynamic-slice_convert_fusion), channel_id=1, source_target_pairs={{0,2},{1,3},{2,0},{3,1},{4,6},{5,7},{6,4},{7,5},{8,10},{9,11},{10,... | collective-permute-start | bytes 1179656 | tf_op jit(solution)/shard_map/ppermute | solution.py:160
  (31 other events, 189.5 us)

commit v7 on v6

--- a/solution.py
+++ b/solution.py
@@ -254,14 +254,16 @@
     query_width = query_weight.shape[1]
     key_width = key_weight.shape[1]
     norm_scale = norm_gain.astype(jnp.float32)
-    query_first = pick_adapters(query_down, block_adapter, index_second)
+    query_first = tree_sum(pick_adapters(query_down, block_adapter, index_second), ("gy",))
     query_second = pick_adapters(query_up, block_adapter, index_first)
-    output_first = pick_adapters(output_down, block_adapter, index_first)
+    output_first = tree_sum(pick_adapters(output_down, block_adapter, index_first), ("gx",))
     output_second = pick_adapters(output_up, block_adapter, index_second)
 
+    own_wide = inputs.astype(jnp.float32)
+    own_squares = tree_sum(jnp.sum(own_wide * own_wide, axis=2), ("gx",))
+    squares = doubling_gather(own_squares, "gy", across_second, 1)
     rows_all = doubling_gather(inputs, "gy", across_second, 1)
     rows_wide = rows_all.astype(jnp.float32)
-    squares = tree_sum(jnp.sum(rows_wide * rows_wide, axis=2), ("gx",))
     factor_rows = lax.rsqrt(squares / width + EPS)
     normed = (rows_wide * factor_rows[..., None] * norm_scale).astype(jnp.bfloat16)
 
@@ -269,7 +271,7 @@
     rank_part = jnp.einsum(
         "tbnd,bdr->tbnr", blocked, query_first, preferred_element_type=jnp.float32
     )
-    rank_query = tree_sum(rank_part, ("gy", "gx")).astype(jnp.bfloat16)
+    rank_query = tree_sum(rank_part, ("gx",)).astype(jnp.bfloat16)
     delta_query = jnp.einsum(
         "tbnr,bre->tbne", rank_query, query_second, preferred_element_type=jnp.float32
     ).reshape(steps, request_count, -1)
@@ -320,7 +322,7 @@
         output_first,
         preferred_element_type=jnp.float32,
     )
-    rank_output = tree_sum(rank_part_out, ("gy", "gx")).astype(jnp.bfloat16)
+    rank_output = tree_sum(rank_part_out, ("gy",)).astype(jnp.bfloat16)
     delta_output = jnp.einsum(
         "tbnr,bre->tbne", rank_output, output_second, preferred_element_type=jnp.float32
     ).reshape(steps, request_count, -1)

time: 296 us -> 303 us (1.024)
  waiting for transfers between devices: 160 us -> 151 us
  other arithmetic: 19.2 us -> 28.1 us
  local copies, waits for them, and re-layouts: 32.3 us -> 36.9 us
    ppermute x13, waiting for transfers between devices: 50.9 us -> 24.5 us  [tree_sum(): value = value + lax.ppermute(value, axis_name, pairs)]
    ppermute x3, waiting for transfers between devices: 10.6 us -> 29 us  [split_half_gather(): lax.ppermute(value, axis_name, [(i, i ^ half) for i in range(axis_size)])]
    ppermute x2 -> x4, waiting for transfers between devices: 10.9 us -> 17 us  [doubling_gather(): lax.ppermute(held, axis_name, [(i, i ^ distance) for i in range(axis_size)])]
    ppermute x9, waiting for transfers between devices: 20 us -> 15.1 us  [split_half_gather(): lax.ppermute(pair, axis_name, [(i, i ^ offset) for i in range(axis_size)])]
    unnamed x59 -> x65, local copies, waits for them, and re-layouts: 16 us -> 19.6 us
  transfers between devices with their start and end apart: 43 -> 45, of which waited for: 34 -> 28; matrix products, arithmetic and copies ran while one was open for 7% -> 22% of each run, Pallas kernels for 0% -> 0%
where the time goes in v7:
time: 303 us; the launch traced here: 302 us
  waiting for transfers between devices  151 us (50%)
  starting transfers between devices  59.5 us (20%)
  local copies, waits for them, and re-layouts  36.9 us (12%)
  other arithmetic  28.1 us (9%)
  matrix products  20.5 us (7%)
  between operations  6.06 us (2%)
    ppermute x9, waiting for transfers between devices, split_half_scatter(): lax.ppermute(outgoing, axis_name, [(i, i ^ offset) for i in range(axis_si...  34.3 us
    ppermute x3, waiting for transfers between devices, split_half_gather(): lax.ppermute(value, axis_name, [(i, i ^ half) for i in range(axis_size)])  29 us
    ppermute x13, waiting for transfers between devices, tree_sum(): value = value + lax.ppermute(value, axis_name, pairs)  24.5 us
    unnamed x65, local copies, waits for them, and re-layouts  19.6 us
    ppermute x13, starting transfers between devices, tree_sum(): value = value + lax.ppermute(value, axis_name, pairs)  19.6 us
    ppermute x4, waiting for transfers between devices, doubling_gather(): lax.ppermute(held, axis_name, [(i, i ^ distance) for i in range(axis_size)])  17 us
    ppermute x9, waiting for transfers between devices, split_half_gather(): lax.ppermute(pair, axis_name, [(i, i ^ offset) for i in range(axis_size)])  15.1 us
    ppermute x2, waiting for transfers between devices, halving_scatter(): held = keep + lax.ppermute(give, axis_name, swap).astype(jnp.float32)  13.2 us
  transfers between devices with their start and end apart: 45, of which 28 were waited for; matrix products, arithmetic and copies ran while one was open for 22% of the time, Pallas kernels for 0%

profile of v7, /device:TPU:0, one launch (start us, length us, event | category | flops | bytes accessed | tf_op | source)
XLA Modules:
  0.0 302.1 jit_solution(220344840094142331)
XLA Ops:
  9.9 3.0 %collective-permute-start.2 = (f32[3,64]{1,0:T(4,128)S(1)}, f32[3,64]{1,0:T(4,128)S(1)}, u32[]{:S(2)}, u32[]{:S(2)}) collective-permute-start(f32[3,64]{1,0:T(4,128)S(1)} %multiply_reduce_fusion), channel_id=1, source_target_pairs={{0,4},{4,0},{8,12},{12,8},{16,20},{20,16},{24,28},{28,24},{1,5},{5... | collective-permute-start | bytes 2312 | tf_op jit(solution)/shard_map/ppermute | solution.py:139
  21.6 3.0 %collective-permute-start.4 = (f32[3,64]{1,0:T(4,128)S(1)}, f32[3,64]{1,0:T(4,128)S(1)}, u32[]{:S(2)}, u32[]{:S(2)}) collective-permute-start(f32[3,64]{1,0:T(4,128)S(1)} %add.455), channel_id=1, source_target_pairs={{0,16},{4,20},{8,24},{12,28},{16,0},{20,4},{24,8},{28,12},{1,17},{... | collective-permute-start | bytes 2312 | tf_op jit(solution)/shard_map/ppermute | solution.py:139
  31.7 17.0 %collective-permute-done.6 = f32[3,128]{1,0:T(4,128)S(1)} collective-permute-done((f32[3,128]{1,0:T(4,128)S(1)}, f32[3,128]{1,0:T(4,128)S(1)}, u32[]{:S(2)}, u32[]{:S(2)}) %collective-permute-start.6) | collective-permute-done | bytes 1568 | tf_op jit(solution)/shard_map/ppermute | solution.py:102
  53.5 4.4 %collective-permute-done.8 = bf16[2,1024,64]{1,2,0:T(8,128)(2,1)S(1)} collective-permute-done((bf16[2,1024,64]{1,2,0:T(8,128)(2,1)S(1)}, bf16[2,1024,64]{1,2,0:T(8,128)(2,1)S(1)}, u32[]{:S(2)}, u32[]{:S(2)}) %collective-permute-start.8) | collective-permute-done | bytes 262176 | tf_op jit(solution)/shard_map/ppermute | solution.py:139
  60.8 3.7 %collective-permute-done.9 = f32[3,2,128,64]{2,3,0,1:T(8,128)S(1)} collective-permute-done((f32[3,2,128,64]{2,3,0,1:T(8,128)S(1)}, f32[3,2,128,64]{2,3,0,1:T(8,128)S(1)}, u32[]{:S(2)}, u32[]{:S(2)}) %collective-permute-start.9) | collective-permute-done | bytes 196640 | tf_op jit(solution)/shard_map/ppermute | solution.py:139
  66.8 3.5 %collective-permute-done.10 = f32[3,2,128,64]{2,3,0,1:T(8,128)S(1)} collective-permute-done((f32[3,2,128,64]{2,3,0,1:T(8,128)S(1)}, f32[3,2,128,64]{2,3,0,1:T(8,128)S(1)}, u32[]{:S(2)}, u32[]{:S(2)}) %collective-permute-start.10) | collective-permute-done | bytes 196640 | tf_op jit(solution)/shard_map/ppermute | solution.py:139
  70.3 3.5 %collective-permute-start.11 = (f32[3,2,128,64]{2,3,0,1:T(8,128)S(1)}, f32[3,2,128,64]{2,3,0,1:T(8,128)S(1)}, u32[]{:S(2)}, u32[]{:S(2)}) collective-permute-start(f32[3,2,128,64]{2,3,0,1:T(8,128)S(1)} %add.472), channel_id=1, source_target_pairs={{0,16},{4,20},{8,24},{12,28},{16,0},{20,4},{24,8},{28,12},{1,17},{... | collective-permute-start | bytes 589832 | tf_op jit(solution)/shard_map/ppermute | solution.py:139
  75.4 4.2 %collective-permute-done.11 = f32[3,2,128,64]{2,3,0,1:T(8,128)S(1)} collective-permute-done((f32[3,2,128,64]{2,3,0,1:T(8,128)S(1)}, f32[3,2,128,64]{2,3,0,1:T(8,128)S(1)}, u32[]{:S(2)}, u32[]{:S(2)}) %collective-permute-start.11) | collective-permute-done | bytes 196640 | tf_op jit(solution)/shard_map/ppermute | solution.py:139
  82.7 3.5 %bitcast_add_fusion = f32[3,256,2048]{2,1,0:T(8,128)S(1)} fusion(f32[3,2,128,2048]{3,2,1,0:T(8,128)S(1)} %copy.78, bf16[1024,2048]{1,0:T(8,128)(2,1)S(1)} %copy-done.19, f32[1024]{0:T(1024)S(1)} %copy-done.15, f32[3,256]{1,0:T(4,128)S(1)} %fusion.105, bf16[3,128,1024]{2,1,0:T(8,128)(2,1)S(1)} %get-tuple-element.20, ...), kind=kOutput, calls=%fused_computation.4 | convolution fusion | flops 3228303360 | bytes 18357248 | tf_op jit(solution)/shard_map/tnd,de->tne/dot_general | solution.py:279
  93.9 14.5 %collective-permute-done.12 = bf16[2,1,32,2560]{3,2,1,0:T(8,128)(2,1)S(1)} collective-permute-done((bf16[2,1,32,2560]{3,2,1,0:T(8,128)(2,1)S(1)}, bf16[2,1,32,2560]{3,2,1,0:T(8,128)(2,1)S(1)}, u32[]{:S(2)}, u32[]{:S(2)}) %collective-permute-start.12) | collective-permute-done | bytes 327712 | tf_op jit(solution)/shard_map/ppermute | solution.py:84
  112.2 2.7 collective-permute-done.16
  114.9 2.8 collective-permute-start.21
  117.7 4.2 %collective-permute-done.17 = bf16[2,1,32,2560]{3,2,1,0:T(8,128)(2,1)S(1)} collective-permute-done((bf16[2,1,32,2560]{3,2,1,0:T(8,128)(2,1)S(1)}, bf16[2,1,32,2560]{3,2,1,0:T(8,128)(2,1)S(1)}, u32[]{:S(2)}, u32[]{:S(2)}) %collective-permute-start.17) | collective-permute-done | bytes 327712 | tf_op jit(solution)/shard_map/ppermute | solution.py:84
  122.0 3.8 %collective-permute-done.18 = bf16[2,1,32,2560]{3,2,1,0:T(8,128)(2,1)S(1)} collective-permute-done((bf16[2,1,32,2560]{3,2,1,0:T(8,128)(2,1)S(1)}, bf16[2,1,32,2560]{3,2,1,0:T(8,128)(2,1)S(1)}, u32[]{:S(2)}, u32[]{:S(2)}) %collective-permute-start.18) | collective-permute-done | bytes 327712 | tf_op jit(solution)/shard_map/ppermute | solution.py:84
  129.0 3.5 %collective-permute-done.21 = bf16[2,1,32,2560]{3,2,1,0:T(8,128)(2,1)S(1)} collective-permute-done((bf16[2,1,32,2560]{3,2,1,0:T(8,128)(2,1)S(1)}, bf16[2,1,32,2560]{3,2,1,0:T(8,128)(2,1)S(1)}, u32[]{:S(2)}, u32[]{:S(2)}) %collective-permute-start.21) | collective-permute-done | bytes 327712 | tf_op jit(solution)/shard_map/ppermute | solution.py:84
  132.6 5.6 %collective-permute-done.22 = bf16[2,1,32,2560]{3,2,1,0:T(8,128)(2,1)S(1)} collective-permute-done((bf16[2,1,32,2560]{3,2,1,0:T(8,128)(2,1)S(1)}, bf16[2,1,32,2560]{3,2,1,0:T(8,128)(2,1)S(1)}, u32[]{:S(2)}, u32[]{:S(2)}) %collective-permute-start.22) | collective-permute-done | bytes 327712 | tf_op jit(solution)/shard_map/ppermute | solution.py:84
  139.7 5.2 %collective-permute-done.23 = bf16[1,32,2560]{2,1,0:T(8,128)(2,1)S(1)} collective-permute-done((bf16[1,32,2560]{2,1,0:T(8,128)(2,1)S(1)}, bf16[1,32,2560]{2,1,0:T(8,128)(2,1)S(1)}, u32[]{:S(2)}, u32[]{:S(2)}) %collective-permute-start.23) | collective-permute-done | bytes 163872 | tf_op jit(solution)/shard_map/ppermute | solution.py:89
  145.9 3.6 %all-to-all-start = ((bf16[3,4,8,1,2560]{4,2,3,0,1:T(8,128)(2,1)}), bf16[3,4,8,1,2560]{4,2,3,0,1:T(8,128)(2,1)S(1)}, u32[]{:S(2)}, u32[]{:S(2)}) async-start(bf16[3,4,8,1,2560]{4,2,3,0,1:T(8,128)(2,1)} %copy.83), calls=%async_computation | async-start | bytes 983040 | tf_op jit(solution)/shard_map/all_to_all | solution.py:289
  150.5 7.5 %all-to-all-done = bf16[3,4,8,1,2560]{4,2,3,0,1:T(8,128)(2,1)S(1)} async-done(((bf16[3,4,8,1,2560]{4,2,3,0,1:T(8,128)(2,1)}), bf16[3,4,8,1,2560]{4,2,3,0,1:T(8,128)(2,1)S(1)}, u32[]{:S(2)}, u32[]{:S(2)}) %all-to-all-start) | async-done | bytes 491552 | tf_op jit(solution)/shard_map/all_to_all | solution.py:289
  160.5 4.6 %fusion.121 = (f32[8,8,24]{2,1,0:T(8,128)S(1)}, f32[8,8,24,256]{3,2,1,0:T(8,128)S(1)}) fusion(pred[8,256]{1,0:T(8,128)(4,1)S(1)} %iota_compare_fusion, bf16[8,256,1024]{2,1,0:T(8,128)(2,1)} %param.28, bf16[3,8,8,8,64]{4,3,2,1,0:T(8,128)(2,1)S(1)} %bitcast.228, bf16[3,8,8,8,64]{4,3,2,1,0:T(8,128)(2,1)S(1)} %bitcast.226), kind=kOutput, calls=%fused_computation.251 | convolution fusion | flops 102627840 | bytes 6168576 | tf_op jit(solution)/shard_map/rhqd,rchd->rhqc/dot_general | solution.py:186
  169.5 3.7 %all-to-all-start.1 = ((bf16[3,1,8,4,2048]{4,2,0,1,3:T(8,128)(2,1)}), bf16[3,1,8,4,2048]{4,2,0,1,3:T(8,128)(2,1)S(1)}, u32[]{:S(2)}, u32[]{:S(2)}) async-start(bf16[3,1,8,4,2048]{4,2,0,1,3:T(8,128)(2,1)} %copy.94), calls=%async_computation.1 | async-start | bytes 786432 | tf_op jit(solution)/shard_map/all_to_all | solution.py:315
  175.3 5.1 %all-to-all-done.1 = bf16[3,1,8,4,2048]{4,2,0,1,3:T(8,128)(2,1)S(1)} async-done(((bf16[3,1,8,4,2048]{4,2,0,1,3:T(8,128)(2,1)}), bf16[3,1,8,4,2048]{4,2,0,1,3:T(8,128)(2,1)S(1)}, u32[]{:S(2)}, u32[]{:S(2)}) %all-to-all-start.1) | async-done | bytes 393248 | tf_op jit(solution)/shard_map/all_to_all | solution.py:315
  185.1 26.7 %collective-permute-done.32 = bf16[1,32,2048]{2,1,0:T(8,128)(2,1)S(1)} collective-permute-done((bf16[1,32,2048]{2,1,0:T(8,128)(2,1)S(1)}, bf16[1,32,2048]{2,1,0:T(8,128)(2,1)S(1)}, u32[]{:S(2)}, u32[]{:S(2)}) %collective-permute-start.32) | collective-permute-done | bytes 131104 | tf_op jit(solution)/shard_map/ppermute | solution.py:116
  220.1 3.0 collective-permute-done.34
  223.7 6.1 %collective-permute-done.35 = bf16[2,1,32,2048]{3,2,1,0:T(8,128)(2,1)S(1)} collective-permute-done((bf16[2,1,32,2048]{3,2,1,0:T(8,128)(2,1)S(1)}, bf16[2,1,32,2048]{3,2,1,0:T(8,128)(2,1)S(1)}, u32[]{:S(2)}, u32[]{:S(2)}) %collective-permute-start.35) | collective-permute-done | bytes 262176 | tf_op jit(solution)/shard_map/ppermute | solution.py:121
  234.5 2.9 collective-permute-start.27
  238.3 2.9 collective-permute-done.31
  258.3 2.9 gather_fusion
  269.7 4.3 %collective-permute-done.40 = f32[3,2,128,64]{2,3,0,1:T(8,128)S(1)} collective-permute-done((f32[3,2,128,64]{2,3,0,1:T(8,128)S(1)}, f32[3,2,128,64]{2,3,0,1:T(8,128)S(1)}, u32[]{:S(2)}, u32[]{:S(2)}) %collective-permute-start.40) | collective-permute-done | bytes 196640 | tf_op jit(solution)/shard_map/ppermute | solution.py:139
  277.2 3.4 %bitcast_add_fusion.1 = f32[3,256,1024]{2,1,0:T(8,128)S(1)} fusion(f32[3,2,128,1024]{3,2,1,0:T(8,128)S(1)} %copy.96, bf16[2048,1024]{1,0:T(8,128)(2,1)S(1)} %copy-done.21, bf16[1,256,2048]{2,1,0:T(8,128)(2,1)S(1)} %bitcast.239, bf16[1,256,2048]{2,1,0:T(8,128)(2,1)S(1)} %bitcast.237, bf16[1,256,2048]{2,1,0:T(8,128)(2,1)S(1)} %bitcast.235), kind=kOutput, calls=%fused_computation.27 | convolution fusion | flops 3225157632 | bytes 13631488 | tf_op jit(solution)/shard_map/tnq,qe->tne/dot_general | solution.py:330
  282.2 3.7 %collective-permute-done.41 = f32[3,2,64,1024]{3,2,0,1:T(8,128)} collective-permute-done((f32[3,2,64,1024]{3,2,0,1:T(8,128)}, f32[3,2,64,1024]{3,2,0,1:T(8,128)}, u32[]{:S(2)}, u32[]{:S(2)}) %collective-permute-start.41) | collective-permute-done | bytes 1572896 | tf_op jit(solution)/shard_map/ppermute | solution.py:160
  290.6 9.5 %collective-permute-done.42 = bf16[3,1,64,1024]{3,2,0,1:T(8,128)(2,1)S(1)} collective-permute-done((bf16[3,1,64,1024]{3,2,0,1:T(8,128)(2,1)S(1)}, bf16[3,1,64,1024]{3,2,0,1:T(8,128)(2,1)S(1)}, u32[]{:S(2)}, u32[]{:S(2)}) %collective-permute-start.42) | collective-permute-done | bytes 393248 | tf_op jit(solution)/shard_map/ppermute | solution.py:160
  (243 shorter events, 118.1 us)
Async XLA Ops:
  0.0 26.2 %collective-permute-start = (bf16[3,64,1024]{2,1,0:T(8,128)(2,1)}, bf16[3,64,1024]{2,1,0:T(8,128)(2,1)}, u32[]{:S(2)}, u32[]{:S(2)}) collective-permute-start(bf16[3,64,1024]{2,1,0:T(8,128)(2,1)} %param.16), channel_id=1, source_target_pairs={{0,1},{1,0},{2,3},{3,2},{4,5},{5,4},{6,7},{7,6},{8,9},{9,8},{10,11... | collective-permute-start | bytes 1179656 | tf_op jit(solution)/shard_map/ppermute | solution.py:102
  8.7 40.1 %collective-permute-start.7 = (bf16[2,1024,64]{1,2,0:T(8,128)(2,1)}, bf16[2,1024,64]{1,2,0:T(8,128)(2,1)}, u32[]{:S(2)}, u32[]{:S(2)}) collective-permute-start(bf16[2,1024,64]{1,2,0:T(8,128)(2,1)} %pad_maximum_fusion.13), channel_id=1, source_target_pairs={{0,1},{1,0},{2,3},{3,2},{4,5},{5,4},{6,7},{7,6},{8,9},{9,8},{10,11... | collective-permute-start | bytes 786440 | tf_op jit(solution)/shard_map/ppermute | solution.py:139
  14.9 134.7 %collective-permute-start.36 = (bf16[2,2048,64]{1,2,0:T(8,128)(2,1)}, bf16[2,2048,64]{1,2,0:T(8,128)(2,1)S(1)}, u32[]{:S(2)}, u32[]{:S(2)}) collective-permute-start(bf16[2,2048,64]{1,2,0:T(8,128)(2,1)} %pad_maximum_fusion.2), channel_id=1, source_target_pairs={{0,4},{4,0},{8,12},{12,8},{16,20},{20,16},{24,28},{28,24},{1,5},{5... | collective-permute-start | bytes 1572872 | tf_op jit(solution)/shard_map/ppermute | solution.py:139
  28.3 23.3 %collective-permute-start.1 = (bf16[3,128,1024]{2,1,0:T(8,128)(2,1)}, bf16[3,128,1024]{2,1,0:T(8,128)(2,1)}, u32[]{:S(2)}, u32[]{:S(2)}) collective-permute-start(bf16[3,128,1024]{2,1,0:T(8,128)(2,1)} %pad_maximum_fusion.1), channel_id=1, source_target_pairs={{0,2},{1,3},{2,0},{3,1},{4,6},{5,7},{6,4},{7,5},{8,10},{9,11},{10,... | collective-permute-start | bytes 2359304 | tf_op jit(solution)/shard_map/ppermute | solution.py:102
  30.2 18.5 %collective-permute-start.6 = (f32[3,128]{1,0:T(4,128)S(1)}, f32[3,128]{1,0:T(4,128)S(1)}, u32[]{:S(2)}, u32[]{:S(2)}) collective-permute-start(f32[3,128]{1,0:T(4,128)S(1)} %pad_maximum_fusion.17), channel_id=1, source_target_pairs={{0,2},{1,3},{2,0},{3,1},{4,6},{5,7},{6,4},{7,5},{8,10},{9,11},{10,... | collective-permute-start | bytes 4616 | tf_op jit(solution)/shard_map/ppermute | solution.py:102
  87.9 20.5 %collective-permute-start.12 = (bf16[2,1,32,2560]{3,2,1,0:T(8,128)(2,1)S(1)}, bf16[2,1,32,2560]{3,2,1,0:T(8,128)(2,1)S(1)}, u32[]{:S(2)}, u32[]{:S(2)}) collective-permute-start(bf16[2,1,32,2560]{3,2,1,0:T(8,128)(2,1)S(1)} %pad_maximum_fusion.4), channel_id=1, source_target_pairs={{0,4},{4,0},{8,12},{12,8},{16,20},{20,16},{24,28},{28,24},{1,5},{5... | collective-permute-start | bytes 983048 | tf_op jit(solution)/shard_map/ppermute | solution.py:84
  89.5 19.5 %collective-permute-start.13 = (bf16[2,1,32,2560]{3,2,1,0:T(8,128)(2,1)S(1)}, bf16[2,1,32,2560]{3,2,1,0:T(8,128)(2,1)S(1)}, u32[]{:S(2)}, u32[]{:S(2)}) collective-permute-start(bf16[2,1,32,2560]{3,2,1,0:T(8,128)(2,1)S(1)} %pad_maximum_fusion.5), channel_id=1, source_target_pairs={{0,8},{4,12},{8,0},{12,4},{16,24},{20,28},{24,16},{28,20},{1,9},{5... | collective-permute-start | bytes 983048 | tf_op jit(solution)/shard_map/ppermute | solution.py:84
  89.9 21.2 %collective-permute-start.14 = (bf16[2,1,32,2560]{3,2,1,0:T(8,128)(2,1)S(1)}, bf16[2,1,32,2560]{3,2,1,0:T(8,128)(2,1)S(1)}, u32[]{:S(2)}, u32[]{:S(2)}) collective-permute-start(bf16[2,1,32,2560]{3,2,1,0:T(8,128)(2,1)S(1)} %pad_maximum_fusion.6), channel_id=1, source_target_pairs={{0,12},{4,8},{8,4},{12,0},{16,28},{20,24},{24,20},{28,16},{1,13},{... | collective-permute-start | bytes 983048 | tf_op jit(solution)/shard_map/ppermute | solution.py:84
  92.2 22.7 %collective-permute-start.16 = (bf16[2,1,32,2560]{3,2,1,0:T(8,128)(2,1)S(1)}, bf16[2,1,32,2560]{3,2,1,0:T(8,128)(2,1)S(1)}, u32[]{:S(2)}, u32[]{:S(2)}) collective-permute-start(bf16[2,1,32,2560]{3,2,1,0:T(8,128)(2,1)S(1)} %pad_maximum_fusion.7), channel_id=1, source_target_pairs={{0,4},{4,0},{8,12},{12,8},{16,20},{20,16},{24,28},{28,24},{1,5},{5... | collective-permute-start | bytes 983048 | tf_op jit(solution)/shard_map/ppermute | solution.py:84
  108.4 13.6 %collective-permute-start.17 = (bf16[2,1,32,2560]{3,2,1,0:T(8,128)(2,1)S(1)}, bf16[2,1,32,2560]{3,2,1,0:T(8,128)(2,1)S(1)}, u32[]{:S(2)}, u32[]{:S(2)}) collective-permute-start(bf16[2,1,32,2560]{3,2,1,0:T(8,128)(2,1)S(1)} %pad_maximum_fusion.8), channel_id=1, source_target_pairs={{0,8},{4,12},{8,0},{12,4},{16,24},{20,28},{24,16},{28,20},{1,9},{5... | collective-permute-start | bytes 983048 | tf_op jit(solution)/shard_map/ppermute | solution.py:84
  109.0 16.9 %collective-permute-start.18 = (bf16[2,1,32,2560]{3,2,1,0:T(8,128)(2,1)S(1)}, bf16[2,1,32,2560]{3,2,1,0:T(8,128)(2,1)S(1)}, u32[]{:S(2)}, u32[]{:S(2)}) collective-permute-start(bf16[2,1,32,2560]{3,2,1,0:T(8,128)(2,1)S(1)} %pad_maximum_fusion.9), channel_id=1, source_target_pairs={{0,12},{4,8},{8,4},{12,0},{16,28},{20,24},{24,20},{28,16},{1,13},{... | collective-permute-start | bytes 983048 | tf_op jit(solution)/shard_map/ppermute | solution.py:84
  111.1 17.1 %collective-permute-start.20 = (bf16[2,1,32,2560]{3,2,1,0:T(8,128)(2,1)S(1)}, bf16[2,1,32,2560]{3,2,1,0:T(8,128)(2,1)S(1)}, u32[]{:S(2)}, u32[]{:S(2)}) collective-permute-start(bf16[2,1,32,2560]{3,2,1,0:T(8,128)(2,1)S(1)} %pad_maximum_fusion.10), channel_id=1, source_target_pairs={{0,4},{4,0},{8,12},{12,8},{16,20},{20,16},{24,28},{28,24},{1,5},{5... | collective-permute-start | bytes 983048 | tf_op jit(solution)/shard_map/ppermute | solution.py:84
  114.9 17.6 %collective-permute-start.21 = (bf16[2,1,32,2560]{3,2,1,0:T(8,128)(2,1)S(1)}, bf16[2,1,32,2560]{3,2,1,0:T(8,128)(2,1)S(1)}, u32[]{:S(2)}, u32[]{:S(2)}) collective-permute-start(bf16[2,1,32,2560]{3,2,1,0:T(8,128)(2,1)S(1)} %pad_maximum_fusion.11), channel_id=1, source_target_pairs={{0,8},{4,12},{8,0},{12,4},{16,24},{20,28},{24,16},{28,20},{1,9},{5... | collective-permute-start | bytes 983048 | tf_op jit(solution)/shard_map/ppermute | solution.py:84
  122.0 16.2 %collective-permute-start.22 = (bf16[2,1,32,2560]{3,2,1,0:T(8,128)(2,1)S(1)}, bf16[2,1,32,2560]{3,2,1,0:T(8,128)(2,1)S(1)}, u32[]{:S(2)}, u32[]{:S(2)}) collective-permute-start(bf16[2,1,32,2560]{3,2,1,0:T(8,128)(2,1)S(1)} %pad_maximum_fusion.12), channel_id=1, source_target_pairs={{0,12},{4,8},{8,4},{12,0},{16,28},{20,24},{24,20},{28,16},{1,13},{... | collective-permute-start | bytes 983048 | tf_op jit(solution)/shard_map/ppermute | solution.py:84
  125.9 13.7 %collective-permute-start.15 = (bf16[1,32,2560]{2,1,0:T(8,128)(2,1)S(1)}, bf16[1,32,2560]{2,1,0:T(8,128)(2,1)S(1)}, u32[]{:S(2)}, u32[]{:S(2)}) collective-permute-start(bf16[1,32,2560]{2,1,0:T(8,128)(2,1)S(1)} %fusion.88), channel_id=1, source_target_pairs={{0,16},{4,20},{8,24},{12,28},{16,0},{20,4},{24,8},{28,12},{1,17},{... | collective-permute-start | bytes 491528 | tf_op jit(solution)/shard_map/ppermute | solution.py:89
  128.3 11.4 %collective-permute-start.19 = (bf16[1,32,2560]{2,1,0:T(8,128)(2,1)S(1)}, bf16[1,32,2560]{2,1,0:T(8,128)(2,1)S(1)}, u32[]{:S(2)}, u32[]{:S(2)}) collective-permute-start(bf16[1,32,2560]{2,1,0:T(8,128)(2,1)S(1)} %fusion.90), channel_id=1, source_target_pairs={{0,16},{4,20},{8,24},{12,28},{16,0},{20,4},{24,8},{28,12},{1,17},{... | collective-permute-start | bytes 491528 | tf_op jit(solution)/shard_map/ppermute | solution.py:89
  145.9 12.1 %all-to-all-start = ((bf16[3,4,8,1,2560]{4,2,3,0,1:T(8,128)(2,1)}), bf16[3,4,8,1,2560]{4,2,3,0,1:T(8,128)(2,1)S(1)}, u32[]{:S(2)}, u32[]{:S(2)}) async-start(bf16[3,4,8,1,2560]{4,2,3,0,1:T(8,128)(2,1)} %copy.83), calls=%async_computation | async-start | bytes 983040 | tf_op jit(solution)/shard_map/all_to_all | solution.py:289
  150.4 22.7 %collective-permute-start.37 = (bf16[2,2048,64]{1,2,0:T(8,128)(2,1)}, bf16[2,2048,64]{1,2,0:T(8,128)(2,1)}, u32[]{:S(2)}, u32[]{:S(2)}) collective-permute-start(bf16[2,2048,64]{1,2,0:T(8,128)(2,1)} %fusion.117), channel_id=1, source_target_pairs={{0,8},{4,12},{8,0},{12,4},{16,24},{20,28},{24,16},{28,20},{1,9},{5... | collective-permute-start | bytes 1572872 | tf_op jit(solution)/shard_map/ppermute | solution.py:139
  169.5 10.9 %all-to-all-start.1 = ((bf16[3,1,8,4,2048]{4,2,0,1,3:T(8,128)(2,1)}), bf16[3,1,8,4,2048]{4,2,0,1,3:T(8,128)(2,1)S(1)}, u32[]{:S(2)}, u32[]{:S(2)}) async-start(bf16[3,1,8,4,2048]{4,2,0,1,3:T(8,128)(2,1)} %copy.94), calls=%async_computation.1 | async-start | bytes 786432 | tf_op jit(solution)/shard_map/all_to_all | solution.py:315
  174.3 88.6 %collective-permute-start.38 = (bf16[2,2048,64]{1,2,0:T(8,128)(2,1)S(1)}, bf16[2,2048,64]{1,2,0:T(8,128)(2,1)}, u32[]{:S(2)}, u32[]{:S(2)}) collective-permute-start(bf16[2,2048,64]{1,2,0:T(8,128)(2,1)S(1)} %fusion.123), channel_id=1, source_target_pairs={{0,16},{4,20},{8,24},{12,28},{16,0},{20,4},{24,8},{28,12},{1,17},{... | collective-permute-start | bytes 1572872 | tf_op jit(solution)/shard_map/ppermute | solution.py:139
  180.5 31.3 %collective-permute-start.32 = (bf16[1,32,2048]{2,1,0:T(8,128)(2,1)S(1)}, bf16[1,32,2048]{2,1,0:T(8,128)(2,1)S(1)}, u32[]{:S(2)}, u32[]{:S(2)}) collective-permute-start(bf16[1,32,2048]{2,1,0:T(8,128)(2,1)S(1)} %get-tuple-element.48), channel_id=1, source_target_pairs={{0,16},{4,20},{8,24},{12,28},{16,0},{20,4},{24,8},{28,12},{1,17},{... | collective-permute-start | bytes 393224 | tf_op jit(solution)/shard_map/ppermute | solution.py:116
  182.1 32.4 %collective-permute-start.28 = (bf16[1,32,2048]{2,1,0:T(8,128)(2,1)S(1)}, bf16[1,32,2048]{2,1,0:T(8,128)(2,1)S(1)}, u32[]{:S(2)}, u32[]{:S(2)}) collective-permute-start(bf16[1,32,2048]{2,1,0:T(8,128)(2,1)S(1)} %get-tuple-element.47), channel_id=1, source_target_pairs={{0,16},{4,20},{8,24},{12,28},{16,0},{20,4},{24,8},{28,12},{1,17},{... | collective-permute-start | bytes 393224 | tf_op jit(solution)/shard_map/ppermute | solution.py:116
  184.1 33.3 %collective-permute-start.24 = (bf16[1,32,2048]{2,1,0:T(8,128)(2,1)S(1)}, bf16[1,32,2048]{2,1,0:T(8,128)(2,1)S(1)}, u32[]{:S(2)}, u32[]{:S(2)}) collective-permute-start(bf16[1,32,2048]{2,1,0:T(8,128)(2,1)S(1)} %get-tuple-element.46), channel_id=1, source_target_pairs={{0,16},{4,20},{8,24},{12,28},{16,0},{20,4},{24,8},{28,12},{1,17},{... | collective-permute-start | bytes 393224 | tf_op jit(solution)/shard_map/ppermute | solution.py:116
  213.5 9.5 %collective-permute-start.34 = (bf16[2,1,32,2048]{3,2,1,0:T(8,128)(2,1)S(1)}, bf16[2,1,32,2048]{3,2,1,0:T(8,128)(2,1)S(1)}, u32[]{:S(2)}, u32[]{:S(2)}) collective-permute-start(bf16[2,1,32,2048]{3,2,1,0:T(8,128)(2,1)S(1)} %pad_maximum_fusion.16), channel_id=1, source_target_pairs={{0,8},{4,12},{8,0},{12,4},{16,24},{20,28},{24,16},{28,20},{1,9},{5... | collective-permute-start | bytes 786440 | tf_op jit(solution)/shard_map/ppermute | solution.py:121
  214.6 15.3 %collective-permute-start.35 = (bf16[2,1,32,2048]{3,2,1,0:T(8,128)(2,1)S(1)}, bf16[2,1,32,2048]{3,2,1,0:T(8,128)(2,1)S(1)}, u32[]{:S(2)}, u32[]{:S(2)}) collective-permute-start(bf16[2,1,32,2048]{3,2,1,0:T(8,128)(2,1)S(1)} %pad_maximum_fusion.16), channel_id=1, source_target_pairs={{0,12},{4,8},{8,4},{12,0},{16,28},{20,24},{24,20},{28,16},{1,13},{... | collective-permute-start | bytes 786440 | tf_op jit(solution)/shard_map/ppermute | solution.py:121
  217.4 15.8 %collective-permute-start.29 = (bf16[2,1,32,2048]{3,2,1,0:T(8,128)(2,1)}, bf16[2,1,32,2048]{3,2,1,0:T(8,128)(2,1)}, u32[]{:S(2)}, u32[]{:S(2)}) collective-permute-start(bf16[2,1,32,2048]{3,2,1,0:T(8,128)(2,1)} %pad_maximum_fusion.15), channel_id=1, source_target_pairs={{0,4},{4,0},{8,12},{12,8},{16,20},{20,16},{24,28},{28,24},{1,5},{5... | collective-permute-start | bytes 786440 | tf_op jit(solution)/shard_map/ppermute | solution.py:121
  220.0 14.5 %collective-permute-start.30 = (bf16[2,1,32,2048]{3,2,1,0:T(8,128)(2,1)}, bf16[2,1,32,2048]{3,2,1,0:T(8,128)(2,1)}, u32[]{:S(2)}, u32[]{:S(2)}) collective-permute-start(bf16[2,1,32,2048]{3,2,1,0:T(8,128)(2,1)} %pad_maximum_fusion.15), channel_id=1, source_target_pairs={{0,8},{4,12},{8,0},{12,4},{16,24},{20,28},{24,16},{28,20},{1,9},{5... | collective-permute-start | bytes 786440 | tf_op jit(solution)/shard_map/ppermute | solution.py:121
  223.0 18.2 %collective-permute-start.31 = (bf16[2,1,32,2048]{3,2,1,0:T(8,128)(2,1)}, bf16[2,1,32,2048]{3,2,1,0:T(8,128)(2,1)}, u32[]{:S(2)}, u32[]{:S(2)}) collective-permute-start(bf16[2,1,32,2048]{3,2,1,0:T(8,128)(2,1)} %pad_maximum_fusion.15), channel_id=1, source_target_pairs={{0,12},{4,8},{8,4},{12,0},{16,28},{20,24},{24,20},{28,16},{1,13},{... | collective-permute-start | bytes 786440 | tf_op jit(solution)/shard_map/ppermute | solution.py:121
  229.8 18.0 %collective-permute-start.25 = (bf16[2,1,32,2048]{3,2,1,0:T(8,128)(2,1)S(1)}, bf16[2,1,32,2048]{3,2,1,0:T(8,128)(2,1)S(1)}, u32[]{:S(2)}, u32[]{:S(2)}) collective-permute-start(bf16[2,1,32,2048]{3,2,1,0:T(8,128)(2,1)S(1)} %pad_maximum_fusion.14), channel_id=1, source_target_pairs={{0,4},{4,0},{8,12},{12,8},{16,20},{20,16},{24,28},{28,24},{1,5},{5... | collective-permute-start | bytes 786440 | tf_op jit(solution)/shard_map/ppermute | solution.py:121
  233.2 15.3 %collective-permute-start.26 = (bf16[2,1,32,2048]{3,2,1,0:T(8,128)(2,1)S(1)}, bf16[2,1,32,2048]{3,2,1,0:T(8,128)(2,1)}, u32[]{:S(2)}, u32[]{:S(2)}) collective-permute-start(bf16[2,1,32,2048]{3,2,1,0:T(8,128)(2,1)S(1)} %pad_maximum_fusion.14), channel_id=1, source_target_pairs={{0,8},{4,12},{8,0},{12,4},{16,24},{20,28},{24,16},{28,20},{1,9},{5... | collective-permute-start | bytes 786440 | tf_op jit(solution)/shard_map/ppermute | solution.py:121
  234.5 17.8 %collective-permute-start.27 = (bf16[2,1,32,2048]{3,2,1,0:T(8,128)(2,1)S(1)}, bf16[2,1,32,2048]{3,2,1,0:T(8,128)(2,1)}, u32[]{:S(2)}, u32[]{:S(2)}) collective-permute-start(bf16[2,1,32,2048]{3,2,1,0:T(8,128)(2,1)S(1)} %pad_maximum_fusion.14), channel_id=1, source_target_pairs={{0,12},{4,8},{8,4},{12,0},{16,28},{20,24},{24,20},{28,16},{1,13},{... | collective-permute-start | bytes 786440 | tf_op jit(solution)/shard_map/ppermute | solution.py:121
  288.9 11.2 %collective-permute-start.42 = (bf16[3,1,64,1024]{3,2,0,1:T(8,128)(2,1)S(1)}, bf16[3,1,64,1024]{3,2,0,1:T(8,128)(2,1)S(1)}, u32[]{:S(2)}, u32[]{:S(2)}) collective-permute-start(bf16[3,1,64,1024]{3,2,0,1:T(8,128)(2,1)S(1)} %dynamic-slice_convert_fusion), channel_id=1, source_target_pairs={{0,2},{1,3},{2,0},{3,1},{4,6},{5,7},{6,4},{7,5},{8,10},{9,11},{10,... | collective-permute-start | bytes 1179656 | tf_op jit(solution)/shard_map/ppermute | solution.py:160
  (36 other events, 274.8 us)

commit v8 on v6

--- a/solution.py
+++ b/solution.py
@@ -256,7 +256,7 @@
     norm_scale = norm_gain.astype(jnp.float32)
     query_first = pick_adapters(query_down, block_adapter, index_second)
     query_second = pick_adapters(query_up, block_adapter, index_first)
-    output_first = pick_adapters(output_down, block_adapter, index_first)
+    output_first = tree_sum(pick_adapters(output_down, block_adapter, index_first), ("gx",))
     output_second = pick_adapters(output_up, block_adapter, index_second)
 
     rows_all = doubling_gather(inputs, "gy", across_second, 1)
@@ -282,6 +282,7 @@
         "tnd,de->tne", normed, value_weight, preferred_element_type=jnp.float32
     )
     joined = jnp.concatenate([part_query, part_key, part_value], axis=-1)
+    output_first, joined = lax.optimization_barrier((output_first, joined))
     summed = split_half_scatter_steps(joined, "gx", across_first).astype(jnp.bfloat16)
     chunk_rows = summed.shape[1] // across_second
     spread = lax.all_to_all(
@@ -320,7 +321,7 @@
         output_first,
         preferred_element_type=jnp.float32,
     )
-    rank_output = tree_sum(rank_part_out, ("gy", "gx")).astype(jnp.bfloat16)
+    rank_output = tree_sum(rank_part_out, ("gy",)).astype(jnp.bfloat16)
     delta_output = jnp.einsum(
         "tbnr,bre->tbne", rank_output, output_second, preferred_element_type=jnp.float32
     ).reshape(steps, request_count, -1)

time: 296 us -> 305 us (1.030)
  local copies, waits for them, and re-layouts: 32.3 us -> 36.3 us
  other arithmetic: 19.2 us -> 22.5 us
    ppermute x9, waiting for transfers between devices: 33.4 us -> 44.2 us  [split_half_scatter(): lax.ppermute(outgoing, axis_name, [(i, i ^ offset) for i in range(axis_si...]
    ppermute x13, waiting for transfers between devices: 50.9 us -> 42 us  [tree_sum(): value = value + lax.ppermute(value, axis_name, pairs)]
    ppermute x13, starting transfers between devices: 17.3 us -> 25 us  [tree_sum(): value = value + lax.ppermute(value, axis_name, pairs)]
    ppermute x9, starting transfers between devices: 13.3 us -> 6.31 us  [split_half_scatter(): lax.ppermute(outgoing, axis_name, [(i, i ^ offset) for i in range(axis_si...]
    unnamed x59 -> x57, local copies, waits for them, and re-layouts: 16 us -> 19.3 us
    ppermute x3, starting transfers between devices: 5.28 us -> 2.18 us  [split_half_scatter(): lax.ppermute(mirror.astype(jnp.bfloat16), axis_name, [(i, i ^ half) for i...]
  transfers between devices with their start and end apart: 43 -> 43, of which waited for: 34 -> 29; matrix products, arithmetic and copies ran while one was open for 7% -> 10% of each run, Pallas kernels for 0% -> 0%
where the time goes in v8:
time: 305 us; the launch traced here: 303 us
  waiting for transfers between devices  163 us (53%)
  starting transfers between devices  55 us (18%)
  local copies, waits for them, and re-layouts  36.3 us (12%)
  other arithmetic  22.5 us (7%)
  matrix products  20.3 us (7%)
  between operations  6.07 us (2%)
    ppermute x9, waiting for transfers between devices, split_half_scatter(): lax.ppermute(outgoing, axis_name, [(i, i ^ offset) for i in range(axis_si...  44.2 us
    ppermute x13, waiting for transfers between devices, tree_sum(): value = value + lax.ppermute(value, axis_name, pairs)  42 us
    ppermute x13, starting transfers between devices, tree_sum(): value = value + lax.ppermute(value, axis_name, pairs)  25 us
    unnamed x57, local copies, waits for them, and re-layouts  19.3 us
    ppermute x9, waiting for transfers between devices, split_half_gather(): lax.ppermute(pair, axis_name, [(i, i ^ offset) for i in range(axis_size)])  17.4 us
    ppermute x2, waiting for transfers between devices, halving_scatter(): held = keep + lax.ppermute(give, axis_name, swap).astype(jnp.float32)  14.4 us
    ppermute x2, waiting for transfers between devices, doubling_gather(): lax.ppermute(held, axis_name, [(i, i ^ distance) for i in range(axis_size)])  11.4 us
    ppermute x3, waiting for transfers between devices, split_half_gather(): lax.ppermute(value, axis_name, [(i, i ^ half) for i in range(axis_size)])  10.8 us
  transfers between devices with their start and end apart: 43, of which 29 were waited for; matrix products, arithmetic and copies ran while one was open for 10% of the time, Pallas kernels for 0%

profile of v8, /device:TPU:0, one launch (start us, length us, event | category | flops | bytes accessed | tf_op | source)
XLA Modules:
  0.0 303.4 jit_solution(9407871903040133813)
XLA Ops:
  17.6 11.4 %collective-permute-done.4 = bf16[3,128,1024]{2,1,0:T(8,128)(2,1)} collective-permute-done((bf16[3,128,1024]{2,1,0:T(8,128)(2,1)S(1)}, bf16[3,128,1024]{2,1,0:T(8,128)(2,1)}, u32[]{:S(2)}, u32[]{:S(2)}) %collective-permute-start.4) | collective-permute-done | bytes 786464 | tf_op jit(solution)/shard_map/ppermute | solution.py:102
  38.2 2.8 collective-permute-start.7
  41.4 6.4 %collective-permute-done.7 = f32[3,256]{1,0:T(4,128)S(1)} collective-permute-done((f32[3,256]{1,0:T(4,128)S(1)}, f32[3,256]{1,0:T(4,128)S(1)}, u32[]{:S(2)}, u32[]{:S(2)}) %collective-permute-start.7) | collective-permute-done | bytes 3104 | tf_op jit(solution)/shard_map/ppermute | solution.py:139
  51.7 5.3 %collective-permute-done.9 = f32[3,2,128,64]{2,3,0,1:T(8,128)S(1)} collective-permute-done((f32[3,2,128,64]{2,3,0,1:T(8,128)S(1)}, f32[3,2,128,64]{2,3,0,1:T(8,128)S(1)}, u32[]{:S(2)}, u32[]{:S(2)}) %collective-permute-start.9) | collective-permute-done | bytes 196640 | tf_op jit(solution)/shard_map/ppermute | solution.py:139
  59.8 3.4 %collective-permute-start.2 = (bf16[2,2048,64]{1,2,0:T(8,128)(2,1)S(1)}, bf16[2,2048,64]{1,2,0:T(8,128)(2,1)S(1)}, u32[]{:S(2)}, u32[]{:S(2)}) collective-permute-start(bf16[2,2048,64]{1,2,0:T(8,128)(2,1)S(1)} %fusion.117), channel_id=1, source_target_pairs={{0,16},{4,20},{8,24},{12,28},{16,0},{20,4},{24,8},{28,12},{1,17},{... | collective-permute-start | bytes 1572872 | tf_op jit(solution)/shard_map/ppermute | solution.py:139
  63.3 4.6 %collective-permute-start.11 = (f32[3,2,128,64]{2,3,0,1:T(8,128)S(1)}, f32[3,2,128,64]{2,3,0,1:T(8,128)S(1)}, u32[]{:S(2)}, u32[]{:S(2)}) collective-permute-start(f32[3,2,128,64]{2,3,0,1:T(8,128)S(1)} %add.460), channel_id=1, source_target_pairs={{0,8},{4,12},{8,0},{12,4},{16,24},{20,28},{24,16},{28,20},{1,9},{5... | collective-permute-start | bytes 589832 | tf_op jit(solution)/shard_map/ppermute | solution.py:139
  68.6 9.3 %collective-permute-done.11 = f32[3,2,128,64]{2,3,0,1:T(8,128)S(1)} collective-permute-done((f32[3,2,128,64]{2,3,0,1:T(8,128)S(1)}, f32[3,2,128,64]{2,3,0,1:T(8,128)S(1)}, u32[]{:S(2)}, u32[]{:S(2)}) %collective-permute-start.11) | collective-permute-done | bytes 196640 | tf_op jit(solution)/shard_map/ppermute | solution.py:139
  78.0 4.9 %collective-permute-start.12 = (f32[3,2,128,64]{2,3,0,1:T(8,128)S(1)}, f32[3,2,128,64]{2,3,0,1:T(8,128)S(1)}, u32[]{:S(2)}, u32[]{:S(2)}) collective-permute-start(f32[3,2,128,64]{2,3,0,1:T(8,128)S(1)} %add.461), channel_id=1, source_target_pairs={{0,16},{4,20},{8,24},{12,28},{16,0},{20,4},{24,8},{28,12},{1,17},{... | collective-permute-start | bytes 589832 | tf_op jit(solution)/shard_map/ppermute | solution.py:139
  83.5 8.1 %collective-permute-done.2 = bf16[2,2048,64]{1,2,0:T(8,128)(2,1)S(1)} collective-permute-done((bf16[2,2048,64]{1,2,0:T(8,128)(2,1)S(1)}, bf16[2,2048,64]{1,2,0:T(8,128)(2,1)S(1)}, u32[]{:S(2)}, u32[]{:S(2)}) %collective-permute-start.2) | collective-permute-done | bytes 524320 | tf_op jit(solution)/shard_map/ppermute | solution.py:139
  97.3 3.5 %bitcast_add_fusion = f32[3,256,2048]{2,1,0:T(8,128)S(1)} fusion(f32[3,2,128,2048]{3,2,1,0:T(8,128)S(1)} %copy.78, bf16[1024,2048]{1,0:T(8,128)(2,1)S(1)} %copy-done.16, f32[1024]{0:T(1024)S(1)} %convert_element_type.196, f32[3,256]{1,0:T(4,128)S(1)} %add_rsqrt_fusion, bf16[3,128,1024]{2,1,0:T(8,128)(2,1)S(1)} %get-tuple-element.24, ...), kind=kOutput, calls=%fused_computation.4 | convolution fusion | flops 3228303360 | bytes 18357248 | tf_op jit(solution)/shard_map/tnd,de->tne/dot_general | solution.py:277
  108.5 10.3 %collective-permute-done.13 = bf16[2,1,32,2560]{3,2,1,0:T(8,128)(2,1)S(1)} collective-permute-done((bf16[2,1,32,2560]{3,2,1,0:T(8,128)(2,1)S(1)}, bf16[2,1,32,2560]{3,2,1,0:T(8,128)(2,1)S(1)}, u32[]{:S(2)}, u32[]{:S(2)}) %collective-permute-start.13) | collective-permute-done | bytes 327712 | tf_op jit(solution)/shard_map/ppermute | solution.py:84
  122.8 9.2 %collective-permute-done.17 = bf16[2,1,32,2560]{3,2,1,0:T(8,128)(2,1)S(1)} collective-permute-done((bf16[2,1,32,2560]{3,2,1,0:T(8,128)(2,1)S(1)}, bf16[2,1,32,2560]{3,2,1,0:T(8,128)(2,1)S(1)}, u32[]{:S(2)}, u32[]{:S(2)}) %collective-permute-start.17) | collective-permute-done | bytes 327712 | tf_op jit(solution)/shard_map/ppermute | solution.py:84
  132.4 8.9 %collective-permute-done.19 = bf16[2,1,32,2560]{3,2,1,0:T(8,128)(2,1)S(1)} collective-permute-done((bf16[2,1,32,2560]{3,2,1,0:T(8,128)(2,1)S(1)}, bf16[2,1,32,2560]{3,2,1,0:T(8,128)(2,1)S(1)}, u32[]{:S(2)}, u32[]{:S(2)}) %collective-permute-start.19) | collective-permute-done | bytes 327712 | tf_op jit(solution)/shard_map/ppermute | solution.py:84
  141.6 7.6 %collective-permute-done.22 = bf16[2,1,32,2560]{3,2,1,0:T(8,128)(2,1)S(1)} collective-permute-done((bf16[2,1,32,2560]{3,2,1,0:T(8,128)(2,1)S(1)}, bf16[2,1,32,2560]{3,2,1,0:T(8,128)(2,1)S(1)}, u32[]{:S(2)}, u32[]{:S(2)}) %collective-permute-start.22) | collective-permute-done | bytes 327712 | tf_op jit(solution)/shard_map/ppermute | solution.py:84
  149.2 5.6 %collective-permute-done.23 = bf16[2,1,32,2560]{3,2,1,0:T(8,128)(2,1)S(1)} collective-permute-done((bf16[2,1,32,2560]{3,2,1,0:T(8,128)(2,1)S(1)}, bf16[2,1,32,2560]{3,2,1,0:T(8,128)(2,1)S(1)}, u32[]{:S(2)}, u32[]{:S(2)}) %collective-permute-start.23) | collective-permute-done | bytes 327712 | tf_op jit(solution)/shard_map/ppermute | solution.py:84
  157.0 7.6 %collective-permute-done.24 = bf16[1,32,2560]{2,1,0:T(8,128)(2,1)S(1)} collective-permute-done((bf16[1,32,2560]{2,1,0:T(8,128)(2,1)S(1)}, bf16[1,32,2560]{2,1,0:T(8,128)(2,1)S(1)}, u32[]{:S(2)}, u32[]{:S(2)}) %collective-permute-start.24) | collective-permute-done | bytes 163872 | tf_op jit(solution)/shard_map/ppermute | solution.py:89
  165.6 3.5 %all-to-all-start = ((bf16[3,4,8,1,2560]{4,2,3,0,1:T(8,128)(2,1)}), bf16[3,4,8,1,2560]{4,2,3,0,1:T(8,128)(2,1)S(1)}, u32[]{:S(2)}, u32[]{:S(2)}) async-start(bf16[3,4,8,1,2560]{4,2,3,0,1:T(8,128)(2,1)} %copy.83), calls=%async_computation | async-start | bytes 983040 | tf_op jit(solution)/shard_map/all_to_all | solution.py:288
  169.3 8.2 %all-to-all-done = bf16[3,4,8,1,2560]{4,2,3,0,1:T(8,128)(2,1)S(1)} async-done(((bf16[3,4,8,1,2560]{4,2,3,0,1:T(8,128)(2,1)}), bf16[3,4,8,1,2560]{4,2,3,0,1:T(8,128)(2,1)S(1)}, u32[]{:S(2)}, u32[]{:S(2)}) %all-to-all-start) | async-done | bytes 491552 | tf_op jit(solution)/shard_map/all_to_all | solution.py:288
  179.2 4.6 %fusion.115 = (f32[8,8,24]{2,1,0:T(8,128)S(1)}, f32[8,8,24,256]{3,2,1,0:T(8,128)S(1)}) fusion(pred[8,256]{1,0:T(8,128)(4,1)S(1)} %iota_compare_fusion, bf16[8,256,1024]{2,1,0:T(8,128)(2,1)} %param.28, bf16[3,8,8,8,64]{4,3,2,1,0:T(8,128)(2,1)S(1)} %bitcast.225, bf16[3,8,8,8,64]{4,3,2,1,0:T(8,128)(2,1)S(1)} %bitcast.223), kind=kOutput, calls=%fused_computation.239 | convolution fusion | flops 102627840 | bytes 6168576 | tf_op jit(solution)/shard_map/rhqd,rchd->rhqc/dot_general | solution.py:186
  185.4 3.1 %fusion.51 = bf16[8,8,3,8,128]{4,3,2,1,0:T(8,128)(2,1)S(1)} fusion(f32[8,8,24,128]{3,2,1,0:T(8,128)S(1)} %fusion.94, f32[8,8,24,256]{3,2,1,0:T(8,128)S(1)} %get-tuple-element.68, f32[8,8,24]{2,1,0:T(8,128)S(1)} %max.7, pred[8,256]{1,0:T(8,128)(4,1)S(1)} %iota_compare_fusion, f32[8,8,24]{2,1,0:T(8,128)S(1)} %add.502, bf16[8,256,1024]{2,1,0:T(8,128)(2,1)} %param.29), kind=kOutput, calls=%fused_computation.52 | convolution fusion | flops 102432768 | bytes 6961152 | tf_op jit(solution)/shard_map/rhqc,rchd->rhqd/dot_general | solution.py:210
  189.7 3.7 %all-to-all-start.1 = ((bf16[3,1,8,4,2048]{4,2,0,1,3:T(8,128)(2,1)}), bf16[3,1,8,4,2048]{4,2,0,1,3:T(8,128)(2,1)S(1)}, u32[]{:S(2)}, u32[]{:S(2)}) async-start(bf16[3,1,8,4,2048]{4,2,0,1,3:T(8,128)(2,1)} %copy.94), calls=%async_computation.1 | async-start | bytes 786432 | tf_op jit(solution)/shard_map/all_to_all | solution.py:314
  193.4 7.1 %all-to-all-done.1 = bf16[3,1,8,4,2048]{4,2,0,1,3:T(8,128)(2,1)S(1)} async-done(((bf16[3,1,8,4,2048]{4,2,0,1,3:T(8,128)(2,1)}), bf16[3,1,8,4,2048]{4,2,0,1,3:T(8,128)(2,1)S(1)}, u32[]{:S(2)}, u32[]{:S(2)}) %all-to-all-start.1) | async-done | bytes 393248 | tf_op jit(solution)/shard_map/all_to_all | solution.py:314
  201.4 2.9 collective-permute-start.29
  204.4 10.8 %collective-permute-done.33 = bf16[1,32,2048]{2,1,0:T(8,128)(2,1)S(1)} collective-permute-done((bf16[1,32,2048]{2,1,0:T(8,128)(2,1)S(1)}, bf16[1,32,2048]{2,1,0:T(8,128)(2,1)S(1)}, u32[]{:S(2)}, u32[]{:S(2)}) %collective-permute-start.33) | collective-permute-done | bytes 131104 | tf_op jit(solution)/shard_map/ppermute | solution.py:116
  220.9 3.6 %collective-permute-done.34 = bf16[2,1,32,2048]{3,2,1,0:T(8,128)(2,1)S(1)} collective-permute-done((bf16[2,1,32,2048]{3,2,1,0:T(8,128)(2,1)S(1)}, bf16[2,1,32,2048]{3,2,1,0:T(8,128)(2,1)S(1)}, u32[]{:S(2)}, u32[]{:S(2)}) %collective-permute-start.34) | collective-permute-done | bytes 262176 | tf_op jit(solution)/shard_map/ppermute | solution.py:121
  227.1 5.1 %collective-permute-done.36 = bf16[2,1,32,2048]{3,2,1,0:T(8,128)(2,1)S(1)} collective-permute-done((bf16[2,1,32,2048]{3,2,1,0:T(8,128)(2,1)S(1)}, bf16[2,1,32,2048]{3,2,1,0:T(8,128)(2,1)S(1)}, u32[]{:S(2)}, u32[]{:S(2)}) %collective-permute-start.36) | collective-permute-done | bytes 262176 | tf_op jit(solution)/shard_map/ppermute | solution.py:121
  239.9 3.7 %collective-permute-done.32 = bf16[2,1,32,2048]{3,2,1,0:T(8,128)(2,1)} collective-permute-done((bf16[2,1,32,2048]{3,2,1,0:T(8,128)(2,1)}, bf16[2,1,32,2048]{3,2,1,0:T(8,128)(2,1)}, u32[]{:S(2)}, u32[]{:S(2)}) %collective-permute-start.32) | collective-permute-done | bytes 262176 | tf_op jit(solution)/shard_map/ppermute | solution.py:121
  260.7 2.8 gather_fusion
  269.8 5.5 %collective-permute-done.38 = f32[3,2,128,64]{2,3,0,1:T(8,128)S(1)} collective-permute-done((f32[3,2,128,64]{2,3,0,1:T(8,128)S(1)}, f32[3,2,128,64]{2,3,0,1:T(8,128)S(1)}, u32[]{:S(2)}, u32[]{:S(2)}) %collective-permute-start.38) | collective-permute-done | bytes 196640 | tf_op jit(solution)/shard_map/ppermute | solution.py:139
  278.6 3.4 %bitcast_add_fusion.1 = f32[3,256,1024]{2,1,0:T(8,128)S(1)} fusion(f32[3,2,128,1024]{3,2,1,0:T(8,128)S(1)} %copy.96, bf16[2048,1024]{1,0:T(8,128)(2,1)S(1)} %copy-done.17, bf16[1,256,2048]{2,1,0:T(8,128)(2,1)S(1)} %bitcast.236, bf16[1,256,2048]{2,1,0:T(8,128)(2,1)S(1)} %bitcast.234, bf16[1,256,2048]{2,1,0:T(8,128)(2,1)S(1)} %bitcast.232), kind=kOutput, calls=%fused_computation.27 | convolution fusion | flops 3225157632 | bytes 13631488 | tf_op jit(solution)/shard_map/tnq,qe->tne/dot_general | solution.py:329
  283.5 3.7 %collective-permute-done.39 = f32[3,2,64,1024]{3,2,0,1:T(8,128)} collective-permute-done((f32[3,2,64,1024]{3,2,0,1:T(8,128)}, f32[3,2,64,1024]{3,2,0,1:T(8,128)}, u32[]{:S(2)}, u32[]{:S(2)}) %collective-permute-start.39) | collective-permute-done | bytes 1572896 | tf_op jit(solution)/shard_map/ppermute | solution.py:160
  290.8 10.7 %collective-permute-done.40 = bf16[3,1,64,1024]{3,2,0,1:T(8,128)(2,1)S(1)} collective-permute-done((bf16[3,1,64,1024]{3,2,0,1:T(8,128)(2,1)S(1)}, bf16[3,1,64,1024]{3,2,0,1:T(8,128)(2,1)S(1)}, u32[]{:S(2)}, u32[]{:S(2)}) %collective-permute-start.40) | collective-permute-done | bytes 393248 | tf_op jit(solution)/shard_map/ppermute | solution.py:160
  (227 shorter events, 105.9 us)
Async XLA Ops:
  8.1 20.9 %collective-permute-start.4 = (bf16[3,128,1024]{2,1,0:T(8,128)(2,1)S(1)}, bf16[3,128,1024]{2,1,0:T(8,128)(2,1)}, u32[]{:S(2)}, u32[]{:S(2)}) collective-permute-start(bf16[3,128,1024]{2,1,0:T(8,128)(2,1)S(1)} %pad_maximum_fusion.1), channel_id=1, source_target_pairs={{0,2},{1,3},{2,0},{3,1},{4,6},{5,7},{6,4},{7,5},{8,10},{9,11},{10,... | collective-permute-start | bytes 2359304 | tf_op jit(solution)/shard_map/ppermute | solution.py:102
  12.6 23.8 %collective-permute-start = (bf16[2,2048,64]{1,2,0:T(8,128)(2,1)}, bf16[2,2048,64]{1,2,0:T(8,128)(2,1)}, u32[]{:S(2)}, u32[]{:S(2)}) collective-permute-start(bf16[2,2048,64]{1,2,0:T(8,128)(2,1)} %pad_maximum_fusion.2), channel_id=1, source_target_pairs={{0,4},{4,0},{8,12},{12,8},{16,20},{20,16},{24,28},{28,24},{1,5},{5... | collective-permute-start | bytes 1572872 | tf_op jit(solution)/shard_map/ppermute | solution.py:139
  37.5 21.1 %collective-permute-start.1 = (bf16[2,2048,64]{1,2,0:T(8,128)(2,1)S(1)}, bf16[2,2048,64]{1,2,0:T(8,128)(2,1)S(1)}, u32[]{:S(2)}, u32[]{:S(2)}) collective-permute-start(bf16[2,2048,64]{1,2,0:T(8,128)(2,1)S(1)} %fusion.111), channel_id=1, source_target_pairs={{0,8},{4,12},{8,0},{12,4},{16,24},{20,28},{24,16},{28,20},{1,9},{5... | collective-permute-start | bytes 1572872 | tf_op jit(solution)/shard_map/ppermute | solution.py:139
  59.8 31.7 %collective-permute-start.2 = (bf16[2,2048,64]{1,2,0:T(8,128)(2,1)S(1)}, bf16[2,2048,64]{1,2,0:T(8,128)(2,1)S(1)}, u32[]{:S(2)}, u32[]{:S(2)}) collective-permute-start(bf16[2,2048,64]{1,2,0:T(8,128)(2,1)S(1)} %fusion.117), channel_id=1, source_target_pairs={{0,16},{4,20},{8,24},{12,28},{16,0},{20,4},{24,8},{28,12},{1,17},{... | collective-permute-start | bytes 1572872 | tf_op jit(solution)/shard_map/ppermute | solution.py:139
  63.3 14.6 %collective-permute-start.11 = (f32[3,2,128,64]{2,3,0,1:T(8,128)S(1)}, f32[3,2,128,64]{2,3,0,1:T(8,128)S(1)}, u32[]{:S(2)}, u32[]{:S(2)}) collective-permute-start(f32[3,2,128,64]{2,3,0,1:T(8,128)S(1)} %add.460), channel_id=1, source_target_pairs={{0,8},{4,12},{8,0},{12,4},{16,24},{20,28},{24,16},{28,20},{1,9},{5... | collective-permute-start | bytes 589832 | tf_op jit(solution)/shard_map/ppermute | solution.py:139
  78.0 16.1 %collective-permute-start.12 = (f32[3,2,128,64]{2,3,0,1:T(8,128)S(1)}, f32[3,2,128,64]{2,3,0,1:T(8,128)S(1)}, u32[]{:S(2)}, u32[]{:S(2)}) collective-permute-start(f32[3,2,128,64]{2,3,0,1:T(8,128)S(1)} %add.461), channel_id=1, source_target_pairs={{0,16},{4,20},{8,24},{12,28},{16,0},{20,4},{24,8},{28,12},{1,17},{... | collective-permute-start | bytes 589832 | tf_op jit(solution)/shard_map/ppermute | solution.py:139
  102.6 16.1 %collective-permute-start.13 = (bf16[2,1,32,2560]{3,2,1,0:T(8,128)(2,1)S(1)}, bf16[2,1,32,2560]{3,2,1,0:T(8,128)(2,1)S(1)}, u32[]{:S(2)}, u32[]{:S(2)}) collective-permute-start(bf16[2,1,32,2560]{3,2,1,0:T(8,128)(2,1)S(1)} %pad_maximum_fusion.4), channel_id=1, source_target_pairs={{0,4},{4,0},{8,12},{12,8},{16,20},{20,16},{24,28},{28,24},{1,5},{5... | collective-permute-start | bytes 983048 | tf_op jit(solution)/shard_map/ppermute | solution.py:84
  103.3 15.6 %collective-permute-start.14 = (bf16[2,1,32,2560]{3,2,1,0:T(8,128)(2,1)S(1)}, bf16[2,1,32,2560]{3,2,1,0:T(8,128)(2,1)S(1)}, u32[]{:S(2)}, u32[]{:S(2)}) collective-permute-start(bf16[2,1,32,2560]{3,2,1,0:T(8,128)(2,1)S(1)} %pad_maximum_fusion.5), channel_id=1, source_target_pairs={{0,8},{4,12},{8,0},{12,4},{16,24},{20,28},{24,16},{28,20},{1,9},{5... | collective-permute-start | bytes 983048 | tf_op jit(solution)/shard_map/ppermute | solution.py:84
  104.1 17.9 %collective-permute-start.15 = (bf16[2,1,32,2560]{3,2,1,0:T(8,128)(2,1)S(1)}, bf16[2,1,32,2560]{3,2,1,0:T(8,128)(2,1)S(1)}, u32[]{:S(2)}, u32[]{:S(2)}) collective-permute-start(bf16[2,1,32,2560]{3,2,1,0:T(8,128)(2,1)S(1)} %pad_maximum_fusion.6), channel_id=1, source_target_pairs={{0,12},{4,8},{8,4},{12,0},{16,28},{20,24},{24,20},{28,16},{1,13},{... | collective-permute-start | bytes 983048 | tf_op jit(solution)/shard_map/ppermute | solution.py:84
  106.9 25.1 %collective-permute-start.17 = (bf16[2,1,32,2560]{3,2,1,0:T(8,128)(2,1)S(1)}, bf16[2,1,32,2560]{3,2,1,0:T(8,128)(2,1)S(1)}, u32[]{:S(2)}, u32[]{:S(2)}) collective-permute-start(bf16[2,1,32,2560]{3,2,1,0:T(8,128)(2,1)S(1)} %pad_maximum_fusion.7), channel_id=1, source_target_pairs={{0,4},{4,0},{8,12},{12,8},{16,20},{20,16},{24,28},{28,24},{1,5},{5... | collective-permute-start | bytes 983048 | tf_op jit(solution)/shard_map/ppermute | solution.py:84
  107.5 24.6 %collective-permute-start.18 = (bf16[2,1,32,2560]{3,2,1,0:T(8,128)(2,1)S(1)}, bf16[2,1,32,2560]{3,2,1,0:T(8,128)(2,1)S(1)}, u32[]{:S(2)}, u32[]{:S(2)}) collective-permute-start(bf16[2,1,32,2560]{3,2,1,0:T(8,128)(2,1)S(1)} %pad_maximum_fusion.8), channel_id=1, source_target_pairs={{0,8},{4,12},{8,0},{12,4},{16,24},{20,28},{24,16},{28,20},{1,9},{5... | collective-permute-start | bytes 983048 | tf_op jit(solution)/shard_map/ppermute | solution.py:84
  118.8 22.6 %collective-permute-start.19 = (bf16[2,1,32,2560]{3,2,1,0:T(8,128)(2,1)S(1)}, bf16[2,1,32,2560]{3,2,1,0:T(8,128)(2,1)S(1)}, u32[]{:S(2)}, u32[]{:S(2)}) collective-permute-start(bf16[2,1,32,2560]{3,2,1,0:T(8,128)(2,1)S(1)} %pad_maximum_fusion.9), channel_id=1, source_target_pairs={{0,12},{4,8},{8,4},{12,0},{16,28},{20,24},{24,20},{28,16},{1,13},{... | collective-permute-start | bytes 983048 | tf_op jit(solution)/shard_map/ppermute | solution.py:84
  118.8 22.7 %collective-permute-start.21 = (bf16[2,1,32,2560]{3,2,1,0:T(8,128)(2,1)S(1)}, bf16[2,1,32,2560]{3,2,1,0:T(8,128)(2,1)S(1)}, u32[]{:S(2)}, u32[]{:S(2)}) collective-permute-start(bf16[2,1,32,2560]{3,2,1,0:T(8,128)(2,1)S(1)} %pad_maximum_fusion.10), channel_id=1, source_target_pairs={{0,4},{4,0},{8,12},{12,8},{16,20},{20,16},{24,28},{28,24},{1,5},{5... | collective-permute-start | bytes 983048 | tf_op jit(solution)/shard_map/ppermute | solution.py:84
  122.0 27.2 %collective-permute-start.22 = (bf16[2,1,32,2560]{3,2,1,0:T(8,128)(2,1)S(1)}, bf16[2,1,32,2560]{3,2,1,0:T(8,128)(2,1)S(1)}, u32[]{:S(2)}, u32[]{:S(2)}) collective-permute-start(bf16[2,1,32,2560]{3,2,1,0:T(8,128)(2,1)S(1)} %pad_maximum_fusion.11), channel_id=1, source_target_pairs={{0,8},{4,12},{8,0},{12,4},{16,24},{20,28},{24,16},{28,20},{1,9},{5... | collective-permute-start | bytes 983048 | tf_op jit(solution)/shard_map/ppermute | solution.py:84
  132.0 22.8 %collective-permute-start.23 = (bf16[2,1,32,2560]{3,2,1,0:T(8,128)(2,1)S(1)}, bf16[2,1,32,2560]{3,2,1,0:T(8,128)(2,1)S(1)}, u32[]{:S(2)}, u32[]{:S(2)}) collective-permute-start(bf16[2,1,32,2560]{3,2,1,0:T(8,128)(2,1)S(1)} %pad_maximum_fusion.12), channel_id=1, source_target_pairs={{0,12},{4,8},{8,4},{12,0},{16,28},{20,24},{24,20},{28,16},{1,13},{... | collective-permute-start | bytes 983048 | tf_op jit(solution)/shard_map/ppermute | solution.py:84
  132.1 24.7 %collective-permute-start.16 = (bf16[1,32,2560]{2,1,0:T(8,128)(2,1)S(1)}, bf16[1,32,2560]{2,1,0:T(8,128)(2,1)S(1)}, u32[]{:S(2)}, u32[]{:S(2)}) collective-permute-start(bf16[1,32,2560]{2,1,0:T(8,128)(2,1)S(1)} %fusion.87), channel_id=1, source_target_pairs={{0,16},{4,20},{8,24},{12,28},{16,0},{20,4},{24,8},{28,12},{1,17},{... | collective-permute-start | bytes 491528 | tf_op jit(solution)/shard_map/ppermute | solution.py:89
  141.5 15.4 %collective-permute-start.20 = (bf16[1,32,2560]{2,1,0:T(8,128)(2,1)S(1)}, bf16[1,32,2560]{2,1,0:T(8,128)(2,1)S(1)}, u32[]{:S(2)}, u32[]{:S(2)}) collective-permute-start(bf16[1,32,2560]{2,1,0:T(8,128)(2,1)S(1)} %fusion.89), channel_id=1, source_target_pairs={{0,16},{4,20},{8,24},{12,28},{16,0},{20,4},{24,8},{28,12},{1,17},{... | collective-permute-start | bytes 491528 | tf_op jit(solution)/shard_map/ppermute | solution.py:89
  155.0 9.6 %collective-permute-start.24 = (bf16[1,32,2560]{2,1,0:T(8,128)(2,1)S(1)}, bf16[1,32,2560]{2,1,0:T(8,128)(2,1)S(1)}, u32[]{:S(2)}, u32[]{:S(2)}) collective-permute-start(bf16[1,32,2560]{2,1,0:T(8,128)(2,1)S(1)} %fusion.91), channel_id=1, source_target_pairs={{0,16},{4,20},{8,24},{12,28},{16,0},{20,4},{24,8},{28,12},{1,17},{... | collective-permute-start | bytes 491528 | tf_op jit(solution)/shard_map/ppermute | solution.py:89
  165.6 11.9 %all-to-all-start = ((bf16[3,4,8,1,2560]{4,2,3,0,1:T(8,128)(2,1)}), bf16[3,4,8,1,2560]{4,2,3,0,1:T(8,128)(2,1)S(1)}, u32[]{:S(2)}, u32[]{:S(2)}) async-start(bf16[3,4,8,1,2560]{4,2,3,0,1:T(8,128)(2,1)} %copy.83), calls=%async_computation | async-start | bytes 983040 | tf_op jit(solution)/shard_map/all_to_all | solution.py:288
  189.7 10.9 %all-to-all-start.1 = ((bf16[3,1,8,4,2048]{4,2,0,1,3:T(8,128)(2,1)}), bf16[3,1,8,4,2048]{4,2,0,1,3:T(8,128)(2,1)S(1)}, u32[]{:S(2)}, u32[]{:S(2)}) async-start(bf16[3,1,8,4,2048]{4,2,0,1,3:T(8,128)(2,1)} %copy.94), calls=%async_computation.1 | async-start | bytes 786432 | tf_op jit(solution)/shard_map/all_to_all | solution.py:314
  200.7 14.5 %collective-permute-start.33 = (bf16[1,32,2048]{2,1,0:T(8,128)(2,1)S(1)}, bf16[1,32,2048]{2,1,0:T(8,128)(2,1)S(1)}, u32[]{:S(2)}, u32[]{:S(2)}) collective-permute-start(bf16[1,32,2048]{2,1,0:T(8,128)(2,1)S(1)} %get-tuple-element.52), channel_id=1, source_target_pairs={{0,16},{4,20},{8,24},{12,28},{16,0},{20,4},{24,8},{28,12},{1,17},{... | collective-permute-start | bytes 393224 | tf_op jit(solution)/shard_map/ppermute | solution.py:116
  201.4 17.4 %collective-permute-start.29 = (bf16[1,32,2048]{2,1,0:T(8,128)(2,1)S(1)}, bf16[1,32,2048]{2,1,0:T(8,128)(2,1)S(1)}, u32[]{:S(2)}, u32[]{:S(2)}) collective-permute-start(bf16[1,32,2048]{2,1,0:T(8,128)(2,1)S(1)} %get-tuple-element.51), channel_id=1, source_target_pairs={{0,16},{4,20},{8,24},{12,28},{16,0},{20,4},{24,8},{28,12},{1,17},{... | collective-permute-start | bytes 393224 | tf_op jit(solution)/shard_map/ppermute | solution.py:116
  204.4 16.5 %collective-permute-start.25 = (bf16[1,32,2048]{2,1,0:T(8,128)(2,1)S(1)}, bf16[1,32,2048]{2,1,0:T(8,128)(2,1)S(1)}, u32[]{:S(2)}, u32[]{:S(2)}) collective-permute-start(bf16[1,32,2048]{2,1,0:T(8,128)(2,1)S(1)} %get-tuple-element.50), channel_id=1, source_target_pairs={{0,16},{4,20},{8,24},{12,28},{16,0},{20,4},{24,8},{28,12},{1,17},{... | collective-permute-start | bytes 393224 | tf_op jit(solution)/shard_map/ppermute | solution.py:116
  216.7 9.8 %collective-permute-start.35 = (bf16[2,1,32,2048]{3,2,1,0:T(8,128)(2,1)S(1)}, bf16[2,1,32,2048]{3,2,1,0:T(8,128)(2,1)S(1)}, u32[]{:S(2)}, u32[]{:S(2)}) collective-permute-start(bf16[2,1,32,2048]{3,2,1,0:T(8,128)(2,1)S(1)} %pad_maximum_fusion.15), channel_id=1, source_target_pairs={{0,8},{4,12},{8,0},{12,4},{16,24},{20,28},{24,16},{28,20},{1,9},{5... | collective-permute-start | bytes 786440 | tf_op jit(solution)/shard_map/ppermute | solution.py:121
  216.7 15.5 %collective-permute-start.36 = (bf16[2,1,32,2048]{3,2,1,0:T(8,128)(2,1)S(1)}, bf16[2,1,32,2048]{3,2,1,0:T(8,128)(2,1)S(1)}, u32[]{:S(2)}, u32[]{:S(2)}) collective-permute-start(bf16[2,1,32,2048]{3,2,1,0:T(8,128)(2,1)S(1)} %pad_maximum_fusion.15), channel_id=1, source_target_pairs={{0,12},{4,8},{8,4},{12,0},{16,28},{20,24},{24,20},{28,16},{1,13},{... | collective-permute-start | bytes 786440 | tf_op jit(solution)/shard_map/ppermute | solution.py:121
  219.5 16.3 %collective-permute-start.30 = (bf16[2,1,32,2048]{3,2,1,0:T(8,128)(2,1)}, bf16[2,1,32,2048]{3,2,1,0:T(8,128)(2,1)}, u32[]{:S(2)}, u32[]{:S(2)}) collective-permute-start(bf16[2,1,32,2048]{3,2,1,0:T(8,128)(2,1)} %pad_maximum_fusion.14), channel_id=1, source_target_pairs={{0,4},{4,0},{8,12},{12,8},{16,20},{20,16},{24,28},{28,24},{1,5},{5... | collective-permute-start | bytes 786440 | tf_op jit(solution)/shard_map/ppermute | solution.py:121
  220.9 18.1 %collective-permute-start.31 = (bf16[2,1,32,2048]{3,2,1,0:T(8,128)(2,1)}, bf16[2,1,32,2048]{3,2,1,0:T(8,128)(2,1)}, u32[]{:S(2)}, u32[]{:S(2)}) collective-permute-start(bf16[2,1,32,2048]{3,2,1,0:T(8,128)(2,1)} %pad_maximum_fusion.14), channel_id=1, source_target_pairs={{0,8},{4,12},{8,0},{12,4},{16,24},{20,28},{24,16},{28,20},{1,9},{5... | collective-permute-start | bytes 786440 | tf_op jit(solution)/shard_map/ppermute | solution.py:121
  224.5 19.1 %collective-permute-start.32 = (bf16[2,1,32,2048]{3,2,1,0:T(8,128)(2,1)}, bf16[2,1,32,2048]{3,2,1,0:T(8,128)(2,1)}, u32[]{:S(2)}, u32[]{:S(2)}) collective-permute-start(bf16[2,1,32,2048]{3,2,1,0:T(8,128)(2,1)} %pad_maximum_fusion.14), channel_id=1, source_target_pairs={{0,12},{4,8},{8,4},{12,0},{16,28},{20,24},{24,20},{28,16},{1,13},{... | collective-permute-start | bytes 786440 | tf_op jit(solution)/shard_map/ppermute | solution.py:121
  226.5 23.7 %collective-permute-start.26 = (bf16[2,1,32,2048]{3,2,1,0:T(8,128)(2,1)S(1)}, bf16[2,1,32,2048]{3,2,1,0:T(8,128)(2,1)S(1)}, u32[]{:S(2)}, u32[]{:S(2)}) collective-permute-start(bf16[2,1,32,2048]{3,2,1,0:T(8,128)(2,1)S(1)} %pad_maximum_fusion.13), channel_id=1, source_target_pairs={{0,4},{4,0},{8,12},{12,8},{16,20},{20,16},{24,28},{28,24},{1,5},{5... | collective-permute-start | bytes 786440 | tf_op jit(solution)/shard_map/ppermute | solution.py:121
  232.2 18.6 %collective-permute-start.27 = (bf16[2,1,32,2048]{3,2,1,0:T(8,128)(2,1)S(1)}, bf16[2,1,32,2048]{3,2,1,0:T(8,128)(2,1)}, u32[]{:S(2)}, u32[]{:S(2)}) collective-permute-start(bf16[2,1,32,2048]{3,2,1,0:T(8,128)(2,1)S(1)} %pad_maximum_fusion.13), channel_id=1, source_target_pairs={{0,8},{4,12},{8,0},{12,4},{16,24},{20,28},{24,16},{28,20},{1,9},{5... | collective-permute-start | bytes 786440 | tf_op jit(solution)/shard_map/ppermute | solution.py:121
  235.8 18.9 %collective-permute-start.28 = (bf16[2,1,32,2048]{3,2,1,0:T(8,128)(2,1)S(1)}, bf16[2,1,32,2048]{3,2,1,0:T(8,128)(2,1)}, u32[]{:S(2)}, u32[]{:S(2)}) collective-permute-start(bf16[2,1,32,2048]{3,2,1,0:T(8,128)(2,1)S(1)} %pad_maximum_fusion.13), channel_id=1, source_target_pairs={{0,12},{4,8},{8,4},{12,0},{16,28},{20,24},{24,20},{28,16},{1,13},{... | collective-permute-start | bytes 786440 | tf_op jit(solution)/shard_map/ppermute | solution.py:121
  290.2 11.2 %collective-permute-start.40 = (bf16[3,1,64,1024]{3,2,0,1:T(8,128)(2,1)S(1)}, bf16[3,1,64,1024]{3,2,0,1:T(8,128)(2,1)S(1)}, u32[]{:S(2)}, u32[]{:S(2)}) collective-permute-start(bf16[3,1,64,1024]{3,2,0,1:T(8,128)(2,1)S(1)} %dynamic-slice_convert_fusion), channel_id=1, source_target_pairs={{0,2},{1,3},{2,0},{3,1},{4,6},{5,7},{6,4},{7,5},{8,10},{9,11},{10,... | collective-permute-start | bytes 1179656 | tf_op jit(solution)/shard_map/ppermute | solution.py:160
  (30 other events, 256.8 us)

commit v9 on v6

--- a/solution.py
+++ b/solution.py
@@ -139,6 +139,10 @@
             value = value + lax.ppermute(value, axis_name, pairs)
             distance *= 2
     return value
+
+
+def sum_then_spread(value, sum_axes, spread_axes):
+    return tree_sum(tree_sum(value, sum_axes).astype(jnp.bfloat16), spread_axes)
 
 
 def halving_scatter(partial, axis_name, axis_size):
@@ -269,7 +273,7 @@
     rank_part = jnp.einsum(
         "tbnd,bdr->tbnr", blocked, query_first, preferred_element_type=jnp.float32
     )
-    rank_query = tree_sum(rank_part, ("gy", "gx")).astype(jnp.bfloat16)
+    rank_query = sum_then_spread(rank_part, ("gx",), ("gy",))
     delta_query = jnp.einsum(
         "tbnr,bre->tbne", rank_query, query_second, preferred_element_type=jnp.float32
     ).reshape(steps, request_count, -1)
@@ -320,7 +324,7 @@
         output_first,
         preferred_element_type=jnp.float32,
     )
-    rank_output = tree_sum(rank_part_out, ("gy", "gx")).astype(jnp.bfloat16)
+    rank_output = sum_then_spread(rank_part_out, ("gy",), ("gx",))
     delta_output = jnp.einsum(
         "tbnr,bre->tbne", rank_output, output_second, preferred_element_type=jnp.float32
     ).reshape(steps, request_count, -1)

time: 296 us -> 291 us (0.983)
  waiting for transfers between devices: 160 us -> 154 us
    ppermute x13, waiting for transfers between devices: 50.9 us -> 43.7 us  [tree_sum(): value = value + lax.ppermute(value, axis_name, pairs)]
where the time goes in v9:
time: 291 us; the launch traced here: 290 us
  waiting for transfers between devices  154 us (53%)
  starting transfers between devices  58.1 us (20%)
  local copies, waits for them, and re-layouts  32.3 us (11%)
  matrix products  20.2 us (7%)
  other arithmetic  19.2 us (7%)
  between operations  6.17 us (2%)
    ppermute x13, waiting for transfers between devices, tree_sum(): value = value + lax.ppermute(value, axis_name, pairs)  43.7 us
    ppermute x9, waiting for transfers between devices, split_half_scatter(): lax.ppermute(outgoing, axis_name, [(i, i ^ offset) for i in range(axis_si...  33.4 us
    ppermute x9, waiting for transfers between devices, split_half_gather(): lax.ppermute(pair, axis_name, [(i, i ^ offset) for i in range(axis_size)])  20 us
    ppermute x13, starting transfers between devices, tree_sum(): value = value + lax.ppermute(value, axis_name, pairs)  17.1 us
    unnamed x59, local copies, waits for them, and re-layouts  16 us
    ppermute x2, waiting for transfers between devices, halving_scatter(): held = keep + lax.ppermute(give, axis_name, swap).astype(jnp.float32)  14.4 us
    ppermute x9, starting transfers between devices, split_half_scatter(): lax.ppermute(outgoing, axis_name, [(i, i ^ offset) for i in range(axis_si...  12.7 us
    ppermute x3, waiting for transfers between devices, split_half_gather(): lax.ppermute(value, axis_name, [(i, i ^ half) for i in range(axis_size)])  11.1 us
  transfers between devices with their start and end apart: 43, of which 34 were waited for; matrix products, arithmetic and copies ran while one was open for 7% of the time, Pallas kernels for 0%

profile of v9, /device:TPU:0, one launch (start us, length us, event | category | flops | bytes accessed | tf_op | source)
XLA Modules:
  0.0 289.7 jit_solution(13772339584417704241)
XLA Ops:
  3.1 3.0 %collective-permute-start.1 = (bf16[3,128,1024]{2,1,0:T(8,128)(2,1)S(1)}, bf16[3,128,1024]{2,1,0:T(8,128)(2,1)}, u32[]{:S(2)}, u32[]{:S(2)}) collective-permute-start(bf16[3,128,1024]{2,1,0:T(8,128)(2,1)S(1)} %pad_maximum_fusion.1), channel_id=1, source_target_pairs={{0,2},{1,3},{2,0},{3,1},{4,6},{5,7},{6,4},{7,5},{8,10},{9,11},{10,... | collective-permute-start | bytes 2359304 | tf_op jit(solution)/shard_map/ppermute | solution.py:102
  14.7 9.3 %collective-permute-done.1 = bf16[3,128,1024]{2,1,0:T(8,128)(2,1)} collective-permute-done((bf16[3,128,1024]{2,1,0:T(8,128)(2,1)S(1)}, bf16[3,128,1024]{2,1,0:T(8,128)(2,1)}, u32[]{:S(2)}, u32[]{:S(2)}) %collective-permute-start.1) | collective-permute-done | bytes 786464 | tf_op jit(solution)/shard_map/ppermute | solution.py:102
  40.3 4.0 %collective-permute-done.5 = f32[3,2,128,64]{2,3,0,1:T(8,128)S(1)} collective-permute-done((f32[3,2,128,64]{2,3,0,1:T(8,128)S(1)}, f32[3,2,128,64]{2,3,0,1:T(8,128)S(1)}, u32[]{:S(2)}, u32[]{:S(2)}) %collective-permute-start.5) | collective-permute-done | bytes 196640 | tf_op jit(solution)/shard_map/ppermute | solution.py:139
  46.2 5.2 %collective-permute-done.6 = f32[3,2,128,64]{2,3,0,1:T(8,128)S(1)} collective-permute-done((f32[3,2,128,64]{2,3,0,1:T(8,128)S(1)}, f32[3,2,128,64]{2,3,0,1:T(8,128)S(1)}, u32[]{:S(2)}, u32[]{:S(2)}) %collective-permute-start.6) | collective-permute-done | bytes 196640 | tf_op jit(solution)/shard_map/ppermute | solution.py:139
  54.0 6.2 %collective-permute-done.7 = f32[3,2,128,64]{2,3,0,1:T(8,128)S(1)} collective-permute-done((f32[3,2,128,64]{2,3,0,1:T(8,128)S(1)}, f32[3,2,128,64]{2,3,0,1:T(8,128)S(1)}, u32[]{:S(2)}, u32[]{:S(2)}) %collective-permute-start.7) | collective-permute-done | bytes 196640 | tf_op jit(solution)/shard_map/ppermute | solution.py:139
  69.8 3.6 %bitcast_add_fusion = f32[3,256,2048]{2,1,0:T(8,128)S(1)} fusion(f32[3,2,128,2048]{3,2,1,0:T(8,128)S(1)} %copy.78, bf16[1024,2048]{1,0:T(8,128)(2,1)S(1)} %copy-done.17, f32[1024]{0:T(1024)S(1)} %convert_element_type.196, f32[3,256]{1,0:T(4,128)S(1)} %add_rsqrt_fusion, bf16[3,128,1024]{2,1,0:T(8,128)(2,1)S(1)} %get-tuple-element.20, ...), kind=kOutput, calls=%fused_computation.4 | convolution fusion | flops 3228303360 | bytes 18357248 | tf_op jit(solution)/shard_map/tnd,de->tne/dot_general | solution.py:281
  81.6 9.5 %collective-permute-done.10 = bf16[2,1,32,2560]{3,2,1,0:T(8,128)(2,1)S(1)} collective-permute-done((bf16[2,1,32,2560]{3,2,1,0:T(8,128)(2,1)S(1)}, bf16[2,1,32,2560]{3,2,1,0:T(8,128)(2,1)S(1)}, u32[]{:S(2)}, u32[]{:S(2)}) %collective-permute-start.10) | collective-permute-done | bytes 327712 | tf_op jit(solution)/shard_map/ppermute | solution.py:84
  95.0 7.5 %collective-permute-done.14 = bf16[2,1,32,2560]{3,2,1,0:T(8,128)(2,1)S(1)} collective-permute-done((bf16[2,1,32,2560]{3,2,1,0:T(8,128)(2,1)S(1)}, bf16[2,1,32,2560]{3,2,1,0:T(8,128)(2,1)S(1)}, u32[]{:S(2)}, u32[]{:S(2)}) %collective-permute-start.14) | collective-permute-done | bytes 327712 | tf_op jit(solution)/shard_map/ppermute | solution.py:84
  102.5 4.1 %collective-permute-start.20 = (bf16[2,1,32,2560]{3,2,1,0:T(8,128)(2,1)S(1)}, bf16[2,1,32,2560]{3,2,1,0:T(8,128)(2,1)S(1)}, u32[]{:S(2)}, u32[]{:S(2)}) collective-permute-start(bf16[2,1,32,2560]{3,2,1,0:T(8,128)(2,1)S(1)} %pad_maximum_fusion.11), channel_id=1, source_target_pairs={{0,12},{4,8},{8,4},{12,0},{16,28},{20,24},{24,20},{28,16},{1,13},{... | collective-permute-start | bytes 983048 | tf_op jit(solution)/shard_map/ppermute | solution.py:84
  106.8 3.4 %collective-permute-done.16 = bf16[2,1,32,2560]{3,2,1,0:T(8,128)(2,1)S(1)} collective-permute-done((bf16[2,1,32,2560]{3,2,1,0:T(8,128)(2,1)S(1)}, bf16[2,1,32,2560]{3,2,1,0:T(8,128)(2,1)S(1)}, u32[]{:S(2)}, u32[]{:S(2)}) %collective-permute-start.16) | collective-permute-done | bytes 327712 | tf_op jit(solution)/shard_map/ppermute | solution.py:84
  110.3 5.1 %collective-permute-start.17 = (bf16[1,32,2560]{2,1,0:T(8,128)(2,1)S(1)}, bf16[1,32,2560]{2,1,0:T(8,128)(2,1)S(1)}, u32[]{:S(2)}, u32[]{:S(2)}) collective-permute-start(bf16[1,32,2560]{2,1,0:T(8,128)(2,1)S(1)} %fusion.86), channel_id=1, source_target_pairs={{0,16},{4,20},{8,24},{12,28},{16,0},{20,4},{24,8},{28,12},{1,17},{... | collective-permute-start | bytes 491528 | tf_op jit(solution)/shard_map/ppermute | solution.py:89
  115.4 7.1 %collective-permute-done.19 = bf16[2,1,32,2560]{3,2,1,0:T(8,128)(2,1)S(1)} collective-permute-done((bf16[2,1,32,2560]{3,2,1,0:T(8,128)(2,1)S(1)}, bf16[2,1,32,2560]{3,2,1,0:T(8,128)(2,1)S(1)}, u32[]{:S(2)}, u32[]{:S(2)}) %collective-permute-start.19) | collective-permute-done | bytes 327712 | tf_op jit(solution)/shard_map/ppermute | solution.py:84
  122.5 5.0 %collective-permute-done.20 = bf16[2,1,32,2560]{3,2,1,0:T(8,128)(2,1)S(1)} collective-permute-done((bf16[2,1,32,2560]{3,2,1,0:T(8,128)(2,1)S(1)}, bf16[2,1,32,2560]{3,2,1,0:T(8,128)(2,1)S(1)}, u32[]{:S(2)}, u32[]{:S(2)}) %collective-permute-start.20) | collective-permute-done | bytes 327712 | tf_op jit(solution)/shard_map/ppermute | solution.py:84
  129.3 7.0 %collective-permute-done.21 = bf16[1,32,2560]{2,1,0:T(8,128)(2,1)S(1)} collective-permute-done((bf16[1,32,2560]{2,1,0:T(8,128)(2,1)S(1)}, bf16[1,32,2560]{2,1,0:T(8,128)(2,1)S(1)}, u32[]{:S(2)}, u32[]{:S(2)}) %collective-permute-start.21) | collective-permute-done | bytes 163872 | tf_op jit(solution)/shard_map/ppermute | solution.py:89
  137.3 3.6 %all-to-all-start = ((bf16[3,4,8,1,2560]{4,2,3,0,1:T(8,128)(2,1)}), bf16[3,4,8,1,2560]{4,2,3,0,1:T(8,128)(2,1)S(1)}, u32[]{:S(2)}, u32[]{:S(2)}) async-start(bf16[3,4,8,1,2560]{4,2,3,0,1:T(8,128)(2,1)} %copy.83), calls=%async_computation | async-start | bytes 983040 | tf_op jit(solution)/shard_map/all_to_all | solution.py:291
  141.2 8.0 %all-to-all-done = bf16[3,4,8,1,2560]{4,2,3,0,1:T(8,128)(2,1)S(1)} async-done(((bf16[3,4,8,1,2560]{4,2,3,0,1:T(8,128)(2,1)}), bf16[3,4,8,1,2560]{4,2,3,0,1:T(8,128)(2,1)S(1)}, u32[]{:S(2)}, u32[]{:S(2)}) %all-to-all-start) | async-done | bytes 491552 | tf_op jit(solution)/shard_map/all_to_all | solution.py:291
  150.9 4.6 %fusion.117 = (f32[8,8,24]{2,1,0:T(8,128)S(1)}, f32[8,8,24,256]{3,2,1,0:T(8,128)S(1)}) fusion(pred[8,256]{1,0:T(8,128)(4,1)S(1)} %iota_compare_fusion, bf16[8,256,1024]{2,1,0:T(8,128)(2,1)} %param.28, bf16[3,8,8,8,64]{4,3,2,1,0:T(8,128)(2,1)S(1)} %bitcast.225, bf16[3,8,8,8,64]{4,3,2,1,0:T(8,128)(2,1)S(1)} %bitcast.223), kind=kOutput, calls=%fused_computation.241 | convolution fusion | flops 102627840 | bytes 6168576 | tf_op jit(solution)/shard_map/rhqd,rchd->rhqc/dot_general | solution.py:190
  157.2 3.1 %fusion.47 = bf16[8,8,3,8,128]{4,3,2,1,0:T(8,128)(2,1)S(1)} fusion(f32[8,8,24,128]{3,2,1,0:T(8,128)S(1)} %fusion.93, f32[8,8,24,256]{3,2,1,0:T(8,128)S(1)} %get-tuple-element.64, f32[8,8,24]{2,1,0:T(8,128)S(1)} %max.7, pred[8,256]{1,0:T(8,128)(4,1)S(1)} %iota_compare_fusion, f32[8,8,24]{2,1,0:T(8,128)S(1)} %add.499, bf16[8,256,1024]{2,1,0:T(8,128)(2,1)} %param.29), kind=kOutput, calls=%fused_computation.52 | convolution fusion | flops 102432768 | bytes 6961152 | tf_op jit(solution)/shard_map/rhqc,rchd->rhqd/dot_general | solution.py:214
  161.4 3.7 %all-to-all-start.1 = ((bf16[3,1,8,4,2048]{4,2,0,1,3:T(8,128)(2,1)}), bf16[3,1,8,4,2048]{4,2,0,1,3:T(8,128)(2,1)S(1)}, u32[]{:S(2)}, u32[]{:S(2)}) async-start(bf16[3,1,8,4,2048]{4,2,0,1,3:T(8,128)(2,1)} %copy.94), calls=%async_computation.1 | async-start | bytes 786432 | tf_op jit(solution)/shard_map/all_to_all | solution.py:317
  167.0 5.3 %all-to-all-done.1 = bf16[3,1,8,4,2048]{4,2,0,1,3:T(8,128)(2,1)S(1)} async-done(((bf16[3,1,8,4,2048]{4,2,0,1,3:T(8,128)(2,1)}), bf16[3,1,8,4,2048]{4,2,0,1,3:T(8,128)(2,1)S(1)}, u32[]{:S(2)}, u32[]{:S(2)}) %all-to-all-start.1) | async-done | bytes 393248 | tf_op jit(solution)/shard_map/all_to_all | solution.py:317
  176.1 10.5 %collective-permute-done.30 = bf16[1,32,2048]{2,1,0:T(8,128)(2,1)S(1)} collective-permute-done((bf16[1,32,2048]{2,1,0:T(8,128)(2,1)S(1)}, bf16[1,32,2048]{2,1,0:T(8,128)(2,1)S(1)}, u32[]{:S(2)}, u32[]{:S(2)}) %collective-permute-start.30) | collective-permute-done | bytes 131104 | tf_op jit(solution)/shard_map/ppermute | solution.py:116
  192.3 3.6 %collective-permute-done.31 = bf16[2,1,32,2048]{3,2,1,0:T(8,128)(2,1)S(1)} collective-permute-done((bf16[2,1,32,2048]{3,2,1,0:T(8,128)(2,1)S(1)}, bf16[2,1,32,2048]{3,2,1,0:T(8,128)(2,1)S(1)}, u32[]{:S(2)}, u32[]{:S(2)}) %collective-permute-start.31) | collective-permute-done | bytes 262176 | tf_op jit(solution)/shard_map/ppermute | solution.py:121
  198.6 5.1 %collective-permute-done.33 = bf16[2,1,32,2048]{3,2,1,0:T(8,128)(2,1)S(1)} collective-permute-done((bf16[2,1,32,2048]{3,2,1,0:T(8,128)(2,1)S(1)}, bf16[2,1,32,2048]{3,2,1,0:T(8,128)(2,1)S(1)}, u32[]{:S(2)}, u32[]{:S(2)}) %collective-permute-start.33) | collective-permute-done | bytes 262176 | tf_op jit(solution)/shard_map/ppermute | solution.py:121
  210.4 4.7 %collective-permute-done.29 = bf16[2,1,32,2048]{3,2,1,0:T(8,128)(2,1)} collective-permute-done((bf16[2,1,32,2048]{3,2,1,0:T(8,128)(2,1)}, bf16[2,1,32,2048]{3,2,1,0:T(8,128)(2,1)}, u32[]{:S(2)}, u32[]{:S(2)}) %collective-permute-start.29) | collective-permute-done | bytes 262176 | tf_op jit(solution)/shard_map/ppermute | solution.py:121
  222.1 4.2 %collective-permute-done.25 = bf16[2,1,32,2048]{3,2,1,0:T(8,128)(2,1)} collective-permute-done((bf16[2,1,32,2048]{3,2,1,0:T(8,128)(2,1)S(1)}, bf16[2,1,32,2048]{3,2,1,0:T(8,128)(2,1)}, u32[]{:S(2)}, u32[]{:S(2)}) %collective-permute-start.25) | collective-permute-done | bytes 262176 | tf_op jit(solution)/shard_map/ppermute | solution.py:121
  239.6 6.5 %collective-permute-done.35 = f32[3,2,128,64]{2,3,0,1:T(8,128)S(1)} collective-permute-done((f32[3,2,128,64]{2,3,0,1:T(8,128)S(1)}, f32[3,2,128,64]{2,3,0,1:T(8,128)S(1)}, u32[]{:S(2)}, u32[]{:S(2)}) %collective-permute-start.35) | collective-permute-done | bytes 196640 | tf_op jit(solution)/shard_map/ppermute | solution.py:139
  247.4 3.3 %collective-permute-done.36 = bf16[3,2,128,64]{2,3,0,1:T(8,128)(2,1)S(1)} collective-permute-done((bf16[3,2,128,64]{2,3,0,1:T(8,128)(2,1)S(1)}, bf16[3,2,128,64]{2,3,0,1:T(8,128)(2,1)S(1)}, u32[]{:S(2)}, u32[]{:S(2)}) %collective-permute-start.36) | collective-permute-done | bytes 98336 | tf_op jit(solution)/shard_map/ppermute | solution.py:139
  250.8 4.6 %collective-permute-done.37 = bf16[3,2,128,64]{2,3,0,1:T(8,128)(2,1)S(1)} collective-permute-done((bf16[3,2,128,64]{2,3,0,1:T(8,128)(2,1)S(1)}, bf16[3,2,128,64]{2,3,0,1:T(8,128)(2,1)S(1)}, u32[]{:S(2)}, u32[]{:S(2)}) %collective-permute-start.37) | collective-permute-done | bytes 98336 | tf_op jit(solution)/shard_map/ppermute | solution.py:139
  257.4 4.2 %collective-permute-done.38 = bf16[3,2,128,64]{2,3,0,1:T(8,128)(2,1)S(1)} collective-permute-done((bf16[3,2,128,64]{2,3,0,1:T(8,128)(2,1)S(1)}, bf16[3,2,128,64]{2,3,0,1:T(8,128)(2,1)S(1)}, u32[]{:S(2)}, u32[]{:S(2)}) %collective-permute-start.38) | collective-permute-done | bytes 98336 | tf_op jit(solution)/shard_map/ppermute | solution.py:139
  264.8 3.4 %bitcast_add_fusion.1 = f32[3,256,1024]{2,1,0:T(8,128)S(1)} fusion(f32[3,2,128,1024]{3,2,1,0:T(8,128)S(1)} %copy.96, bf16[2048,1024]{1,0:T(8,128)(2,1)S(1)} %copy-done.18, bf16[1,256,2048]{2,1,0:T(8,128)(2,1)S(1)} %bitcast.236, bf16[1,256,2048]{2,1,0:T(8,128)(2,1)S(1)} %bitcast.234, bf16[1,256,2048]{2,1,0:T(8,128)(2,1)S(1)} %bitcast.232), kind=kOutput, calls=%fused_computation.27 | convolution fusion | flops 3225157632 | bytes 13631488 | tf_op jit(solution)/shard_map/tnq,qe->tne/dot_general | solution.py:332
  269.8 3.7 %collective-permute-done.39 = f32[3,2,64,1024]{3,2,0,1:T(8,128)} collective-permute-done((f32[3,2,64,1024]{3,2,0,1:T(8,128)}, f32[3,2,64,1024]{3,2,0,1:T(8,128)}, u32[]{:S(2)}, u32[]{:S(2)}) %collective-permute-start.39) | collective-permute-done | bytes 1572896 | tf_op jit(solution)/shard_map/ppermute | solution.py:164
  277.1 10.7 %collective-permute-done.40 = bf16[3,1,64,1024]{3,2,0,1:T(8,128)(2,1)S(1)} collective-permute-done((bf16[3,1,64,1024]{3,2,0,1:T(8,128)(2,1)S(1)}, bf16[3,1,64,1024]{3,2,0,1:T(8,128)(2,1)S(1)}, u32[]{:S(2)}, u32[]{:S(2)}) %collective-permute-start.40) | collective-permute-done | bytes 393248 | tf_op jit(solution)/shard_map/ppermute | solution.py:164
  (228 shorter events, 111.0 us)
Async XLA Ops:
  3.1 20.9 %collective-permute-start.1 = (bf16[3,128,1024]{2,1,0:T(8,128)(2,1)S(1)}, bf16[3,128,1024]{2,1,0:T(8,128)(2,1)}, u32[]{:S(2)}, u32[]{:S(2)}) collective-permute-start(bf16[3,128,1024]{2,1,0:T(8,128)(2,1)S(1)} %pad_maximum_fusion.1), channel_id=1, source_target_pairs={{0,2},{1,3},{2,0},{3,1},{4,6},{5,7},{6,4},{7,5},{8,10},{9,11},{10,... | collective-permute-start | bytes 2359304 | tf_op jit(solution)/shard_map/ppermute | solution.py:102
  44.3 7.2 %collective-permute-start.6 = (f32[3,2,128,64]{2,3,0,1:T(8,128)S(1)}, f32[3,2,128,64]{2,3,0,1:T(8,128)S(1)}, u32[]{:S(2)}, u32[]{:S(2)}) collective-permute-start(f32[3,2,128,64]{2,3,0,1:T(8,128)S(1)} %add.455), channel_id=1, source_target_pairs={{0,8},{4,12},{8,0},{12,4},{16,24},{20,28},{24,16},{28,20},{1,9},{5... | collective-permute-start | bytes 589832 | tf_op jit(solution)/shard_map/ppermute | solution.py:139
  51.5 8.7 %collective-permute-start.7 = (f32[3,2,128,64]{2,3,0,1:T(8,128)S(1)}, f32[3,2,128,64]{2,3,0,1:T(8,128)S(1)}, u32[]{:S(2)}, u32[]{:S(2)}) collective-permute-start(f32[3,2,128,64]{2,3,0,1:T(8,128)S(1)} %add.456), channel_id=1, source_target_pairs={{0,16},{4,20},{8,24},{12,28},{16,0},{20,4},{24,8},{28,12},{1,17},{... | collective-permute-start | bytes 589832 | tf_op jit(solution)/shard_map/ppermute | solution.py:139
  75.0 16.1 %collective-permute-start.10 = (bf16[2,1,32,2560]{3,2,1,0:T(8,128)(2,1)S(1)}, bf16[2,1,32,2560]{3,2,1,0:T(8,128)(2,1)S(1)}, u32[]{:S(2)}, u32[]{:S(2)}) collective-permute-start(bf16[2,1,32,2560]{3,2,1,0:T(8,128)(2,1)S(1)} %pad_maximum_fusion.3), channel_id=1, source_target_pairs={{0,4},{4,0},{8,12},{12,8},{16,20},{20,16},{24,28},{28,24},{1,5},{5... | collective-permute-start | bytes 983048 | tf_op jit(solution)/shard_map/ppermute | solution.py:84
  76.6 16.1 %collective-permute-start.11 = (bf16[2,1,32,2560]{3,2,1,0:T(8,128)(2,1)S(1)}, bf16[2,1,32,2560]{3,2,1,0:T(8,128)(2,1)S(1)}, u32[]{:S(2)}, u32[]{:S(2)}) collective-permute-start(bf16[2,1,32,2560]{3,2,1,0:T(8,128)(2,1)S(1)} %pad_maximum_fusion.4), channel_id=1, source_target_pairs={{0,8},{4,12},{8,0},{12,4},{16,24},{20,28},{24,16},{28,20},{1,9},{5... | collective-permute-start | bytes 983048 | tf_op jit(solution)/shard_map/ppermute | solution.py:84
  77.2 17.1 %collective-permute-start.12 = (bf16[2,1,32,2560]{3,2,1,0:T(8,128)(2,1)S(1)}, bf16[2,1,32,2560]{3,2,1,0:T(8,128)(2,1)S(1)}, u32[]{:S(2)}, u32[]{:S(2)}) collective-permute-start(bf16[2,1,32,2560]{3,2,1,0:T(8,128)(2,1)S(1)} %pad_maximum_fusion.5), channel_id=1, source_target_pairs={{0,12},{4,8},{8,4},{12,0},{16,28},{20,24},{24,20},{28,16},{1,13},{... | collective-permute-start | bytes 983048 | tf_op jit(solution)/shard_map/ppermute | solution.py:84
  79.2 23.2 %collective-permute-start.14 = (bf16[2,1,32,2560]{3,2,1,0:T(8,128)(2,1)S(1)}, bf16[2,1,32,2560]{3,2,1,0:T(8,128)(2,1)S(1)}, u32[]{:S(2)}, u32[]{:S(2)}) collective-permute-start(bf16[2,1,32,2560]{3,2,1,0:T(8,128)(2,1)S(1)} %pad_maximum_fusion.6), channel_id=1, source_target_pairs={{0,4},{4,0},{8,12},{12,8},{16,20},{20,16},{24,28},{28,24},{1,5},{5... | collective-permute-start | bytes 983048 | tf_op jit(solution)/shard_map/ppermute | solution.py:84
  80.8 25.8 %collective-permute-start.15 = (bf16[2,1,32,2560]{3,2,1,0:T(8,128)(2,1)S(1)}, bf16[2,1,32,2560]{3,2,1,0:T(8,128)(2,1)S(1)}, u32[]{:S(2)}, u32[]{:S(2)}) collective-permute-start(bf16[2,1,32,2560]{3,2,1,0:T(8,128)(2,1)S(1)} %pad_maximum_fusion.7), channel_id=1, source_target_pairs={{0,8},{4,12},{8,0},{12,4},{16,24},{20,28},{24,16},{28,20},{1,9},{5... | collective-permute-start | bytes 983048 | tf_op jit(solution)/shard_map/ppermute | solution.py:84
  91.1 19.1 %collective-permute-start.16 = (bf16[2,1,32,2560]{3,2,1,0:T(8,128)(2,1)S(1)}, bf16[2,1,32,2560]{3,2,1,0:T(8,128)(2,1)S(1)}, u32[]{:S(2)}, u32[]{:S(2)}) collective-permute-start(bf16[2,1,32,2560]{3,2,1,0:T(8,128)(2,1)S(1)} %pad_maximum_fusion.8), channel_id=1, source_target_pairs={{0,12},{4,8},{8,4},{12,0},{16,28},{20,24},{24,20},{28,16},{1,13},{... | collective-permute-start | bytes 983048 | tf_op jit(solution)/shard_map/ppermute | solution.py:84
  92.7 22.7 %collective-permute-start.18 = (bf16[2,1,32,2560]{3,2,1,0:T(8,128)(2,1)S(1)}, bf16[2,1,32,2560]{3,2,1,0:T(8,128)(2,1)S(1)}, u32[]{:S(2)}, u32[]{:S(2)}) collective-permute-start(bf16[2,1,32,2560]{3,2,1,0:T(8,128)(2,1)S(1)} %pad_maximum_fusion.9), channel_id=1, source_target_pairs={{0,4},{4,0},{8,12},{12,8},{16,20},{20,16},{24,28},{28,24},{1,5},{5... | collective-permute-start | bytes 983048 | tf_op jit(solution)/shard_map/ppermute | solution.py:84
  94.3 28.2 %collective-permute-start.19 = (bf16[2,1,32,2560]{3,2,1,0:T(8,128)(2,1)S(1)}, bf16[2,1,32,2560]{3,2,1,0:T(8,128)(2,1)S(1)}, u32[]{:S(2)}, u32[]{:S(2)}) collective-permute-start(bf16[2,1,32,2560]{3,2,1,0:T(8,128)(2,1)S(1)} %pad_maximum_fusion.10), channel_id=1, source_target_pairs={{0,8},{4,12},{8,0},{12,4},{16,24},{20,28},{24,16},{28,20},{1,9},{5... | collective-permute-start | bytes 983048 | tf_op jit(solution)/shard_map/ppermute | solution.py:84
  102.5 25.0 %collective-permute-start.20 = (bf16[2,1,32,2560]{3,2,1,0:T(8,128)(2,1)S(1)}, bf16[2,1,32,2560]{3,2,1,0:T(8,128)(2,1)S(1)}, u32[]{:S(2)}, u32[]{:S(2)}) collective-permute-start(bf16[2,1,32,2560]{3,2,1,0:T(8,128)(2,1)S(1)} %pad_maximum_fusion.11), channel_id=1, source_target_pairs={{0,12},{4,8},{8,4},{12,0},{16,28},{20,24},{24,20},{28,16},{1,13},{... | collective-permute-start | bytes 983048 | tf_op jit(solution)/shard_map/ppermute | solution.py:84
  106.7 22.5 %collective-permute-start.13 = (bf16[1,32,2560]{2,1,0:T(8,128)(2,1)S(1)}, bf16[1,32,2560]{2,1,0:T(8,128)(2,1)S(1)}, u32[]{:S(2)}, u32[]{:S(2)}) collective-permute-start(bf16[1,32,2560]{2,1,0:T(8,128)(2,1)S(1)} %fusion.84), channel_id=1, source_target_pairs={{0,16},{4,20},{8,24},{12,28},{16,0},{20,4},{24,8},{28,12},{1,17},{... | collective-permute-start | bytes 491528 | tf_op jit(solution)/shard_map/ppermute | solution.py:89
  110.3 19.0 %collective-permute-start.17 = (bf16[1,32,2560]{2,1,0:T(8,128)(2,1)S(1)}, bf16[1,32,2560]{2,1,0:T(8,128)(2,1)S(1)}, u32[]{:S(2)}, u32[]{:S(2)}) collective-permute-start(bf16[1,32,2560]{2,1,0:T(8,128)(2,1)S(1)} %fusion.86), channel_id=1, source_target_pairs={{0,16},{4,20},{8,24},{12,28},{16,0},{20,4},{24,8},{28,12},{1,17},{... | collective-permute-start | bytes 491528 | tf_op jit(solution)/shard_map/ppermute | solution.py:89
  127.6 8.7 %collective-permute-start.21 = (bf16[1,32,2560]{2,1,0:T(8,128)(2,1)S(1)}, bf16[1,32,2560]{2,1,0:T(8,128)(2,1)S(1)}, u32[]{:S(2)}, u32[]{:S(2)}) collective-permute-start(bf16[1,32,2560]{2,1,0:T(8,128)(2,1)S(1)} %fusion.88), channel_id=1, source_target_pairs={{0,16},{4,20},{8,24},{12,28},{16,0},{20,4},{24,8},{28,12},{1,17},{... | collective-permute-start | bytes 491528 | tf_op jit(solution)/shard_map/ppermute | solution.py:89
  137.3 11.9 %all-to-all-start = ((bf16[3,4,8,1,2560]{4,2,3,0,1:T(8,128)(2,1)}), bf16[3,4,8,1,2560]{4,2,3,0,1:T(8,128)(2,1)S(1)}, u32[]{:S(2)}, u32[]{:S(2)}) async-start(bf16[3,4,8,1,2560]{4,2,3,0,1:T(8,128)(2,1)} %copy.83), calls=%async_computation | async-start | bytes 983040 | tf_op jit(solution)/shard_map/all_to_all | solution.py:291
  161.4 10.9 %all-to-all-start.1 = ((bf16[3,1,8,4,2048]{4,2,0,1,3:T(8,128)(2,1)}), bf16[3,1,8,4,2048]{4,2,0,1,3:T(8,128)(2,1)S(1)}, u32[]{:S(2)}, u32[]{:S(2)}) async-start(bf16[3,1,8,4,2048]{4,2,0,1,3:T(8,128)(2,1)} %copy.94), calls=%async_computation.1 | async-start | bytes 786432 | tf_op jit(solution)/shard_map/all_to_all | solution.py:317
  172.4 14.2 %collective-permute-start.30 = (bf16[1,32,2048]{2,1,0:T(8,128)(2,1)S(1)}, bf16[1,32,2048]{2,1,0:T(8,128)(2,1)S(1)}, u32[]{:S(2)}, u32[]{:S(2)}) collective-permute-start(bf16[1,32,2048]{2,1,0:T(8,128)(2,1)S(1)} %get-tuple-element.48), channel_id=1, source_target_pairs={{0,16},{4,20},{8,24},{12,28},{16,0},{20,4},{24,8},{28,12},{1,17},{... | collective-permute-start | bytes 393224 | tf_op jit(solution)/shard_map/ppermute | solution.py:116
  173.2 17.0 %collective-permute-start.26 = (bf16[1,32,2048]{2,1,0:T(8,128)(2,1)S(1)}, bf16[1,32,2048]{2,1,0:T(8,128)(2,1)S(1)}, u32[]{:S(2)}, u32[]{:S(2)}) collective-permute-start(bf16[1,32,2048]{2,1,0:T(8,128)(2,1)S(1)} %get-tuple-element.47), channel_id=1, source_target_pairs={{0,16},{4,20},{8,24},{12,28},{16,0},{20,4},{24,8},{28,12},{1,17},{... | collective-permute-start | bytes 393224 | tf_op jit(solution)/shard_map/ppermute | solution.py:116
  176.1 16.2 %collective-permute-start.22 = (bf16[1,32,2048]{2,1,0:T(8,128)(2,1)S(1)}, bf16[1,32,2048]{2,1,0:T(8,128)(2,1)S(1)}, u32[]{:S(2)}, u32[]{:S(2)}) collective-permute-start(bf16[1,32,2048]{2,1,0:T(8,128)(2,1)S(1)} %get-tuple-element.46), channel_id=1, source_target_pairs={{0,16},{4,20},{8,24},{12,28},{16,0},{20,4},{24,8},{28,12},{1,17},{... | collective-permute-start | bytes 393224 | tf_op jit(solution)/shard_map/ppermute | solution.py:116
  186.7 9.2 %collective-permute-start.31 = (bf16[2,1,32,2048]{3,2,1,0:T(8,128)(2,1)S(1)}, bf16[2,1,32,2048]{3,2,1,0:T(8,128)(2,1)S(1)}, u32[]{:S(2)}, u32[]{:S(2)}) collective-permute-start(bf16[2,1,32,2048]{3,2,1,0:T(8,128)(2,1)S(1)} %pad_maximum_fusion.14), channel_id=1, source_target_pairs={{0,4},{4,0},{8,12},{12,8},{16,20},{20,16},{24,28},{28,24},{1,5},{5... | collective-permute-start | bytes 786440 | tf_op jit(solution)/shard_map/ppermute | solution.py:121
  187.4 10.4 %collective-permute-start.32 = (bf16[2,1,32,2048]{3,2,1,0:T(8,128)(2,1)S(1)}, bf16[2,1,32,2048]{3,2,1,0:T(8,128)(2,1)S(1)}, u32[]{:S(2)}, u32[]{:S(2)}) collective-permute-start(bf16[2,1,32,2048]{3,2,1,0:T(8,128)(2,1)S(1)} %pad_maximum_fusion.14), channel_id=1, source_target_pairs={{0,8},{4,12},{8,0},{12,4},{16,24},{20,28},{24,16},{28,20},{1,9},{5... | collective-permute-start | bytes 786440 | tf_op jit(solution)/shard_map/ppermute | solution.py:121
  187.4 16.2 %collective-permute-start.33 = (bf16[2,1,32,2048]{3,2,1,0:T(8,128)(2,1)S(1)}, bf16[2,1,32,2048]{3,2,1,0:T(8,128)(2,1)S(1)}, u32[]{:S(2)}, u32[]{:S(2)}) collective-permute-start(bf16[2,1,32,2048]{3,2,1,0:T(8,128)(2,1)S(1)} %pad_maximum_fusion.14), channel_id=1, source_target_pairs={{0,12},{4,8},{8,4},{12,0},{16,28},{20,24},{24,20},{28,16},{1,13},{... | collective-permute-start | bytes 786440 | tf_op jit(solution)/shard_map/ppermute | solution.py:121
  190.9 16.2 %collective-permute-start.27 = (bf16[2,1,32,2048]{3,2,1,0:T(8,128)(2,1)}, bf16[2,1,32,2048]{3,2,1,0:T(8,128)(2,1)S(1)}, u32[]{:S(2)}, u32[]{:S(2)}) collective-permute-start(bf16[2,1,32,2048]{3,2,1,0:T(8,128)(2,1)} %pad_maximum_fusion.13), channel_id=1, source_target_pairs={{0,4},{4,0},{8,12},{12,8},{16,20},{20,16},{24,28},{28,24},{1,5},{5... | collective-permute-start | bytes 786440 | tf_op jit(solution)/shard_map/ppermute | solution.py:121
  192.3 17.2 %collective-permute-start.28 = (bf16[2,1,32,2048]{3,2,1,0:T(8,128)(2,1)}, bf16[2,1,32,2048]{3,2,1,0:T(8,128)(2,1)}, u32[]{:S(2)}, u32[]{:S(2)}) collective-permute-start(bf16[2,1,32,2048]{3,2,1,0:T(8,128)(2,1)} %pad_maximum_fusion.13), channel_id=1, source_target_pairs={{0,8},{4,12},{8,0},{12,4},{16,24},{20,28},{24,16},{28,20},{1,9},{5... | collective-permute-start | bytes 786440 | tf_op jit(solution)/shard_map/ppermute | solution.py:121
  195.9 19.2 %collective-permute-start.29 = (bf16[2,1,32,2048]{3,2,1,0:T(8,128)(2,1)}, bf16[2,1,32,2048]{3,2,1,0:T(8,128)(2,1)}, u32[]{:S(2)}, u32[]{:S(2)}) collective-permute-start(bf16[2,1,32,2048]{3,2,1,0:T(8,128)(2,1)} %pad_maximum_fusion.13), channel_id=1, source_target_pairs={{0,12},{4,8},{8,4},{12,0},{16,28},{20,24},{24,20},{28,16},{1,13},{... | collective-permute-start | bytes 786440 | tf_op jit(solution)/shard_map/ppermute | solution.py:121
  197.9 22.9 %collective-permute-start.23 = (bf16[2,1,32,2048]{3,2,1,0:T(8,128)(2,1)S(1)}, bf16[2,1,32,2048]{3,2,1,0:T(8,128)(2,1)S(1)}, u32[]{:S(2)}, u32[]{:S(2)}) collective-permute-start(bf16[2,1,32,2048]{3,2,1,0:T(8,128)(2,1)S(1)} %pad_maximum_fusion.12), channel_id=1, source_target_pairs={{0,4},{4,0},{8,12},{12,8},{16,20},{20,16},{24,28},{28,24},{1,5},{5... | collective-permute-start | bytes 786440 | tf_op jit(solution)/shard_map/ppermute | solution.py:121
  203.7 17.7 %collective-permute-start.24 = (bf16[2,1,32,2048]{3,2,1,0:T(8,128)(2,1)S(1)}, bf16[2,1,32,2048]{3,2,1,0:T(8,128)(2,1)S(1)}, u32[]{:S(2)}, u32[]{:S(2)}) collective-permute-start(bf16[2,1,32,2048]{3,2,1,0:T(8,128)(2,1)S(1)} %pad_maximum_fusion.12), channel_id=1, source_target_pairs={{0,8},{4,12},{8,0},{12,4},{16,24},{20,28},{24,16},{28,20},{1,9},{5... | collective-permute-start | bytes 786440 | tf_op jit(solution)/shard_map/ppermute | solution.py:121
  207.1 19.1 %collective-permute-start.25 = (bf16[2,1,32,2048]{3,2,1,0:T(8,128)(2,1)S(1)}, bf16[2,1,32,2048]{3,2,1,0:T(8,128)(2,1)}, u32[]{:S(2)}, u32[]{:S(2)}) collective-permute-start(bf16[2,1,32,2048]{3,2,1,0:T(8,128)(2,1)S(1)} %pad_maximum_fusion.12), channel_id=1, source_target_pairs={{0,12},{4,8},{8,4},{12,0},{16,28},{20,24},{24,20},{28,16},{1,13},{... | collective-permute-start | bytes 786440 | tf_op jit(solution)/shard_map/ppermute | solution.py:121
  239.0 7.0 %collective-permute-start.35 = (f32[3,2,128,64]{2,3,0,1:T(8,128)S(1)}, f32[3,2,128,64]{2,3,0,1:T(8,128)S(1)}, u32[]{:S(2)}, u32[]{:S(2)}) collective-permute-start(f32[3,2,128,64]{2,3,0,1:T(8,128)S(1)} %add.500), channel_id=1, source_target_pairs={{0,2},{1,3},{2,0},{3,1},{4,6},{5,7},{6,4},{7,5},{8,10},{9,11},{10,... | collective-permute-start | bytes 589832 | tf_op jit(solution)/shard_map/ppermute | solution.py:139
  255.5 6.1 %collective-permute-start.38 = (bf16[3,2,128,64]{2,3,0,1:T(8,128)(2,1)S(1)}, bf16[3,2,128,64]{2,3,0,1:T(8,128)(2,1)S(1)}, u32[]{:S(2)}, u32[]{:S(2)}) collective-permute-start(bf16[3,2,128,64]{2,3,0,1:T(8,128)(2,1)S(1)} %add.503), channel_id=1, source_target_pairs={{0,16},{4,20},{8,24},{12,28},{16,0},{20,4},{24,8},{28,12},{1,17},{... | collective-permute-start | bytes 294920 | tf_op jit(solution)/shard_map/ppermute | solution.py:139
  276.5 11.2 %collective-permute-start.40 = (bf16[3,1,64,1024]{3,2,0,1:T(8,128)(2,1)S(1)}, bf16[3,1,64,1024]{3,2,0,1:T(8,128)(2,1)S(1)}, u32[]{:S(2)}, u32[]{:S(2)}) collective-permute-start(bf16[3,1,64,1024]{3,2,0,1:T(8,128)(2,1)S(1)} %dynamic-slice_convert_fusion), channel_id=1, source_target_pairs={{0,2},{1,3},{2,0},{3,1},{4,6},{5,7},{6,4},{7,5},{8,10},{9,11},{10,... | collective-permute-start | bytes 1179656 | tf_op jit(solution)/shard_map/ppermute | solution.py:164
  (31 other events, 192.9 us)

commit v10 on v9

--- a/solution.py
+++ b/solution.py
@@ -61,6 +61,33 @@
             for step in range(value.shape[0])
         ]
     )
+
+
+def ring_gather(value, axis_name, axis_size):
+    if axis_size < 4 or axis_size % 2:
+        return lax.all_gather(value, axis_name, axis=1, tiled=True)
+    ring = list(range(0, axis_size, 2)) + list(range(axis_size - 1, 0, -2))
+    place = [0] * axis_size
+    for position, index in enumerate(ring):
+        place[index] = position
+    ahead = [(ring[p], ring[(p + 1) % axis_size]) for p in range(axis_size)]
+    behind = [(ring[p], ring[(p - 1) % axis_size]) for p in range(axis_size)]
+    slots = [None] * axis_size
+    slots[0] = value
+    forward = backward = value
+    for hop in range(1, axis_size // 2 + 1):
+        forward = lax.ppermute(forward, axis_name, ahead)
+        slots[(-hop) % axis_size] = forward
+        if hop < axis_size - hop:
+            backward = lax.ppermute(backward, axis_name, behind)
+            slots[hop] = backward
+    stacked = jnp.stack(slots)
+    places = jnp.asarray(place, dtype=jnp.int32)
+    me = lax.axis_index(axis_name)
+    order = (places - places[me]) % axis_size
+    gathered = jnp.take(stacked, order, axis=0)
+    steps, rows, columns = value.shape
+    return gathered.transpose(1, 0, 2, 3).reshape(steps, axis_size * rows, columns)
 
 
 def split_half_scatter(partial, axis_name, axis_size):
@@ -317,7 +344,7 @@
     head_group = lax.all_to_all(
         mixed_local.reshape(steps, local_rows, across_second, -1), "gy", 2, 1, tiled=False
     ).reshape(steps, across_second * local_rows, -1)
-    mixed_all = split_half_gather_steps(head_group, "gx", across_first)
+    mixed_all = ring_gather(head_group, "gx", across_first)
     rank_part_out = jnp.einsum(
         "tbnq,bqr->tbnr",
         mixed_all.reshape(steps, block_count, block_rows, -1),

time: 291 us -> 274 us (0.942)
  local copies, waits for them, and re-layouts: 32.3 us -> 22.1 us
  waiting for transfers between devices: 154 us -> 151 us
    unnamed x59 -> x27, local copies, waits for them, and re-layouts: 16 us -> 9.43 us
    gather x3 -> x1, local copies, waits for them, and re-layouts: 6.51 us -> 2.64 us  [ring_gather(): gathered = jnp.take(stacked, order, axis=0)]
    ppermute x12 -> x7, starting transfers between devices: 10.4 us -> 6.69 us  [the longest x3 4.47 us: ring_gather(): backward = lax.ppermute(backward, axis_name, behind)]
    ppermute x12 -> x7, waiting for transfers between devices: 31.1 us -> 29.2 us  [the longest x3 14.8 us: ring_gather(): backward = lax.ppermute(backward, axis_name, behind)]
  transfers between devices with their start and end apart: 43 -> 38, of which waited for: 34 -> 30; matrix products, arithmetic and copies ran while one was open for 7% -> 5% of each run, Pallas kernels for 0% -> 0%
where the time goes in v10:
time: 274 us; the launch traced here: 273 us
  waiting for transfers between devices  151 us (55%)
  starting transfers between devices  55.7 us (20%)
  local copies, waits for them, and re-layouts  22.1 us (8%)
  matrix products  20.2 us (7%)
  other arithmetic  18.2 us (7%)
  between operations  5.9 us (2%)
    ppermute x13, waiting for transfers between devices, tree_sum(): value = value + lax.ppermute(value, axis_name, pairs)  41.3 us
    ppermute x9, waiting for transfers between devices, split_half_scatter(): lax.ppermute(outgoing, axis_name, [(i, i ^ offset) for i in range(axis_si...  33.4 us
    ppermute x13, starting transfers between devices, tree_sum(): value = value + lax.ppermute(value, axis_name, pairs)  17.9 us
    ppermute x3, waiting for transfers between devices, ring_gather(): backward = lax.ppermute(backward, axis_name, behind)  14.8 us
    ppermute x4, waiting for transfers between devices, ring_gather(): forward = lax.ppermute(forward, axis_name, ahead)  14.4 us
    ppermute x2, waiting for transfers between devices, halving_scatter(): held = keep + lax.ppermute(give, axis_name, swap).astype(jnp.float32)  13.7 us
    ppermute x9, starting transfers between devices, split_half_scatter(): lax.ppermute(outgoing, axis_name, [(i, i ^ offset) for i in range(axis_si...  12.7 us
    ppermute x2, waiting for transfers between devices, doubling_gather(): lax.ppermute(held, axis_name, [(i, i ^ distance) for i in range(axis_size)])  12.6 us
  transfers between devices with their start and end apart: 38, of which 30 were waited for; matrix products, arithmetic and copies ran while one was open for 5% of the time, Pallas kernels for 0%

profile of v10, /device:TPU:0, one launch (start us, length us, event | category | flops | bytes accessed | tf_op | source)
XLA Modules:
  0.0 272.9 jit_solution(11188041989819831981)
XLA Ops:
  3.1 3.0 %collective-permute-start.1 = (bf16[3,128,1024]{2,1,0:T(8,128)(2,1)S(1)}, bf16[3,128,1024]{2,1,0:T(8,128)(2,1)}, u32[]{:S(2)}, u32[]{:S(2)}) collective-permute-start(bf16[3,128,1024]{2,1,0:T(8,128)(2,1)S(1)} %pad_maximum_fusion.1), channel_id=1, source_target_pairs={{0,2},{1,3},{2,0},{3,1},{4,6},{5,7},{6,4},{7,5},{8,10},{9,11},{10,... | collective-permute-start | bytes 2359304 | tf_op jit(solution)/shard_map/ppermute | solution.py:129
  13.0 11.0 %collective-permute-done.1 = bf16[3,128,1024]{2,1,0:T(8,128)(2,1)} collective-permute-done((bf16[3,128,1024]{2,1,0:T(8,128)(2,1)S(1)}, bf16[3,128,1024]{2,1,0:T(8,128)(2,1)}, u32[]{:S(2)}, u32[]{:S(2)}) %collective-permute-start.1) | collective-permute-done | bytes 786464 | tf_op jit(solution)/shard_map/ppermute | solution.py:129
  40.3 4.0 %collective-permute-done.5 = f32[3,2,128,64]{2,3,0,1:T(8,128)S(1)} collective-permute-done((f32[3,2,128,64]{2,3,0,1:T(8,128)S(1)}, f32[3,2,128,64]{2,3,0,1:T(8,128)S(1)}, u32[]{:S(2)}, u32[]{:S(2)}) %collective-permute-start.5) | collective-permute-done | bytes 196640 | tf_op jit(solution)/shard_map/ppermute | solution.py:166
  46.2 5.2 %collective-permute-done.6 = f32[3,2,128,64]{2,3,0,1:T(8,128)S(1)} collective-permute-done((f32[3,2,128,64]{2,3,0,1:T(8,128)S(1)}, f32[3,2,128,64]{2,3,0,1:T(8,128)S(1)}, u32[]{:S(2)}, u32[]{:S(2)}) %collective-permute-start.6) | collective-permute-done | bytes 196640 | tf_op jit(solution)/shard_map/ppermute | solution.py:166
  54.7 5.5 %collective-permute-done.7 = f32[3,2,128,64]{2,3,0,1:T(8,128)S(1)} collective-permute-done((f32[3,2,128,64]{2,3,0,1:T(8,128)S(1)}, f32[3,2,128,64]{2,3,0,1:T(8,128)S(1)}, u32[]{:S(2)}, u32[]{:S(2)}) %collective-permute-start.7) | collective-permute-done | bytes 196640 | tf_op jit(solution)/shard_map/ppermute | solution.py:166
  69.8 3.5 %bitcast_add_fusion = f32[3,256,2048]{2,1,0:T(8,128)S(1)} fusion(f32[3,2,128,2048]{3,2,1,0:T(8,128)S(1)} %copy.76, bf16[1024,2048]{1,0:T(8,128)(2,1)S(1)} %copy-done.7, f32[1024]{0:T(1024)S(1)} %convert_element_type.196, f32[3,256]{1,0:T(4,128)S(1)} %add_rsqrt_fusion, bf16[3,128,1024]{2,1,0:T(8,128)(2,1)S(1)} %get-tuple-element.21, ...), kind=kOutput, calls=%fused_computation.2 | convolution fusion | flops 3228303360 | bytes 18357248 | tf_op jit(solution)/shard_map/tnd,de->tne/dot_general | solution.py:308
  81.5 9.5 %collective-permute-done.10 = bf16[2,1,32,2560]{3,2,1,0:T(8,128)(2,1)S(1)} collective-permute-done((bf16[2,1,32,2560]{3,2,1,0:T(8,128)(2,1)S(1)}, bf16[2,1,32,2560]{3,2,1,0:T(8,128)(2,1)S(1)}, u32[]{:S(2)}, u32[]{:S(2)}) %collective-permute-start.10) | collective-permute-done | bytes 327712 | tf_op jit(solution)/shard_map/ppermute | solution.py:111
  95.0 7.4 %collective-permute-done.14 = bf16[2,1,32,2560]{3,2,1,0:T(8,128)(2,1)S(1)} collective-permute-done((bf16[2,1,32,2560]{3,2,1,0:T(8,128)(2,1)S(1)}, bf16[2,1,32,2560]{3,2,1,0:T(8,128)(2,1)S(1)}, u32[]{:S(2)}, u32[]{:S(2)}) %collective-permute-start.14) | collective-permute-done | bytes 327712 | tf_op jit(solution)/shard_map/ppermute | solution.py:111
  102.4 4.1 %collective-permute-start.20 = (bf16[2,1,32,2560]{3,2,1,0:T(8,128)(2,1)S(1)}, bf16[2,1,32,2560]{3,2,1,0:T(8,128)(2,1)S(1)}, u32[]{:S(2)}, u32[]{:S(2)}) collective-permute-start(bf16[2,1,32,2560]{3,2,1,0:T(8,128)(2,1)S(1)} %pad_maximum_fusion.11), channel_id=1, source_target_pairs={{0,12},{4,8},{8,4},{12,0},{16,28},{20,24},{24,20},{28,16},{1,13},{... | collective-permute-start | bytes 983048 | tf_op jit(solution)/shard_map/ppermute | solution.py:111
  106.7 3.4 %collective-permute-done.16 = bf16[2,1,32,2560]{3,2,1,0:T(8,128)(2,1)S(1)} collective-permute-done((bf16[2,1,32,2560]{3,2,1,0:T(8,128)(2,1)S(1)}, bf16[2,1,32,2560]{3,2,1,0:T(8,128)(2,1)S(1)}, u32[]{:S(2)}, u32[]{:S(2)}) %collective-permute-start.16) | collective-permute-done | bytes 327712 | tf_op jit(solution)/shard_map/ppermute | solution.py:111
  110.2 5.1 %collective-permute-start.17 = (bf16[1,32,2560]{2,1,0:T(8,128)(2,1)S(1)}, bf16[1,32,2560]{2,1,0:T(8,128)(2,1)S(1)}, u32[]{:S(2)}, u32[]{:S(2)}) collective-permute-start(bf16[1,32,2560]{2,1,0:T(8,128)(2,1)S(1)} %fusion.77), channel_id=1, source_target_pairs={{0,16},{4,20},{8,24},{12,28},{16,0},{20,4},{24,8},{28,12},{1,17},{... | collective-permute-start | bytes 491528 | tf_op jit(solution)/shard_map/ppermute | solution.py:116
  115.3 7.1 %collective-permute-done.19 = bf16[2,1,32,2560]{3,2,1,0:T(8,128)(2,1)S(1)} collective-permute-done((bf16[2,1,32,2560]{3,2,1,0:T(8,128)(2,1)S(1)}, bf16[2,1,32,2560]{3,2,1,0:T(8,128)(2,1)S(1)}, u32[]{:S(2)}, u32[]{:S(2)}) %collective-permute-start.19) | collective-permute-done | bytes 327712 | tf_op jit(solution)/shard_map/ppermute | solution.py:111
  122.5 5.0 %collective-permute-done.20 = bf16[2,1,32,2560]{3,2,1,0:T(8,128)(2,1)S(1)} collective-permute-done((bf16[2,1,32,2560]{3,2,1,0:T(8,128)(2,1)S(1)}, bf16[2,1,32,2560]{3,2,1,0:T(8,128)(2,1)S(1)}, u32[]{:S(2)}, u32[]{:S(2)}) %collective-permute-start.20) | collective-permute-done | bytes 327712 | tf_op jit(solution)/shard_map/ppermute | solution.py:111
  129.3 7.0 %collective-permute-done.21 = bf16[1,32,2560]{2,1,0:T(8,128)(2,1)S(1)} collective-permute-done((bf16[1,32,2560]{2,1,0:T(8,128)(2,1)S(1)}, bf16[1,32,2560]{2,1,0:T(8,128)(2,1)S(1)}, u32[]{:S(2)}, u32[]{:S(2)}) %collective-permute-start.21) | collective-permute-done | bytes 163872 | tf_op jit(solution)/shard_map/ppermute | solution.py:116
  137.2 3.6 %all-to-all-start = ((bf16[3,4,8,1,2560]{4,2,3,0,1:T(8,128)(2,1)}), bf16[3,4,8,1,2560]{4,2,3,0,1:T(8,128)(2,1)S(1)}, u32[]{:S(2)}, u32[]{:S(2)}) async-start(bf16[3,4,8,1,2560]{4,2,3,0,1:T(8,128)(2,1)} %copy.81), calls=%async_computation | async-start | bytes 983040 | tf_op jit(solution)/shard_map/all_to_all | solution.py:318
  141.1 8.0 %all-to-all-done = bf16[3,4,8,1,2560]{4,2,3,0,1:T(8,128)(2,1)S(1)} async-done(((bf16[3,4,8,1,2560]{4,2,3,0,1:T(8,128)(2,1)}), bf16[3,4,8,1,2560]{4,2,3,0,1:T(8,128)(2,1)S(1)}, u32[]{:S(2)}, u32[]{:S(2)}) %all-to-all-start) | async-done | bytes 491552 | tf_op jit(solution)/shard_map/all_to_all | solution.py:318
  150.9 4.6 %fusion.104 = (f32[8,8,24]{2,1,0:T(8,128)S(1)}, f32[8,8,24,256]{3,2,1,0:T(8,128)S(1)}) fusion(pred[8,256]{1,0:T(8,128)(4,1)S(1)} %iota_compare_fusion, bf16[8,256,1024]{2,1,0:T(8,128)(2,1)} %param.27, bf16[3,8,8,8,64]{4,3,2,1,0:T(8,128)(2,1)S(1)} %bitcast.211, bf16[3,8,8,8,64]{4,3,2,1,0:T(8,128)(2,1)S(1)} %bitcast.209), kind=kOutput, calls=%fused_computation.206 | convolution fusion | flops 102627840 | bytes 6168576 | tf_op jit(solution)/shard_map/rhqd,rchd->rhqc/dot_general | solution.py:217
  157.1 3.1 %fusion.38 = bf16[8,8,3,8,128]{4,3,2,1,0:T(8,128)(2,1)S(1)} fusion(f32[8,8,24,128]{3,2,1,0:T(8,128)S(1)} %fusion.84, f32[8,8,24,256]{3,2,1,0:T(8,128)S(1)} %get-tuple-element.53, f32[8,8,24]{2,1,0:T(8,128)S(1)} %max.7, pred[8,256]{1,0:T(8,128)(4,1)S(1)} %iota_compare_fusion, f32[8,8,24]{2,1,0:T(8,128)S(1)} %add.509, bf16[8,256,1024]{2,1,0:T(8,128)(2,1)} %param.28), kind=kOutput, calls=%fused_computation.39 | convolution fusion | flops 102432768 | bytes 6961152 | tf_op jit(solution)/shard_map/rhqc,rchd->rhqd/dot_general | solution.py:241
  161.4 3.5 %all-to-all-start.1 = ((bf16[3,1,8,4,2048]{4,2,0,1,3:T(8,128)(2,1)}), bf16[3,1,8,4,2048]{4,2,0,1,3:T(8,128)(2,1)S(1)}, u32[]{:S(2)}, u32[]{:S(2)}) async-start(bf16[3,1,8,4,2048]{4,2,0,1,3:T(8,128)(2,1)} %copy.92), calls=%async_computation.1 | async-start | bytes 786432 | tf_op jit(solution)/shard_map/all_to_all | solution.py:344
  166.6 5.6 %all-to-all-done.1 = bf16[3,1,8,4,2048]{4,2,0,1,3:T(8,128)(2,1)S(1)} async-done(((bf16[3,1,8,4,2048]{4,2,0,1,3:T(8,128)(2,1)}), bf16[3,1,8,4,2048]{4,2,0,1,3:T(8,128)(2,1)S(1)}, u32[]{:S(2)}, u32[]{:S(2)}) %all-to-all-start.1) | async-done | bytes 393248 | tf_op jit(solution)/shard_map/all_to_all | solution.py:344
  175.1 7.9 %collective-permute-done.22 = bf16[3,32,2048]{2,1,0:T(8,128)(2,1)S(1)} collective-permute-done((bf16[3,32,2048]{2,1,0:T(8,128)(2,1)S(1)}, bf16[3,32,2048]{2,1,0:T(8,128)(2,1)S(1)}, u32[]{:S(2)}, u32[]{:S(2)}) %collective-permute-start.22) | collective-permute-done | bytes 393248 | tf_op jit(solution)/shard_map/ppermute | solution.py:82
  185.8 6.9 %collective-permute-done.23 = bf16[3,32,2048]{2,1,0:T(8,128)(2,1)S(1)} collective-permute-done((bf16[3,32,2048]{2,1,0:T(8,128)(2,1)S(1)}, bf16[3,32,2048]{2,1,0:T(8,128)(2,1)S(1)}, u32[]{:S(2)}, u32[]{:S(2)}) %collective-permute-start.23) | collective-permute-done | bytes 393248 | tf_op jit(solution)/shard_map/ppermute | solution.py:82
  195.6 7.9 %collective-permute-done.27 = bf16[3,32,2048]{2,1,0:T(8,128)(2,1)S(1)} collective-permute-done((bf16[3,32,2048]{2,1,0:T(8,128)(2,1)S(1)}, bf16[3,32,2048]{2,1,0:T(8,128)(2,1)S(1)}, u32[]{:S(2)}, u32[]{:S(2)}) %collective-permute-start.27) | collective-permute-done | bytes 393248 | tf_op jit(solution)/shard_map/ppermute | solution.py:79
  204.9 6.4 %collective-permute-done.28 = bf16[3,32,2048]{2,1,0:T(8,128)(2,1)S(1)} collective-permute-done((bf16[3,32,2048]{2,1,0:T(8,128)(2,1)S(1)}, bf16[3,32,2048]{2,1,0:T(8,128)(2,1)S(1)}, u32[]{:S(2)}, u32[]{:S(2)}) %collective-permute-start.28) | collective-permute-done | bytes 393248 | tf_op jit(solution)/shard_map/ppermute | solution.py:79
  222.2 5.8 %collective-permute-done.30 = f32[3,2,128,64]{2,3,0,1:T(8,128)S(1)} collective-permute-done((f32[3,2,128,64]{2,3,0,1:T(8,128)S(1)}, f32[3,2,128,64]{2,3,0,1:T(8,128)S(1)}, u32[]{:S(2)}, u32[]{:S(2)}) %collective-permute-start.30) | collective-permute-done | bytes 196640 | tf_op jit(solution)/shard_map/ppermute | solution.py:166
  228.9 3.8 %collective-permute-done.31 = bf16[3,2,128,64]{2,3,0,1:T(8,128)(2,1)S(1)} collective-permute-done((bf16[3,2,128,64]{2,3,0,1:T(8,128)(2,1)S(1)}, bf16[3,2,128,64]{2,3,0,1:T(8,128)(2,1)S(1)}, u32[]{:S(2)}, u32[]{:S(2)}) %collective-permute-start.31) | collective-permute-done | bytes 98336 | tf_op jit(solution)/shard_map/ppermute | solution.py:166
  233.4 4.1 %collective-permute-done.32 = bf16[3,2,128,64]{2,3,0,1:T(8,128)(2,1)S(1)} collective-permute-done((bf16[3,2,128,64]{2,3,0,1:T(8,128)(2,1)S(1)}, bf16[3,2,128,64]{2,3,0,1:T(8,128)(2,1)S(1)}, u32[]{:S(2)}, u32[]{:S(2)}) %collective-permute-start.32) | collective-permute-done | bytes 98336 | tf_op jit(solution)/shard_map/ppermute | solution.py:166
  239.3 4.8 %collective-permute-done.33 = bf16[3,2,128,64]{2,3,0,1:T(8,128)(2,1)S(1)} collective-permute-done((bf16[3,2,128,64]{2,3,0,1:T(8,128)(2,1)S(1)}, bf16[3,2,128,64]{2,3,0,1:T(8,128)(2,1)S(1)}, u32[]{:S(2)}, u32[]{:S(2)}) %collective-permute-start.33) | collective-permute-done | bytes 98336 | tf_op jit(solution)/shard_map/ppermute | solution.py:166
  246.9 3.5 %bitcast_add_fusion.1 = f32[3,256,1024]{2,1,0:T(8,128)S(1)} fusion(f32[3,2,128,1024]{3,2,1,0:T(8,128)S(1)} %copy.97, bf16[3,256,2048]{2,1,0:T(8,128)(2,1)S(1)} %bitcast.205, bf16[2048,1024]{1,0:T(8,128)(2,1)S(1)} %copy-done.8), kind=kOutput, calls=%fused_computation.14 | convolution fusion | flops 3222011904 | bytes 13631488 | tf_op jit(solution)/shard_map/tnq,qe->tne/dot_general | solution.py:359
  251.9 3.7 %collective-permute-done.34 = f32[3,2,64,1024]{3,2,0,1:T(8,128)} collective-permute-done((f32[3,2,64,1024]{3,2,0,1:T(8,128)}, f32[3,2,64,1024]{3,2,0,1:T(8,128)}, u32[]{:S(2)}, u32[]{:S(2)}) %collective-permute-start.34) | collective-permute-done | bytes 1572896 | tf_op jit(solution)/shard_map/ppermute | solution.py:191
  255.7 2.9 %bitcast_add_fusion.2 = f32[3,2,64,1024]{3,2,0,1:T(8,128)} fusion(f32[3,2,64,1024]{3,2,0,1:T(8,128)} %collective-permute-done.34, f32[3,2,1,64,1024]{4,3,2,1,0:T(8,128)S(1)} %get-tuple-element.18), kind=kLoop, calls=%fused_computation.25 | loop fusion | flops 393216 | bytes 4718592 | tf_op jit(solution)/shard_map/add | solution.py:191
  261.0 10.0 %collective-permute-done.35 = bf16[3,1,64,1024]{3,2,0,1:T(8,128)(2,1)S(1)} collective-permute-done((bf16[3,1,64,1024]{3,2,0,1:T(8,128)(2,1)S(1)}, bf16[3,1,64,1024]{3,2,0,1:T(8,128)(2,1)S(1)}, u32[]{:S(2)}, u32[]{:S(2)}) %collective-permute-start.35) | collective-permute-done | bytes 393248 | tf_op jit(solution)/shard_map/ppermute | solution.py:191
  (179 shorter events, 90.1 us)
Async XLA Ops:
  3.1 20.9 %collective-permute-start.1 = (bf16[3,128,1024]{2,1,0:T(8,128)(2,1)S(1)}, bf16[3,128,1024]{2,1,0:T(8,128)(2,1)}, u32[]{:S(2)}, u32[]{:S(2)}) collective-permute-start(bf16[3,128,1024]{2,1,0:T(8,128)(2,1)S(1)} %pad_maximum_fusion.1), channel_id=1, source_target_pairs={{0,2},{1,3},{2,0},{3,1},{4,6},{5,7},{6,4},{7,5},{8,10},{9,11},{10,... | collective-permute-start | bytes 2359304 | tf_op jit(solution)/shard_map/ppermute | solution.py:129
  33.3 4.5 %collective-permute-start.4 = (f32[3,256]{1,0:T(4,128)S(1)}, f32[3,256]{1,0:T(4,128)S(1)}, u32[]{:S(2)}, u32[]{:S(2)}) collective-permute-start(f32[3,256]{1,0:T(4,128)S(1)} %add.454), channel_id=1, source_target_pairs={{0,16},{4,20},{8,24},{12,28},{16,0},{20,4},{24,8},{28,12},{1,17},{... | collective-permute-start | bytes 9224 | tf_op jit(solution)/shard_map/ppermute | solution.py:166
  38.5 5.7 %collective-permute-start.5 = (f32[3,2,128,64]{2,3,0,1:T(8,128)S(1)}, f32[3,2,128,64]{2,3,0,1:T(8,128)S(1)}, u32[]{:S(2)}, u32[]{:S(2)}) collective-permute-start(f32[3,2,128,64]{2,3,0,1:T(8,128)S(1)} %fusion.25), channel_id=1, source_target_pairs={{0,4},{4,0},{8,12},{12,8},{16,20},{20,16},{24,28},{28,24},{1,5},{5... | collective-permute-start | bytes 589832 | tf_op jit(solution)/shard_map/ppermute | solution.py:166
  44.2 7.2 %collective-permute-start.6 = (f32[3,2,128,64]{2,3,0,1:T(8,128)S(1)}, f32[3,2,128,64]{2,3,0,1:T(8,128)S(1)}, u32[]{:S(2)}, u32[]{:S(2)}) collective-permute-start(f32[3,2,128,64]{2,3,0,1:T(8,128)S(1)} %add.466), channel_id=1, source_target_pairs={{0,8},{4,12},{8,0},{12,4},{16,24},{20,28},{24,16},{28,20},{1,9},{5... | collective-permute-start | bytes 589832 | tf_op jit(solution)/shard_map/ppermute | solution.py:166
  51.5 8.7 %collective-permute-start.7 = (f32[3,2,128,64]{2,3,0,1:T(8,128)S(1)}, f32[3,2,128,64]{2,3,0,1:T(8,128)S(1)}, u32[]{:S(2)}, u32[]{:S(2)}) collective-permute-start(f32[3,2,128,64]{2,3,0,1:T(8,128)S(1)} %add.467), channel_id=1, source_target_pairs={{0,16},{4,20},{8,24},{12,28},{16,0},{20,4},{24,8},{28,12},{1,17},{... | collective-permute-start | bytes 589832 | tf_op jit(solution)/shard_map/ppermute | solution.py:166
  61.6 4.9 %collective-permute-start.9 = (bf16[3,2,128,64]{2,3,0,1:T(8,128)(2,1)S(1)}, bf16[3,2,128,64]{2,3,0,1:T(8,128)(2,1)S(1)}, u32[]{:S(2)}, u32[]{:S(2)}) collective-permute-start(bf16[3,2,128,64]{2,3,0,1:T(8,128)(2,1)S(1)} %add.469), channel_id=1, source_target_pairs={{0,2},{1,3},{2,0},{3,1},{4,6},{5,7},{6,4},{7,5},{8,10},{9,11},{10,... | collective-permute-start | bytes 294920 | tf_op jit(solution)/shard_map/ppermute | solution.py:166
  74.9 16.1 %collective-permute-start.10 = (bf16[2,1,32,2560]{3,2,1,0:T(8,128)(2,1)S(1)}, bf16[2,1,32,2560]{3,2,1,0:T(8,128)(2,1)S(1)}, u32[]{:S(2)}, u32[]{:S(2)}) collective-permute-start(bf16[2,1,32,2560]{3,2,1,0:T(8,128)(2,1)S(1)} %pad_maximum_fusion.3), channel_id=1, source_target_pairs={{0,4},{4,0},{8,12},{12,8},{16,20},{20,16},{24,28},{28,24},{1,5},{5... | collective-permute-start | bytes 983048 | tf_op jit(solution)/shard_map/ppermute | solution.py:111
  76.5 16.1 %collective-permute-start.11 = (bf16[2,1,32,2560]{3,2,1,0:T(8,128)(2,1)S(1)}, bf16[2,1,32,2560]{3,2,1,0:T(8,128)(2,1)S(1)}, u32[]{:S(2)}, u32[]{:S(2)}) collective-permute-start(bf16[2,1,32,2560]{3,2,1,0:T(8,128)(2,1)S(1)} %pad_maximum_fusion.4), channel_id=1, source_target_pairs={{0,8},{4,12},{8,0},{12,4},{16,24},{20,28},{24,16},{28,20},{1,9},{5... | collective-permute-start | bytes 983048 | tf_op jit(solution)/shard_map/ppermute | solution.py:111
  77.2 17.1 %collective-permute-start.12 = (bf16[2,1,32,2560]{3,2,1,0:T(8,128)(2,1)S(1)}, bf16[2,1,32,2560]{3,2,1,0:T(8,128)(2,1)S(1)}, u32[]{:S(2)}, u32[]{:S(2)}) collective-permute-start(bf16[2,1,32,2560]{3,2,1,0:T(8,128)(2,1)S(1)} %pad_maximum_fusion.5), channel_id=1, source_target_pairs={{0,12},{4,8},{8,4},{12,0},{16,28},{20,24},{24,20},{28,16},{1,13},{... | collective-permute-start | bytes 983048 | tf_op jit(solution)/shard_map/ppermute | solution.py:111
  79.1 23.3 %collective-permute-start.14 = (bf16[2,1,32,2560]{3,2,1,0:T(8,128)(2,1)S(1)}, bf16[2,1,32,2560]{3,2,1,0:T(8,128)(2,1)S(1)}, u32[]{:S(2)}, u32[]{:S(2)}) collective-permute-start(bf16[2,1,32,2560]{3,2,1,0:T(8,128)(2,1)S(1)} %pad_maximum_fusion.6), channel_id=1, source_target_pairs={{0,4},{4,0},{8,12},{12,8},{16,20},{20,16},{24,28},{28,24},{1,5},{5... | collective-permute-start | bytes 983048 | tf_op jit(solution)/shard_map/ppermute | solution.py:111
  80.7 25.9 %collective-permute-start.15 = (bf16[2,1,32,2560]{3,2,1,0:T(8,128)(2,1)S(1)}, bf16[2,1,32,2560]{3,2,1,0:T(8,128)(2,1)S(1)}, u32[]{:S(2)}, u32[]{:S(2)}) collective-permute-start(bf16[2,1,32,2560]{3,2,1,0:T(8,128)(2,1)S(1)} %pad_maximum_fusion.7), channel_id=1, source_target_pairs={{0,8},{4,12},{8,0},{12,4},{16,24},{20,28},{24,16},{28,20},{1,9},{5... | collective-permute-start | bytes 983048 | tf_op jit(solution)/shard_map/ppermute | solution.py:111
  91.0 19.1 %collective-permute-start.16 = (bf16[2,1,32,2560]{3,2,1,0:T(8,128)(2,1)S(1)}, bf16[2,1,32,2560]{3,2,1,0:T(8,128)(2,1)S(1)}, u32[]{:S(2)}, u32[]{:S(2)}) collective-permute-start(bf16[2,1,32,2560]{3,2,1,0:T(8,128)(2,1)S(1)} %pad_maximum_fusion.8), channel_id=1, source_target_pairs={{0,12},{4,8},{8,4},{12,0},{16,28},{20,24},{24,20},{28,16},{1,13},{... | collective-permute-start | bytes 983048 | tf_op jit(solution)/shard_map/ppermute | solution.py:111
  92.6 22.7 %collective-permute-start.18 = (bf16[2,1,32,2560]{3,2,1,0:T(8,128)(2,1)S(1)}, bf16[2,1,32,2560]{3,2,1,0:T(8,128)(2,1)S(1)}, u32[]{:S(2)}, u32[]{:S(2)}) collective-permute-start(bf16[2,1,32,2560]{3,2,1,0:T(8,128)(2,1)S(1)} %pad_maximum_fusion.9), channel_id=1, source_target_pairs={{0,4},{4,0},{8,12},{12,8},{16,20},{20,16},{24,28},{28,24},{1,5},{5... | collective-permute-start | bytes 983048 | tf_op jit(solution)/shard_map/ppermute | solution.py:111
  94.3 28.2 %collective-permute-start.19 = (bf16[2,1,32,2560]{3,2,1,0:T(8,128)(2,1)S(1)}, bf16[2,1,32,2560]{3,2,1,0:T(8,128)(2,1)S(1)}, u32[]{:S(2)}, u32[]{:S(2)}) collective-permute-start(bf16[2,1,32,2560]{3,2,1,0:T(8,128)(2,1)S(1)} %pad_maximum_fusion.10), channel_id=1, source_target_pairs={{0,8},{4,12},{8,0},{12,4},{16,24},{20,28},{24,16},{28,20},{1,9},{5... | collective-permute-start | bytes 983048 | tf_op jit(solution)/shard_map/ppermute | solution.py:111
  102.4 25.0 %collective-permute-start.20 = (bf16[2,1,32,2560]{3,2,1,0:T(8,128)(2,1)S(1)}, bf16[2,1,32,2560]{3,2,1,0:T(8,128)(2,1)S(1)}, u32[]{:S(2)}, u32[]{:S(2)}) collective-permute-start(bf16[2,1,32,2560]{3,2,1,0:T(8,128)(2,1)S(1)} %pad_maximum_fusion.11), channel_id=1, source_target_pairs={{0,12},{4,8},{8,4},{12,0},{16,28},{20,24},{24,20},{28,16},{1,13},{... | collective-permute-start | bytes 983048 | tf_op jit(solution)/shard_map/ppermute | solution.py:111
  106.6 22.5 %collective-permute-start.13 = (bf16[1,32,2560]{2,1,0:T(8,128)(2,1)S(1)}, bf16[1,32,2560]{2,1,0:T(8,128)(2,1)S(1)}, u32[]{:S(2)}, u32[]{:S(2)}) collective-permute-start(bf16[1,32,2560]{2,1,0:T(8,128)(2,1)S(1)} %fusion.75), channel_id=1, source_target_pairs={{0,16},{4,20},{8,24},{12,28},{16,0},{20,4},{24,8},{28,12},{1,17},{... | collective-permute-start | bytes 491528 | tf_op jit(solution)/shard_map/ppermute | solution.py:116
  110.2 19.0 %collective-permute-start.17 = (bf16[1,32,2560]{2,1,0:T(8,128)(2,1)S(1)}, bf16[1,32,2560]{2,1,0:T(8,128)(2,1)S(1)}, u32[]{:S(2)}, u32[]{:S(2)}) collective-permute-start(bf16[1,32,2560]{2,1,0:T(8,128)(2,1)S(1)} %fusion.77), channel_id=1, source_target_pairs={{0,16},{4,20},{8,24},{12,28},{16,0},{20,4},{24,8},{28,12},{1,17},{... | collective-permute-start | bytes 491528 | tf_op jit(solution)/shard_map/ppermute | solution.py:116
  127.6 8.7 %collective-permute-start.21 = (bf16[1,32,2560]{2,1,0:T(8,128)(2,1)S(1)}, bf16[1,32,2560]{2,1,0:T(8,128)(2,1)S(1)}, u32[]{:S(2)}, u32[]{:S(2)}) collective-permute-start(bf16[1,32,2560]{2,1,0:T(8,128)(2,1)S(1)} %fusion.79), channel_id=1, source_target_pairs={{0,16},{4,20},{8,24},{12,28},{16,0},{20,4},{24,8},{28,12},{1,17},{... | collective-permute-start | bytes 491528 | tf_op jit(solution)/shard_map/ppermute | solution.py:116
  137.2 11.9 %all-to-all-start = ((bf16[3,4,8,1,2560]{4,2,3,0,1:T(8,128)(2,1)}), bf16[3,4,8,1,2560]{4,2,3,0,1:T(8,128)(2,1)S(1)}, u32[]{:S(2)}, u32[]{:S(2)}) async-start(bf16[3,4,8,1,2560]{4,2,3,0,1:T(8,128)(2,1)} %copy.81), calls=%async_computation | async-start | bytes 983040 | tf_op jit(solution)/shard_map/all_to_all | solution.py:318
  161.4 10.9 %all-to-all-start.1 = ((bf16[3,1,8,4,2048]{4,2,0,1,3:T(8,128)(2,1)}), bf16[3,1,8,4,2048]{4,2,0,1,3:T(8,128)(2,1)S(1)}, u32[]{:S(2)}, u32[]{:S(2)}) async-start(bf16[3,1,8,4,2048]{4,2,0,1,3:T(8,128)(2,1)} %copy.92), calls=%async_computation.1 | async-start | bytes 786432 | tf_op jit(solution)/shard_map/all_to_all | solution.py:344
  172.3 10.7 %collective-permute-start.22 = (bf16[3,32,2048]{2,1,0:T(8,128)(2,1)S(1)}, bf16[3,32,2048]{2,1,0:T(8,128)(2,1)S(1)}, u32[]{:S(2)}, u32[]{:S(2)}) collective-permute-start(bf16[3,32,2048]{2,1,0:T(8,128)(2,1)S(1)} %bitcast.214), channel_id=1, source_target_pairs={{0,4},{8,0},{16,8},{24,16},{28,24},{20,28},{12,20},{4,12},{1,5},{9... | collective-permute-start | bytes 1179656 | tf_op jit(solution)/shard_map/ppermute | solution.py:82
  173.8 10.7 %collective-permute-start.25 = (bf16[3,32,2048]{2,1,0:T(8,128)(2,1)S(1)}, bf16[3,32,2048]{2,1,0:T(8,128)(2,1)S(1)}, u32[]{:S(2)}, u32[]{:S(2)}) collective-permute-start(bf16[3,32,2048]{2,1,0:T(8,128)(2,1)S(1)} %bitcast.215), channel_id=1, source_target_pairs={{0,8},{8,16},{16,24},{24,28},{28,20},{20,12},{12,4},{4,0},{1,9},{9... | collective-permute-start | bytes 1179656 | tf_op jit(solution)/shard_map/ppermute | solution.py:79
  183.0 9.8 %collective-permute-start.23 = (bf16[3,32,2048]{2,1,0:T(8,128)(2,1)S(1)}, bf16[3,32,2048]{2,1,0:T(8,128)(2,1)S(1)}, u32[]{:S(2)}, u32[]{:S(2)}) collective-permute-start(bf16[3,32,2048]{2,1,0:T(8,128)(2,1)S(1)} %collective-permute-done.22), channel_id=1, source_target_pairs={{0,4},{8,0},{16,8},{24,16},{28,24},{20,28},{12,20},{4,12},{1,5},{9... | collective-permute-start | bytes 1179656 | tf_op jit(solution)/shard_map/ppermute | solution.py:82
  184.5 9.8 %collective-permute-start.26 = (bf16[3,32,2048]{2,1,0:T(8,128)(2,1)S(1)}, bf16[3,32,2048]{2,1,0:T(8,128)(2,1)S(1)}, u32[]{:S(2)}, u32[]{:S(2)}) collective-permute-start(bf16[3,32,2048]{2,1,0:T(8,128)(2,1)S(1)} %collective-permute-done.25), channel_id=1, source_target_pairs={{0,8},{8,16},{16,24},{24,28},{28,20},{20,12},{12,4},{4,0},{1,9},{9... | collective-permute-start | bytes 1179656 | tf_op jit(solution)/shard_map/ppermute | solution.py:79
  192.8 11.3 %collective-permute-start.24 = (bf16[3,32,2048]{2,1,0:T(8,128)(2,1)S(1)}, bf16[3,32,2048]{2,1,0:T(8,128)(2,1)S(1)}, u32[]{:S(2)}, u32[]{:S(2)}) collective-permute-start(bf16[3,32,2048]{2,1,0:T(8,128)(2,1)S(1)} %collective-permute-done.23), channel_id=1, source_target_pairs={{0,4},{8,0},{16,8},{24,16},{28,24},{20,28},{12,20},{4,12},{1,5},{9... | collective-permute-start | bytes 1179656 | tf_op jit(solution)/shard_map/ppermute | solution.py:82
  194.2 9.3 %collective-permute-start.27 = (bf16[3,32,2048]{2,1,0:T(8,128)(2,1)S(1)}, bf16[3,32,2048]{2,1,0:T(8,128)(2,1)S(1)}, u32[]{:S(2)}, u32[]{:S(2)}) collective-permute-start(bf16[3,32,2048]{2,1,0:T(8,128)(2,1)S(1)} %collective-permute-done.26), channel_id=1, source_target_pairs={{0,8},{8,16},{16,24},{24,28},{28,20},{20,12},{12,4},{4,0},{1,9},{9... | collective-permute-start | bytes 1179656 | tf_op jit(solution)/shard_map/ppermute | solution.py:79
  203.5 7.8 %collective-permute-start.28 = (bf16[3,32,2048]{2,1,0:T(8,128)(2,1)S(1)}, bf16[3,32,2048]{2,1,0:T(8,128)(2,1)S(1)}, u32[]{:S(2)}, u32[]{:S(2)}) collective-permute-start(bf16[3,32,2048]{2,1,0:T(8,128)(2,1)S(1)} %collective-permute-done.27), channel_id=1, source_target_pairs={{0,8},{8,16},{16,24},{24,28},{28,20},{20,12},{12,4},{4,0},{1,9},{9... | collective-permute-start | bytes 1179656 | tf_op jit(solution)/shard_map/ppermute | solution.py:79
  221.0 7.0 %collective-permute-start.30 = (f32[3,2,128,64]{2,3,0,1:T(8,128)S(1)}, f32[3,2,128,64]{2,3,0,1:T(8,128)S(1)}, u32[]{:S(2)}, u32[]{:S(2)}) collective-permute-start(f32[3,2,128,64]{2,3,0,1:T(8,128)S(1)} %add.510), channel_id=1, source_target_pairs={{0,2},{1,3},{2,0},{3,1},{4,6},{5,7},{6,4},{7,5},{8,10},{9,11},{10,... | collective-permute-start | bytes 589832 | tf_op jit(solution)/shard_map/ppermute | solution.py:166
  228.0 4.7 %collective-permute-start.31 = (bf16[3,2,128,64]{2,3,0,1:T(8,128)(2,1)S(1)}, bf16[3,2,128,64]{2,3,0,1:T(8,128)(2,1)S(1)}, u32[]{:S(2)}, u32[]{:S(2)}) collective-permute-start(bf16[3,2,128,64]{2,3,0,1:T(8,128)(2,1)S(1)} %add_convert_fusion.2), channel_id=1, source_target_pairs={{0,4},{4,0},{8,12},{12,8},{16,20},{20,16},{24,28},{28,24},{1,5},{5... | collective-permute-start | bytes 294920 | tf_op jit(solution)/shard_map/ppermute | solution.py:166
  232.7 4.7 %collective-permute-start.32 = (bf16[3,2,128,64]{2,3,0,1:T(8,128)(2,1)S(1)}, bf16[3,2,128,64]{2,3,0,1:T(8,128)(2,1)S(1)}, u32[]{:S(2)}, u32[]{:S(2)}) collective-permute-start(bf16[3,2,128,64]{2,3,0,1:T(8,128)(2,1)S(1)} %add.512), channel_id=1, source_target_pairs={{0,8},{4,12},{8,0},{12,4},{16,24},{20,28},{24,16},{28,20},{1,9},{5... | collective-permute-start | bytes 294920 | tf_op jit(solution)/shard_map/ppermute | solution.py:166
  237.4 6.6 %collective-permute-start.33 = (bf16[3,2,128,64]{2,3,0,1:T(8,128)(2,1)S(1)}, bf16[3,2,128,64]{2,3,0,1:T(8,128)(2,1)S(1)}, u32[]{:S(2)}, u32[]{:S(2)}) collective-permute-start(bf16[3,2,128,64]{2,3,0,1:T(8,128)(2,1)S(1)} %add.513), channel_id=1, source_target_pairs={{0,16},{4,20},{8,24},{12,28},{16,0},{20,4},{24,8},{28,12},{1,17},{... | collective-permute-start | bytes 294920 | tf_op jit(solution)/shard_map/ppermute | solution.py:166
  259.7 11.2 %collective-permute-start.35 = (bf16[3,1,64,1024]{3,2,0,1:T(8,128)(2,1)S(1)}, bf16[3,1,64,1024]{3,2,0,1:T(8,128)(2,1)S(1)}, u32[]{:S(2)}, u32[]{:S(2)}) collective-permute-start(bf16[3,1,64,1024]{3,2,0,1:T(8,128)(2,1)S(1)} %dynamic-slice_convert_fusion), channel_id=1, source_target_pairs={{0,2},{1,3},{2,0},{3,1},{4,6},{5,7},{6,4},{7,5},{8,10},{9,11},{10,... | collective-permute-start | bytes 1179656 | tf_op jit(solution)/shard_map/ppermute | solution.py:191
  (16 other events, 159.5 us)

commit v11 on v10

--- a/solution.py
+++ b/solution.py
@@ -61,6 +61,21 @@
             for step in range(value.shape[0])
         ]
     )
+
+
+def permute_all_to_all(value, axis_name, axis_size, split_axis, concat_axis):
+    if axis_size & (axis_size - 1):
+        return lax.all_to_all(value, axis_name, split_axis, concat_axis, tiled=False)
+    me = lax.axis_index(axis_name)
+    received = []
+    for offset in range(axis_size):
+        piece = lax.dynamic_index_in_dim(value, me ^ offset, axis=split_axis, keepdims=False)
+        if offset:
+            piece = lax.ppermute(piece, axis_name, [(i, i ^ offset) for i in range(axis_size)])
+        received.append(piece)
+    stacked = jnp.stack(received)
+    order = jnp.arange(axis_size, dtype=jnp.int32) ^ me
+    return jnp.moveaxis(jnp.take(stacked, order, axis=0), 0, concat_axis)
 
 
 def ring_gather(value, axis_name, axis_size):
@@ -315,8 +330,8 @@
     joined = jnp.concatenate([part_query, part_key, part_value], axis=-1)
     summed = split_half_scatter_steps(joined, "gx", across_first).astype(jnp.bfloat16)
     chunk_rows = summed.shape[1] // across_second
-    spread = lax.all_to_all(
-        summed.reshape(steps, across_second, chunk_rows, -1), "gy", 1, 2, tiled=False
+    spread = permute_all_to_all(
+        summed.reshape(steps, across_second, chunk_rows, -1), "gy", across_second, 1, 2
     )
     query_full = spread[..., :query_width].reshape(steps, local_rows, -1)
     key_full = spread[..., query_width : query_width + key_width].reshape(steps, local_rows, -1)
@@ -341,8 +356,8 @@
         value_full,
         cache_lengths,
     )
-    head_group = lax.all_to_all(
-        mixed_local.reshape(steps, local_rows, across_second, -1), "gy", 2, 1, tiled=False
+    head_group = permute_all_to_all(
+        mixed_local.reshape(steps, local_rows, across_second, -1), "gy", across_second, 2, 1
     ).reshape(steps, across_second * local_rows, -1)
     mixed_all = ring_gather(head_group, "gx", across_first)
     rank_part_out = jnp.einsum(

time: 274 us -> 276 us (level)
  waiting for transfers between devices: 151 us -> 161 us
  starting transfers between devices: 55.7 us -> 46.3 us
    all_to_all x2 -> x0, waiting for transfers between devices: 13.7 us -> none  [the longest x1 8.04 us: local(): lax.all_to_all(summed.reshape(steps, across_second, chunk_rows, -1), 'gy'...]
    ppermute x0 -> x6, waiting for transfers between devices: none -> 11 us  [permute_all_to_all(): lax.ppermute(piece, axis_name, [(i, i ^ offset) for i in range(axis_size)])]
    all_to_all x2 -> x0, starting transfers between devices: 7.11 us -> none  [the longest x1 3.65 us: local(): lax.all_to_all(summed.reshape(steps, across_second, chunk_rows, -1), 'gy'...]
    ppermute x9, waiting for transfers between devices: 33.4 us -> 39.6 us  [split_half_scatter(): lax.ppermute(outgoing, axis_name, [(i, i ^ offset) for i in range(axis_si...]
    ppermute x9, starting transfers between devices: 12.7 us -> 8.21 us  [split_half_scatter(): lax.ppermute(outgoing, axis_name, [(i, i ^ offset) for i in range(axis_si...]
    ppermute x0 -> x6, starting transfers between devices: none -> 4.03 us  [permute_all_to_all(): lax.ppermute(piece, axis_name, [(i, i ^ offset) for i in range(axis_size)])]
    unnamed x27 -> x28, local copies, waits for them, and re-layouts: 9.43 us -> 8.88 us
  transfers between devices with their start and end apart: 38 -> 42, of which waited for: 30 -> 32; matrix products, arithmetic and copies ran while one was open for 5% -> 5% of each run, Pallas kernels for 0% -> 0%
where the time goes in v11:
time: 276 us; the launch traced here: 275 us
  waiting for transfers between devices  161 us (58%)
  starting transfers between devices  46.3 us (17%)
  local copies, waits for them, and re-layouts  22.7 us (8%)
  matrix products  20.2 us (7%)
  other arithmetic  19.2 us (7%)
  between operations  6.17 us (2%)
    ppermute x13, waiting for transfers between devices, tree_sum(): value = value + lax.ppermute(value, axis_name, pairs)  43 us
    ppermute x9, waiting for transfers between devices, split_half_scatter(): lax.ppermute(outgoing, axis_name, [(i, i ^ offset) for i in range(axis_si...  39.6 us
    ppermute x13, starting transfers between devices, tree_sum(): value = value + lax.ppermute(value, axis_name, pairs)  18.7 us
    ppermute x4, waiting for transfers between devices, ring_gather(): forward = lax.ppermute(forward, axis_name, ahead)  15.7 us
    ppermute x3, waiting for transfers between devices, ring_gather(): backward = lax.ppermute(backward, axis_name, behind)  15.7 us
    ppermute x2, waiting for transfers between devices, doubling_gather(): lax.ppermute(held, axis_name, [(i, i ^ distance) for i in range(axis_size)])  15.2 us
    ppermute x2, waiting for transfers between devices, halving_scatter(): held = keep + lax.ppermute(give, axis_name, swap).astype(jnp.float32)  13.2 us
    ppermute x6, waiting for transfers between devices, permute_all_to_all(): lax.ppermute(piece, axis_name, [(i, i ^ offset) for i in range(axis_size)])  11 us
  transfers between devices with their start and end apart: 42, of which 32 were waited for; matrix products, arithmetic and copies ran while one was open for 5% of the time, Pallas kernels for 0%

profile of v11, /device:TPU:0, one launch (start us, length us, event | category | flops | bytes accessed | tf_op | source)
XLA Modules:
  0.0 275.2 jit_solution(13530520061015858922)
XLA Ops:
  10.1 2.6 collective-permute-start.1
  15.7 15.2 %collective-permute-done.1 = bf16[3,128,1024]{2,1,0:T(8,128)(2,1)S(1)} collective-permute-done((bf16[3,128,1024]{2,1,0:T(8,128)(2,1)S(1)}, bf16[3,128,1024]{2,1,0:T(8,128)(2,1)S(1)}, u32[]{:S(2)}, u32[]{:S(2)}) %collective-permute-start.1) | collective-permute-done | bytes 786464 | tf_op jit(solution)/shard_map/ppermute | solution.py:144
  39.0 2.8 %collective-permute-start.4 = (f32[3,256]{1,0:T(4,128)S(1)}, f32[3,256]{1,0:T(4,128)S(1)}, u32[]{:S(2)}, u32[]{:S(2)}) collective-permute-start(f32[3,256]{1,0:T(4,128)S(1)} %add.490), channel_id=1, source_target_pairs={{0,16},{4,20},{8,24},{12,28},{16,0},{20,4},{24,8},{28,12},{1,17},{... | collective-permute-start | bytes 9224 | tf_op jit(solution)/shard_map/ppermute | solution.py:181
  46.0 3.9 %collective-permute-done.5 = f32[3,2,128,64]{2,3,0,1:T(8,128)S(1)} collective-permute-done((f32[3,2,128,64]{2,3,0,1:T(8,128)S(1)}, f32[3,2,128,64]{2,3,0,1:T(8,128)S(1)}, u32[]{:S(2)}, u32[]{:S(2)}) %collective-permute-start.5) | collective-permute-done | bytes 196640 | tf_op jit(solution)/shard_map/ppermute | solution.py:181
  52.5 5.2 %collective-permute-done.6 = f32[3,2,128,64]{2,3,0,1:T(8,128)S(1)} collective-permute-done((f32[3,2,128,64]{2,3,0,1:T(8,128)S(1)}, f32[3,2,128,64]{2,3,0,1:T(8,128)S(1)}, u32[]{:S(2)}, u32[]{:S(2)}) %collective-permute-start.6) | collective-permute-done | bytes 196640 | tf_op jit(solution)/shard_map/ppermute | solution.py:181
  59.7 6.7 %collective-permute-done.7 = f32[3,2,128,64]{2,3,0,1:T(8,128)S(1)} collective-permute-done((f32[3,2,128,64]{2,3,0,1:T(8,128)S(1)}, f32[3,2,128,64]{2,3,0,1:T(8,128)S(1)}, u32[]{:S(2)}, u32[]{:S(2)}) %collective-permute-start.7) | collective-permute-done | bytes 196640 | tf_op jit(solution)/shard_map/ppermute | solution.py:181
  76.1 3.5 %bitcast_add_fusion = f32[3,256,2048]{2,1,0:T(8,128)S(1)} fusion(f32[3,2,128,2048]{3,2,1,0:T(8,128)S(1)} %copy.51, bf16[1024,2048]{1,0:T(8,128)(2,1)S(1)} %copy-done.6, f32[1024]{0:T(1024)S(1)} %convert_element_type.190, f32[3,256]{1,0:T(4,128)S(1)} %add_rsqrt_fusion, bf16[3,128,1024]{2,1,0:T(8,128)(2,1)S(1)} %get-tuple-element.21, ...), kind=kOutput, calls=%fused_computation.4 | convolution fusion | flops 3228303360 | bytes 18357248 | tf_op jit(solution)/shard_map/tnd,de->tne/dot_general | solution.py:323
  87.7 9.8 %collective-permute-done.10 = bf16[2,1,32,2560]{3,2,1,0:T(8,128)(2,1)S(1)} collective-permute-done((bf16[2,1,32,2560]{3,2,1,0:T(8,128)(2,1)S(1)}, bf16[2,1,32,2560]{3,2,1,0:T(8,128)(2,1)S(1)}, u32[]{:S(2)}, u32[]{:S(2)}) %collective-permute-start.10) | collective-permute-done | bytes 327712 | tf_op jit(solution)/shard_map/ppermute | solution.py:126
  101.4 6.7 %collective-permute-done.14 = bf16[2,1,32,2560]{3,2,1,0:T(8,128)(2,1)S(1)} collective-permute-done((bf16[2,1,32,2560]{3,2,1,0:T(8,128)(2,1)S(1)}, bf16[2,1,32,2560]{3,2,1,0:T(8,128)(2,1)S(1)}, u32[]{:S(2)}, u32[]{:S(2)}) %collective-permute-start.14) | collective-permute-done | bytes 327712 | tf_op jit(solution)/shard_map/ppermute | solution.py:126
  109.8 2.6 collective-permute-start.13
  112.4 7.7 %collective-permute-done.16 = bf16[2,1,32,2560]{3,2,1,0:T(8,128)(2,1)S(1)} collective-permute-done((bf16[2,1,32,2560]{3,2,1,0:T(8,128)(2,1)S(1)}, bf16[2,1,32,2560]{3,2,1,0:T(8,128)(2,1)S(1)}, u32[]{:S(2)}, u32[]{:S(2)}) %collective-permute-start.16) | collective-permute-done | bytes 327712 | tf_op jit(solution)/shard_map/ppermute | solution.py:126
  121.2 7.9 %collective-permute-done.19 = bf16[2,1,32,2560]{3,2,1,0:T(8,128)(2,1)S(1)} collective-permute-done((bf16[2,1,32,2560]{3,2,1,0:T(8,128)(2,1)S(1)}, bf16[2,1,32,2560]{3,2,1,0:T(8,128)(2,1)S(1)}, u32[]{:S(2)}, u32[]{:S(2)}) %collective-permute-start.19) | collective-permute-done | bytes 327712 | tf_op jit(solution)/shard_map/ppermute | solution.py:126
  129.2 4.8 %collective-permute-done.20 = bf16[2,1,32,2560]{3,2,1,0:T(8,128)(2,1)S(1)} collective-permute-done((bf16[2,1,32,2560]{3,2,1,0:T(8,128)(2,1)S(1)}, bf16[2,1,32,2560]{3,2,1,0:T(8,128)(2,1)S(1)}, u32[]{:S(2)}, u32[]{:S(2)}) %collective-permute-start.20) | collective-permute-done | bytes 327712 | tf_op jit(solution)/shard_map/ppermute | solution.py:126
  135.2 7.2 %collective-permute-done.21 = bf16[1,32,2560]{2,1,0:T(8,128)(2,1)S(1)} collective-permute-done((bf16[1,32,2560]{2,1,0:T(8,128)(2,1)S(1)}, bf16[1,32,2560]{2,1,0:T(8,128)(2,1)S(1)}, u32[]{:S(2)}, u32[]{:S(2)}) %collective-permute-start.21) | collective-permute-done | bytes 163872 | tf_op jit(solution)/shard_map/ppermute | solution.py:131
  144.5 4.3 %collective-permute-done.23 = bf16[3,8,2560]{2,1,0:T(8,128)(2,1)S(1)} collective-permute-done((bf16[3,8,2560]{2,1,0:T(8,128)(2,1)S(1)}, bf16[3,8,2560]{2,1,0:T(8,128)(2,1)S(1)}, u32[]{:S(2)}, u32[]{:S(2)}) %collective-permute-start.23) | collective-permute-done | bytes 122912 | tf_op jit(solution)/shard_map/ppermute | solution.py:74
  153.0 4.6 %fusion.105 = (f32[8,8,24]{2,1,0:T(8,128)S(1)}, f32[8,8,24,256]{3,2,1,0:T(8,128)S(1)}) fusion(pred[8,256]{1,0:T(8,128)(4,1)S(1)} %iota_compare_fusion, bf16[8,256,1024]{2,1,0:T(8,128)(2,1)} %param.27, bf16[3,8,8,8,64]{4,3,2,1,0:T(8,128)(2,1)S(1)} %bitcast.238, bf16[3,8,8,8,64]{4,3,2,1,0:T(8,128)(2,1)S(1)} %bitcast.236), kind=kOutput, calls=%fused_computation.229 | convolution fusion | flops 102627840 | bytes 6168576 | tf_op jit(solution)/shard_map/rhqd,rchd->rhqc/dot_general | solution.py:232
  159.3 3.1 %fusion.38 = bf16[8,8,3,8,128]{4,3,2,1,0:T(8,128)(2,1)S(1)} fusion(f32[8,8,24,128]{3,2,1,0:T(8,128)S(1)} %fusion.84, f32[8,8,24,256]{3,2,1,0:T(8,128)S(1)} %get-tuple-element.61, f32[8,8,24]{2,1,0:T(8,128)S(1)} %max.7, pred[8,256]{1,0:T(8,128)(4,1)S(1)} %iota_compare_fusion, f32[8,8,24]{2,1,0:T(8,128)S(1)} %add.550, bf16[8,256,1024]{2,1,0:T(8,128)(2,1)} %param.28), kind=kOutput, calls=%fused_computation.41 | convolution fusion | flops 102432768 | bytes 6961152 | tf_op jit(solution)/shard_map/rhqc,rchd->rhqd/dot_general | solution.py:256
  165.9 3.2 %collective-permute-done.26 = bf16[3,8,2048]{2,1,0:T(8,128)(2,1)S(1)} collective-permute-done((bf16[3,8,2048]{2,1,0:T(8,128)(2,1)S(1)}, bf16[3,8,2048]{2,1,0:T(8,128)(2,1)S(1)}, u32[]{:S(2)}, u32[]{:S(2)}) %collective-permute-start.26) | collective-permute-done | bytes 98336 | tf_op jit(solution)/shard_map/ppermute | solution.py:74
  174.6 8.2 %collective-permute-done.28 = bf16[3,32,2048]{2,1,0:T(8,128)(2,1)S(1)} collective-permute-done((bf16[3,32,2048]{2,1,0:T(8,128)(2,1)S(1)}, bf16[3,32,2048]{2,1,0:T(8,128)(2,1)S(1)}, u32[]{:S(2)}, u32[]{:S(2)}) %collective-permute-start.28) | collective-permute-done | bytes 393248 | tf_op jit(solution)/shard_map/ppermute | solution.py:97
  185.7 7.5 %collective-permute-done.29 = bf16[3,32,2048]{2,1,0:T(8,128)(2,1)S(1)} collective-permute-done((bf16[3,32,2048]{2,1,0:T(8,128)(2,1)S(1)}, bf16[3,32,2048]{2,1,0:T(8,128)(2,1)S(1)}, u32[]{:S(2)}, u32[]{:S(2)}) %collective-permute-start.29) | collective-permute-done | bytes 393248 | tf_op jit(solution)/shard_map/ppermute | solution.py:97
  196.0 8.4 %collective-permute-done.33 = bf16[3,32,2048]{2,1,0:T(8,128)(2,1)S(1)} collective-permute-done((bf16[3,32,2048]{2,1,0:T(8,128)(2,1)S(1)}, bf16[3,32,2048]{2,1,0:T(8,128)(2,1)S(1)}, u32[]{:S(2)}, u32[]{:S(2)}) %collective-permute-start.33) | collective-permute-done | bytes 393248 | tf_op jit(solution)/shard_map/ppermute | solution.py:94
  205.3 7.3 %collective-permute-done.34 = bf16[3,32,2048]{2,1,0:T(8,128)(2,1)S(1)} collective-permute-done((bf16[3,32,2048]{2,1,0:T(8,128)(2,1)S(1)}, bf16[3,32,2048]{2,1,0:T(8,128)(2,1)S(1)}, u32[]{:S(2)}, u32[]{:S(2)}) %collective-permute-start.34) | collective-permute-done | bytes 393248 | tf_op jit(solution)/shard_map/ppermute | solution.py:94
  215.7 2.6 gather_fusion.2
  222.3 2.8 %collective-permute-start.36 = (f32[3,2,128,64]{2,3,0,1:T(8,128)S(1)}, f32[3,2,128,64]{2,3,0,1:T(8,128)S(1)}, u32[]{:S(2)}, u32[]{:S(2)}) collective-permute-start(f32[3,2,128,64]{2,3,0,1:T(8,128)S(1)} %add.551), channel_id=1, source_target_pairs={{0,2},{1,3},{2,0},{3,1},{4,6},{5,7},{6,4},{7,5},{8,10},{9,11},{10,... | collective-permute-start | bytes 589832 | tf_op jit(solution)/shard_map/ppermute | solution.py:181
  225.0 5.2 %collective-permute-done.36 = f32[3,2,128,64]{2,3,0,1:T(8,128)S(1)} collective-permute-done((f32[3,2,128,64]{2,3,0,1:T(8,128)S(1)}, f32[3,2,128,64]{2,3,0,1:T(8,128)S(1)}, u32[]{:S(2)}, u32[]{:S(2)}) %collective-permute-start.36) | collective-permute-done | bytes 196640 | tf_op jit(solution)/shard_map/ppermute | solution.py:181
  231.3 3.7 %collective-permute-done.37 = bf16[3,2,128,64]{2,3,0,1:T(8,128)(2,1)S(1)} collective-permute-done((bf16[3,2,128,64]{2,3,0,1:T(8,128)(2,1)S(1)}, bf16[3,2,128,64]{2,3,0,1:T(8,128)(2,1)S(1)}, u32[]{:S(2)}, u32[]{:S(2)}) %collective-permute-start.37) | collective-permute-done | bytes 98336 | tf_op jit(solution)/shard_map/ppermute | solution.py:181
  235.5 4.2 %collective-permute-done.38 = bf16[3,2,128,64]{2,3,0,1:T(8,128)(2,1)S(1)} collective-permute-done((bf16[3,2,128,64]{2,3,0,1:T(8,128)(2,1)S(1)}, bf16[3,2,128,64]{2,3,0,1:T(8,128)(2,1)S(1)}, u32[]{:S(2)}, u32[]{:S(2)}) %collective-permute-start.38) | collective-permute-done | bytes 98336 | tf_op jit(solution)/shard_map/ppermute | solution.py:181
  241.0 5.4 %collective-permute-done.39 = bf16[3,2,128,64]{2,3,0,1:T(8,128)(2,1)S(1)} collective-permute-done((bf16[3,2,128,64]{2,3,0,1:T(8,128)(2,1)S(1)}, bf16[3,2,128,64]{2,3,0,1:T(8,128)(2,1)S(1)}, u32[]{:S(2)}, u32[]{:S(2)}) %collective-permute-start.39) | collective-permute-done | bytes 98336 | tf_op jit(solution)/shard_map/ppermute | solution.py:181
  249.1 3.5 %bitcast_add_fusion.1 = f32[3,256,1024]{2,1,0:T(8,128)S(1)} fusion(f32[3,2,128,1024]{3,2,1,0:T(8,128)S(1)} %copy.74, bf16[3,256,2048]{2,1,0:T(8,128)(2,1)S(1)} %bitcast.234, bf16[2048,1024]{1,0:T(8,128)(2,1)S(1)} %copy-done.7), kind=kOutput, calls=%fused_computation.16 | convolution fusion | flops 3222011904 | bytes 13631488 | tf_op jit(solution)/shard_map/tnq,qe->tne/dot_general | solution.py:374
  254.2 3.7 %collective-permute-done.40 = f32[3,2,64,1024]{3,2,0,1:T(8,128)} collective-permute-done((f32[3,2,64,1024]{3,2,0,1:T(8,128)}, f32[3,2,64,1024]{3,2,0,1:T(8,128)}, u32[]{:S(2)}, u32[]{:S(2)}) %collective-permute-start.40) | collective-permute-done | bytes 1572896 | tf_op jit(solution)/shard_map/ppermute | solution.py:206
  258.0 2.9 %bitcast_add_fusion.2 = f32[3,2,64,1024]{3,2,0,1:T(8,128)} fusion(f32[3,2,64,1024]{3,2,0,1:T(8,128)} %collective-permute-done.40, f32[3,2,1,64,1024]{4,3,2,1,0:T(8,128)S(1)} %get-tuple-element.18), kind=kLoop, calls=%fused_computation.27 | loop fusion | flops 393216 | bytes 4718592 | tf_op jit(solution)/shard_map/add | solution.py:206
  263.8 9.4 %collective-permute-done.41 = bf16[3,1,64,1024]{3,2,0,1:T(8,128)(2,1)S(1)} collective-permute-done((bf16[3,1,64,1024]{3,2,0,1:T(8,128)(2,1)S(1)}, bf16[3,1,64,1024]{3,2,0,1:T(8,128)(2,1)S(1)}, u32[]{:S(2)}, u32[]{:S(2)}) %collective-permute-start.41) | collective-permute-done | bytes 393248 | tf_op jit(solution)/shard_map/ppermute | solution.py:206
  (197 shorter events, 92.5 us)
Async XLA Ops:
  0.0 9.0 %collective-permute-start = (bf16[3,64,1024]{2,1,0:T(8,128)(2,1)}, bf16[3,64,1024]{2,1,0:T(8,128)(2,1)S(1)}, u32[]{:S(2)}, u32[]{:S(2)}) collective-permute-start(bf16[3,64,1024]{2,1,0:T(8,128)(2,1)} %param.15), channel_id=1, source_target_pairs={{0,1},{1,0},{2,3},{3,2},{4,5},{5,4},{6,7},{7,6},{8,9},{9,8},{10,11... | collective-permute-start | bytes 1179656 | tf_op jit(solution)/shard_map/ppermute | solution.py:144
  10.1 20.8 %collective-permute-start.1 = (bf16[3,128,1024]{2,1,0:T(8,128)(2,1)S(1)}, bf16[3,128,1024]{2,1,0:T(8,128)(2,1)S(1)}, u32[]{:S(2)}, u32[]{:S(2)}) collective-permute-start(bf16[3,128,1024]{2,1,0:T(8,128)(2,1)S(1)} %pad_maximum_fusion.1), channel_id=1, source_target_pairs={{0,2},{1,3},{2,0},{3,1},{4,6},{5,7},{6,4},{7,5},{8,10},{9,11},{10,... | collective-permute-start | bytes 2359304 | tf_op jit(solution)/shard_map/ppermute | solution.py:144
  44.2 5.7 %collective-permute-start.5 = (f32[3,2,128,64]{2,3,0,1:T(8,128)S(1)}, f32[3,2,128,64]{2,3,0,1:T(8,128)S(1)}, u32[]{:S(2)}, u32[]{:S(2)}) collective-permute-start(f32[3,2,128,64]{2,3,0,1:T(8,128)S(1)} %fusion.25), channel_id=1, source_target_pairs={{0,4},{4,0},{8,12},{12,8},{16,20},{20,16},{24,28},{28,24},{1,5},{5... | collective-permute-start | bytes 589832 | tf_op jit(solution)/shard_map/ppermute | solution.py:181
  50.0 7.7 %collective-permute-start.6 = (f32[3,2,128,64]{2,3,0,1:T(8,128)S(1)}, f32[3,2,128,64]{2,3,0,1:T(8,128)S(1)}, u32[]{:S(2)}, u32[]{:S(2)}) collective-permute-start(f32[3,2,128,64]{2,3,0,1:T(8,128)S(1)} %add.502), channel_id=1, source_target_pairs={{0,8},{4,12},{8,0},{12,4},{16,24},{20,28},{24,16},{28,20},{1,9},{5... | collective-permute-start | bytes 589832 | tf_op jit(solution)/shard_map/ppermute | solution.py:181
  57.7 8.7 %collective-permute-start.7 = (f32[3,2,128,64]{2,3,0,1:T(8,128)S(1)}, f32[3,2,128,64]{2,3,0,1:T(8,128)S(1)}, u32[]{:S(2)}, u32[]{:S(2)}) collective-permute-start(f32[3,2,128,64]{2,3,0,1:T(8,128)S(1)} %add.503), channel_id=1, source_target_pairs={{0,16},{4,20},{8,24},{12,28},{16,0},{20,4},{24,8},{28,12},{1,17},{... | collective-permute-start | bytes 589832 | tf_op jit(solution)/shard_map/ppermute | solution.py:181
  67.9 5.0 %collective-permute-start.9 = (bf16[3,2,128,64]{2,3,0,1:T(8,128)(2,1)S(1)}, bf16[3,2,128,64]{2,3,0,1:T(8,128)(2,1)S(1)}, u32[]{:S(2)}, u32[]{:S(2)}) collective-permute-start(bf16[3,2,128,64]{2,3,0,1:T(8,128)(2,1)S(1)} %add.505), channel_id=1, source_target_pairs={{0,2},{1,3},{2,0},{3,1},{4,6},{5,7},{6,4},{7,5},{8,10},{9,11},{10,... | collective-permute-start | bytes 294920 | tf_op jit(solution)/shard_map/ppermute | solution.py:181
  81.4 16.1 %collective-permute-start.10 = (bf16[2,1,32,2560]{3,2,1,0:T(8,128)(2,1)S(1)}, bf16[2,1,32,2560]{3,2,1,0:T(8,128)(2,1)S(1)}, u32[]{:S(2)}, u32[]{:S(2)}) collective-permute-start(bf16[2,1,32,2560]{3,2,1,0:T(8,128)(2,1)S(1)} %pad_maximum_fusion.5), channel_id=1, source_target_pairs={{0,4},{4,0},{8,12},{12,8},{16,20},{20,16},{24,28},{28,24},{1,5},{5... | collective-permute-start | bytes 983048 | tf_op jit(solution)/shard_map/ppermute | solution.py:126
  83.2 14.4 %collective-permute-start.11 = (bf16[2,1,32,2560]{3,2,1,0:T(8,128)(2,1)S(1)}, bf16[2,1,32,2560]{3,2,1,0:T(8,128)(2,1)S(1)}, u32[]{:S(2)}, u32[]{:S(2)}) collective-permute-start(bf16[2,1,32,2560]{3,2,1,0:T(8,128)(2,1)S(1)} %pad_maximum_fusion.6), channel_id=1, source_target_pairs={{0,8},{4,12},{8,0},{12,4},{16,24},{20,28},{24,16},{28,20},{1,9},{5... | collective-permute-start | bytes 983048 | tf_op jit(solution)/shard_map/ppermute | solution.py:126
  83.4 17.4 %collective-permute-start.12 = (bf16[2,1,32,2560]{3,2,1,0:T(8,128)(2,1)S(1)}, bf16[2,1,32,2560]{3,2,1,0:T(8,128)(2,1)S(1)}, u32[]{:S(2)}, u32[]{:S(2)}) collective-permute-start(bf16[2,1,32,2560]{3,2,1,0:T(8,128)(2,1)S(1)} %pad_maximum_fusion.7), channel_id=1, source_target_pairs={{0,12},{4,8},{8,4},{12,0},{16,28},{20,24},{24,20},{28,16},{1,13},{... | collective-permute-start | bytes 983048 | tf_op jit(solution)/shard_map/ppermute | solution.py:126
  85.7 22.5 %collective-permute-start.14 = (bf16[2,1,32,2560]{3,2,1,0:T(8,128)(2,1)S(1)}, bf16[2,1,32,2560]{3,2,1,0:T(8,128)(2,1)S(1)}, u32[]{:S(2)}, u32[]{:S(2)}) collective-permute-start(bf16[2,1,32,2560]{3,2,1,0:T(8,128)(2,1)S(1)} %pad_maximum_fusion.8), channel_id=1, source_target_pairs={{0,4},{4,0},{8,12},{12,8},{16,20},{20,16},{24,28},{28,24},{1,5},{5... | collective-permute-start | bytes 983048 | tf_op jit(solution)/shard_map/ppermute | solution.py:126
  87.5 22.3 %collective-permute-start.15 = (bf16[2,1,32,2560]{3,2,1,0:T(8,128)(2,1)S(1)}, bf16[2,1,32,2560]{3,2,1,0:T(8,128)(2,1)S(1)}, u32[]{:S(2)}, u32[]{:S(2)}) collective-permute-start(bf16[2,1,32,2560]{3,2,1,0:T(8,128)(2,1)S(1)} %pad_maximum_fusion.9), channel_id=1, source_target_pairs={{0,8},{4,12},{8,0},{12,4},{16,24},{20,28},{24,16},{28,20},{1,9},{5... | collective-permute-start | bytes 983048 | tf_op jit(solution)/shard_map/ppermute | solution.py:126
  97.6 22.6 %collective-permute-start.16 = (bf16[2,1,32,2560]{3,2,1,0:T(8,128)(2,1)S(1)}, bf16[2,1,32,2560]{3,2,1,0:T(8,128)(2,1)S(1)}, u32[]{:S(2)}, u32[]{:S(2)}) collective-permute-start(bf16[2,1,32,2560]{3,2,1,0:T(8,128)(2,1)S(1)} %pad_maximum_fusion.10), channel_id=1, source_target_pairs={{0,12},{4,8},{8,4},{12,0},{16,28},{20,24},{24,20},{28,16},{1,13},{... | collective-permute-start | bytes 983048 | tf_op jit(solution)/shard_map/ppermute | solution.py:126
  97.6 23.6 %collective-permute-start.18 = (bf16[2,1,32,2560]{3,2,1,0:T(8,128)(2,1)S(1)}, bf16[2,1,32,2560]{3,2,1,0:T(8,128)(2,1)S(1)}, u32[]{:S(2)}, u32[]{:S(2)}) collective-permute-start(bf16[2,1,32,2560]{3,2,1,0:T(8,128)(2,1)S(1)} %pad_maximum_fusion.11), channel_id=1, source_target_pairs={{0,4},{4,0},{8,12},{12,8},{16,20},{20,16},{24,28},{28,24},{1,5},{5... | collective-permute-start | bytes 983048 | tf_op jit(solution)/shard_map/ppermute | solution.py:126
  100.8 28.4 %collective-permute-start.19 = (bf16[2,1,32,2560]{3,2,1,0:T(8,128)(2,1)S(1)}, bf16[2,1,32,2560]{3,2,1,0:T(8,128)(2,1)S(1)}, u32[]{:S(2)}, u32[]{:S(2)}) collective-permute-start(bf16[2,1,32,2560]{3,2,1,0:T(8,128)(2,1)S(1)} %pad_maximum_fusion.12), channel_id=1, source_target_pairs={{0,8},{4,12},{8,0},{12,4},{16,24},{20,28},{24,16},{28,20},{1,9},{5... | collective-permute-start | bytes 983048 | tf_op jit(solution)/shard_map/ppermute | solution.py:126
  108.2 25.9 %collective-permute-start.20 = (bf16[2,1,32,2560]{3,2,1,0:T(8,128)(2,1)S(1)}, bf16[2,1,32,2560]{3,2,1,0:T(8,128)(2,1)S(1)}, u32[]{:S(2)}, u32[]{:S(2)}) collective-permute-start(bf16[2,1,32,2560]{3,2,1,0:T(8,128)(2,1)S(1)} %pad_maximum_fusion.13), channel_id=1, source_target_pairs={{0,12},{4,8},{8,4},{12,0},{16,28},{20,24},{24,20},{28,16},{1,13},{... | collective-permute-start | bytes 983048 | tf_op jit(solution)/shard_map/ppermute | solution.py:126
  109.8 25.2 %collective-permute-start.13 = (bf16[1,32,2560]{2,1,0:T(8,128)(2,1)S(1)}, bf16[1,32,2560]{2,1,0:T(8,128)(2,1)S(1)}, u32[]{:S(2)}, u32[]{:S(2)}) collective-permute-start(bf16[1,32,2560]{2,1,0:T(8,128)(2,1)S(1)} %fusion.75), channel_id=1, source_target_pairs={{0,16},{4,20},{8,24},{12,28},{16,0},{20,4},{24,8},{28,12},{1,17},{... | collective-permute-start | bytes 491528 | tf_op jit(solution)/shard_map/ppermute | solution.py:131
  120.3 14.8 %collective-permute-start.17 = (bf16[1,32,2560]{2,1,0:T(8,128)(2,1)S(1)}, bf16[1,32,2560]{2,1,0:T(8,128)(2,1)S(1)}, u32[]{:S(2)}, u32[]{:S(2)}) collective-permute-start(bf16[1,32,2560]{2,1,0:T(8,128)(2,1)S(1)} %fusion.77), channel_id=1, source_target_pairs={{0,16},{4,20},{8,24},{12,28},{16,0},{20,4},{24,8},{28,12},{1,17},{... | collective-permute-start | bytes 491528 | tf_op jit(solution)/shard_map/ppermute | solution.py:131
  134.2 8.2 %collective-permute-start.21 = (bf16[1,32,2560]{2,1,0:T(8,128)(2,1)S(1)}, bf16[1,32,2560]{2,1,0:T(8,128)(2,1)S(1)}, u32[]{:S(2)}, u32[]{:S(2)}) collective-permute-start(bf16[1,32,2560]{2,1,0:T(8,128)(2,1)S(1)} %fusion.79), channel_id=1, source_target_pairs={{0,16},{4,20},{8,24},{12,28},{16,0},{20,4},{24,8},{28,12},{1,17},{... | collective-permute-start | bytes 491528 | tf_op jit(solution)/shard_map/ppermute | solution.py:131
  142.6 6.2 %collective-permute-start.23 = (bf16[3,8,2560]{2,1,0:T(8,128)(2,1)S(1)}, bf16[3,8,2560]{2,1,0:T(8,128)(2,1)S(1)}, u32[]{:S(2)}, u32[]{:S(2)}) collective-permute-start(bf16[3,8,2560]{2,1,0:T(8,128)(2,1)S(1)} %get-tuple-element.48), channel_id=1, source_target_pairs={{0,2},{1,3},{2,0},{3,1},{4,6},{5,7},{6,4},{7,5},{8,10},{9,11},{10,... | collective-permute-start | bytes 368648 | tf_op jit(solution)/shard_map/ppermute | solution.py:74
  144.3 6.2 %collective-permute-start.24 = (bf16[3,8,2560]{2,1,0:T(8,128)(2,1)S(1)}, bf16[3,8,2560]{2,1,0:T(8,128)(2,1)S(1)}, u32[]{:S(2)}, u32[]{:S(2)}) collective-permute-start(bf16[3,8,2560]{2,1,0:T(8,128)(2,1)S(1)} %get-tuple-element.47), channel_id=1, source_target_pairs={{0,3},{1,2},{2,1},{3,0},{4,7},{5,6},{6,5},{7,4},{8,11},{9,10},{10,... | collective-permute-start | bytes 368648 | tf_op jit(solution)/shard_map/ppermute | solution.py:74
  163.9 5.2 %collective-permute-start.26 = (bf16[3,8,2048]{2,1,0:T(8,128)(2,1)S(1)}, bf16[3,8,2048]{2,1,0:T(8,128)(2,1)S(1)}, u32[]{:S(2)}, u32[]{:S(2)}) collective-permute-start(bf16[3,8,2048]{2,1,0:T(8,128)(2,1)S(1)} %bitcast.251), channel_id=1, source_target_pairs={{0,2},{1,3},{2,0},{3,1},{4,6},{5,7},{6,4},{7,5},{8,10},{9,11},{10,... | collective-permute-start | bytes 294920 | tf_op jit(solution)/shard_map/ppermute | solution.py:74
  165.7 5.2 %collective-permute-start.27 = (bf16[3,8,2048]{2,1,0:T(8,128)(2,1)S(1)}, bf16[3,8,2048]{2,1,0:T(8,128)(2,1)S(1)}, u32[]{:S(2)}, u32[]{:S(2)}) collective-permute-start(bf16[3,8,2048]{2,1,0:T(8,128)(2,1)S(1)} %bitcast.252), channel_id=1, source_target_pairs={{0,3},{1,2},{2,1},{3,0},{4,7},{5,6},{6,5},{7,4},{8,11},{9,10},{10,... | collective-permute-start | bytes 294920 | tf_op jit(solution)/shard_map/ppermute | solution.py:74
  171.7 11.2 %collective-permute-start.28 = (bf16[3,32,2048]{2,1,0:T(8,128)(2,1)S(1)}, bf16[3,32,2048]{2,1,0:T(8,128)(2,1)S(1)}, u32[]{:S(2)}, u32[]{:S(2)}) collective-permute-start(bf16[3,32,2048]{2,1,0:T(8,128)(2,1)S(1)} %copy_bitcast_fusion.2), channel_id=1, source_target_pairs={{0,4},{8,0},{16,8},{24,16},{28,24},{20,28},{12,20},{4,12},{1,5},{9... | collective-permute-start | bytes 1179656 | tf_op jit(solution)/shard_map/ppermute | solution.py:97
  173.6 11.1 %collective-permute-start.31 = (bf16[3,32,2048]{2,1,0:T(8,128)(2,1)S(1)}, bf16[3,32,2048]{2,1,0:T(8,128)(2,1)S(1)}, u32[]{:S(2)}, u32[]{:S(2)}) collective-permute-start(bf16[3,32,2048]{2,1,0:T(8,128)(2,1)S(1)} %copy_bitcast_fusion.2), channel_id=1, source_target_pairs={{0,8},{8,16},{16,24},{24,28},{28,20},{20,12},{12,4},{4,0},{1,9},{9... | collective-permute-start | bytes 1179656 | tf_op jit(solution)/shard_map/ppermute | solution.py:94
  182.8 10.3 %collective-permute-start.29 = (bf16[3,32,2048]{2,1,0:T(8,128)(2,1)S(1)}, bf16[3,32,2048]{2,1,0:T(8,128)(2,1)S(1)}, u32[]{:S(2)}, u32[]{:S(2)}) collective-permute-start(bf16[3,32,2048]{2,1,0:T(8,128)(2,1)S(1)} %collective-permute-done.28), channel_id=1, source_target_pairs={{0,4},{8,0},{16,8},{24,16},{28,24},{20,28},{12,20},{4,12},{1,5},{9... | collective-permute-start | bytes 1179656 | tf_op jit(solution)/shard_map/ppermute | solution.py:97
  184.8 10.3 %collective-permute-start.32 = (bf16[3,32,2048]{2,1,0:T(8,128)(2,1)S(1)}, bf16[3,32,2048]{2,1,0:T(8,128)(2,1)S(1)}, u32[]{:S(2)}, u32[]{:S(2)}) collective-permute-start(bf16[3,32,2048]{2,1,0:T(8,128)(2,1)S(1)} %collective-permute-done.31), channel_id=1, source_target_pairs={{0,8},{8,16},{16,24},{24,28},{28,20},{20,12},{12,4},{4,0},{1,9},{9... | collective-permute-start | bytes 1179656 | tf_op jit(solution)/shard_map/ppermute | solution.py:94
  193.1 11.3 %collective-permute-start.30 = (bf16[3,32,2048]{2,1,0:T(8,128)(2,1)S(1)}, bf16[3,32,2048]{2,1,0:T(8,128)(2,1)S(1)}, u32[]{:S(2)}, u32[]{:S(2)}) collective-permute-start(bf16[3,32,2048]{2,1,0:T(8,128)(2,1)S(1)} %collective-permute-done.29), channel_id=1, source_target_pairs={{0,4},{8,0},{16,8},{24,16},{28,24},{20,28},{12,20},{4,12},{1,5},{9... | collective-permute-start | bytes 1179656 | tf_op jit(solution)/shard_map/ppermute | solution.py:97
  195.1 9.3 %collective-permute-start.33 = (bf16[3,32,2048]{2,1,0:T(8,128)(2,1)S(1)}, bf16[3,32,2048]{2,1,0:T(8,128)(2,1)S(1)}, u32[]{:S(2)}, u32[]{:S(2)}) collective-permute-start(bf16[3,32,2048]{2,1,0:T(8,128)(2,1)S(1)} %collective-permute-done.32), channel_id=1, source_target_pairs={{0,8},{8,16},{16,24},{24,28},{28,20},{20,12},{12,4},{4,0},{1,9},{9... | collective-permute-start | bytes 1179656 | tf_op jit(solution)/shard_map/ppermute | solution.py:94
  204.3 8.2 %collective-permute-start.34 = (bf16[3,32,2048]{2,1,0:T(8,128)(2,1)S(1)}, bf16[3,32,2048]{2,1,0:T(8,128)(2,1)S(1)}, u32[]{:S(2)}, u32[]{:S(2)}) collective-permute-start(bf16[3,32,2048]{2,1,0:T(8,128)(2,1)S(1)} %collective-permute-done.33), channel_id=1, source_target_pairs={{0,8},{8,16},{16,24},{24,28},{28,20},{20,12},{12,4},{4,0},{1,9},{9... | collective-permute-start | bytes 1179656 | tf_op jit(solution)/shard_map/ppermute | solution.py:94
  222.3 8.0 %collective-permute-start.36 = (f32[3,2,128,64]{2,3,0,1:T(8,128)S(1)}, f32[3,2,128,64]{2,3,0,1:T(8,128)S(1)}, u32[]{:S(2)}, u32[]{:S(2)}) collective-permute-start(f32[3,2,128,64]{2,3,0,1:T(8,128)S(1)} %add.551), channel_id=1, source_target_pairs={{0,2},{1,3},{2,0},{3,1},{4,6},{5,7},{6,4},{7,5},{8,10},{9,11},{10,... | collective-permute-start | bytes 589832 | tf_op jit(solution)/shard_map/ppermute | solution.py:181
  239.7 6.6 %collective-permute-start.39 = (bf16[3,2,128,64]{2,3,0,1:T(8,128)(2,1)S(1)}, bf16[3,2,128,64]{2,3,0,1:T(8,128)(2,1)S(1)}, u32[]{:S(2)}, u32[]{:S(2)}) collective-permute-start(bf16[3,2,128,64]{2,3,0,1:T(8,128)(2,1)S(1)} %add.554), channel_id=1, source_target_pairs={{0,16},{4,20},{8,24},{12,28},{16,0},{20,4},{24,8},{28,12},{1,17},{... | collective-permute-start | bytes 294920 | tf_op jit(solution)/shard_map/ppermute | solution.py:181
  262.0 11.2 %collective-permute-start.41 = (bf16[3,1,64,1024]{3,2,0,1:T(8,128)(2,1)S(1)}, bf16[3,1,64,1024]{3,2,0,1:T(8,128)(2,1)S(1)}, u32[]{:S(2)}, u32[]{:S(2)}) collective-permute-start(bf16[3,1,64,1024]{3,2,0,1:T(8,128)(2,1)S(1)} %dynamic-slice_convert_fusion), channel_id=1, source_target_pairs={{0,2},{1,3},{2,0},{3,1},{4,6},{5,7},{6,4},{7,5},{8,10},{9,11},{10,... | collective-permute-start | bytes 1179656 | tf_op jit(solution)/shard_map/ppermute | solution.py:206
  (19 other events, 184.7 us)

commit v12 on v10

--- a/solution.py
+++ b/solution.py
@@ -304,10 +304,10 @@
     delta_query = jnp.einsum(
         "tbnr,bre->tbne", rank_query, query_second, preferred_element_type=jnp.float32
     ).reshape(steps, request_count, -1)
-    part_query = (
+    query_main = lax.optimization_barrier(
         jnp.einsum("tnd,de->tne", normed, query_weight, preferred_element_type=jnp.float32)
-        + delta_query
-    )
+    )
+    part_query = query_main + delta_query
     part_key = jnp.einsum("tnd,de->tne", normed, key_weight, preferred_element_type=jnp.float32)
     part_value = jnp.einsum(
         "tnd,de->tne", normed, value_weight, preferred_element_type=jnp.float32
@@ -355,10 +355,10 @@
     delta_output = jnp.einsum(
         "tbnr,bre->tbne", rank_output, output_second, preferred_element_type=jnp.float32
     ).reshape(steps, request_count, -1)
-    partial_out = (
+    output_main = lax.optimization_barrier(
         jnp.einsum("tnq,qe->tne", mixed_all, output_weight, preferred_element_type=jnp.float32)
-        + delta_output
-    )
+    )
+    partial_out = output_main + delta_output
     return halving_scatter(partial_out, "gy", across_second).astype(jnp.bfloat16)
 
 

time: 274 us -> 269 us (0.982)
  waiting for transfers between devices: 151 us -> 140 us
  other arithmetic: 18.2 us -> 22.9 us
  matrix products: 20.2 us -> 23.8 us
    ppermute x13, waiting for transfers between devices: 41.3 us -> 28 us  [tree_sum(): value = value + lax.ppermute(value, axis_name, pairs)]
    ppermute x9, waiting for transfers between devices: 33.4 us -> 36.7 us  [split_half_scatter(): lax.ppermute(outgoing, axis_name, [(i, i ^ offset) for i in range(axis_si...]
    add x0 -> x2, other arithmetic: none -> 2.99 us  [the longest x1 1.99 us: local(): part_query = query_main + delta_query]
    unnamed x27 -> x31, local copies, waits for them, and re-layouts: 9.43 us -> 8.44 us
  transfers between devices with their start and end apart: 38 -> 38, of which waited for: 30 -> 28; matrix products, arithmetic and copies ran while one was open for 5% -> 10% of each run, Pallas kernels for 0% -> 0%
where the time goes in v12:
time: 269 us; the launch traced here: 268 us
  waiting for transfers between devices  140 us (52%)
  starting transfers between devices  55 us (20%)
  matrix products  23.8 us (9%)
  other arithmetic  22.9 us (9%)
  local copies, waits for them, and re-layouts  20.6 us (8%)
  between operations  6.13 us (2%)
    ppermute x9, waiting for transfers between devices, split_half_scatter(): lax.ppermute(outgoing, axis_name, [(i, i ^ offset) for i in range(axis_si...  36.7 us
    ppermute x13, waiting for transfers between devices, tree_sum(): value = value + lax.ppermute(value, axis_name, pairs)  28 us
    ppermute x13, starting transfers between devices, tree_sum(): value = value + lax.ppermute(value, axis_name, pairs)  19.3 us
    ppermute x3, waiting for transfers between devices, ring_gather(): backward = lax.ppermute(backward, axis_name, behind)  14.8 us
    ppermute x2, waiting for transfers between devices, halving_scatter(): held = keep + lax.ppermute(give, axis_name, swap).astype(jnp.float32)  13.5 us
    ppermute x4, waiting for transfers between devices, ring_gather(): forward = lax.ppermute(forward, axis_name, ahead)  13.1 us
    ppermute x2, waiting for transfers between devices, doubling_gather(): lax.ppermute(held, axis_name, [(i, i ^ distance) for i in range(axis_size)])  12.3 us
    ppermute x9, starting transfers between devices, split_half_scatter(): lax.ppermute(outgoing, axis_name, [(i, i ^ offset) for i in range(axis_si...  11.8 us
  transfers between devices with their start and end apart: 38, of which 28 were waited for; matrix products, arithmetic and copies ran while one was open for 10% of the time, Pallas kernels for 0%

profile of v12, /device:TPU:0, one launch (start us, length us, event | category | flops | bytes accessed | tf_op | source)
XLA Modules:
  0.0 268.2 jit_solution(16457886584719730299)
XLA Ops:
  3.2 3.0 %collective-permute-start.1 = (bf16[3,128,1024]{2,1,0:T(8,128)(2,1)S(1)}, bf16[3,128,1024]{2,1,0:T(8,128)(2,1)}, u32[]{:S(2)}, u32[]{:S(2)}) collective-permute-start(bf16[3,128,1024]{2,1,0:T(8,128)(2,1)S(1)} %pad_maximum_fusion.1), channel_id=1, source_target_pairs={{0,2},{1,3},{2,0},{3,1},{4,6},{5,7},{6,4},{7,5},{8,10},{9,11},{10,... | collective-permute-start | bytes 2359304 | tf_op jit(solution)/shard_map/ppermute | solution.py:129
  13.3 10.8 %collective-permute-done.1 = bf16[3,128,1024]{2,1,0:T(8,128)(2,1)} collective-permute-done((bf16[3,128,1024]{2,1,0:T(8,128)(2,1)S(1)}, bf16[3,128,1024]{2,1,0:T(8,128)(2,1)}, u32[]{:S(2)}, u32[]{:S(2)}) %collective-permute-start.1) | collective-permute-done | bytes 786464 | tf_op jit(solution)/shard_map/ppermute | solution.py:129
  33.3 2.8 %collective-permute-start.4 = (f32[3,256]{1,0:T(4,128)S(1)}, f32[3,256]{1,0:T(4,128)S(1)}, u32[]{:S(2)}, u32[]{:S(2)}) collective-permute-start(f32[3,256]{1,0:T(4,128)S(1)} %add.454), channel_id=1, source_target_pairs={{0,16},{4,20},{8,24},{12,28},{16,0},{20,4},{24,8},{28,12},{1,17},{... | collective-permute-start | bytes 9224 | tf_op jit(solution)/shard_map/ppermute | solution.py:166
  40.4 3.9 %collective-permute-done.5 = f32[3,2,128,64]{2,3,0,1:T(8,128)S(1)} collective-permute-done((f32[3,2,128,64]{2,3,0,1:T(8,128)S(1)}, f32[3,2,128,64]{2,3,0,1:T(8,128)S(1)}, u32[]{:S(2)}, u32[]{:S(2)}) %collective-permute-start.5) | collective-permute-done | bytes 196640 | tf_op jit(solution)/shard_map/ppermute | solution.py:166
  46.8 4.7 %collective-permute-done.6 = f32[3,2,128,64]{2,3,0,1:T(8,128)S(1)} collective-permute-done((f32[3,2,128,64]{2,3,0,1:T(8,128)S(1)}, f32[3,2,128,64]{2,3,0,1:T(8,128)S(1)}, u32[]{:S(2)}, u32[]{:S(2)}) %collective-permute-start.6) | collective-permute-done | bytes 196640 | tf_op jit(solution)/shard_map/ppermute | solution.py:166
  51.5 2.5 collective-permute-start.7
  54.1 5.6 %fusion.8 = f32[3,256,2048]{2,1,0:T(8,128)} fusion(bf16[1024,2048]{1,0:T(8,128)(2,1)S(1)} %copy-done.7, f32[1024]{0:T(1024)S(1)} %convert_element_type.196, f32[3,256]{1,0:T(4,128)S(1)} %add_rsqrt_fusion, bf16[3,128,1024]{2,1,0:T(8,128)(2,1)S(1)} %get-tuple-element.21, bf16[3,128,1024]{2,1,0:T(8,128)(2,1)S(1)} %get-tuple-element.20), kind=kOutput, calls=%fused_computation.11 | convolution fusion | flops 3226730496 | bytes 12065792 | tf_op jit(solution)/shard_map/tnd,de->tne/dot_general | solution.py:308
  75.8 2.8 %collective-permute-start.20 = (bf16[2,1,32,2560]{3,2,1,0:T(8,128)(2,1)S(1)}, bf16[2,1,32,2560]{3,2,1,0:T(8,128)(2,1)S(1)}, u32[]{:S(2)}, u32[]{:S(2)}) collective-permute-start(bf16[2,1,32,2560]{3,2,1,0:T(8,128)(2,1)S(1)} %pad_maximum_fusion.11), channel_id=1, source_target_pairs={{0,12},{4,8},{8,4},{12,0},{16,28},{20,24},{24,20},{28,16},{1,13},{... | collective-permute-start | bytes 983048 | tf_op jit(solution)/shard_map/ppermute | solution.py:111
  79.6 2.8 %collective-permute-start.16 = (bf16[2,1,32,2560]{3,2,1,0:T(8,128)(2,1)S(1)}, bf16[2,1,32,2560]{3,2,1,0:T(8,128)(2,1)S(1)}, u32[]{:S(2)}, u32[]{:S(2)}) collective-permute-start(bf16[2,1,32,2560]{3,2,1,0:T(8,128)(2,1)S(1)} %pad_maximum_fusion.8), channel_id=1, source_target_pairs={{0,12},{4,8},{8,4},{12,0},{16,28},{20,24},{24,20},{28,16},{1,13},{... | collective-permute-start | bytes 983048 | tf_op jit(solution)/shard_map/ppermute | solution.py:111
  83.1 4.3 %collective-permute-done.20 = bf16[2,1,32,2560]{3,2,1,0:T(8,128)(2,1)S(1)} collective-permute-done((bf16[2,1,32,2560]{3,2,1,0:T(8,128)(2,1)S(1)}, bf16[2,1,32,2560]{3,2,1,0:T(8,128)(2,1)S(1)}, u32[]{:S(2)}, u32[]{:S(2)}) %collective-permute-start.20) | collective-permute-done | bytes 327712 | tf_op jit(solution)/shard_map/ppermute | solution.py:111
  89.0 5.5 %collective-permute-done.19 = bf16[2,1,32,2560]{3,2,1,0:T(8,128)(2,1)S(1)} collective-permute-done((bf16[2,1,32,2560]{3,2,1,0:T(8,128)(2,1)S(1)}, bf16[2,1,32,2560]{3,2,1,0:T(8,128)(2,1)S(1)}, u32[]{:S(2)}, u32[]{:S(2)}) %collective-permute-start.19) | collective-permute-done | bytes 327712 | tf_op jit(solution)/shard_map/ppermute | solution.py:111
  96.7 4.8 %collective-permute-done.16 = bf16[2,1,32,2560]{3,2,1,0:T(8,128)(2,1)S(1)} collective-permute-done((bf16[2,1,32,2560]{3,2,1,0:T(8,128)(2,1)S(1)}, bf16[2,1,32,2560]{3,2,1,0:T(8,128)(2,1)S(1)}, u32[]{:S(2)}, u32[]{:S(2)}) %collective-permute-start.16) | collective-permute-done | bytes 327712 | tf_op jit(solution)/shard_map/ppermute | solution.py:111
  103.0 5.5 %collective-permute-done.15 = bf16[2,1,32,2560]{3,2,1,0:T(8,128)(2,1)S(1)} collective-permute-done((bf16[2,1,32,2560]{3,2,1,0:T(8,128)(2,1)S(1)}, bf16[2,1,32,2560]{3,2,1,0:T(8,128)(2,1)S(1)}, u32[]{:S(2)}, u32[]{:S(2)}) %collective-permute-start.15) | collective-permute-done | bytes 327712 | tf_op jit(solution)/shard_map/ppermute | solution.py:111
  111.7 10.9 %collective-permute-done.12 = bf16[2,1,32,2560]{3,2,1,0:T(8,128)(2,1)S(1)} collective-permute-done((bf16[2,1,32,2560]{3,2,1,0:T(8,128)(2,1)S(1)}, bf16[2,1,32,2560]{3,2,1,0:T(8,128)(2,1)S(1)}, u32[]{:S(2)}, u32[]{:S(2)}) %collective-permute-start.12) | collective-permute-done | bytes 327712 | tf_op jit(solution)/shard_map/ppermute | solution.py:111
  122.7 5.7 %collective-permute-done.11 = bf16[2,1,32,2560]{3,2,1,0:T(8,128)(2,1)S(1)} collective-permute-done((bf16[2,1,32,2560]{3,2,1,0:T(8,128)(2,1)S(1)}, bf16[2,1,32,2560]{3,2,1,0:T(8,128)(2,1)S(1)}, u32[]{:S(2)}, u32[]{:S(2)}) %collective-permute-start.11) | collective-permute-done | bytes 327712 | tf_op jit(solution)/shard_map/ppermute | solution.py:111
  130.3 7.7 %collective-permute-done.13 = bf16[1,32,2560]{2,1,0:T(8,128)(2,1)S(1)} collective-permute-done((bf16[1,32,2560]{2,1,0:T(8,128)(2,1)S(1)}, bf16[1,32,2560]{2,1,0:T(8,128)(2,1)S(1)}, u32[]{:S(2)}, u32[]{:S(2)}) %collective-permute-start.13) | collective-permute-done | bytes 163872 | tf_op jit(solution)/shard_map/ppermute | solution.py:116
  138.9 3.7 %all-to-all-start = ((bf16[3,4,8,1,2560]{4,2,3,0,1:T(8,128)(2,1)}), bf16[3,4,8,1,2560]{4,2,3,0,1:T(8,128)(2,1)S(1)}, u32[]{:S(2)}, u32[]{:S(2)}) async-start(bf16[3,4,8,1,2560]{4,2,3,0,1:T(8,128)(2,1)} %copy.81), calls=%async_computation | async-start | bytes 983040 | tf_op jit(solution)/shard_map/all_to_all | solution.py:318
  142.9 8.0 %all-to-all-done = bf16[3,4,8,1,2560]{4,2,3,0,1:T(8,128)(2,1)S(1)} async-done(((bf16[3,4,8,1,2560]{4,2,3,0,1:T(8,128)(2,1)}), bf16[3,4,8,1,2560]{4,2,3,0,1:T(8,128)(2,1)S(1)}, u32[]{:S(2)}, u32[]{:S(2)}) %all-to-all-start) | async-done | bytes 491552 | tf_op jit(solution)/shard_map/all_to_all | solution.py:318
  152.6 4.6 %fusion.102 = (f32[8,8,24]{2,1,0:T(8,128)S(1)}, f32[8,8,24,256]{3,2,1,0:T(8,128)S(1)}) fusion(pred[8,256]{1,0:T(8,128)(4,1)S(1)} %iota_compare_fusion, bf16[8,256,1024]{2,1,0:T(8,128)(2,1)} %param.27, bf16[3,8,8,8,64]{4,3,2,1,0:T(8,128)(2,1)S(1)} %bitcast.209, bf16[3,8,8,8,64]{4,3,2,1,0:T(8,128)(2,1)S(1)} %bitcast.207), kind=kOutput, calls=%fused_computation.206 | convolution fusion | flops 102627840 | bytes 6168576 | tf_op jit(solution)/shard_map/rhqd,rchd->rhqc/dot_general | solution.py:217
  161.6 3.5 %all-to-all-start.1 = ((bf16[3,1,8,4,2048]{4,2,0,1,3:T(8,128)(2,1)}), bf16[3,1,8,4,2048]{4,2,0,1,3:T(8,128)(2,1)S(1)}, u32[]{:S(2)}, u32[]{:S(2)}) async-start(bf16[3,1,8,4,2048]{4,2,0,1,3:T(8,128)(2,1)} %copy.92), calls=%async_computation.1 | async-start | bytes 786432 | tf_op jit(solution)/shard_map/all_to_all | solution.py:344
  166.9 5.6 %all-to-all-done.1 = bf16[3,1,8,4,2048]{4,2,0,1,3:T(8,128)(2,1)S(1)} async-done(((bf16[3,1,8,4,2048]{4,2,0,1,3:T(8,128)(2,1)}), bf16[3,1,8,4,2048]{4,2,0,1,3:T(8,128)(2,1)S(1)}, u32[]{:S(2)}, u32[]{:S(2)}) %all-to-all-start.1) | async-done | bytes 393248 | tf_op jit(solution)/shard_map/all_to_all | solution.py:344
  175.4 7.8 %collective-permute-done.22 = bf16[3,32,2048]{2,1,0:T(8,128)(2,1)S(1)} collective-permute-done((bf16[3,32,2048]{2,1,0:T(8,128)(2,1)S(1)}, bf16[3,32,2048]{2,1,0:T(8,128)(2,1)S(1)}, u32[]{:S(2)}, u32[]{:S(2)}) %collective-permute-start.22) | collective-permute-done | bytes 393248 | tf_op jit(solution)/shard_map/ppermute | solution.py:82
  186.1 6.9 %collective-permute-done.23 = bf16[3,32,2048]{2,1,0:T(8,128)(2,1)S(1)} collective-permute-done((bf16[3,32,2048]{2,1,0:T(8,128)(2,1)S(1)}, bf16[3,32,2048]{2,1,0:T(8,128)(2,1)S(1)}, u32[]{:S(2)}, u32[]{:S(2)}) %collective-permute-start.23) | collective-permute-done | bytes 393248 | tf_op jit(solution)/shard_map/ppermute | solution.py:82
  195.8 7.3 %collective-permute-done.27 = bf16[3,32,2048]{2,1,0:T(8,128)(2,1)S(1)} collective-permute-done((bf16[3,32,2048]{2,1,0:T(8,128)(2,1)S(1)}, bf16[3,32,2048]{2,1,0:T(8,128)(2,1)S(1)}, u32[]{:S(2)}, u32[]{:S(2)}) %collective-permute-start.27) | collective-permute-done | bytes 393248 | tf_op jit(solution)/shard_map/ppermute | solution.py:79
  205.1 5.8 %collective-permute-done.28 = bf16[3,32,2048]{2,1,0:T(8,128)(2,1)S(1)} collective-permute-done((bf16[3,32,2048]{2,1,0:T(8,128)(2,1)S(1)}, bf16[3,32,2048]{2,1,0:T(8,128)(2,1)S(1)}, u32[]{:S(2)}, u32[]{:S(2)}) %collective-permute-start.28) | collective-permute-done | bytes 393248 | tf_op jit(solution)/shard_map/ppermute | solution.py:79
  214.0 2.6 gather_fusion
  221.8 5.8 %collective-permute-done.30 = f32[3,2,128,64]{2,3,0,1:T(8,128)S(1)} collective-permute-done((f32[3,2,128,64]{2,3,0,1:T(8,128)S(1)}, f32[3,2,128,64]{2,3,0,1:T(8,128)S(1)}, u32[]{:S(2)}, u32[]{:S(2)}) %collective-permute-start.30) | collective-permute-done | bytes 196640 | tf_op jit(solution)/shard_map/ppermute | solution.py:166
  228.5 3.8 %collective-permute-done.31 = bf16[3,2,128,64]{2,3,0,1:T(8,128)(2,1)S(1)} collective-permute-done((bf16[3,2,128,64]{2,3,0,1:T(8,128)(2,1)S(1)}, bf16[3,2,128,64]{2,3,0,1:T(8,128)(2,1)S(1)}, u32[]{:S(2)}, u32[]{:S(2)}) %collective-permute-start.31) | collective-permute-done | bytes 98336 | tf_op jit(solution)/shard_map/ppermute | solution.py:166
  238.6 5.2 %fusion.6 = f32[3,256,1024]{2,1,0:T(8,128)S(1)} fusion(bf16[3,256,2048]{2,1,0:T(8,128)(2,1)S(1)} %bitcast.204, bf16[2048,1024]{1,0:T(8,128)(2,1)} %param.20), kind=kOutput, calls=%fused_computation.9 | convolution fusion | flops 3221225472 | bytes 10485760 | tf_op jit(solution)/shard_map/tnq,qe->tne/dot_general | solution.py:359
  247.2 3.7 %collective-permute-done.34 = f32[3,2,64,1024]{3,2,0,1:T(8,128)} collective-permute-done((f32[3,2,64,1024]{3,2,0,1:T(8,128)}, f32[3,2,64,1024]{3,2,0,1:T(8,128)}, u32[]{:S(2)}, u32[]{:S(2)}) %collective-permute-start.34) | collective-permute-done | bytes 1572896 | tf_op jit(solution)/shard_map/ppermute | solution.py:191
  250.9 2.9 %bitcast_add_fusion.2 = f32[3,2,64,1024]{3,2,0,1:T(8,128)} fusion(f32[3,2,64,1024]{3,2,0,1:T(8,128)} %collective-permute-done.34, f32[3,2,1,64,1024]{4,3,2,1,0:T(8,128)S(1)} %get-tuple-element.18), kind=kLoop, calls=%fused_computation.25 | loop fusion | flops 393216 | bytes 4718592 | tf_op jit(solution)/shard_map/add | solution.py:191
  256.4 9.8 %collective-permute-done.35 = bf16[3,1,64,1024]{3,2,0,1:T(8,128)(2,1)S(1)} collective-permute-done((bf16[3,1,64,1024]{3,2,0,1:T(8,128)(2,1)S(1)}, bf16[3,1,64,1024]{3,2,0,1:T(8,128)(2,1)S(1)}, u32[]{:S(2)}, u32[]{:S(2)}) %collective-permute-start.35) | collective-permute-done | bytes 393248 | tf_op jit(solution)/shard_map/ppermute | solution.py:191
  (186 shorter events, 91.9 us)
Async XLA Ops:
  3.2 20.9 %collective-permute-start.1 = (bf16[3,128,1024]{2,1,0:T(8,128)(2,1)S(1)}, bf16[3,128,1024]{2,1,0:T(8,128)(2,1)}, u32[]{:S(2)}, u32[]{:S(2)}) collective-permute-start(bf16[3,128,1024]{2,1,0:T(8,128)(2,1)S(1)} %pad_maximum_fusion.1), channel_id=1, source_target_pairs={{0,2},{1,3},{2,0},{3,1},{4,6},{5,7},{6,4},{7,5},{8,10},{9,11},{10,... | collective-permute-start | bytes 2359304 | tf_op jit(solution)/shard_map/ppermute | solution.py:129
  33.3 4.5 %collective-permute-start.4 = (f32[3,256]{1,0:T(4,128)S(1)}, f32[3,256]{1,0:T(4,128)S(1)}, u32[]{:S(2)}, u32[]{:S(2)}) collective-permute-start(f32[3,256]{1,0:T(4,128)S(1)} %add.454), channel_id=1, source_target_pairs={{0,16},{4,20},{8,24},{12,28},{16,0},{20,4},{24,8},{28,12},{1,17},{... | collective-permute-start | bytes 9224 | tf_op jit(solution)/shard_map/ppermute | solution.py:166
  38.5 5.7 %collective-permute-start.5 = (f32[3,2,128,64]{2,3,0,1:T(8,128)S(1)}, f32[3,2,128,64]{2,3,0,1:T(8,128)S(1)}, u32[]{:S(2)}, u32[]{:S(2)}) collective-permute-start(f32[3,2,128,64]{2,3,0,1:T(8,128)S(1)} %fusion.23), channel_id=1, source_target_pairs={{0,4},{4,0},{8,12},{12,8},{16,20},{20,16},{24,28},{28,24},{1,5},{5... | collective-permute-start | bytes 589832 | tf_op jit(solution)/shard_map/ppermute | solution.py:166
  44.3 7.2 %collective-permute-start.6 = (f32[3,2,128,64]{2,3,0,1:T(8,128)S(1)}, f32[3,2,128,64]{2,3,0,1:T(8,128)S(1)}, u32[]{:S(2)}, u32[]{:S(2)}) collective-permute-start(f32[3,2,128,64]{2,3,0,1:T(8,128)S(1)} %add.466), channel_id=1, source_target_pairs={{0,8},{4,12},{8,0},{12,4},{16,24},{20,28},{24,16},{28,20},{1,9},{5... | collective-permute-start | bytes 589832 | tf_op jit(solution)/shard_map/ppermute | solution.py:166
  51.5 8.7 %collective-permute-start.7 = (f32[3,2,128,64]{2,3,0,1:T(8,128)S(1)}, f32[3,2,128,64]{2,3,0,1:T(8,128)S(1)}, u32[]{:S(2)}, u32[]{:S(2)}) collective-permute-start(f32[3,2,128,64]{2,3,0,1:T(8,128)S(1)} %add.467), channel_id=1, source_target_pairs={{0,16},{4,20},{8,24},{12,28},{16,0},{20,4},{24,8},{28,12},{1,17},{... | collective-permute-start | bytes 589832 | tf_op jit(solution)/shard_map/ppermute | solution.py:166
  61.9 5.3 %collective-permute-start.9 = (bf16[3,2,128,64]{2,3,0,1:T(8,128)(2,1)S(1)}, bf16[3,2,128,64]{2,3,0,1:T(8,128)(2,1)S(1)}, u32[]{:S(2)}, u32[]{:S(2)}) collective-permute-start(bf16[3,2,128,64]{2,3,0,1:T(8,128)(2,1)S(1)} %add.469), channel_id=1, source_target_pairs={{0,2},{1,3},{2,0},{3,1},{4,6},{5,7},{6,4},{7,5},{8,10},{9,11},{10,... | collective-permute-start | bytes 294920 | tf_op jit(solution)/shard_map/ppermute | solution.py:166
  75.8 11.6 %collective-permute-start.20 = (bf16[2,1,32,2560]{3,2,1,0:T(8,128)(2,1)S(1)}, bf16[2,1,32,2560]{3,2,1,0:T(8,128)(2,1)S(1)}, u32[]{:S(2)}, u32[]{:S(2)}) collective-permute-start(bf16[2,1,32,2560]{3,2,1,0:T(8,128)(2,1)S(1)} %pad_maximum_fusion.11), channel_id=1, source_target_pairs={{0,12},{4,8},{8,4},{12,0},{16,28},{20,24},{24,20},{28,16},{1,13},{... | collective-permute-start | bytes 983048 | tf_op jit(solution)/shard_map/ppermute | solution.py:111
  78.6 15.8 %collective-permute-start.19 = (bf16[2,1,32,2560]{3,2,1,0:T(8,128)(2,1)S(1)}, bf16[2,1,32,2560]{3,2,1,0:T(8,128)(2,1)S(1)}, u32[]{:S(2)}, u32[]{:S(2)}) collective-permute-start(bf16[2,1,32,2560]{3,2,1,0:T(8,128)(2,1)S(1)} %pad_maximum_fusion.10), channel_id=1, source_target_pairs={{0,8},{4,12},{8,0},{12,4},{16,24},{20,28},{24,16},{28,20},{1,9},{5... | collective-permute-start | bytes 983048 | tf_op jit(solution)/shard_map/ppermute | solution.py:111
  79.0 17.4 %collective-permute-start.18 = (bf16[2,1,32,2560]{3,2,1,0:T(8,128)(2,1)S(1)}, bf16[2,1,32,2560]{3,2,1,0:T(8,128)(2,1)S(1)}, u32[]{:S(2)}, u32[]{:S(2)}) collective-permute-start(bf16[2,1,32,2560]{3,2,1,0:T(8,128)(2,1)S(1)} %pad_maximum_fusion.9), channel_id=1, source_target_pairs={{0,4},{4,0},{8,12},{12,8},{16,20},{20,16},{24,28},{28,24},{1,5},{5... | collective-permute-start | bytes 983048 | tf_op jit(solution)/shard_map/ppermute | solution.py:111
  79.6 21.9 %collective-permute-start.16 = (bf16[2,1,32,2560]{3,2,1,0:T(8,128)(2,1)S(1)}, bf16[2,1,32,2560]{3,2,1,0:T(8,128)(2,1)S(1)}, u32[]{:S(2)}, u32[]{:S(2)}) collective-permute-start(bf16[2,1,32,2560]{3,2,1,0:T(8,128)(2,1)S(1)} %pad_maximum_fusion.8), channel_id=1, source_target_pairs={{0,12},{4,8},{8,4},{12,0},{16,28},{20,24},{24,20},{28,16},{1,13},{... | collective-permute-start | bytes 983048 | tf_op jit(solution)/shard_map/ppermute | solution.py:111
  82.4 26.1 %collective-permute-start.15 = (bf16[2,1,32,2560]{3,2,1,0:T(8,128)(2,1)S(1)}, bf16[2,1,32,2560]{3,2,1,0:T(8,128)(2,1)S(1)}, u32[]{:S(2)}, u32[]{:S(2)}) collective-permute-start(bf16[2,1,32,2560]{3,2,1,0:T(8,128)(2,1)S(1)} %pad_maximum_fusion.7), channel_id=1, source_target_pairs={{0,8},{4,12},{8,0},{12,4},{16,24},{20,28},{24,16},{28,20},{1,9},{5... | collective-permute-start | bytes 983048 | tf_op jit(solution)/shard_map/ppermute | solution.py:111
  87.4 22.7 %collective-permute-start.14 = (bf16[2,1,32,2560]{3,2,1,0:T(8,128)(2,1)S(1)}, bf16[2,1,32,2560]{3,2,1,0:T(8,128)(2,1)S(1)}, u32[]{:S(2)}, u32[]{:S(2)}) collective-permute-start(bf16[2,1,32,2560]{3,2,1,0:T(8,128)(2,1)S(1)} %pad_maximum_fusion.6), channel_id=1, source_target_pairs={{0,4},{4,0},{8,12},{12,8},{16,20},{20,16},{24,28},{28,24},{1,5},{5... | collective-permute-start | bytes 983048 | tf_op jit(solution)/shard_map/ppermute | solution.py:111
  94.5 28.2 %collective-permute-start.12 = (bf16[2,1,32,2560]{3,2,1,0:T(8,128)(2,1)S(1)}, bf16[2,1,32,2560]{3,2,1,0:T(8,128)(2,1)S(1)}, u32[]{:S(2)}, u32[]{:S(2)}) collective-permute-start(bf16[2,1,32,2560]{3,2,1,0:T(8,128)(2,1)S(1)} %pad_maximum_fusion.5), channel_id=1, source_target_pairs={{0,12},{4,8},{8,4},{12,0},{16,28},{20,24},{24,20},{28,16},{1,13},{... | collective-permute-start | bytes 983048 | tf_op jit(solution)/shard_map/ppermute | solution.py:111
  96.3 32.1 %collective-permute-start.11 = (bf16[2,1,32,2560]{3,2,1,0:T(8,128)(2,1)S(1)}, bf16[2,1,32,2560]{3,2,1,0:T(8,128)(2,1)S(1)}, u32[]{:S(2)}, u32[]{:S(2)}) collective-permute-start(bf16[2,1,32,2560]{3,2,1,0:T(8,128)(2,1)S(1)} %pad_maximum_fusion.4), channel_id=1, source_target_pairs={{0,8},{4,12},{8,0},{12,4},{16,24},{20,28},{24,16},{28,20},{1,9},{5... | collective-permute-start | bytes 983048 | tf_op jit(solution)/shard_map/ppermute | solution.py:111
  101.5 26.9 %collective-permute-start.10 = (bf16[2,1,32,2560]{3,2,1,0:T(8,128)(2,1)S(1)}, bf16[2,1,32,2560]{3,2,1,0:T(8,128)(2,1)S(1)}, u32[]{:S(2)}, u32[]{:S(2)}) collective-permute-start(bf16[2,1,32,2560]{3,2,1,0:T(8,128)(2,1)S(1)} %pad_maximum_fusion.3), channel_id=1, source_target_pairs={{0,4},{4,0},{8,12},{12,8},{16,20},{20,16},{24,28},{28,24},{1,5},{5... | collective-permute-start | bytes 983048 | tf_op jit(solution)/shard_map/ppermute | solution.py:111
  108.6 21.5 %collective-permute-start.21 = (bf16[1,32,2560]{2,1,0:T(8,128)(2,1)S(1)}, bf16[1,32,2560]{2,1,0:T(8,128)(2,1)S(1)}, u32[]{:S(2)}, u32[]{:S(2)}) collective-permute-start(bf16[1,32,2560]{2,1,0:T(8,128)(2,1)S(1)} %fusion.77), channel_id=1, source_target_pairs={{0,16},{4,20},{8,24},{12,28},{16,0},{20,4},{24,8},{28,12},{1,17},{... | collective-permute-start | bytes 491528 | tf_op jit(solution)/shard_map/ppermute | solution.py:116
  110.2 20.0 %collective-permute-start.17 = (bf16[1,32,2560]{2,1,0:T(8,128)(2,1)S(1)}, bf16[1,32,2560]{2,1,0:T(8,128)(2,1)S(1)}, u32[]{:S(2)}, u32[]{:S(2)}) collective-permute-start(bf16[1,32,2560]{2,1,0:T(8,128)(2,1)S(1)} %fusion.75), channel_id=1, source_target_pairs={{0,16},{4,20},{8,24},{12,28},{16,0},{20,4},{24,8},{28,12},{1,17},{... | collective-permute-start | bytes 491528 | tf_op jit(solution)/shard_map/ppermute | solution.py:116
  128.6 9.4 %collective-permute-start.13 = (bf16[1,32,2560]{2,1,0:T(8,128)(2,1)S(1)}, bf16[1,32,2560]{2,1,0:T(8,128)(2,1)S(1)}, u32[]{:S(2)}, u32[]{:S(2)}) collective-permute-start(bf16[1,32,2560]{2,1,0:T(8,128)(2,1)S(1)} %fusion.73), channel_id=1, source_target_pairs={{0,16},{4,20},{8,24},{12,28},{16,0},{20,4},{24,8},{28,12},{1,17},{... | collective-permute-start | bytes 491528 | tf_op jit(solution)/shard_map/ppermute | solution.py:116
  138.9 11.9 %all-to-all-start = ((bf16[3,4,8,1,2560]{4,2,3,0,1:T(8,128)(2,1)}), bf16[3,4,8,1,2560]{4,2,3,0,1:T(8,128)(2,1)S(1)}, u32[]{:S(2)}, u32[]{:S(2)}) async-start(bf16[3,4,8,1,2560]{4,2,3,0,1:T(8,128)(2,1)} %copy.81), calls=%async_computation | async-start | bytes 983040 | tf_op jit(solution)/shard_map/all_to_all | solution.py:318
  161.6 10.9 %all-to-all-start.1 = ((bf16[3,1,8,4,2048]{4,2,0,1,3:T(8,128)(2,1)}), bf16[3,1,8,4,2048]{4,2,0,1,3:T(8,128)(2,1)S(1)}, u32[]{:S(2)}, u32[]{:S(2)}) async-start(bf16[3,1,8,4,2048]{4,2,0,1,3:T(8,128)(2,1)} %copy.92), calls=%async_computation.1 | async-start | bytes 786432 | tf_op jit(solution)/shard_map/all_to_all | solution.py:344
  172.5 10.7 %collective-permute-start.22 = (bf16[3,32,2048]{2,1,0:T(8,128)(2,1)S(1)}, bf16[3,32,2048]{2,1,0:T(8,128)(2,1)S(1)}, u32[]{:S(2)}, u32[]{:S(2)}) collective-permute-start(bf16[3,32,2048]{2,1,0:T(8,128)(2,1)S(1)} %bitcast.212), channel_id=1, source_target_pairs={{0,4},{8,0},{16,8},{24,16},{28,24},{20,28},{12,20},{4,12},{1,5},{9... | collective-permute-start | bytes 1179656 | tf_op jit(solution)/shard_map/ppermute | solution.py:82
  173.4 10.7 %collective-permute-start.25 = (bf16[3,32,2048]{2,1,0:T(8,128)(2,1)S(1)}, bf16[3,32,2048]{2,1,0:T(8,128)(2,1)S(1)}, u32[]{:S(2)}, u32[]{:S(2)}) collective-permute-start(bf16[3,32,2048]{2,1,0:T(8,128)(2,1)S(1)} %bitcast.213), channel_id=1, source_target_pairs={{0,8},{8,16},{16,24},{24,28},{28,20},{20,12},{12,4},{4,0},{1,9},{9... | collective-permute-start | bytes 1179656 | tf_op jit(solution)/shard_map/ppermute | solution.py:79
  183.2 9.8 %collective-permute-start.23 = (bf16[3,32,2048]{2,1,0:T(8,128)(2,1)S(1)}, bf16[3,32,2048]{2,1,0:T(8,128)(2,1)S(1)}, u32[]{:S(2)}, u32[]{:S(2)}) collective-permute-start(bf16[3,32,2048]{2,1,0:T(8,128)(2,1)S(1)} %collective-permute-done.22), channel_id=1, source_target_pairs={{0,4},{8,0},{16,8},{24,16},{28,24},{20,28},{12,20},{4,12},{1,5},{9... | collective-permute-start | bytes 1179656 | tf_op jit(solution)/shard_map/ppermute | solution.py:82
  184.1 9.8 %collective-permute-start.26 = (bf16[3,32,2048]{2,1,0:T(8,128)(2,1)S(1)}, bf16[3,32,2048]{2,1,0:T(8,128)(2,1)S(1)}, u32[]{:S(2)}, u32[]{:S(2)}) collective-permute-start(bf16[3,32,2048]{2,1,0:T(8,128)(2,1)S(1)} %collective-permute-done.25), channel_id=1, source_target_pairs={{0,8},{8,16},{16,24},{24,28},{28,20},{20,12},{12,4},{4,0},{1,9},{9... | collective-permute-start | bytes 1179656 | tf_op jit(solution)/shard_map/ppermute | solution.py:79
  193.0 11.3 %collective-permute-start.24 = (bf16[3,32,2048]{2,1,0:T(8,128)(2,1)S(1)}, bf16[3,32,2048]{2,1,0:T(8,128)(2,1)S(1)}, u32[]{:S(2)}, u32[]{:S(2)}) collective-permute-start(bf16[3,32,2048]{2,1,0:T(8,128)(2,1)S(1)} %collective-permute-done.23), channel_id=1, source_target_pairs={{0,4},{8,0},{16,8},{24,16},{28,24},{20,28},{12,20},{4,12},{1,5},{9... | collective-permute-start | bytes 1179656 | tf_op jit(solution)/shard_map/ppermute | solution.py:82
  193.8 9.3 %collective-permute-start.27 = (bf16[3,32,2048]{2,1,0:T(8,128)(2,1)S(1)}, bf16[3,32,2048]{2,1,0:T(8,128)(2,1)S(1)}, u32[]{:S(2)}, u32[]{:S(2)}) collective-permute-start(bf16[3,32,2048]{2,1,0:T(8,128)(2,1)S(1)} %collective-permute-done.26), channel_id=1, source_target_pairs={{0,8},{8,16},{16,24},{24,28},{28,20},{20,12},{12,4},{4,0},{1,9},{9... | collective-permute-start | bytes 1179656 | tf_op jit(solution)/shard_map/ppermute | solution.py:79
  203.1 7.8 %collective-permute-start.28 = (bf16[3,32,2048]{2,1,0:T(8,128)(2,1)S(1)}, bf16[3,32,2048]{2,1,0:T(8,128)(2,1)S(1)}, u32[]{:S(2)}, u32[]{:S(2)}) collective-permute-start(bf16[3,32,2048]{2,1,0:T(8,128)(2,1)S(1)} %collective-permute-done.27), channel_id=1, source_target_pairs={{0,8},{8,16},{16,24},{24,28},{28,20},{20,12},{12,4},{4,0},{1,9},{9... | collective-permute-start | bytes 1179656 | tf_op jit(solution)/shard_map/ppermute | solution.py:79
  220.6 7.0 %collective-permute-start.30 = (f32[3,2,128,64]{2,3,0,1:T(8,128)S(1)}, f32[3,2,128,64]{2,3,0,1:T(8,128)S(1)}, u32[]{:S(2)}, u32[]{:S(2)}) collective-permute-start(f32[3,2,128,64]{2,3,0,1:T(8,128)S(1)} %add.510), channel_id=1, source_target_pairs={{0,2},{1,3},{2,0},{3,1},{4,6},{5,7},{6,4},{7,5},{8,10},{9,11},{10,... | collective-permute-start | bytes 589832 | tf_op jit(solution)/shard_map/ppermute | solution.py:166
  227.6 4.7 %collective-permute-start.31 = (bf16[3,2,128,64]{2,3,0,1:T(8,128)(2,1)S(1)}, bf16[3,2,128,64]{2,3,0,1:T(8,128)(2,1)S(1)}, u32[]{:S(2)}, u32[]{:S(2)}) collective-permute-start(bf16[3,2,128,64]{2,3,0,1:T(8,128)(2,1)S(1)} %add_convert_fusion.2), channel_id=1, source_target_pairs={{0,4},{4,0},{8,12},{12,8},{16,20},{20,16},{24,28},{28,24},{1,5},{5... | collective-permute-start | bytes 294920 | tf_op jit(solution)/shard_map/ppermute | solution.py:166
  232.3 4.7 %collective-permute-start.32 = (bf16[3,2,128,64]{2,3,0,1:T(8,128)(2,1)S(1)}, bf16[3,2,128,64]{2,3,0,1:T(8,128)(2,1)S(1)}, u32[]{:S(2)}, u32[]{:S(2)}) collective-permute-start(bf16[3,2,128,64]{2,3,0,1:T(8,128)(2,1)S(1)} %add.512), channel_id=1, source_target_pairs={{0,8},{4,12},{8,0},{12,4},{16,24},{20,28},{24,16},{28,20},{1,9},{5... | collective-permute-start | bytes 294920 | tf_op jit(solution)/shard_map/ppermute | solution.py:166
  237.0 6.8 %collective-permute-start.33 = (bf16[3,2,128,64]{2,3,0,1:T(8,128)(2,1)S(1)}, bf16[3,2,128,64]{2,3,0,1:T(8,128)(2,1)S(1)}, u32[]{:S(2)}, u32[]{:S(2)}) collective-permute-start(bf16[3,2,128,64]{2,3,0,1:T(8,128)(2,1)S(1)} %add.513), channel_id=1, source_target_pairs={{0,16},{4,20},{8,24},{12,28},{16,0},{20,4},{24,8},{28,12},{1,17},{... | collective-permute-start | bytes 294920 | tf_op jit(solution)/shard_map/ppermute | solution.py:166
  255.0 11.2 %collective-permute-start.35 = (bf16[3,1,64,1024]{3,2,0,1:T(8,128)(2,1)S(1)}, bf16[3,1,64,1024]{3,2,0,1:T(8,128)(2,1)S(1)}, u32[]{:S(2)}, u32[]{:S(2)}) collective-permute-start(bf16[3,1,64,1024]{3,2,0,1:T(8,128)(2,1)S(1)} %dynamic-slice_convert_fusion), channel_id=1, source_target_pairs={{0,2},{1,3},{2,0},{3,1},{4,6},{5,7},{6,4},{7,5},{8,10},{9,11},{10,... | collective-permute-start | bytes 1179656 | tf_op jit(solution)/shard_map/ppermute | solution.py:191
  (18 other events, 179.6 us)

commit v13 on v12

--- a/solution.py
+++ b/solution.py
@@ -359,7 +359,12 @@
         jnp.einsum("tnq,qe->tne", mixed_all, output_weight, preferred_element_type=jnp.float32)
     )
     partial_out = output_main + delta_output
-    return halving_scatter(partial_out, "gy", across_second).astype(jnp.bfloat16)
+    return jnp.concatenate(
+        [
+            halving_scatter(partial_out[step : step + 1], "gy", across_second)
+            for step in range(steps)
+        ]
+    ).astype(jnp.bfloat16)
 
 
 def solution(mesh):

time: 269 us -> 264 us (0.981)
  waiting for transfers between devices: 140 us -> 134 us
  starting transfers between devices: 55 us -> 57.9 us
    ppermute x2 -> x6, waiting for transfers between devices: 13.5 us -> 7.83 us  [halving_scatter(): held = keep + lax.ppermute(give, axis_name, swap).astype(jnp.float32)]
    ppermute x2 -> x6, starting transfers between devices: 1.47 us -> 4.29 us  [halving_scatter(): held = keep + lax.ppermute(give, axis_name, swap).astype(jnp.float32)]
  transfers between devices with their start and end apart: 38 -> 42, of which waited for: 28 -> 30; matrix products, arithmetic and copies ran while one was open for 10% -> 11% of each run, Pallas kernels for 0% -> 0%
where the time goes in v13:
time: 264 us
  waiting for transfers between devices  134 us (51%)
  starting transfers between devices  57.9 us (22%)
  matrix products  23.8 us (9%)
  local copies, waits for them, and re-layouts  21.3 us (8%)
  other arithmetic  20.4 us (8%)
  between operations  6.26 us (2%)
    ppermute x9, waiting for transfers between devices, split_half_scatter(): lax.ppermute(outgoing, axis_name, [(i, i ^ offset) for i in range(axis_si...  36.7 us
    ppermute x13, waiting for transfers between devices, tree_sum(): value = value + lax.ppermute(value, axis_name, pairs)  28 us
    ppermute x13, starting transfers between devices, tree_sum(): value = value + lax.ppermute(value, axis_name, pairs)  19.3 us
    ppermute x3, waiting for transfers between devices, ring_gather(): backward = lax.ppermute(backward, axis_name, behind)  14.8 us
    ppermute x4, waiting for transfers between devices, ring_gather(): forward = lax.ppermute(forward, axis_name, ahead)  13.1 us
    ppermute x2, waiting for transfers between devices, doubling_gather(): lax.ppermute(held, axis_name, [(i, i ^ distance) for i in range(axis_size)])  12.2 us
    ppermute x9, starting transfers between devices, split_half_scatter(): lax.ppermute(outgoing, axis_name, [(i, i ^ offset) for i in range(axis_si...  11.8 us
    unnamed x31, local copies, waits for them, and re-layouts  8.42 us
  transfers between devices with their start and end apart: 42, of which 30 were waited for; matrix products, arithmetic and copies ran while one was open for 11% of the time, Pallas kernels for 0%

profile of v13, /device:TPU:0, one launch (start us, length us, event | category | flops | bytes accessed | tf_op | source)
XLA Modules:
  0.0 263.6 jit_solution(10060632445965822952)
XLA Ops:
  3.2 3.0 %collective-permute-start.1 = (bf16[3,128,1024]{2,1,0:T(8,128)(2,1)S(1)}, bf16[3,128,1024]{2,1,0:T(8,128)(2,1)}, u32[]{:S(2)}, u32[]{:S(2)}) collective-permute-start(bf16[3,128,1024]{2,1,0:T(8,128)(2,1)S(1)} %pad_maximum_fusion.1), channel_id=1, source_target_pairs={{0,2},{1,3},{2,0},{3,1},{4,6},{5,7},{6,4},{7,5},{8,10},{9,11},{10,... | collective-permute-start | bytes 2359304 | tf_op jit(solution)/shard_map/ppermute | solution.py:129
  13.4 10.7 %collective-permute-done.1 = bf16[3,128,1024]{2,1,0:T(8,128)(2,1)} collective-permute-done((bf16[3,128,1024]{2,1,0:T(8,128)(2,1)S(1)}, bf16[3,128,1024]{2,1,0:T(8,128)(2,1)}, u32[]{:S(2)}, u32[]{:S(2)}) %collective-permute-start.1) | collective-permute-done | bytes 786464 | tf_op jit(solution)/shard_map/ppermute | solution.py:129
  33.3 2.8 %collective-permute-start.4 = (f32[3,256]{1,0:T(4,128)S(1)}, f32[3,256]{1,0:T(4,128)S(1)}, u32[]{:S(2)}, u32[]{:S(2)}) collective-permute-start(f32[3,256]{1,0:T(4,128)S(1)} %add.478), channel_id=1, source_target_pairs={{0,16},{4,20},{8,24},{12,28},{16,0},{20,4},{24,8},{28,12},{1,17},{... | collective-permute-start | bytes 9224 | tf_op jit(solution)/shard_map/ppermute | solution.py:166
  40.4 3.9 %collective-permute-done.5 = f32[3,2,128,64]{2,3,0,1:T(8,128)S(1)} collective-permute-done((f32[3,2,128,64]{2,3,0,1:T(8,128)S(1)}, f32[3,2,128,64]{2,3,0,1:T(8,128)S(1)}, u32[]{:S(2)}, u32[]{:S(2)}) %collective-permute-start.5) | collective-permute-done | bytes 196640 | tf_op jit(solution)/shard_map/ppermute | solution.py:166
  46.8 4.7 %collective-permute-done.6 = f32[3,2,128,64]{2,3,0,1:T(8,128)S(1)} collective-permute-done((f32[3,2,128,64]{2,3,0,1:T(8,128)S(1)}, f32[3,2,128,64]{2,3,0,1:T(8,128)S(1)}, u32[]{:S(2)}, u32[]{:S(2)}) %collective-permute-start.6) | collective-permute-done | bytes 196640 | tf_op jit(solution)/shard_map/ppermute | solution.py:166
  51.5 2.5 collective-permute-start.7
  54.1 5.6 %fusion.8 = f32[3,256,2048]{2,1,0:T(8,128)} fusion(bf16[1024,2048]{1,0:T(8,128)(2,1)S(1)} %copy-done.7, f32[1024]{0:T(1024)S(1)} %convert_element_type.207, f32[3,256]{1,0:T(4,128)S(1)} %add_rsqrt_fusion, bf16[3,128,1024]{2,1,0:T(8,128)(2,1)S(1)} %get-tuple-element.22, bf16[3,128,1024]{2,1,0:T(8,128)(2,1)S(1)} %get-tuple-element.21), kind=kOutput, calls=%fused_computation.11 | convolution fusion | flops 3226730496 | bytes 12065792 | tf_op jit(solution)/shard_map/tnd,de->tne/dot_general | solution.py:308
  72.3 2.5 pad_maximum_fusion
  75.8 2.8 %collective-permute-start.20 = (bf16[2,1,32,2560]{3,2,1,0:T(8,128)(2,1)S(1)}, bf16[2,1,32,2560]{3,2,1,0:T(8,128)(2,1)S(1)}, u32[]{:S(2)}, u32[]{:S(2)}) collective-permute-start(bf16[2,1,32,2560]{3,2,1,0:T(8,128)(2,1)S(1)} %pad_maximum_fusion.12), channel_id=1, source_target_pairs={{0,12},{4,8},{8,4},{12,0},{16,28},{20,24},{24,20},{28,16},{1,13},{... | collective-permute-start | bytes 983048 | tf_op jit(solution)/shard_map/ppermute | solution.py:111
  79.6 2.8 %collective-permute-start.16 = (bf16[2,1,32,2560]{3,2,1,0:T(8,128)(2,1)S(1)}, bf16[2,1,32,2560]{3,2,1,0:T(8,128)(2,1)S(1)}, u32[]{:S(2)}, u32[]{:S(2)}) collective-permute-start(bf16[2,1,32,2560]{3,2,1,0:T(8,128)(2,1)S(1)} %pad_maximum_fusion.9), channel_id=1, source_target_pairs={{0,12},{4,8},{8,4},{12,0},{16,28},{20,24},{24,20},{28,16},{1,13},{... | collective-permute-start | bytes 983048 | tf_op jit(solution)/shard_map/ppermute | solution.py:111
  83.1 4.3 %collective-permute-done.20 = bf16[2,1,32,2560]{3,2,1,0:T(8,128)(2,1)S(1)} collective-permute-done((bf16[2,1,32,2560]{3,2,1,0:T(8,128)(2,1)S(1)}, bf16[2,1,32,2560]{3,2,1,0:T(8,128)(2,1)S(1)}, u32[]{:S(2)}, u32[]{:S(2)}) %collective-permute-start.20) | collective-permute-done | bytes 327712 | tf_op jit(solution)/shard_map/ppermute | solution.py:111
  89.0 5.5 %collective-permute-done.19 = bf16[2,1,32,2560]{3,2,1,0:T(8,128)(2,1)S(1)} collective-permute-done((bf16[2,1,32,2560]{3,2,1,0:T(8,128)(2,1)S(1)}, bf16[2,1,32,2560]{3,2,1,0:T(8,128)(2,1)S(1)}, u32[]{:S(2)}, u32[]{:S(2)}) %collective-permute-start.19) | collective-permute-done | bytes 327712 | tf_op jit(solution)/shard_map/ppermute | solution.py:111
  96.7 4.8 %collective-permute-done.16 = bf16[2,1,32,2560]{3,2,1,0:T(8,128)(2,1)S(1)} collective-permute-done((bf16[2,1,32,2560]{3,2,1,0:T(8,128)(2,1)S(1)}, bf16[2,1,32,2560]{3,2,1,0:T(8,128)(2,1)S(1)}, u32[]{:S(2)}, u32[]{:S(2)}) %collective-permute-start.16) | collective-permute-done | bytes 327712 | tf_op jit(solution)/shard_map/ppermute | solution.py:111
  103.0 5.5 %collective-permute-done.15 = bf16[2,1,32,2560]{3,2,1,0:T(8,128)(2,1)S(1)} collective-permute-done((bf16[2,1,32,2560]{3,2,1,0:T(8,128)(2,1)S(1)}, bf16[2,1,32,2560]{3,2,1,0:T(8,128)(2,1)S(1)}, u32[]{:S(2)}, u32[]{:S(2)}) %collective-permute-start.15) | collective-permute-done | bytes 327712 | tf_op jit(solution)/shard_map/ppermute | solution.py:111
  111.7 10.9 %collective-permute-done.12 = bf16[2,1,32,2560]{3,2,1,0:T(8,128)(2,1)S(1)} collective-permute-done((bf16[2,1,32,2560]{3,2,1,0:T(8,128)(2,1)S(1)}, bf16[2,1,32,2560]{3,2,1,0:T(8,128)(2,1)S(1)}, u32[]{:S(2)}, u32[]{:S(2)}) %collective-permute-start.12) | collective-permute-done | bytes 327712 | tf_op jit(solution)/shard_map/ppermute | solution.py:111
  122.7 5.7 %collective-permute-done.11 = bf16[2,1,32,2560]{3,2,1,0:T(8,128)(2,1)S(1)} collective-permute-done((bf16[2,1,32,2560]{3,2,1,0:T(8,128)(2,1)S(1)}, bf16[2,1,32,2560]{3,2,1,0:T(8,128)(2,1)S(1)}, u32[]{:S(2)}, u32[]{:S(2)}) %collective-permute-start.11) | collective-permute-done | bytes 327712 | tf_op jit(solution)/shard_map/ppermute | solution.py:111
  130.3 7.7 %collective-permute-done.13 = bf16[1,32,2560]{2,1,0:T(8,128)(2,1)S(1)} collective-permute-done((bf16[1,32,2560]{2,1,0:T(8,128)(2,1)S(1)}, bf16[1,32,2560]{2,1,0:T(8,128)(2,1)S(1)}, u32[]{:S(2)}, u32[]{:S(2)}) %collective-permute-start.13) | collective-permute-done | bytes 163872 | tf_op jit(solution)/shard_map/ppermute | solution.py:116
  138.9 3.7 %all-to-all-start = ((bf16[3,4,8,1,2560]{4,2,3,0,1:T(8,128)(2,1)}), bf16[3,4,8,1,2560]{4,2,3,0,1:T(8,128)(2,1)S(1)}, u32[]{:S(2)}, u32[]{:S(2)}) async-start(bf16[3,4,8,1,2560]{4,2,3,0,1:T(8,128)(2,1)} %copy.75), calls=%async_computation | async-start | bytes 983040 | tf_op jit(solution)/shard_map/all_to_all | solution.py:318
  142.9 8.0 %all-to-all-done = bf16[3,4,8,1,2560]{4,2,3,0,1:T(8,128)(2,1)S(1)} async-done(((bf16[3,4,8,1,2560]{4,2,3,0,1:T(8,128)(2,1)}), bf16[3,4,8,1,2560]{4,2,3,0,1:T(8,128)(2,1)S(1)}, u32[]{:S(2)}, u32[]{:S(2)}) %all-to-all-start) | async-done | bytes 491552 | tf_op jit(solution)/shard_map/all_to_all | solution.py:318
  152.6 4.6 %fusion.105 = (f32[8,8,24]{2,1,0:T(8,128)S(1)}, f32[8,8,24,256]{3,2,1,0:T(8,128)S(1)}) fusion(pred[8,256]{1,0:T(8,128)(4,1)S(1)} %iota_compare_fusion, bf16[8,256,1024]{2,1,0:T(8,128)(2,1)} %param.27, bf16[3,8,8,8,64]{4,3,2,1,0:T(8,128)(2,1)S(1)} %bitcast.225, bf16[3,8,8,8,64]{4,3,2,1,0:T(8,128)(2,1)S(1)} %bitcast.223), kind=kOutput, calls=%fused_computation.216 | convolution fusion | flops 102627840 | bytes 6168576 | tf_op jit(solution)/shard_map/rhqd,rchd->rhqc/dot_general | solution.py:217
  161.6 3.5 %all-to-all-start.1 = ((bf16[3,1,8,4,2048]{4,2,0,1,3:T(8,128)(2,1)}), bf16[3,1,8,4,2048]{4,2,0,1,3:T(8,128)(2,1)S(1)}, u32[]{:S(2)}, u32[]{:S(2)}) async-start(bf16[3,1,8,4,2048]{4,2,0,1,3:T(8,128)(2,1)} %copy.86), calls=%async_computation.1 | async-start | bytes 786432 | tf_op jit(solution)/shard_map/all_to_all | solution.py:344
  166.9 5.6 %all-to-all-done.1 = bf16[3,1,8,4,2048]{4,2,0,1,3:T(8,128)(2,1)S(1)} async-done(((bf16[3,1,8,4,2048]{4,2,0,1,3:T(8,128)(2,1)}), bf16[3,1,8,4,2048]{4,2,0,1,3:T(8,128)(2,1)S(1)}, u32[]{:S(2)}, u32[]{:S(2)}) %all-to-all-start.1) | async-done | bytes 393248 | tf_op jit(solution)/shard_map/all_to_all | solution.py:344
  175.4 7.9 %collective-permute-done.22 = bf16[3,32,2048]{2,1,0:T(8,128)(2,1)S(1)} collective-permute-done((bf16[3,32,2048]{2,1,0:T(8,128)(2,1)S(1)}, bf16[3,32,2048]{2,1,0:T(8,128)(2,1)S(1)}, u32[]{:S(2)}, u32[]{:S(2)}) %collective-permute-start.22) | collective-permute-done | bytes 393248 | tf_op jit(solution)/shard_map/ppermute | solution.py:82
  186.1 6.9 %collective-permute-done.23 = bf16[3,32,2048]{2,1,0:T(8,128)(2,1)S(1)} collective-permute-done((bf16[3,32,2048]{2,1,0:T(8,128)(2,1)S(1)}, bf16[3,32,2048]{2,1,0:T(8,128)(2,1)S(1)}, u32[]{:S(2)}, u32[]{:S(2)}) %collective-permute-start.23) | collective-permute-done | bytes 393248 | tf_op jit(solution)/shard_map/ppermute | solution.py:82
  195.8 7.3 %collective-permute-done.27 = bf16[3,32,2048]{2,1,0:T(8,128)(2,1)S(1)} collective-permute-done((bf16[3,32,2048]{2,1,0:T(8,128)(2,1)S(1)}, bf16[3,32,2048]{2,1,0:T(8,128)(2,1)S(1)}, u32[]{:S(2)}, u32[]{:S(2)}) %collective-permute-start.27) | collective-permute-done | bytes 393248 | tf_op jit(solution)/shard_map/ppermute | solution.py:79
  205.1 5.8 %collective-permute-done.28 = bf16[3,32,2048]{2,1,0:T(8,128)(2,1)S(1)} collective-permute-done((bf16[3,32,2048]{2,1,0:T(8,128)(2,1)S(1)}, bf16[3,32,2048]{2,1,0:T(8,128)(2,1)S(1)}, u32[]{:S(2)}, u32[]{:S(2)}) %collective-permute-start.28) | collective-permute-done | bytes 393248 | tf_op jit(solution)/shard_map/ppermute | solution.py:79
  214.0 2.6 %gather_fusion = bf16[8,3,32,2048]{3,2,1,0:T(8,128)(2,1)S(1)} fusion(bf16[8,3,32,2048]{3,2,1,0:T(8,128)(2,1)} %bitcast_dynamic-update-slice_fusion.1, s32[1024]{0:T(1024)S(1)} %pad_clamp_fusion), kind=kCustom, calls=%fused_computation | custom fusion | bytes 6291488 | tf_op jit(solution)/shard_map/jit(_take)/gather | solution.py:88
  221.9 5.8 %collective-permute-done.30 = f32[3,2,128,64]{2,3,0,1:T(8,128)S(1)} collective-permute-done((f32[3,2,128,64]{2,3,0,1:T(8,128)S(1)}, f32[3,2,128,64]{2,3,0,1:T(8,128)S(1)}, u32[]{:S(2)}, u32[]{:S(2)}) %collective-permute-start.30) | collective-permute-done | bytes 196640 | tf_op jit(solution)/shard_map/ppermute | solution.py:166
  228.6 3.8 %collective-permute-done.31 = bf16[3,2,128,64]{2,3,0,1:T(8,128)(2,1)S(1)} collective-permute-done((bf16[3,2,128,64]{2,3,0,1:T(8,128)(2,1)S(1)}, bf16[3,2,128,64]{2,3,0,1:T(8,128)(2,1)S(1)}, u32[]{:S(2)}, u32[]{:S(2)}) %collective-permute-start.31) | collective-permute-done | bytes 98336 | tf_op jit(solution)/shard_map/ppermute | solution.py:166
  238.6 5.2 %fusion.6 = f32[3,256,1024]{2,1,0:T(8,128)S(1)} fusion(bf16[3,256,2048]{2,1,0:T(8,128)(2,1)S(1)} %bitcast.220, bf16[2048,1024]{1,0:T(8,128)(2,1)} %param.20), kind=kOutput, calls=%fused_computation.9 | convolution fusion | flops 3221225472 | bytes 10485760 | tf_op jit(solution)/shard_map/tnq,qe->tne/dot_general | solution.py:359
  255.5 2.5 collective-permute-done.39
  258.0 2.8 %collective-permute-done.37 = bf16[1,1,64,1024]{3,2,1,0:T(8,128)(2,1)S(1)} collective-permute-done((bf16[1,1,64,1024]{3,2,1,0:T(8,128)(2,1)S(1)}, bf16[1,1,64,1024]{3,2,1,0:T(8,128)(2,1)S(1)}, u32[]{:S(2)}, u32[]{:S(2)}) %collective-permute-start.37) | collective-permute-done | bytes 131104 | tf_op jit(solution)/shard_map/ppermute | solution.py:191
  (203 shorter events, 95.8 us)
Async XLA Ops:
  3.2 20.9 %collective-permute-start.1 = (bf16[3,128,1024]{2,1,0:T(8,128)(2,1)S(1)}, bf16[3,128,1024]{2,1,0:T(8,128)(2,1)}, u32[]{:S(2)}, u32[]{:S(2)}) collective-permute-start(bf16[3,128,1024]{2,1,0:T(8,128)(2,1)S(1)} %pad_maximum_fusion.1), channel_id=1, source_target_pairs={{0,2},{1,3},{2,0},{3,1},{4,6},{5,7},{6,4},{7,5},{8,10},{9,11},{10,... | collective-permute-start | bytes 2359304 | tf_op jit(solution)/shard_map/ppermute | solution.py:129
  38.5 5.7 %collective-permute-start.5 = (f32[3,2,128,64]{2,3,0,1:T(8,128)S(1)}, f32[3,2,128,64]{2,3,0,1:T(8,128)S(1)}, u32[]{:S(2)}, u32[]{:S(2)}) collective-permute-start(f32[3,2,128,64]{2,3,0,1:T(8,128)S(1)} %fusion.23), channel_id=1, source_target_pairs={{0,4},{4,0},{8,12},{12,8},{16,20},{20,16},{24,28},{28,24},{1,5},{5... | collective-permute-start | bytes 589832 | tf_op jit(solution)/shard_map/ppermute | solution.py:166
  44.3 7.2 %collective-permute-start.6 = (f32[3,2,128,64]{2,3,0,1:T(8,128)S(1)}, f32[3,2,128,64]{2,3,0,1:T(8,128)S(1)}, u32[]{:S(2)}, u32[]{:S(2)}) collective-permute-start(f32[3,2,128,64]{2,3,0,1:T(8,128)S(1)} %add.490), channel_id=1, source_target_pairs={{0,8},{4,12},{8,0},{12,4},{16,24},{20,28},{24,16},{28,20},{1,9},{5... | collective-permute-start | bytes 589832 | tf_op jit(solution)/shard_map/ppermute | solution.py:166
  51.5 8.7 %collective-permute-start.7 = (f32[3,2,128,64]{2,3,0,1:T(8,128)S(1)}, f32[3,2,128,64]{2,3,0,1:T(8,128)S(1)}, u32[]{:S(2)}, u32[]{:S(2)}) collective-permute-start(f32[3,2,128,64]{2,3,0,1:T(8,128)S(1)} %add.491), channel_id=1, source_target_pairs={{0,16},{4,20},{8,24},{12,28},{16,0},{20,4},{24,8},{28,12},{1,17},{... | collective-permute-start | bytes 589832 | tf_op jit(solution)/shard_map/ppermute | solution.py:166
  61.9 5.3 %collective-permute-start.9 = (bf16[3,2,128,64]{2,3,0,1:T(8,128)(2,1)S(1)}, bf16[3,2,128,64]{2,3,0,1:T(8,128)(2,1)S(1)}, u32[]{:S(2)}, u32[]{:S(2)}) collective-permute-start(bf16[3,2,128,64]{2,3,0,1:T(8,128)(2,1)S(1)} %add.493), channel_id=1, source_target_pairs={{0,2},{1,3},{2,0},{3,1},{4,6},{5,7},{6,4},{7,5},{8,10},{9,11},{10,... | collective-permute-start | bytes 294920 | tf_op jit(solution)/shard_map/ppermute | solution.py:166
  75.8 11.6 %collective-permute-start.20 = (bf16[2,1,32,2560]{3,2,1,0:T(8,128)(2,1)S(1)}, bf16[2,1,32,2560]{3,2,1,0:T(8,128)(2,1)S(1)}, u32[]{:S(2)}, u32[]{:S(2)}) collective-permute-start(bf16[2,1,32,2560]{3,2,1,0:T(8,128)(2,1)S(1)} %pad_maximum_fusion.12), channel_id=1, source_target_pairs={{0,12},{4,8},{8,4},{12,0},{16,28},{20,24},{24,20},{28,16},{1,13},{... | collective-permute-start | bytes 983048 | tf_op jit(solution)/shard_map/ppermute | solution.py:111
  78.6 15.8 %collective-permute-start.19 = (bf16[2,1,32,2560]{3,2,1,0:T(8,128)(2,1)S(1)}, bf16[2,1,32,2560]{3,2,1,0:T(8,128)(2,1)S(1)}, u32[]{:S(2)}, u32[]{:S(2)}) collective-permute-start(bf16[2,1,32,2560]{3,2,1,0:T(8,128)(2,1)S(1)} %pad_maximum_fusion.11), channel_id=1, source_target_pairs={{0,8},{4,12},{8,0},{12,4},{16,24},{20,28},{24,16},{28,20},{1,9},{5... | collective-permute-start | bytes 983048 | tf_op jit(solution)/shard_map/ppermute | solution.py:111
  78.9 17.4 %collective-permute-start.18 = (bf16[2,1,32,2560]{3,2,1,0:T(8,128)(2,1)S(1)}, bf16[2,1,32,2560]{3,2,1,0:T(8,128)(2,1)S(1)}, u32[]{:S(2)}, u32[]{:S(2)}) collective-permute-start(bf16[2,1,32,2560]{3,2,1,0:T(8,128)(2,1)S(1)} %pad_maximum_fusion.10), channel_id=1, source_target_pairs={{0,4},{4,0},{8,12},{12,8},{16,20},{20,16},{24,28},{28,24},{1,5},{5... | collective-permute-start | bytes 983048 | tf_op jit(solution)/shard_map/ppermute | solution.py:111
  79.6 21.9 %collective-permute-start.16 = (bf16[2,1,32,2560]{3,2,1,0:T(8,128)(2,1)S(1)}, bf16[2,1,32,2560]{3,2,1,0:T(8,128)(2,1)S(1)}, u32[]{:S(2)}, u32[]{:S(2)}) collective-permute-start(bf16[2,1,32,2560]{3,2,1,0:T(8,128)(2,1)S(1)} %pad_maximum_fusion.9), channel_id=1, source_target_pairs={{0,12},{4,8},{8,4},{12,0},{16,28},{20,24},{24,20},{28,16},{1,13},{... | collective-permute-start | bytes 983048 | tf_op jit(solution)/shard_map/ppermute | solution.py:111
  82.4 26.1 %collective-permute-start.15 = (bf16[2,1,32,2560]{3,2,1,0:T(8,128)(2,1)S(1)}, bf16[2,1,32,2560]{3,2,1,0:T(8,128)(2,1)S(1)}, u32[]{:S(2)}, u32[]{:S(2)}) collective-permute-start(bf16[2,1,32,2560]{3,2,1,0:T(8,128)(2,1)S(1)} %pad_maximum_fusion.8), channel_id=1, source_target_pairs={{0,8},{4,12},{8,0},{12,4},{16,24},{20,28},{24,16},{28,20},{1,9},{5... | collective-permute-start | bytes 983048 | tf_op jit(solution)/shard_map/ppermute | solution.py:111
  87.4 22.7 %collective-permute-start.14 = (bf16[2,1,32,2560]{3,2,1,0:T(8,128)(2,1)S(1)}, bf16[2,1,32,2560]{3,2,1,0:T(8,128)(2,1)S(1)}, u32[]{:S(2)}, u32[]{:S(2)}) collective-permute-start(bf16[2,1,32,2560]{3,2,1,0:T(8,128)(2,1)S(1)} %pad_maximum_fusion.7), channel_id=1, source_target_pairs={{0,4},{4,0},{8,12},{12,8},{16,20},{20,16},{24,28},{28,24},{1,5},{5... | collective-permute-start | bytes 983048 | tf_op jit(solution)/shard_map/ppermute | solution.py:111
  94.5 28.2 %collective-permute-start.12 = (bf16[2,1,32,2560]{3,2,1,0:T(8,128)(2,1)S(1)}, bf16[2,1,32,2560]{3,2,1,0:T(8,128)(2,1)S(1)}, u32[]{:S(2)}, u32[]{:S(2)}) collective-permute-start(bf16[2,1,32,2560]{3,2,1,0:T(8,128)(2,1)S(1)} %pad_maximum_fusion.6), channel_id=1, source_target_pairs={{0,12},{4,8},{8,4},{12,0},{16,28},{20,24},{24,20},{28,16},{1,13},{... | collective-permute-start | bytes 983048 | tf_op jit(solution)/shard_map/ppermute | solution.py:111
  96.3 32.1 %collective-permute-start.11 = (bf16[2,1,32,2560]{3,2,1,0:T(8,128)(2,1)S(1)}, bf16[2,1,32,2560]{3,2,1,0:T(8,128)(2,1)S(1)}, u32[]{:S(2)}, u32[]{:S(2)}) collective-permute-start(bf16[2,1,32,2560]{3,2,1,0:T(8,128)(2,1)S(1)} %pad_maximum_fusion.5), channel_id=1, source_target_pairs={{0,8},{4,12},{8,0},{12,4},{16,24},{20,28},{24,16},{28,20},{1,9},{5... | collective-permute-start | bytes 983048 | tf_op jit(solution)/shard_map/ppermute | solution.py:111
  101.5 26.9 %collective-permute-start.10 = (bf16[2,1,32,2560]{3,2,1,0:T(8,128)(2,1)S(1)}, bf16[2,1,32,2560]{3,2,1,0:T(8,128)(2,1)S(1)}, u32[]{:S(2)}, u32[]{:S(2)}) collective-permute-start(bf16[2,1,32,2560]{3,2,1,0:T(8,128)(2,1)S(1)} %pad_maximum_fusion.4), channel_id=1, source_target_pairs={{0,4},{4,0},{8,12},{12,8},{16,20},{20,16},{24,28},{28,24},{1,5},{5... | collective-permute-start | bytes 983048 | tf_op jit(solution)/shard_map/ppermute | solution.py:111
  108.6 21.5 %collective-permute-start.21 = (bf16[1,32,2560]{2,1,0:T(8,128)(2,1)S(1)}, bf16[1,32,2560]{2,1,0:T(8,128)(2,1)S(1)}, u32[]{:S(2)}, u32[]{:S(2)}) collective-permute-start(bf16[1,32,2560]{2,1,0:T(8,128)(2,1)S(1)} %fusion.76), channel_id=1, source_target_pairs={{0,16},{4,20},{8,24},{12,28},{16,0},{20,4},{24,8},{28,12},{1,17},{... | collective-permute-start | bytes 491528 | tf_op jit(solution)/shard_map/ppermute | solution.py:116
  110.2 20.0 %collective-permute-start.17 = (bf16[1,32,2560]{2,1,0:T(8,128)(2,1)S(1)}, bf16[1,32,2560]{2,1,0:T(8,128)(2,1)S(1)}, u32[]{:S(2)}, u32[]{:S(2)}) collective-permute-start(bf16[1,32,2560]{2,1,0:T(8,128)(2,1)S(1)} %fusion.74), channel_id=1, source_target_pairs={{0,16},{4,20},{8,24},{12,28},{16,0},{20,4},{24,8},{28,12},{1,17},{... | collective-permute-start | bytes 491528 | tf_op jit(solution)/shard_map/ppermute | solution.py:116
  128.6 9.4 %collective-permute-start.13 = (bf16[1,32,2560]{2,1,0:T(8,128)(2,1)S(1)}, bf16[1,32,2560]{2,1,0:T(8,128)(2,1)S(1)}, u32[]{:S(2)}, u32[]{:S(2)}) collective-permute-start(bf16[1,32,2560]{2,1,0:T(8,128)(2,1)S(1)} %fusion.72), channel_id=1, source_target_pairs={{0,16},{4,20},{8,24},{12,28},{16,0},{20,4},{24,8},{28,12},{1,17},{... | collective-permute-start | bytes 491528 | tf_op jit(solution)/shard_map/ppermute | solution.py:116
  138.9 11.9 %all-to-all-start = ((bf16[3,4,8,1,2560]{4,2,3,0,1:T(8,128)(2,1)}), bf16[3,4,8,1,2560]{4,2,3,0,1:T(8,128)(2,1)S(1)}, u32[]{:S(2)}, u32[]{:S(2)}) async-start(bf16[3,4,8,1,2560]{4,2,3,0,1:T(8,128)(2,1)} %copy.75), calls=%async_computation | async-start | bytes 983040 | tf_op jit(solution)/shard_map/all_to_all | solution.py:318
  161.6 10.9 %all-to-all-start.1 = ((bf16[3,1,8,4,2048]{4,2,0,1,3:T(8,128)(2,1)}), bf16[3,1,8,4,2048]{4,2,0,1,3:T(8,128)(2,1)S(1)}, u32[]{:S(2)}, u32[]{:S(2)}) async-start(bf16[3,1,8,4,2048]{4,2,0,1,3:T(8,128)(2,1)} %copy.86), calls=%async_computation.1 | async-start | bytes 786432 | tf_op jit(solution)/shard_map/all_to_all | solution.py:344
  172.5 10.7 %collective-permute-start.22 = (bf16[3,32,2048]{2,1,0:T(8,128)(2,1)S(1)}, bf16[3,32,2048]{2,1,0:T(8,128)(2,1)S(1)}, u32[]{:S(2)}, u32[]{:S(2)}) collective-permute-start(bf16[3,32,2048]{2,1,0:T(8,128)(2,1)S(1)} %bitcast.228), channel_id=1, source_target_pairs={{0,4},{8,0},{16,8},{24,16},{28,24},{20,28},{12,20},{4,12},{1,5},{9... | collective-permute-start | bytes 1179656 | tf_op jit(solution)/shard_map/ppermute | solution.py:82
  173.4 10.7 %collective-permute-start.25 = (bf16[3,32,2048]{2,1,0:T(8,128)(2,1)S(1)}, bf16[3,32,2048]{2,1,0:T(8,128)(2,1)S(1)}, u32[]{:S(2)}, u32[]{:S(2)}) collective-permute-start(bf16[3,32,2048]{2,1,0:T(8,128)(2,1)S(1)} %bitcast.229), channel_id=1, source_target_pairs={{0,8},{8,16},{16,24},{24,28},{28,20},{20,12},{12,4},{4,0},{1,9},{9... | collective-permute-start | bytes 1179656 | tf_op jit(solution)/shard_map/ppermute | solution.py:79
  183.2 9.8 %collective-permute-start.23 = (bf16[3,32,2048]{2,1,0:T(8,128)(2,1)S(1)}, bf16[3,32,2048]{2,1,0:T(8,128)(2,1)S(1)}, u32[]{:S(2)}, u32[]{:S(2)}) collective-permute-start(bf16[3,32,2048]{2,1,0:T(8,128)(2,1)S(1)} %collective-permute-done.22), channel_id=1, source_target_pairs={{0,4},{8,0},{16,8},{24,16},{28,24},{20,28},{12,20},{4,12},{1,5},{9... | collective-permute-start | bytes 1179656 | tf_op jit(solution)/shard_map/ppermute | solution.py:82
  184.1 9.8 %collective-permute-start.26 = (bf16[3,32,2048]{2,1,0:T(8,128)(2,1)S(1)}, bf16[3,32,2048]{2,1,0:T(8,128)(2,1)S(1)}, u32[]{:S(2)}, u32[]{:S(2)}) collective-permute-start(bf16[3,32,2048]{2,1,0:T(8,128)(2,1)S(1)} %collective-permute-done.25), channel_id=1, source_target_pairs={{0,8},{8,16},{16,24},{24,28},{28,20},{20,12},{12,4},{4,0},{1,9},{9... | collective-permute-start | bytes 1179656 | tf_op jit(solution)/shard_map/ppermute | solution.py:79
  193.0 11.3 %collective-permute-start.24 = (bf16[3,32,2048]{2,1,0:T(8,128)(2,1)S(1)}, bf16[3,32,2048]{2,1,0:T(8,128)(2,1)S(1)}, u32[]{:S(2)}, u32[]{:S(2)}) collective-permute-start(bf16[3,32,2048]{2,1,0:T(8,128)(2,1)S(1)} %collective-permute-done.23), channel_id=1, source_target_pairs={{0,4},{8,0},{16,8},{24,16},{28,24},{20,28},{12,20},{4,12},{1,5},{9... | collective-permute-start | bytes 1179656 | tf_op jit(solution)/shard_map/ppermute | solution.py:82
  193.8 9.3 %collective-permute-start.27 = (bf16[3,32,2048]{2,1,0:T(8,128)(2,1)S(1)}, bf16[3,32,2048]{2,1,0:T(8,128)(2,1)S(1)}, u32[]{:S(2)}, u32[]{:S(2)}) collective-permute-start(bf16[3,32,2048]{2,1,0:T(8,128)(2,1)S(1)} %collective-permute-done.26), channel_id=1, source_target_pairs={{0,8},{8,16},{16,24},{24,28},{28,20},{20,12},{12,4},{4,0},{1,9},{9... | collective-permute-start | bytes 1179656 | tf_op jit(solution)/shard_map/ppermute | solution.py:79
  203.1 7.8 %collective-permute-start.28 = (bf16[3,32,2048]{2,1,0:T(8,128)(2,1)S(1)}, bf16[3,32,2048]{2,1,0:T(8,128)(2,1)S(1)}, u32[]{:S(2)}, u32[]{:S(2)}) collective-permute-start(bf16[3,32,2048]{2,1,0:T(8,128)(2,1)S(1)} %collective-permute-done.27), channel_id=1, source_target_pairs={{0,8},{8,16},{16,24},{24,28},{28,20},{20,12},{12,4},{4,0},{1,9},{9... | collective-permute-start | bytes 1179656 | tf_op jit(solution)/shard_map/ppermute | solution.py:79
  220.6 7.0 %collective-permute-start.30 = (f32[3,2,128,64]{2,3,0,1:T(8,128)S(1)}, f32[3,2,128,64]{2,3,0,1:T(8,128)S(1)}, u32[]{:S(2)}, u32[]{:S(2)}) collective-permute-start(f32[3,2,128,64]{2,3,0,1:T(8,128)S(1)} %add.534), channel_id=1, source_target_pairs={{0,2},{1,3},{2,0},{3,1},{4,6},{5,7},{6,4},{7,5},{8,10},{9,11},{10,... | collective-permute-start | bytes 589832 | tf_op jit(solution)/shard_map/ppermute | solution.py:166
  232.4 4.7 %collective-permute-start.32 = (bf16[3,2,128,64]{2,3,0,1:T(8,128)(2,1)S(1)}, bf16[3,2,128,64]{2,3,0,1:T(8,128)(2,1)S(1)}, u32[]{:S(2)}, u32[]{:S(2)}) collective-permute-start(bf16[3,2,128,64]{2,3,0,1:T(8,128)(2,1)S(1)} %add.536), channel_id=1, source_target_pairs={{0,8},{4,12},{8,0},{12,4},{16,24},{20,28},{24,16},{28,20},{1,9},{5... | collective-permute-start | bytes 294920 | tf_op jit(solution)/shard_map/ppermute | solution.py:166
  237.1 6.8 %collective-permute-start.33 = (bf16[3,2,128,64]{2,3,0,1:T(8,128)(2,1)S(1)}, bf16[3,2,128,64]{2,3,0,1:T(8,128)(2,1)S(1)}, u32[]{:S(2)}, u32[]{:S(2)}) collective-permute-start(bf16[3,2,128,64]{2,3,0,1:T(8,128)(2,1)S(1)} %add.537), channel_id=1, source_target_pairs={{0,16},{4,20},{8,24},{12,28},{16,0},{20,4},{24,8},{28,12},{1,17},{... | collective-permute-start | bytes 294920 | tf_op jit(solution)/shard_map/ppermute | solution.py:166
  251.6 6.4 %collective-permute-start.39 = (bf16[1,1,64,1024]{3,2,1,0:T(8,128)(2,1)S(1)}, bf16[1,1,64,1024]{3,2,1,0:T(8,128)(2,1)S(1)}, u32[]{:S(2)}, u32[]{:S(2)}) collective-permute-start(bf16[1,1,64,1024]{3,2,1,0:T(8,128)(2,1)S(1)} %dynamic-slice_convert_fusion), channel_id=1, source_target_pairs={{0,2},{1,3},{2,0},{3,1},{4,6},{5,7},{6,4},{7,5},{8,10},{9,11},{10,... | collective-permute-start | bytes 393224 | tf_op jit(solution)/shard_map/ppermute | solution.py:191
  253.2 7.6 %collective-permute-start.37 = (bf16[1,1,64,1024]{3,2,1,0:T(8,128)(2,1)S(1)}, bf16[1,1,64,1024]{3,2,1,0:T(8,128)(2,1)S(1)}, u32[]{:S(2)}, u32[]{:S(2)}) collective-permute-start(bf16[1,1,64,1024]{3,2,1,0:T(8,128)(2,1)S(1)} %dynamic-slice_convert_fusion.1), channel_id=1, source_target_pairs={{0,2},{1,3},{2,0},{3,1},{4,6},{5,7},{6,4},{7,5},{8,10},{9,11},{10,... | collective-permute-start | bytes 393224 | tf_op jit(solution)/shard_map/ppermute | solution.py:191
  254.0 8.8 %collective-permute-start.35 = (bf16[1,1,64,1024]{3,2,1,0:T(8,128)(2,1)S(1)}, bf16[1,1,64,1024]{3,2,1,0:T(8,128)(2,1)S(1)}, u32[]{:S(2)}, u32[]{:S(2)}) collective-permute-start(bf16[1,1,64,1024]{3,2,1,0:T(8,128)(2,1)S(1)} %dynamic-slice_convert_fusion.2), channel_id=1, source_target_pairs={{0,2},{1,3},{2,0},{3,1},{4,6},{5,7},{6,4},{7,5},{8,10},{9,11},{10,... | collective-permute-start | bytes 393224 | tf_op jit(solution)/shard_map/ppermute | solution.py:191
  (22 other events, 191.4 us)

commit v14 on v13

--- a/solution.py
+++ b/solution.py
@@ -312,8 +312,11 @@
     part_value = jnp.einsum(
         "tnd,de->tne", normed, value_weight, preferred_element_type=jnp.float32
     )
-    joined = jnp.concatenate([part_query, part_key, part_value], axis=-1)
-    summed = split_half_scatter_steps(joined, "gx", across_first).astype(jnp.bfloat16)
+    summed_kv = split_half_scatter_steps(
+        jnp.concatenate([part_key, part_value], axis=-1), "gx", across_first
+    )
+    summed_q = split_half_scatter_steps(part_query, "gx", across_first)
+    summed = jnp.concatenate([summed_q, summed_kv], axis=-1).astype(jnp.bfloat16)
     chunk_rows = summed.shape[1] // across_second
     spread = lax.all_to_all(
         summed.reshape(steps, across_second, chunk_rows, -1), "gy", 1, 2, tiled=False

time: 264 us -> 285 us (1.080)
  other arithmetic: 20.4 us -> 32 us
  starting transfers between devices: 57.9 us -> 64.5 us
  local copies, waits for them, and re-layouts: 21.3 us -> 25.1 us
  waiting for transfers between devices: 134 us -> 131 us
    ppermute x9 -> x18, starting transfers between devices: 11.8 us -> 20.3 us  [split_half_scatter(): lax.ppermute(outgoing, axis_name, [(i, i ^ offset) for i in range(axis_si...]
    ppermute x9 -> x18, waiting for transfers between devices: 36.7 us -> 28.4 us  [split_half_scatter(): lax.ppermute(outgoing, axis_name, [(i, i ^ offset) for i in range(axis_si...]
    ppermute x13, waiting for transfers between devices: 28 us -> 34.6 us  [tree_sum(): value = value + lax.ppermute(value, axis_name, pairs)]
    convert_element_type x9 -> x18, other arithmetic: 0.4 us -> 4.61 us  [split_half_scatter(): incoming = lax.ppermute(outgoing, axis_name, [(i, i ^ offset) for i in ra...]
    ppermute x13, starting transfers between devices: 19.3 us -> 15.2 us  [tree_sum(): value = value + lax.ppermute(value, axis_name, pairs)]
    ppermute x3 -> x6, starting transfers between devices: 4.51 us -> 7.9 us  [split_half_scatter(): lax.ppermute(mirror.astype(jnp.bfloat16), axis_name, [(i, i ^ half) for i...]
    another operation x9 -> x18, other arithmetic: 0.3 us -> 3.44 us  [split_half_scatter(): jnp.stack([lax.dynamic_index_in_dim(narrow, peer, axis=1, keepdims=False)...]
    ppermute x3 -> x6, waiting for transfers between devices: 7.68 us -> 6.57 us  [split_half_scatter(): lax.ppermute(mirror.astype(jnp.bfloat16), axis_name, [(i, i ^ half) for i...]
  transfers between devices with their start and end apart: 42 -> 54, of which waited for: 30 -> 31; matrix products, arithmetic and copies ran while one was open for 11% -> 15% of each run, Pallas kernels for 0% -> 0%
where the time goes in v14:
time: 285 us; the launch traced here: 284 us
  waiting for transfers between devices  131 us (46%)
  starting transfers between devices  64.5 us (23%)
  other arithmetic  32 us (11%)
  local copies, waits for them, and re-layouts  25.1 us (9%)
  matrix products  24.9 us (9%)
  between operations  5.97 us (2%)
    ppermute x13, waiting for transfers between devices, tree_sum(): value = value + lax.ppermute(value, axis_name, pairs)  34.6 us
    ppermute x18, waiting for transfers between devices, split_half_scatter(): lax.ppermute(outgoing, axis_name, [(i, i ^ offset) for i in range(axis_si...  28.4 us
    ppermute x18, starting transfers between devices, split_half_scatter(): lax.ppermute(outgoing, axis_name, [(i, i ^ offset) for i in range(axis_si...  20.3 us
    ppermute x13, starting transfers between devices, tree_sum(): value = value + lax.ppermute(value, axis_name, pairs)  15.2 us
    ppermute x3, waiting for transfers between devices, ring_gather(): backward = lax.ppermute(backward, axis_name, behind)  14.8 us
    ppermute x4, waiting for transfers between devices, ring_gather(): forward = lax.ppermute(forward, axis_name, ahead)  14.3 us
    ppermute x2, waiting for transfers between devices, doubling_gather(): lax.ppermute(held, axis_name, [(i, i ^ distance) for i in range(axis_size)])  10.9 us
    unnamed x43, local copies, waits for them, and re-layouts  8.68 us
  transfers between devices with their start and end apart: 54, of which 31 were waited for; matrix products, arithmetic and copies ran while one was open for 15% of the time, Pallas kernels for 0%

profile of v14, /device:TPU:0, one launch (start us, length us, event | category | flops | bytes accessed | tf_op | source)
XLA Modules:
  0.0 283.7 jit_solution(6988430373272654949)
XLA Ops:
  4.7 2.6 collective-permute-start.1
  14.7 10.9 %collective-permute-done.1 = bf16[3,128,1024]{2,1,0:T(8,128)(2,1)} collective-permute-done((bf16[3,128,1024]{2,1,0:T(8,128)(2,1)S(1)}, bf16[3,128,1024]{2,1,0:T(8,128)(2,1)}, u32[]{:S(2)}, u32[]{:S(2)}) %collective-permute-start.1) | collective-permute-done | bytes 786464 | tf_op jit(solution)/shard_map/ppermute | solution.py:129
  34.8 2.8 collective-permute-start.4
  45.9 2.5 collective-permute-start.32
  56.2 8.2 %fusion.8 = f32[3,256,2048]{2,1,0:T(8,128)} fusion(bf16[1024,2048]{1,0:T(8,128)(2,1)} %param.17, f32[1024]{0:T(1024)S(1)} %convert_element_type.318, f32[3,256]{1,0:T(4,128)S(1)} %add_rsqrt_fusion, bf16[3,128,1024]{2,1,0:T(8,128)(2,1)S(1)} %get-tuple-element.25, bf16[3,128,1024]{2,1,0:T(8,128)(2,1)S(1)} %get-tuple-element.24), kind=kOutput, calls=%fused_computation.10 | convolution fusion | flops 3226730496 | bytes 12065792 | tf_op jit(solution)/shard_map/tnd,de->tne/dot_general | solution.py:308
  66.7 2.6 collective-permute-start.24
  82.6 5.9 %collective-permute-done.6 = f32[3,2,128,64]{2,3,0,1:T(8,128)S(1)} collective-permute-done((f32[3,2,128,64]{2,3,0,1:T(8,128)S(1)}, f32[3,2,128,64]{2,3,0,1:T(8,128)S(1)}, u32[]{:S(2)}, u32[]{:S(2)}) %collective-permute-start.6) | collective-permute-done | bytes 196640 | tf_op jit(solution)/shard_map/ppermute | solution.py:166
  89.1 7.6 %collective-permute-done.7 = f32[3,2,128,64]{2,3,0,1:T(8,128)S(1)} collective-permute-done((f32[3,2,128,64]{2,3,0,1:T(8,128)S(1)}, f32[3,2,128,64]{2,3,0,1:T(8,128)S(1)}, u32[]{:S(2)}, u32[]{:S(2)}) %collective-permute-start.7) | collective-permute-done | bytes 196640 | tf_op jit(solution)/shard_map/ppermute | solution.py:166
  99.8 3.3 %collective-permute-done.9 = bf16[3,2,128,64]{2,3,0,1:T(8,128)(2,1)S(1)} collective-permute-done((bf16[3,2,128,64]{2,3,0,1:T(8,128)(2,1)S(1)}, bf16[3,2,128,64]{2,3,0,1:T(8,128)(2,1)S(1)}, u32[]{:S(2)}, u32[]{:S(2)}) %collective-permute-start.9) | collective-permute-done | bytes 98336 | tf_op jit(solution)/shard_map/ppermute | solution.py:166
  115.5 3.9 %collective-permute-done.20 = bf16[2,1,32,2048]{3,2,1,0:T(8,128)(2,1)S(1)} collective-permute-done((bf16[2,1,32,2048]{3,2,1,0:T(8,128)(2,1)S(1)}, bf16[2,1,32,2048]{3,2,1,0:T(8,128)(2,1)S(1)}, u32[]{:S(2)}, u32[]{:S(2)}) %collective-permute-start.20) | collective-permute-done | bytes 262176 | tf_op jit(solution)/shard_map/ppermute | solution.py:111
  120.0 4.1 %collective-permute-done.19 = bf16[2,1,32,2048]{3,2,1,0:T(8,128)(2,1)S(1)} collective-permute-done((bf16[2,1,32,2048]{3,2,1,0:T(8,128)(2,1)S(1)}, bf16[2,1,32,2048]{3,2,1,0:T(8,128)(2,1)S(1)}, u32[]{:S(2)}, u32[]{:S(2)}) %collective-permute-start.19) | collective-permute-done | bytes 262176 | tf_op jit(solution)/shard_map/ppermute | solution.py:111
  127.2 3.5 %collective-permute-done.16 = bf16[2,1,32,2048]{3,2,1,0:T(8,128)(2,1)S(1)} collective-permute-done((bf16[2,1,32,2048]{3,2,1,0:T(8,128)(2,1)S(1)}, bf16[2,1,32,2048]{3,2,1,0:T(8,128)(2,1)S(1)}, u32[]{:S(2)}, u32[]{:S(2)}) %collective-permute-start.16) | collective-permute-done | bytes 262176 | tf_op jit(solution)/shard_map/ppermute | solution.py:111
  131.3 4.0 %collective-permute-done.15 = bf16[2,1,32,2048]{3,2,1,0:T(8,128)(2,1)S(1)} collective-permute-done((bf16[2,1,32,2048]{3,2,1,0:T(8,128)(2,1)S(1)}, bf16[2,1,32,2048]{3,2,1,0:T(8,128)(2,1)S(1)}, u32[]{:S(2)}, u32[]{:S(2)}) %collective-permute-start.15) | collective-permute-done | bytes 262176 | tf_op jit(solution)/shard_map/ppermute | solution.py:111
  138.6 9.0 %collective-permute-done.12 = bf16[2,1,32,2048]{3,2,1,0:T(8,128)(2,1)S(1)} collective-permute-done((bf16[2,1,32,2048]{3,2,1,0:T(8,128)(2,1)S(1)}, bf16[2,1,32,2048]{3,2,1,0:T(8,128)(2,1)S(1)}, u32[]{:S(2)}, u32[]{:S(2)}) %collective-permute-start.12) | collective-permute-done | bytes 262176 | tf_op jit(solution)/shard_map/ppermute | solution.py:111
  147.6 3.0 %collective-permute-done.11 = bf16[2,1,32,2048]{3,2,1,0:T(8,128)(2,1)S(1)} collective-permute-done((bf16[2,1,32,2048]{3,2,1,0:T(8,128)(2,1)S(1)}, bf16[2,1,32,2048]{3,2,1,0:T(8,128)(2,1)S(1)}, u32[]{:S(2)}, u32[]{:S(2)}) %collective-permute-start.11) | collective-permute-done | bytes 262176 | tf_op jit(solution)/shard_map/ppermute | solution.py:111
  151.0 6.6 %collective-permute-done.13 = bf16[1,32,2048]{2,1,0:T(8,128)(2,1)S(1)} collective-permute-done((bf16[1,32,2048]{2,1,0:T(8,128)(2,1)S(1)}, bf16[1,32,2048]{2,1,0:T(8,128)(2,1)S(1)}, u32[]{:S(2)}, u32[]{:S(2)}) %collective-permute-start.13) | collective-permute-done | bytes 131104 | tf_op jit(solution)/shard_map/ppermute | solution.py:116
  158.6 3.7 %all-to-all-start = ((bf16[3,4,8,1,2560]{4,2,0,3,1:T(8,128)(2,1)}), bf16[3,4,8,1,2560]{4,2,0,3,1:T(8,128)(2,1)S(1)}, u32[]{:S(2)}, u32[]{:S(2)}) async-start(bf16[3,4,8,1,2560]{4,2,0,3,1:T(8,128)(2,1)} %copy.89), calls=%async_computation | async-start | bytes 983040 | tf_op jit(solution)/shard_map/all_to_all | solution.py:321
  162.6 8.0 %all-to-all-done = bf16[3,4,8,1,2560]{4,2,0,3,1:T(8,128)(2,1)S(1)} async-done(((bf16[3,4,8,1,2560]{4,2,0,3,1:T(8,128)(2,1)}), bf16[3,4,8,1,2560]{4,2,0,3,1:T(8,128)(2,1)S(1)}, u32[]{:S(2)}, u32[]{:S(2)}) %all-to-all-start) | async-done | bytes 491552 | tf_op jit(solution)/shard_map/all_to_all | solution.py:321
  172.3 4.6 %fusion.119 = (f32[8,8,24]{2,1,0:T(8,128)S(1)}, f32[8,8,24,256]{3,2,1,0:T(8,128)S(1)}) fusion(pred[8,256]{1,0:T(8,128)(4,1)S(1)} %iota_compare_fusion, bf16[8,256,1024]{2,1,0:T(8,128)(2,1)} %param.27, bf16[3,8,8,8,64]{4,3,2,1,0:T(8,128)(2,1)S(1)} %bitcast.253, bf16[3,8,8,8,64]{4,3,2,1,0:T(8,128)(2,1)S(1)} %bitcast.251), kind=kOutput, calls=%fused_computation.281 | convolution fusion | flops 102627840 | bytes 6168576 | tf_op jit(solution)/shard_map/rhqd,rchd->rhqc/dot_general | solution.py:217
  181.3 3.5 %all-to-all-start.1 = ((bf16[3,1,8,4,2048]{4,2,0,1,3:T(8,128)(2,1)}), bf16[3,1,8,4,2048]{4,2,0,1,3:T(8,128)(2,1)S(1)}, u32[]{:S(2)}, u32[]{:S(2)}) async-start(bf16[3,1,8,4,2048]{4,2,0,1,3:T(8,128)(2,1)} %copy.100), calls=%async_computation.1 | async-start | bytes 786432 | tf_op jit(solution)/shard_map/all_to_all | solution.py:347
  186.6 5.6 %all-to-all-done.1 = bf16[3,1,8,4,2048]{4,2,0,1,3:T(8,128)(2,1)S(1)} async-done(((bf16[3,1,8,4,2048]{4,2,0,1,3:T(8,128)(2,1)}), bf16[3,1,8,4,2048]{4,2,0,1,3:T(8,128)(2,1)S(1)}, u32[]{:S(2)}, u32[]{:S(2)}) %all-to-all-start.1) | async-done | bytes 393248 | tf_op jit(solution)/shard_map/all_to_all | solution.py:347
  195.1 7.8 %collective-permute-done.34 = bf16[3,32,2048]{2,1,0:T(8,128)(2,1)S(1)} collective-permute-done((bf16[3,32,2048]{2,1,0:T(8,128)(2,1)S(1)}, bf16[3,32,2048]{2,1,0:T(8,128)(2,1)S(1)}, u32[]{:S(2)}, u32[]{:S(2)}) %collective-permute-start.34) | collective-permute-done | bytes 393248 | tf_op jit(solution)/shard_map/ppermute | solution.py:82
  205.7 7.0 %collective-permute-done.35 = bf16[3,32,2048]{2,1,0:T(8,128)(2,1)S(1)} collective-permute-done((bf16[3,32,2048]{2,1,0:T(8,128)(2,1)S(1)}, bf16[3,32,2048]{2,1,0:T(8,128)(2,1)S(1)}, u32[]{:S(2)}, u32[]{:S(2)}) %collective-permute-start.35) | collective-permute-done | bytes 393248 | tf_op jit(solution)/shard_map/ppermute | solution.py:82
  215.5 7.9 %collective-permute-done.39 = bf16[3,32,2048]{2,1,0:T(8,128)(2,1)S(1)} collective-permute-done((bf16[3,32,2048]{2,1,0:T(8,128)(2,1)S(1)}, bf16[3,32,2048]{2,1,0:T(8,128)(2,1)S(1)}, u32[]{:S(2)}, u32[]{:S(2)}) %collective-permute-start.39) | collective-permute-done | bytes 393248 | tf_op jit(solution)/shard_map/ppermute | solution.py:79
  224.8 6.4 %collective-permute-done.40 = bf16[3,32,2048]{2,1,0:T(8,128)(2,1)S(1)} collective-permute-done((bf16[3,32,2048]{2,1,0:T(8,128)(2,1)S(1)}, bf16[3,32,2048]{2,1,0:T(8,128)(2,1)S(1)}, u32[]{:S(2)}, u32[]{:S(2)}) %collective-permute-start.40) | collective-permute-done | bytes 393248 | tf_op jit(solution)/shard_map/ppermute | solution.py:79
  234.3 2.6 gather_fusion
  242.1 5.8 %collective-permute-done.42 = f32[3,2,128,64]{2,3,0,1:T(8,128)S(1)} collective-permute-done((f32[3,2,128,64]{2,3,0,1:T(8,128)S(1)}, f32[3,2,128,64]{2,3,0,1:T(8,128)S(1)}, u32[]{:S(2)}, u32[]{:S(2)}) %collective-permute-start.42) | collective-permute-done | bytes 196640 | tf_op jit(solution)/shard_map/ppermute | solution.py:166
  248.9 3.8 %collective-permute-done.43 = bf16[3,2,128,64]{2,3,0,1:T(8,128)(2,1)S(1)} collective-permute-done((bf16[3,2,128,64]{2,3,0,1:T(8,128)(2,1)S(1)}, bf16[3,2,128,64]{2,3,0,1:T(8,128)(2,1)S(1)}, u32[]{:S(2)}, u32[]{:S(2)}) %collective-permute-start.43) | collective-permute-done | bytes 98336 | tf_op jit(solution)/shard_map/ppermute | solution.py:166
  254.3 3.0 %collective-permute-done.44 = bf16[3,2,128,64]{2,3,0,1:T(8,128)(2,1)S(1)} collective-permute-done((bf16[3,2,128,64]{2,3,0,1:T(8,128)(2,1)S(1)}, bf16[3,2,128,64]{2,3,0,1:T(8,128)(2,1)S(1)}, u32[]{:S(2)}, u32[]{:S(2)}) %collective-permute-start.44) | collective-permute-done | bytes 98336 | tf_op jit(solution)/shard_map/ppermute | solution.py:166
  257.9 5.2 %fusion.6 = f32[3,256,1024]{2,1,0:T(8,128)S(1)} fusion(bf16[3,256,2048]{2,1,0:T(8,128)(2,1)S(1)} %bitcast.239, bf16[2048,1024]{1,0:T(8,128)(2,1)} %param.20), kind=kOutput, calls=%fused_computation.8 | convolution fusion | flops 3221225472 | bytes 10485760 | tf_op jit(solution)/shard_map/tnq,qe->tne/dot_general | solution.py:362
  275.3 2.8 collective-permute-done.51
  278.1 2.8 collective-permute-done.49
  (273 shorter events, 116.8 us)
Async XLA Ops:
  4.7 20.9 %collective-permute-start.1 = (bf16[3,128,1024]{2,1,0:T(8,128)(2,1)S(1)}, bf16[3,128,1024]{2,1,0:T(8,128)(2,1)}, u32[]{:S(2)}, u32[]{:S(2)}) collective-permute-start(bf16[3,128,1024]{2,1,0:T(8,128)(2,1)S(1)} %pad_maximum_fusion), channel_id=1, source_target_pairs={{0,2},{1,3},{2,0},{3,1},{4,6},{5,7},{6,4},{7,5},{8,10},{9,11},{10,... | collective-permute-start | bytes 2359304 | tf_op jit(solution)/shard_map/ppermute | solution.py:129
  45.9 19.3 %collective-permute-start.32 = (bf16[2,1,32,512]{3,2,1,0:T(8,128)(2,1)}, bf16[2,1,32,512]{3,2,1,0:T(8,128)(2,1)}, u32[]{:S(2)}, u32[]{:S(2)}) collective-permute-start(bf16[2,1,32,512]{3,2,1,0:T(8,128)(2,1)} %pad_maximum_fusion.21), channel_id=1, source_target_pairs={{0,12},{4,8},{8,4},{12,0},{16,28},{20,24},{24,20},{28,16},{1,13},{... | collective-permute-start | bytes 196616 | tf_op jit(solution)/shard_map/ppermute | solution.py:111
  49.0 17.7 %collective-permute-start.31 = (bf16[2,1,32,512]{3,2,1,0:T(8,128)(2,1)}, bf16[2,1,32,512]{3,2,1,0:T(8,128)(2,1)}, u32[]{:S(2)}, u32[]{:S(2)}) collective-permute-start(bf16[2,1,32,512]{3,2,1,0:T(8,128)(2,1)} %pad_maximum_fusion.20), channel_id=1, source_target_pairs={{0,8},{4,12},{8,0},{12,4},{16,24},{20,28},{24,16},{28,20},{1,9},{5... | collective-permute-start | bytes 196616 | tf_op jit(solution)/shard_map/ppermute | solution.py:111
  50.1 20.0 %collective-permute-start.30 = (bf16[2,1,32,512]{3,2,1,0:T(8,128)(2,1)}, bf16[2,1,32,512]{3,2,1,0:T(8,128)(2,1)}, u32[]{:S(2)}, u32[]{:S(2)}) collective-permute-start(bf16[2,1,32,512]{3,2,1,0:T(8,128)(2,1)} %pad_maximum_fusion.19), channel_id=1, source_target_pairs={{0,4},{4,0},{8,12},{12,8},{16,20},{20,16},{24,28},{28,24},{1,5},{5... | collective-permute-start | bytes 196616 | tf_op jit(solution)/shard_map/ppermute | solution.py:111
  51.3 20.2 %collective-permute-start.28 = (bf16[2,1,32,512]{3,2,1,0:T(8,128)(2,1)}, bf16[2,1,32,512]{3,2,1,0:T(8,128)(2,1)}, u32[]{:S(2)}, u32[]{:S(2)}) collective-permute-start(bf16[2,1,32,512]{3,2,1,0:T(8,128)(2,1)} %pad_maximum_fusion.18), channel_id=1, source_target_pairs={{0,12},{4,8},{8,4},{12,0},{16,28},{20,24},{24,20},{28,16},{1,13},{... | collective-permute-start | bytes 196616 | tf_op jit(solution)/shard_map/ppermute | solution.py:111
  54.4 18.6 %collective-permute-start.27 = (bf16[2,1,32,512]{3,2,1,0:T(8,128)(2,1)}, bf16[2,1,32,512]{3,2,1,0:T(8,128)(2,1)}, u32[]{:S(2)}, u32[]{:S(2)}) collective-permute-start(bf16[2,1,32,512]{3,2,1,0:T(8,128)(2,1)} %pad_maximum_fusion.17), channel_id=1, source_target_pairs={{0,8},{4,12},{8,0},{12,4},{16,24},{20,28},{24,16},{28,20},{1,9},{5... | collective-permute-start | bytes 196616 | tf_op jit(solution)/shard_map/ppermute | solution.py:111
  65.2 10.2 %collective-permute-start.26 = (bf16[2,1,32,512]{3,2,1,0:T(8,128)(2,1)S(1)}, bf16[2,1,32,512]{3,2,1,0:T(8,128)(2,1)S(1)}, u32[]{:S(2)}, u32[]{:S(2)}) collective-permute-start(bf16[2,1,32,512]{3,2,1,0:T(8,128)(2,1)S(1)} %pad_maximum_fusion.16), channel_id=1, source_target_pairs={{0,4},{4,0},{8,12},{12,8},{16,20},{20,16},{24,28},{28,24},{1,5},{5... | collective-permute-start | bytes 196616 | tf_op jit(solution)/shard_map/ppermute | solution.py:111
  66.7 11.0 %collective-permute-start.24 = (bf16[2,1,32,512]{3,2,1,0:T(8,128)(2,1)S(1)}, bf16[2,1,32,512]{3,2,1,0:T(8,128)(2,1)S(1)}, u32[]{:S(2)}, u32[]{:S(2)}) collective-permute-start(bf16[2,1,32,512]{3,2,1,0:T(8,128)(2,1)S(1)} %pad_maximum_fusion.15), channel_id=1, source_target_pairs={{0,12},{4,8},{8,4},{12,0},{16,28},{20,24},{24,20},{28,16},{1,13},{... | collective-permute-start | bytes 196616 | tf_op jit(solution)/shard_map/ppermute | solution.py:111
  70.1 8.4 %collective-permute-start.23 = (bf16[2,1,32,512]{3,2,1,0:T(8,128)(2,1)S(1)}, bf16[2,1,32,512]{3,2,1,0:T(8,128)(2,1)S(1)}, u32[]{:S(2)}, u32[]{:S(2)}) collective-permute-start(bf16[2,1,32,512]{3,2,1,0:T(8,128)(2,1)S(1)} %pad_maximum_fusion.14), channel_id=1, source_target_pairs={{0,8},{4,12},{8,0},{12,4},{16,24},{20,28},{24,16},{28,20},{1,9},{5... | collective-permute-start | bytes 196616 | tf_op jit(solution)/shard_map/ppermute | solution.py:111
  77.7 11.4 %collective-permute-start.29 = (bf16[1,32,512]{2,1,0:T(8,128)(2,1)S(1)}, bf16[1,32,512]{2,1,0:T(8,128)(2,1)S(1)}, u32[]{:S(2)}, u32[]{:S(2)}) collective-permute-start(bf16[1,32,512]{2,1,0:T(8,128)(2,1)S(1)} %fusion.105), channel_id=1, source_target_pairs={{0,16},{4,20},{8,24},{12,28},{16,0},{20,4},{24,8},{28,12},{1,17},{... | collective-permute-start | bytes 98312 | tf_op jit(solution)/shard_map/ppermute | solution.py:116
  78.6 18.2 %collective-permute-start.25 = (bf16[1,32,512]{2,1,0:T(8,128)(2,1)S(1)}, bf16[1,32,512]{2,1,0:T(8,128)(2,1)S(1)}, u32[]{:S(2)}, u32[]{:S(2)}) collective-permute-start(bf16[1,32,512]{2,1,0:T(8,128)(2,1)S(1)} %fusion.104), channel_id=1, source_target_pairs={{0,16},{4,20},{8,24},{12,28},{16,0},{20,4},{24,8},{28,12},{1,17},{... | collective-permute-start | bytes 98312 | tf_op jit(solution)/shard_map/ppermute | solution.py:116
  88.5 8.2 %collective-permute-start.7 = (f32[3,2,128,64]{2,3,0,1:T(8,128)S(1)}, f32[3,2,128,64]{2,3,0,1:T(8,128)S(1)}, u32[]{:S(2)}, u32[]{:S(2)}) collective-permute-start(f32[3,2,128,64]{2,3,0,1:T(8,128)S(1)} %add.748), channel_id=1, source_target_pairs={{0,16},{4,20},{8,24},{12,28},{16,0},{20,4},{24,8},{28,12},{1,17},{... | collective-permute-start | bytes 589832 | tf_op jit(solution)/shard_map/ppermute | solution.py:166
  109.1 10.3 %collective-permute-start.20 = (bf16[2,1,32,2048]{3,2,1,0:T(8,128)(2,1)S(1)}, bf16[2,1,32,2048]{3,2,1,0:T(8,128)(2,1)S(1)}, u32[]{:S(2)}, u32[]{:S(2)}) collective-permute-start(bf16[2,1,32,2048]{3,2,1,0:T(8,128)(2,1)S(1)} %pad_maximum_fusion.12), channel_id=1, source_target_pairs={{0,12},{4,8},{8,4},{12,0},{16,28},{20,24},{24,20},{28,16},{1,13},{... | collective-permute-start | bytes 786440 | tf_op jit(solution)/shard_map/ppermute | solution.py:111
  109.2 14.9 %collective-permute-start.19 = (bf16[2,1,32,2048]{3,2,1,0:T(8,128)(2,1)S(1)}, bf16[2,1,32,2048]{3,2,1,0:T(8,128)(2,1)S(1)}, u32[]{:S(2)}, u32[]{:S(2)}) collective-permute-start(bf16[2,1,32,2048]{3,2,1,0:T(8,128)(2,1)S(1)} %pad_maximum_fusion.11), channel_id=1, source_target_pairs={{0,8},{4,12},{8,0},{12,4},{16,24},{20,28},{24,16},{28,20},{1,9},{5... | collective-permute-start | bytes 786440 | tf_op jit(solution)/shard_map/ppermute | solution.py:111
  111.4 13.7 %collective-permute-start.18 = (bf16[2,1,32,2048]{3,2,1,0:T(8,128)(2,1)S(1)}, bf16[2,1,32,2048]{3,2,1,0:T(8,128)(2,1)S(1)}, u32[]{:S(2)}, u32[]{:S(2)}) collective-permute-start(bf16[2,1,32,2048]{3,2,1,0:T(8,128)(2,1)S(1)} %pad_maximum_fusion.10), channel_id=1, source_target_pairs={{0,4},{4,0},{8,12},{12,8},{16,20},{20,16},{24,28},{28,24},{1,5},{5... | collective-permute-start | bytes 786440 | tf_op jit(solution)/shard_map/ppermute | solution.py:111
  112.9 17.8 %collective-permute-start.16 = (bf16[2,1,32,2048]{3,2,1,0:T(8,128)(2,1)S(1)}, bf16[2,1,32,2048]{3,2,1,0:T(8,128)(2,1)S(1)}, u32[]{:S(2)}, u32[]{:S(2)}) collective-permute-start(bf16[2,1,32,2048]{3,2,1,0:T(8,128)(2,1)S(1)} %pad_maximum_fusion.9), channel_id=1, source_target_pairs={{0,12},{4,8},{8,4},{12,0},{16,28},{20,24},{24,20},{28,16},{1,13},{... | collective-permute-start | bytes 786440 | tf_op jit(solution)/shard_map/ppermute | solution.py:111
  113.0 22.4 %collective-permute-start.15 = (bf16[2,1,32,2048]{3,2,1,0:T(8,128)(2,1)S(1)}, bf16[2,1,32,2048]{3,2,1,0:T(8,128)(2,1)S(1)}, u32[]{:S(2)}, u32[]{:S(2)}) collective-permute-start(bf16[2,1,32,2048]{3,2,1,0:T(8,128)(2,1)S(1)} %pad_maximum_fusion.8), channel_id=1, source_target_pairs={{0,8},{4,12},{8,0},{12,4},{16,24},{20,28},{24,16},{28,20},{1,9},{5... | collective-permute-start | bytes 786440 | tf_op jit(solution)/shard_map/ppermute | solution.py:111
  119.4 16.9 %collective-permute-start.14 = (bf16[2,1,32,2048]{3,2,1,0:T(8,128)(2,1)S(1)}, bf16[2,1,32,2048]{3,2,1,0:T(8,128)(2,1)S(1)}, u32[]{:S(2)}, u32[]{:S(2)}) collective-permute-start(bf16[2,1,32,2048]{3,2,1,0:T(8,128)(2,1)S(1)} %pad_maximum_fusion.7), channel_id=1, source_target_pairs={{0,4},{4,0},{8,12},{12,8},{16,20},{20,16},{24,28},{28,24},{1,5},{5... | collective-permute-start | bytes 786440 | tf_op jit(solution)/shard_map/ppermute | solution.py:111
  124.1 23.4 %collective-permute-start.12 = (bf16[2,1,32,2048]{3,2,1,0:T(8,128)(2,1)S(1)}, bf16[2,1,32,2048]{3,2,1,0:T(8,128)(2,1)S(1)}, u32[]{:S(2)}, u32[]{:S(2)}) collective-permute-start(bf16[2,1,32,2048]{3,2,1,0:T(8,128)(2,1)S(1)} %pad_maximum_fusion.6), channel_id=1, source_target_pairs={{0,12},{4,8},{8,4},{12,0},{16,28},{20,24},{24,20},{28,16},{1,13},{... | collective-permute-start | bytes 786440 | tf_op jit(solution)/shard_map/ppermute | solution.py:111
  125.0 25.6 %collective-permute-start.11 = (bf16[2,1,32,2048]{3,2,1,0:T(8,128)(2,1)S(1)}, bf16[2,1,32,2048]{3,2,1,0:T(8,128)(2,1)S(1)}, u32[]{:S(2)}, u32[]{:S(2)}) collective-permute-start(bf16[2,1,32,2048]{3,2,1,0:T(8,128)(2,1)S(1)} %pad_maximum_fusion.5), channel_id=1, source_target_pairs={{0,8},{4,12},{8,0},{12,4},{16,24},{20,28},{24,16},{28,20},{1,9},{5... | collective-permute-start | bytes 786440 | tf_op jit(solution)/shard_map/ppermute | solution.py:111
  130.6 20.0 %collective-permute-start.10 = (bf16[2,1,32,2048]{3,2,1,0:T(8,128)(2,1)S(1)}, bf16[2,1,32,2048]{3,2,1,0:T(8,128)(2,1)S(1)}, u32[]{:S(2)}, u32[]{:S(2)}) collective-permute-start(bf16[2,1,32,2048]{3,2,1,0:T(8,128)(2,1)S(1)} %pad_maximum_fusion.4), channel_id=1, source_target_pairs={{0,4},{4,0},{8,12},{12,8},{16,20},{20,16},{24,28},{28,24},{1,5},{5... | collective-permute-start | bytes 786440 | tf_op jit(solution)/shard_map/ppermute | solution.py:111
  135.4 15.4 %collective-permute-start.21 = (bf16[1,32,2048]{2,1,0:T(8,128)(2,1)S(1)}, bf16[1,32,2048]{2,1,0:T(8,128)(2,1)S(1)}, u32[]{:S(2)}, u32[]{:S(2)}) collective-permute-start(bf16[1,32,2048]{2,1,0:T(8,128)(2,1)S(1)} %fusion.78), channel_id=1, source_target_pairs={{0,16},{4,20},{8,24},{12,28},{16,0},{20,4},{24,8},{28,12},{1,17},{... | collective-permute-start | bytes 393224 | tf_op jit(solution)/shard_map/ppermute | solution.py:116
  136.4 14.6 %collective-permute-start.17 = (bf16[1,32,2048]{2,1,0:T(8,128)(2,1)S(1)}, bf16[1,32,2048]{2,1,0:T(8,128)(2,1)S(1)}, u32[]{:S(2)}, u32[]{:S(2)}) collective-permute-start(bf16[1,32,2048]{2,1,0:T(8,128)(2,1)S(1)} %fusion.77), channel_id=1, source_target_pairs={{0,16},{4,20},{8,24},{12,28},{16,0},{20,4},{24,8},{28,12},{1,17},{... | collective-permute-start | bytes 393224 | tf_op jit(solution)/shard_map/ppermute | solution.py:116
  158.6 11.9 %all-to-all-start = ((bf16[3,4,8,1,2560]{4,2,0,3,1:T(8,128)(2,1)}), bf16[3,4,8,1,2560]{4,2,0,3,1:T(8,128)(2,1)S(1)}, u32[]{:S(2)}, u32[]{:S(2)}) async-start(bf16[3,4,8,1,2560]{4,2,0,3,1:T(8,128)(2,1)} %copy.89), calls=%async_computation | async-start | bytes 983040 | tf_op jit(solution)/shard_map/all_to_all | solution.py:321
  181.3 10.9 %all-to-all-start.1 = ((bf16[3,1,8,4,2048]{4,2,0,1,3:T(8,128)(2,1)}), bf16[3,1,8,4,2048]{4,2,0,1,3:T(8,128)(2,1)S(1)}, u32[]{:S(2)}, u32[]{:S(2)}) async-start(bf16[3,1,8,4,2048]{4,2,0,1,3:T(8,128)(2,1)} %copy.100), calls=%async_computation.1 | async-start | bytes 786432 | tf_op jit(solution)/shard_map/all_to_all | solution.py:347
  192.2 10.7 %collective-permute-start.34 = (bf16[3,32,2048]{2,1,0:T(8,128)(2,1)S(1)}, bf16[3,32,2048]{2,1,0:T(8,128)(2,1)S(1)}, u32[]{:S(2)}, u32[]{:S(2)}) collective-permute-start(bf16[3,32,2048]{2,1,0:T(8,128)(2,1)S(1)} %bitcast.256), channel_id=1, source_target_pairs={{0,4},{8,0},{16,8},{24,16},{28,24},{20,28},{12,20},{4,12},{1,5},{9... | collective-permute-start | bytes 1179656 | tf_op jit(solution)/shard_map/ppermute | solution.py:82
  193.7 10.7 %collective-permute-start.37 = (bf16[3,32,2048]{2,1,0:T(8,128)(2,1)S(1)}, bf16[3,32,2048]{2,1,0:T(8,128)(2,1)S(1)}, u32[]{:S(2)}, u32[]{:S(2)}) collective-permute-start(bf16[3,32,2048]{2,1,0:T(8,128)(2,1)S(1)} %bitcast.257), channel_id=1, source_target_pairs={{0,8},{8,16},{16,24},{24,28},{28,20},{20,12},{12,4},{4,0},{1,9},{9... | collective-permute-start | bytes 1179656 | tf_op jit(solution)/shard_map/ppermute | solution.py:79
  202.9 9.8 %collective-permute-start.35 = (bf16[3,32,2048]{2,1,0:T(8,128)(2,1)S(1)}, bf16[3,32,2048]{2,1,0:T(8,128)(2,1)S(1)}, u32[]{:S(2)}, u32[]{:S(2)}) collective-permute-start(bf16[3,32,2048]{2,1,0:T(8,128)(2,1)S(1)} %collective-permute-done.34), channel_id=1, source_target_pairs={{0,4},{8,0},{16,8},{24,16},{28,24},{20,28},{12,20},{4,12},{1,5},{9... | collective-permute-start | bytes 1179656 | tf_op jit(solution)/shard_map/ppermute | solution.py:82
  204.3 9.8 %collective-permute-start.38 = (bf16[3,32,2048]{2,1,0:T(8,128)(2,1)S(1)}, bf16[3,32,2048]{2,1,0:T(8,128)(2,1)S(1)}, u32[]{:S(2)}, u32[]{:S(2)}) collective-permute-start(bf16[3,32,2048]{2,1,0:T(8,128)(2,1)S(1)} %collective-permute-done.37), channel_id=1, source_target_pairs={{0,8},{8,16},{16,24},{24,28},{28,20},{20,12},{12,4},{4,0},{1,9},{9... | collective-permute-start | bytes 1179656 | tf_op jit(solution)/shard_map/ppermute | solution.py:79
  212.7 11.3 %collective-permute-start.36 = (bf16[3,32,2048]{2,1,0:T(8,128)(2,1)S(1)}, bf16[3,32,2048]{2,1,0:T(8,128)(2,1)S(1)}, u32[]{:S(2)}, u32[]{:S(2)}) collective-permute-start(bf16[3,32,2048]{2,1,0:T(8,128)(2,1)S(1)} %collective-permute-done.35), channel_id=1, source_target_pairs={{0,4},{8,0},{16,8},{24,16},{28,24},{20,28},{12,20},{4,12},{1,5},{9... | collective-permute-start | bytes 1179656 | tf_op jit(solution)/shard_map/ppermute | solution.py:82
  214.1 9.3 %collective-permute-start.39 = (bf16[3,32,2048]{2,1,0:T(8,128)(2,1)S(1)}, bf16[3,32,2048]{2,1,0:T(8,128)(2,1)S(1)}, u32[]{:S(2)}, u32[]{:S(2)}) collective-permute-start(bf16[3,32,2048]{2,1,0:T(8,128)(2,1)S(1)} %collective-permute-done.38), channel_id=1, source_target_pairs={{0,8},{8,16},{16,24},{24,28},{28,20},{20,12},{12,4},{4,0},{1,9},{9... | collective-permute-start | bytes 1179656 | tf_op jit(solution)/shard_map/ppermute | solution.py:79
  274.1 8.8 %collective-permute-start.47 = (bf16[1,1,64,1024]{3,2,1,0:T(8,128)(2,1)S(1)}, bf16[1,1,64,1024]{3,2,1,0:T(8,128)(2,1)S(1)}, u32[]{:S(2)}, u32[]{:S(2)}) collective-permute-start(bf16[1,1,64,1024]{3,2,1,0:T(8,128)(2,1)S(1)} %dynamic-slice_convert_fusion.2), channel_id=1, source_target_pairs={{0,2},{1,3},{2,0},{3,1},{4,6},{5,7},{6,4},{7,5},{8,10},{9,11},{10,... | collective-permute-start | bytes 393224 | tf_op jit(solution)/shard_map/ppermute | solution.py:191
  (40 other events, 307.4 us)

commit v15 on v13

--- a/solution.py
+++ b/solution.py
@@ -290,9 +290,11 @@
     output_first = pick_adapters(output_down, block_adapter, index_first)
     output_second = pick_adapters(output_up, block_adapter, index_second)
 
+    own_wide = inputs.astype(jnp.float32)
+    own_squares = tree_sum(jnp.sum(own_wide * own_wide, axis=2), ("gx",))
+    squares = doubling_gather(own_squares, "gy", across_second, 1)
     rows_all = doubling_gather(inputs, "gy", across_second, 1)
     rows_wide = rows_all.astype(jnp.float32)
-    squares = tree_sum(jnp.sum(rows_wide * rows_wide, axis=2), ("gx",))
     factor_rows = lax.rsqrt(squares / width + EPS)
     normed = (rows_wide * factor_rows[..., None] * norm_scale).astype(jnp.bfloat16)
 

time: 264 us -> 266 us (level)
  starting transfers between devices: 57.9 us -> 46.4 us
  waiting for transfers between devices: 134 us -> 141 us
  other arithmetic: 20.4 us -> 25.3 us
    ppermute x13, starting transfers between devices: 19.3 us -> 14.3 us  [tree_sum(): value = value + lax.ppermute(value, axis_name, pairs)]
    ppermute x13, waiting for transfers between devices: 28 us -> 31.4 us  [tree_sum(): value = value + lax.ppermute(value, axis_name, pairs)]
    ppermute x2 -> x4, waiting for transfers between devices: 12.2 us -> 11.3 us  [doubling_gather(): lax.ppermute(held, axis_name, [(i, i ^ distance) for i in range(axis_size)])]
    unnamed x31 -> x29, local copies, waits for them, and re-layouts: 8.42 us -> 8.94 us
  transfers between devices with their start and end apart: 42 -> 44, of which waited for: 30 -> 31; matrix products, arithmetic and copies ran while one was open for 11% -> 14% of each run, Pallas kernels for 0% -> 0%
where the time goes in v15:
time: 266 us; the launch traced here: 265 us
  waiting for transfers between devices  141 us (53%)
  starting transfers between devices  46.4 us (17%)
  other arithmetic  25.3 us (10%)
  matrix products  24 us (9%)
  local copies, waits for them, and re-layouts  23.2 us (9%)
  between operations  5.79 us (2%)
    ppermute x9, waiting for transfers between devices, split_half_scatter(): lax.ppermute(outgoing, axis_name, [(i, i ^ offset) for i in range(axis_si...  39.1 us
    ppermute x13, waiting for transfers between devices, tree_sum(): value = value + lax.ppermute(value, axis_name, pairs)  31.4 us
    ppermute x3, waiting for transfers between devices, ring_gather(): backward = lax.ppermute(backward, axis_name, behind)  14.8 us
    ppermute x4, waiting for transfers between devices, ring_gather(): forward = lax.ppermute(forward, axis_name, ahead)  14.3 us
    ppermute x13, starting transfers between devices, tree_sum(): value = value + lax.ppermute(value, axis_name, pairs)  14.3 us
    ppermute x4, waiting for transfers between devices, doubling_gather(): lax.ppermute(held, axis_name, [(i, i ^ distance) for i in range(axis_size)])  11.3 us
    ppermute x9, starting transfers between devices, split_half_scatter(): lax.ppermute(outgoing, axis_name, [(i, i ^ offset) for i in range(axis_si...  9.46 us
    unnamed x29, local copies, waits for them, and re-layouts  8.94 us
  transfers between devices with their start and end apart: 44, of which 31 were waited for; matrix products, arithmetic and copies ran while one was open for 14% of the time, Pallas kernels for 0%

profile of v15, /device:TPU:0, one launch (start us, length us, event | category | flops | bytes accessed | tf_op | source)
XLA Modules:
  0.0 265.3 jit_solution(10949693752481102427)
XLA Ops:
  1.6 2.6 collective-permute-start.2
  17.2 2.6 collective-permute-start.4
  29.3 10.0 %collective-permute-done.6 = f32[3,128]{1,0:T(4,128)} collective-permute-done((f32[3,128]{1,0:T(4,128)}, f32[3,128]{1,0:T(4,128)}, u32[]{:S(2)}, u32[]{:S(2)}) %collective-permute-start.6) | collective-permute-done | bytes 1568 | tf_op jit(solution)/shard_map/ppermute | solution.py:129
  43.3 4.5 %collective-permute-done.7 = f32[3,2,128,64]{2,3,0,1:T(8,128)S(1)} collective-permute-done((f32[3,2,128,64]{2,3,0,1:T(8,128)S(1)}, f32[3,2,128,64]{2,3,0,1:T(8,128)S(1)}, u32[]{:S(2)}, u32[]{:S(2)}) %collective-permute-start.7) | collective-permute-done | bytes 196640 | tf_op jit(solution)/shard_map/ppermute | solution.py:166
  49.5 5.1 %collective-permute-done.8 = f32[3,2,128,64]{2,3,0,1:T(8,128)S(1)} collective-permute-done((f32[3,2,128,64]{2,3,0,1:T(8,128)S(1)}, f32[3,2,128,64]{2,3,0,1:T(8,128)S(1)}, u32[]{:S(2)}, u32[]{:S(2)}) %collective-permute-start.8) | collective-permute-done | bytes 196640 | tf_op jit(solution)/shard_map/ppermute | solution.py:166
  54.7 5.8 %fusion.8 = f32[3,256,2048]{2,1,0:T(8,128)} fusion(bf16[1024,2048]{1,0:T(8,128)(2,1)S(1)} %copy-done.6, f32[1024]{0:T(1024)S(1)} %convert_element_type.211, f32[3,256]{1,0:T(4,128)S(1)} %fusion.94, bf16[3,128,1024]{2,1,0:T(8,128)(2,1)S(1)} %get-tuple-element.22, bf16[3,128,1024]{2,1,0:T(8,128)(2,1)S(1)} %get-tuple-element.21), kind=kOutput, calls=%fused_computation.11 | convolution fusion | flops 3226730496 | bytes 12065792 | tf_op jit(solution)/shard_map/tnd,de->tne/dot_general | solution.py:310
  60.5 2.9 %collective-permute-done.9 = f32[3,2,128,64]{2,3,0,1:T(8,128)S(1)} collective-permute-done((f32[3,2,128,64]{2,3,0,1:T(8,128)S(1)}, f32[3,2,128,64]{2,3,0,1:T(8,128)S(1)}, u32[]{:S(2)}, u32[]{:S(2)}) %collective-permute-start.9) | collective-permute-done | bytes 196640 | tf_op jit(solution)/shard_map/ppermute | solution.py:166
  75.4 2.5 pad_maximum_fusion
  85.3 5.3 %collective-permute-done.22 = bf16[2,1,32,2560]{3,2,1,0:T(8,128)(2,1)S(1)} collective-permute-done((bf16[2,1,32,2560]{3,2,1,0:T(8,128)(2,1)S(1)}, bf16[2,1,32,2560]{3,2,1,0:T(8,128)(2,1)S(1)}, u32[]{:S(2)}, u32[]{:S(2)}) %collective-permute-start.22) | collective-permute-done | bytes 327712 | tf_op jit(solution)/shard_map/ppermute | solution.py:111
  91.1 5.5 %collective-permute-done.21 = bf16[2,1,32,2560]{3,2,1,0:T(8,128)(2,1)S(1)} collective-permute-done((bf16[2,1,32,2560]{3,2,1,0:T(8,128)(2,1)S(1)}, bf16[2,1,32,2560]{3,2,1,0:T(8,128)(2,1)S(1)}, u32[]{:S(2)}, u32[]{:S(2)}) %collective-permute-start.21) | collective-permute-done | bytes 327712 | tf_op jit(solution)/shard_map/ppermute | solution.py:111
  99.8 4.8 %collective-permute-done.18 = bf16[2,1,32,2560]{3,2,1,0:T(8,128)(2,1)S(1)} collective-permute-done((bf16[2,1,32,2560]{3,2,1,0:T(8,128)(2,1)S(1)}, bf16[2,1,32,2560]{3,2,1,0:T(8,128)(2,1)S(1)}, u32[]{:S(2)}, u32[]{:S(2)}) %collective-permute-start.18) | collective-permute-done | bytes 327712 | tf_op jit(solution)/shard_map/ppermute | solution.py:111
  105.2 5.5 %collective-permute-done.17 = bf16[2,1,32,2560]{3,2,1,0:T(8,128)(2,1)S(1)} collective-permute-done((bf16[2,1,32,2560]{3,2,1,0:T(8,128)(2,1)S(1)}, bf16[2,1,32,2560]{3,2,1,0:T(8,128)(2,1)S(1)}, u32[]{:S(2)}, u32[]{:S(2)}) %collective-permute-start.17) | collective-permute-done | bytes 327712 | tf_op jit(solution)/shard_map/ppermute | solution.py:111
  111.8 2.1 collective-permute-start.19
  113.9 11.8 %collective-permute-done.14 = bf16[2,1,32,2560]{3,2,1,0:T(8,128)(2,1)S(1)} collective-permute-done((bf16[2,1,32,2560]{3,2,1,0:T(8,128)(2,1)S(1)}, bf16[2,1,32,2560]{3,2,1,0:T(8,128)(2,1)S(1)}, u32[]{:S(2)}, u32[]{:S(2)}) %collective-permute-start.14) | collective-permute-done | bytes 327712 | tf_op jit(solution)/shard_map/ppermute | solution.py:111
  125.8 4.8 %collective-permute-done.13 = bf16[2,1,32,2560]{3,2,1,0:T(8,128)(2,1)S(1)} collective-permute-done((bf16[2,1,32,2560]{3,2,1,0:T(8,128)(2,1)S(1)}, bf16[2,1,32,2560]{3,2,1,0:T(8,128)(2,1)S(1)}, u32[]{:S(2)}, u32[]{:S(2)}) %collective-permute-start.13) | collective-permute-done | bytes 327712 | tf_op jit(solution)/shard_map/ppermute | solution.py:111
  131.1 8.1 %collective-permute-done.15 = bf16[1,32,2560]{2,1,0:T(8,128)(2,1)S(1)} collective-permute-done((bf16[1,32,2560]{2,1,0:T(8,128)(2,1)S(1)}, bf16[1,32,2560]{2,1,0:T(8,128)(2,1)S(1)}, u32[]{:S(2)}, u32[]{:S(2)}) %collective-permute-start.15) | collective-permute-done | bytes 163872 | tf_op jit(solution)/shard_map/ppermute | solution.py:116
  140.1 3.7 %all-to-all-start = ((bf16[3,4,8,1,2560]{4,2,3,0,1:T(8,128)(2,1)}), bf16[3,4,8,1,2560]{4,2,3,0,1:T(8,128)(2,1)S(1)}, u32[]{:S(2)}, u32[]{:S(2)}) async-start(bf16[3,4,8,1,2560]{4,2,3,0,1:T(8,128)(2,1)} %copy.75), calls=%async_computation | async-start | bytes 983040 | tf_op jit(solution)/shard_map/all_to_all | solution.py:320
  144.1 8.0 %all-to-all-done = bf16[3,4,8,1,2560]{4,2,3,0,1:T(8,128)(2,1)S(1)} async-done(((bf16[3,4,8,1,2560]{4,2,3,0,1:T(8,128)(2,1)}), bf16[3,4,8,1,2560]{4,2,3,0,1:T(8,128)(2,1)S(1)}, u32[]{:S(2)}, u32[]{:S(2)}) %all-to-all-start) | async-done | bytes 491552 | tf_op jit(solution)/shard_map/all_to_all | solution.py:320
  153.8 4.6 %fusion.110 = (f32[8,8,24]{2,1,0:T(8,128)S(1)}, f32[8,8,24,256]{3,2,1,0:T(8,128)S(1)}) fusion(pred[8,256]{1,0:T(8,128)(4,1)S(1)} %iota_compare_fusion, bf16[8,256,1024]{2,1,0:T(8,128)(2,1)} %param.27, bf16[3,8,8,8,64]{4,3,2,1,0:T(8,128)(2,1)S(1)} %bitcast.228, bf16[3,8,8,8,64]{4,3,2,1,0:T(8,128)(2,1)S(1)} %bitcast.226), kind=kOutput, calls=%fused_computation.227 | convolution fusion | flops 102627840 | bytes 6168576 | tf_op jit(solution)/shard_map/rhqd,rchd->rhqc/dot_general | solution.py:217
  162.8 3.5 %all-to-all-start.1 = ((bf16[3,1,8,4,2048]{4,2,0,1,3:T(8,128)(2,1)}), bf16[3,1,8,4,2048]{4,2,0,1,3:T(8,128)(2,1)S(1)}, u32[]{:S(2)}, u32[]{:S(2)}) async-start(bf16[3,1,8,4,2048]{4,2,0,1,3:T(8,128)(2,1)} %copy.86), calls=%async_computation.1 | async-start | bytes 786432 | tf_op jit(solution)/shard_map/all_to_all | solution.py:346
  168.1 5.6 %all-to-all-done.1 = bf16[3,1,8,4,2048]{4,2,0,1,3:T(8,128)(2,1)S(1)} async-done(((bf16[3,1,8,4,2048]{4,2,0,1,3:T(8,128)(2,1)}), bf16[3,1,8,4,2048]{4,2,0,1,3:T(8,128)(2,1)S(1)}, u32[]{:S(2)}, u32[]{:S(2)}) %all-to-all-start.1) | async-done | bytes 393248 | tf_op jit(solution)/shard_map/all_to_all | solution.py:346
  176.6 7.8 %collective-permute-done.24 = bf16[3,32,2048]{2,1,0:T(8,128)(2,1)S(1)} collective-permute-done((bf16[3,32,2048]{2,1,0:T(8,128)(2,1)S(1)}, bf16[3,32,2048]{2,1,0:T(8,128)(2,1)S(1)}, u32[]{:S(2)}, u32[]{:S(2)}) %collective-permute-start.24) | collective-permute-done | bytes 393248 | tf_op jit(solution)/shard_map/ppermute | solution.py:82
  187.3 6.9 %collective-permute-done.25 = bf16[3,32,2048]{2,1,0:T(8,128)(2,1)S(1)} collective-permute-done((bf16[3,32,2048]{2,1,0:T(8,128)(2,1)S(1)}, bf16[3,32,2048]{2,1,0:T(8,128)(2,1)S(1)}, u32[]{:S(2)}, u32[]{:S(2)}) %collective-permute-start.25) | collective-permute-done | bytes 393248 | tf_op jit(solution)/shard_map/ppermute | solution.py:82
  197.0 7.9 %collective-permute-done.29 = bf16[3,32,2048]{2,1,0:T(8,128)(2,1)S(1)} collective-permute-done((bf16[3,32,2048]{2,1,0:T(8,128)(2,1)S(1)}, bf16[3,32,2048]{2,1,0:T(8,128)(2,1)S(1)}, u32[]{:S(2)}, u32[]{:S(2)}) %collective-permute-start.29) | collective-permute-done | bytes 393248 | tf_op jit(solution)/shard_map/ppermute | solution.py:79
  206.3 6.4 %collective-permute-done.30 = bf16[3,32,2048]{2,1,0:T(8,128)(2,1)S(1)} collective-permute-done((bf16[3,32,2048]{2,1,0:T(8,128)(2,1)S(1)}, bf16[3,32,2048]{2,1,0:T(8,128)(2,1)S(1)}, u32[]{:S(2)}, u32[]{:S(2)}) %collective-permute-start.30) | collective-permute-done | bytes 393248 | tf_op jit(solution)/shard_map/ppermute | solution.py:79
  215.8 2.6 gather_fusion
  223.7 5.8 %collective-permute-done.32 = f32[3,2,128,64]{2,3,0,1:T(8,128)S(1)} collective-permute-done((f32[3,2,128,64]{2,3,0,1:T(8,128)S(1)}, f32[3,2,128,64]{2,3,0,1:T(8,128)S(1)}, u32[]{:S(2)}, u32[]{:S(2)}) %collective-permute-start.32) | collective-permute-done | bytes 196640 | tf_op jit(solution)/shard_map/ppermute | solution.py:166
  230.4 3.8 %collective-permute-done.33 = bf16[3,2,128,64]{2,3,0,1:T(8,128)(2,1)S(1)} collective-permute-done((bf16[3,2,128,64]{2,3,0,1:T(8,128)(2,1)S(1)}, bf16[3,2,128,64]{2,3,0,1:T(8,128)(2,1)S(1)}, u32[]{:S(2)}, u32[]{:S(2)}) %collective-permute-start.33) | collective-permute-done | bytes 98336 | tf_op jit(solution)/shard_map/ppermute | solution.py:166
  235.8 3.0 %collective-permute-done.34 = bf16[3,2,128,64]{2,3,0,1:T(8,128)(2,1)S(1)} collective-permute-done((bf16[3,2,128,64]{2,3,0,1:T(8,128)(2,1)S(1)}, bf16[3,2,128,64]{2,3,0,1:T(8,128)(2,1)S(1)}, u32[]{:S(2)}, u32[]{:S(2)}) %collective-permute-start.34) | collective-permute-done | bytes 98336 | tf_op jit(solution)/shard_map/ppermute | solution.py:166
  239.5 5.2 %fusion.6 = f32[3,256,1024]{2,1,0:T(8,128)S(1)} fusion(bf16[3,256,2048]{2,1,0:T(8,128)(2,1)S(1)} %bitcast.223, bf16[2048,1024]{1,0:T(8,128)(2,1)} %param.20), kind=kOutput, calls=%fused_computation.9 | convolution fusion | flops 3221225472 | bytes 10485760 | tf_op jit(solution)/shard_map/tnq,qe->tne/dot_general | solution.py:361
  256.9 2.8 %collective-permute-done.41 = bf16[1,1,64,1024]{3,2,1,0:T(8,128)(2,1)S(1)} collective-permute-done((bf16[1,1,64,1024]{3,2,1,0:T(8,128)(2,1)S(1)}, bf16[1,1,64,1024]{3,2,1,0:T(8,128)(2,1)S(1)}, u32[]{:S(2)}, u32[]{:S(2)}) %collective-permute-start.41) | collective-permute-done | bytes 131104 | tf_op jit(solution)/shard_map/ppermute | solution.py:191
  259.7 2.8 %collective-permute-done.39 = bf16[1,1,64,1024]{3,2,1,0:T(8,128)(2,1)S(1)} collective-permute-done((bf16[1,1,64,1024]{3,2,1,0:T(8,128)(2,1)S(1)}, bf16[1,1,64,1024]{3,2,1,0:T(8,128)(2,1)S(1)}, u32[]{:S(2)}, u32[]{:S(2)}) %collective-permute-start.39) | collective-permute-done | bytes 131104 | tf_op jit(solution)/shard_map/ppermute | solution.py:191
  (210 shorter events, 95.2 us)
Async XLA Ops:
  0.0 19.8 %collective-permute-start = (bf16[3,64,1024]{2,1,0:T(8,128)(2,1)}, bf16[3,64,1024]{2,1,0:T(8,128)(2,1)S(1)}, u32[]{:S(2)}, u32[]{:S(2)}) collective-permute-start(bf16[3,64,1024]{2,1,0:T(8,128)(2,1)} %param.15), channel_id=1, source_target_pairs={{0,1},{1,0},{2,3},{3,2},{4,5},{5,4},{6,7},{7,6},{8,9},{9,8},{10,11... | collective-permute-start | bytes 1179656 | tf_op jit(solution)/shard_map/ppermute | solution.py:129
  1.6 11.9 %collective-permute-start.2 = (f32[3,64]{1,0:T(4,128)S(1)}, f32[3,64]{1,0:T(4,128)S(1)}, u32[]{:S(2)}, u32[]{:S(2)}) collective-permute-start(f32[3,64]{1,0:T(4,128)S(1)} %multiply_reduce_fusion), channel_id=1, source_target_pairs={{0,4},{4,0},{8,12},{12,8},{16,20},{20,16},{24,28},{28,24},{1,5},{5... | collective-permute-start | bytes 2312 | tf_op jit(solution)/shard_map/ppermute | solution.py:166
  17.2 7.0 %collective-permute-start.4 = (f32[3,64]{1,0:T(4,128)S(1)}, f32[3,64]{1,0:T(4,128)S(1)}, u32[]{:S(2)}, u32[]{:S(2)}) collective-permute-start(f32[3,64]{1,0:T(4,128)S(1)} %add.490), channel_id=1, source_target_pairs={{0,16},{4,20},{8,24},{12,28},{16,0},{20,4},{24,8},{28,12},{1,17},{... | collective-permute-start | bytes 2312 | tf_op jit(solution)/shard_map/ppermute | solution.py:166
  20.9 19.1 %collective-permute-start.1 = (bf16[3,128,1024]{2,1,0:T(8,128)(2,1)S(1)}, bf16[3,128,1024]{2,1,0:T(8,128)(2,1)S(1)}, u32[]{:S(2)}, u32[]{:S(2)}) collective-permute-start(bf16[3,128,1024]{2,1,0:T(8,128)(2,1)S(1)} %pad_maximum_fusion.1), channel_id=1, source_target_pairs={{0,2},{1,3},{2,0},{3,1},{4,6},{5,7},{6,4},{7,5},{8,10},{9,11},{10,... | collective-permute-start | bytes 2359304 | tf_op jit(solution)/shard_map/ppermute | solution.py:129
  26.8 12.5 %collective-permute-start.6 = (f32[3,128]{1,0:T(4,128)}, f32[3,128]{1,0:T(4,128)}, u32[]{:S(2)}, u32[]{:S(2)}) collective-permute-start(f32[3,128]{1,0:T(4,128)} %pad_maximum_fusion.13), channel_id=1, source_target_pairs={{0,2},{1,3},{2,0},{3,1},{4,6},{5,7},{6,4},{7,5},{8,10},{9,11},{10,... | collective-permute-start | bytes 4616 | tf_op jit(solution)/shard_map/ppermute | solution.py:129
  47.8 6.8 %collective-permute-start.8 = (f32[3,2,128,64]{2,3,0,1:T(8,128)S(1)}, f32[3,2,128,64]{2,3,0,1:T(8,128)S(1)}, u32[]{:S(2)}, u32[]{:S(2)}) collective-permute-start(f32[3,2,128,64]{2,3,0,1:T(8,128)S(1)} %add.504), channel_id=1, source_target_pairs={{0,8},{4,12},{8,0},{12,4},{16,24},{20,28},{24,16},{28,20},{1,9},{5... | collective-permute-start | bytes 589832 | tf_op jit(solution)/shard_map/ppermute | solution.py:166
  54.6 8.7 %collective-permute-start.9 = (f32[3,2,128,64]{2,3,0,1:T(8,128)S(1)}, f32[3,2,128,64]{2,3,0,1:T(8,128)S(1)}, u32[]{:S(2)}, u32[]{:S(2)}) collective-permute-start(f32[3,2,128,64]{2,3,0,1:T(8,128)S(1)} %add.505), channel_id=1, source_target_pairs={{0,16},{4,20},{8,24},{12,28},{16,0},{20,4},{24,8},{28,12},{1,17},{... | collective-permute-start | bytes 589832 | tf_op jit(solution)/shard_map/ppermute | solution.py:166
  78.9 11.6 %collective-permute-start.22 = (bf16[2,1,32,2560]{3,2,1,0:T(8,128)(2,1)S(1)}, bf16[2,1,32,2560]{3,2,1,0:T(8,128)(2,1)S(1)}, u32[]{:S(2)}, u32[]{:S(2)}) collective-permute-start(bf16[2,1,32,2560]{3,2,1,0:T(8,128)(2,1)S(1)} %pad_maximum_fusion.12), channel_id=1, source_target_pairs={{0,12},{4,8},{8,4},{12,0},{16,28},{20,24},{24,20},{28,16},{1,13},{... | collective-permute-start | bytes 983048 | tf_op jit(solution)/shard_map/ppermute | solution.py:111
  79.0 17.6 %collective-permute-start.21 = (bf16[2,1,32,2560]{3,2,1,0:T(8,128)(2,1)S(1)}, bf16[2,1,32,2560]{3,2,1,0:T(8,128)(2,1)S(1)}, u32[]{:S(2)}, u32[]{:S(2)}) collective-permute-start(bf16[2,1,32,2560]{3,2,1,0:T(8,128)(2,1)S(1)} %pad_maximum_fusion.11), channel_id=1, source_target_pairs={{0,8},{4,12},{8,0},{12,4},{16,24},{20,28},{24,16},{28,20},{1,9},{5... | collective-permute-start | bytes 983048 | tf_op jit(solution)/shard_map/ppermute | solution.py:111
  81.1 16.5 %collective-permute-start.20 = (bf16[2,1,32,2560]{3,2,1,0:T(8,128)(2,1)S(1)}, bf16[2,1,32,2560]{3,2,1,0:T(8,128)(2,1)S(1)}, u32[]{:S(2)}, u32[]{:S(2)}) collective-permute-start(bf16[2,1,32,2560]{3,2,1,0:T(8,128)(2,1)S(1)} %pad_maximum_fusion.10), channel_id=1, source_target_pairs={{0,4},{4,0},{8,12},{12,8},{16,20},{20,16},{24,28},{28,24},{1,5},{5... | collective-permute-start | bytes 983048 | tf_op jit(solution)/shard_map/ppermute | solution.py:111
  82.7 21.9 %collective-permute-start.18 = (bf16[2,1,32,2560]{3,2,1,0:T(8,128)(2,1)S(1)}, bf16[2,1,32,2560]{3,2,1,0:T(8,128)(2,1)S(1)}, u32[]{:S(2)}, u32[]{:S(2)}) collective-permute-start(bf16[2,1,32,2560]{3,2,1,0:T(8,128)(2,1)S(1)} %pad_maximum_fusion.9), channel_id=1, source_target_pairs={{0,12},{4,8},{8,4},{12,0},{16,28},{20,24},{24,20},{28,16},{1,13},{... | collective-permute-start | bytes 983048 | tf_op jit(solution)/shard_map/ppermute | solution.py:111
  82.8 27.9 %collective-permute-start.17 = (bf16[2,1,32,2560]{3,2,1,0:T(8,128)(2,1)S(1)}, bf16[2,1,32,2560]{3,2,1,0:T(8,128)(2,1)S(1)}, u32[]{:S(2)}, u32[]{:S(2)}) collective-permute-start(bf16[2,1,32,2560]{3,2,1,0:T(8,128)(2,1)S(1)} %pad_maximum_fusion.8), channel_id=1, source_target_pairs={{0,8},{4,12},{8,0},{12,4},{16,24},{20,28},{24,16},{28,20},{1,9},{5... | collective-permute-start | bytes 983048 | tf_op jit(solution)/shard_map/ppermute | solution.py:111
  90.5 21.1 %collective-permute-start.16 = (bf16[2,1,32,2560]{3,2,1,0:T(8,128)(2,1)S(1)}, bf16[2,1,32,2560]{3,2,1,0:T(8,128)(2,1)S(1)}, u32[]{:S(2)}, u32[]{:S(2)}) collective-permute-start(bf16[2,1,32,2560]{3,2,1,0:T(8,128)(2,1)S(1)} %pad_maximum_fusion.7), channel_id=1, source_target_pairs={{0,4},{4,0},{8,12},{12,8},{16,20},{20,16},{24,28},{28,24},{1,5},{5... | collective-permute-start | bytes 983048 | tf_op jit(solution)/shard_map/ppermute | solution.py:111
  96.6 29.1 %collective-permute-start.14 = (bf16[2,1,32,2560]{3,2,1,0:T(8,128)(2,1)S(1)}, bf16[2,1,32,2560]{3,2,1,0:T(8,128)(2,1)S(1)}, u32[]{:S(2)}, u32[]{:S(2)}) collective-permute-start(bf16[2,1,32,2560]{3,2,1,0:T(8,128)(2,1)S(1)} %pad_maximum_fusion.6), channel_id=1, source_target_pairs={{0,12},{4,8},{8,4},{12,0},{16,28},{20,24},{24,20},{28,16},{1,13},{... | collective-permute-start | bytes 983048 | tf_op jit(solution)/shard_map/ppermute | solution.py:111
  97.6 33.0 %collective-permute-start.13 = (bf16[2,1,32,2560]{3,2,1,0:T(8,128)(2,1)S(1)}, bf16[2,1,32,2560]{3,2,1,0:T(8,128)(2,1)S(1)}, u32[]{:S(2)}, u32[]{:S(2)}) collective-permute-start(bf16[2,1,32,2560]{3,2,1,0:T(8,128)(2,1)S(1)} %pad_maximum_fusion.5), channel_id=1, source_target_pairs={{0,8},{4,12},{8,0},{12,4},{16,24},{20,28},{24,16},{28,20},{1,9},{5... | collective-permute-start | bytes 983048 | tf_op jit(solution)/shard_map/ppermute | solution.py:111
  104.6 26.0 %collective-permute-start.12 = (bf16[2,1,32,2560]{3,2,1,0:T(8,128)(2,1)S(1)}, bf16[2,1,32,2560]{3,2,1,0:T(8,128)(2,1)S(1)}, u32[]{:S(2)}, u32[]{:S(2)}) collective-permute-start(bf16[2,1,32,2560]{3,2,1,0:T(8,128)(2,1)S(1)} %pad_maximum_fusion.4), channel_id=1, source_target_pairs={{0,4},{4,0},{8,12},{12,8},{16,20},{20,16},{24,28},{28,24},{1,5},{5... | collective-permute-start | bytes 983048 | tf_op jit(solution)/shard_map/ppermute | solution.py:111
  110.7 20.1 %collective-permute-start.23 = (bf16[1,32,2560]{2,1,0:T(8,128)(2,1)S(1)}, bf16[1,32,2560]{2,1,0:T(8,128)(2,1)S(1)}, u32[]{:S(2)}, u32[]{:S(2)}) collective-permute-start(bf16[1,32,2560]{2,1,0:T(8,128)(2,1)S(1)} %fusion.76), channel_id=1, source_target_pairs={{0,16},{4,20},{8,24},{12,28},{16,0},{20,4},{24,8},{28,12},{1,17},{... | collective-permute-start | bytes 491528 | tf_op jit(solution)/shard_map/ppermute | solution.py:116
  111.8 19.2 %collective-permute-start.19 = (bf16[1,32,2560]{2,1,0:T(8,128)(2,1)S(1)}, bf16[1,32,2560]{2,1,0:T(8,128)(2,1)S(1)}, u32[]{:S(2)}, u32[]{:S(2)}) collective-permute-start(bf16[1,32,2560]{2,1,0:T(8,128)(2,1)S(1)} %fusion.74), channel_id=1, source_target_pairs={{0,16},{4,20},{8,24},{12,28},{16,0},{20,4},{24,8},{28,12},{1,17},{... | collective-permute-start | bytes 491528 | tf_op jit(solution)/shard_map/ppermute | solution.py:116
  130.8 8.4 %collective-permute-start.15 = (bf16[1,32,2560]{2,1,0:T(8,128)(2,1)S(1)}, bf16[1,32,2560]{2,1,0:T(8,128)(2,1)S(1)}, u32[]{:S(2)}, u32[]{:S(2)}) collective-permute-start(bf16[1,32,2560]{2,1,0:T(8,128)(2,1)S(1)} %fusion.72), channel_id=1, source_target_pairs={{0,16},{4,20},{8,24},{12,28},{16,0},{20,4},{24,8},{28,12},{1,17},{... | collective-permute-start | bytes 491528 | tf_op jit(solution)/shard_map/ppermute | solution.py:116
  140.1 11.9 %all-to-all-start = ((bf16[3,4,8,1,2560]{4,2,3,0,1:T(8,128)(2,1)}), bf16[3,4,8,1,2560]{4,2,3,0,1:T(8,128)(2,1)S(1)}, u32[]{:S(2)}, u32[]{:S(2)}) async-start(bf16[3,4,8,1,2560]{4,2,3,0,1:T(8,128)(2,1)} %copy.75), calls=%async_computation | async-start | bytes 983040 | tf_op jit(solution)/shard_map/all_to_all | solution.py:320
  162.8 10.9 %all-to-all-start.1 = ((bf16[3,1,8,4,2048]{4,2,0,1,3:T(8,128)(2,1)}), bf16[3,1,8,4,2048]{4,2,0,1,3:T(8,128)(2,1)S(1)}, u32[]{:S(2)}, u32[]{:S(2)}) async-start(bf16[3,1,8,4,2048]{4,2,0,1,3:T(8,128)(2,1)} %copy.86), calls=%async_computation.1 | async-start | bytes 786432 | tf_op jit(solution)/shard_map/all_to_all | solution.py:346
  173.7 10.7 %collective-permute-start.24 = (bf16[3,32,2048]{2,1,0:T(8,128)(2,1)S(1)}, bf16[3,32,2048]{2,1,0:T(8,128)(2,1)S(1)}, u32[]{:S(2)}, u32[]{:S(2)}) collective-permute-start(bf16[3,32,2048]{2,1,0:T(8,128)(2,1)S(1)} %bitcast.231), channel_id=1, source_target_pairs={{0,4},{8,0},{16,8},{24,16},{28,24},{20,28},{12,20},{4,12},{1,5},{9... | collective-permute-start | bytes 1179656 | tf_op jit(solution)/shard_map/ppermute | solution.py:82
  175.2 10.7 %collective-permute-start.27 = (bf16[3,32,2048]{2,1,0:T(8,128)(2,1)S(1)}, bf16[3,32,2048]{2,1,0:T(8,128)(2,1)S(1)}, u32[]{:S(2)}, u32[]{:S(2)}) collective-permute-start(bf16[3,32,2048]{2,1,0:T(8,128)(2,1)S(1)} %bitcast.232), channel_id=1, source_target_pairs={{0,8},{8,16},{16,24},{24,28},{28,20},{20,12},{12,4},{4,0},{1,9},{9... | collective-permute-start | bytes 1179656 | tf_op jit(solution)/shard_map/ppermute | solution.py:79
  184.4 9.8 %collective-permute-start.25 = (bf16[3,32,2048]{2,1,0:T(8,128)(2,1)S(1)}, bf16[3,32,2048]{2,1,0:T(8,128)(2,1)S(1)}, u32[]{:S(2)}, u32[]{:S(2)}) collective-permute-start(bf16[3,32,2048]{2,1,0:T(8,128)(2,1)S(1)} %collective-permute-done.24), channel_id=1, source_target_pairs={{0,4},{8,0},{16,8},{24,16},{28,24},{20,28},{12,20},{4,12},{1,5},{9... | collective-permute-start | bytes 1179656 | tf_op jit(solution)/shard_map/ppermute | solution.py:82
  185.9 9.8 %collective-permute-start.28 = (bf16[3,32,2048]{2,1,0:T(8,128)(2,1)S(1)}, bf16[3,32,2048]{2,1,0:T(8,128)(2,1)S(1)}, u32[]{:S(2)}, u32[]{:S(2)}) collective-permute-start(bf16[3,32,2048]{2,1,0:T(8,128)(2,1)S(1)} %collective-permute-done.27), channel_id=1, source_target_pairs={{0,8},{8,16},{16,24},{24,28},{28,20},{20,12},{12,4},{4,0},{1,9},{9... | collective-permute-start | bytes 1179656 | tf_op jit(solution)/shard_map/ppermute | solution.py:79
  194.2 11.3 %collective-permute-start.26 = (bf16[3,32,2048]{2,1,0:T(8,128)(2,1)S(1)}, bf16[3,32,2048]{2,1,0:T(8,128)(2,1)S(1)}, u32[]{:S(2)}, u32[]{:S(2)}) collective-permute-start(bf16[3,32,2048]{2,1,0:T(8,128)(2,1)S(1)} %collective-permute-done.25), channel_id=1, source_target_pairs={{0,4},{8,0},{16,8},{24,16},{28,24},{20,28},{12,20},{4,12},{1,5},{9... | collective-permute-start | bytes 1179656 | tf_op jit(solution)/shard_map/ppermute | solution.py:82
  195.6 9.3 %collective-permute-start.29 = (bf16[3,32,2048]{2,1,0:T(8,128)(2,1)S(1)}, bf16[3,32,2048]{2,1,0:T(8,128)(2,1)S(1)}, u32[]{:S(2)}, u32[]{:S(2)}) collective-permute-start(bf16[3,32,2048]{2,1,0:T(8,128)(2,1)S(1)} %collective-permute-done.28), channel_id=1, source_target_pairs={{0,8},{8,16},{16,24},{24,28},{28,20},{20,12},{12,4},{4,0},{1,9},{9... | collective-permute-start | bytes 1179656 | tf_op jit(solution)/shard_map/ppermute | solution.py:79
  204.9 7.8 %collective-permute-start.30 = (bf16[3,32,2048]{2,1,0:T(8,128)(2,1)S(1)}, bf16[3,32,2048]{2,1,0:T(8,128)(2,1)S(1)}, u32[]{:S(2)}, u32[]{:S(2)}) collective-permute-start(bf16[3,32,2048]{2,1,0:T(8,128)(2,1)S(1)} %collective-permute-done.29), channel_id=1, source_target_pairs={{0,8},{8,16},{16,24},{24,28},{28,20},{20,12},{12,4},{4,0},{1,9},{9... | collective-permute-start | bytes 1179656 | tf_op jit(solution)/shard_map/ppermute | solution.py:79
  222.4 7.0 %collective-permute-start.32 = (f32[3,2,128,64]{2,3,0,1:T(8,128)S(1)}, f32[3,2,128,64]{2,3,0,1:T(8,128)S(1)}, u32[]{:S(2)}, u32[]{:S(2)}) collective-permute-start(f32[3,2,128,64]{2,3,0,1:T(8,128)S(1)} %add.548), channel_id=1, source_target_pairs={{0,2},{1,3},{2,0},{3,1},{4,6},{5,7},{6,4},{7,5},{8,10},{9,11},{10,... | collective-permute-start | bytes 589832 | tf_op jit(solution)/shard_map/ppermute | solution.py:166
  238.9 6.6 %collective-permute-start.35 = (bf16[3,2,128,64]{2,3,0,1:T(8,128)(2,1)S(1)}, bf16[3,2,128,64]{2,3,0,1:T(8,128)(2,1)S(1)}, u32[]{:S(2)}, u32[]{:S(2)}) collective-permute-start(bf16[3,2,128,64]{2,3,0,1:T(8,128)(2,1)S(1)} %add.551), channel_id=1, source_target_pairs={{0,16},{4,20},{8,24},{12,28},{16,0},{20,4},{24,8},{28,12},{1,17},{... | collective-permute-start | bytes 294920 | tf_op jit(solution)/shard_map/ppermute | solution.py:166
  254.6 7.9 %collective-permute-start.39 = (bf16[1,1,64,1024]{3,2,1,0:T(8,128)(2,1)S(1)}, bf16[1,1,64,1024]{3,2,1,0:T(8,128)(2,1)S(1)}, u32[]{:S(2)}, u32[]{:S(2)}) collective-permute-start(bf16[1,1,64,1024]{3,2,1,0:T(8,128)(2,1)S(1)} %dynamic-slice_convert_fusion.1), channel_id=1, source_target_pairs={{0,2},{1,3},{2,0},{3,1},{4,6},{5,7},{6,4},{7,5},{8,10},{9,11},{10,... | collective-permute-start | bytes 393224 | tf_op jit(solution)/shard_map/ppermute | solution.py:191
  255.6 8.8 %collective-permute-start.37 = (bf16[1,1,64,1024]{3,2,1,0:T(8,128)(2,1)S(1)}, bf16[1,1,64,1024]{3,2,1,0:T(8,128)(2,1)S(1)}, u32[]{:S(2)}, u32[]{:S(2)}) collective-permute-start(bf16[1,1,64,1024]{3,2,1,0:T(8,128)(2,1)S(1)} %dynamic-slice_convert_fusion.2), channel_id=1, source_target_pairs={{0,2},{1,3},{2,0},{3,1},{4,6},{5,7},{6,4},{7,5},{8,10},{9,11},{10,... | collective-permute-start | bytes 393224 | tf_op jit(solution)/shard_map/ppermute | solution.py:191
  (23 other events, 165.2 us)

commit v16 on v13

--- a/solution.py
+++ b/solution.py
@@ -186,8 +186,7 @@
         keep = lax.dynamic_index_in_dim(pairs, mine, axis=2, keepdims=False)
         give = lax.dynamic_index_in_dim(pairs, 1 - mine, axis=2, keepdims=False)
         swap = [(i, i ^ distance) for i in range(axis_size)]
-        if distance > 1:
-            give = give.astype(jnp.bfloat16)
+        give = give.astype(jnp.bfloat16)
         held = keep + lax.ppermute(give, axis_name, swap).astype(jnp.float32)
         distance *= 2
     return held.reshape(steps, rows // axis_size, columns)

time: 264 us -> 264 us (level)
  transfers between devices with their start and end apart: 42 -> 42, of which waited for: 30 -> 30; matrix products, arithmetic and copies ran while one was open for 11% -> 10% of each run, Pallas kernels for 0% -> 0%
where the time goes in v16:
time: 264 us; the launch traced here: 263 us
  waiting for transfers between devices  134 us (51%)
  starting transfers between devices  57.9 us (22%)
  matrix products  23.8 us (9%)
  local copies, waits for them, and re-layouts  20.5 us (8%)
  other arithmetic  20.2 us (8%)
  between operations  6.3 us (2%)
    ppermute x9, waiting for transfers between devices, split_half_scatter(): lax.ppermute(outgoing, axis_name, [(i, i ^ offset) for i in range(axis_si...  36.7 us
    ppermute x13, waiting for transfers between devices, tree_sum(): value = value + lax.ppermute(value, axis_name, pairs)  28 us
    ppermute x13, starting transfers between devices, tree_sum(): value = value + lax.ppermute(value, axis_name, pairs)  19.3 us
    ppermute x3, waiting for transfers between devices, ring_gather(): backward = lax.ppermute(backward, axis_name, behind)  14.8 us
    ppermute x4, waiting for transfers between devices, ring_gather(): forward = lax.ppermute(forward, axis_name, ahead)  13.1 us
    ppermute x2, waiting for transfers between devices, doubling_gather(): lax.ppermute(held, axis_name, [(i, i ^ distance) for i in range(axis_size)])  12.2 us
    ppermute x9, starting transfers between devices, split_half_scatter(): lax.ppermute(outgoing, axis_name, [(i, i ^ offset) for i in range(axis_si...  11.8 us
    unnamed x31, local copies, waits for them, and re-layouts  8.42 us
  transfers between devices with their start and end apart: 42, of which 30 were waited for; matrix products, arithmetic and copies ran while one was open for 10% of the time, Pallas kernels for 0%

profile of v16, /device:TPU:0, one launch (start us, length us, event | category | flops | bytes accessed | tf_op | source)
XLA Modules:
  0.0 263.0 jit_solution(964859614064749315)
XLA Ops:
  3.2 3.0 %collective-permute-start.1 = (bf16[3,128,1024]{2,1,0:T(8,128)(2,1)S(1)}, bf16[3,128,1024]{2,1,0:T(8,128)(2,1)}, u32[]{:S(2)}, u32[]{:S(2)}) collective-permute-start(bf16[3,128,1024]{2,1,0:T(8,128)(2,1)S(1)} %pad_maximum_fusion.1), channel_id=1, source_target_pairs={{0,2},{1,3},{2,0},{3,1},{4,6},{5,7},{6,4},{7,5},{8,10},{9,11},{10,... | collective-permute-start | bytes 2359304 | tf_op jit(solution)/shard_map/ppermute | solution.py:129
  13.4 10.7 %collective-permute-done.1 = bf16[3,128,1024]{2,1,0:T(8,128)(2,1)} collective-permute-done((bf16[3,128,1024]{2,1,0:T(8,128)(2,1)S(1)}, bf16[3,128,1024]{2,1,0:T(8,128)(2,1)}, u32[]{:S(2)}, u32[]{:S(2)}) %collective-permute-start.1) | collective-permute-done | bytes 786464 | tf_op jit(solution)/shard_map/ppermute | solution.py:129
  33.3 2.8 %collective-permute-start.4 = (f32[3,256]{1,0:T(4,128)S(1)}, f32[3,256]{1,0:T(4,128)S(1)}, u32[]{:S(2)}, u32[]{:S(2)}) collective-permute-start(f32[3,256]{1,0:T(4,128)S(1)} %add.478), channel_id=1, source_target_pairs={{0,16},{4,20},{8,24},{12,28},{16,0},{20,4},{24,8},{28,12},{1,17},{... | collective-permute-start | bytes 9224 | tf_op jit(solution)/shard_map/ppermute | solution.py:166
  40.4 3.9 %collective-permute-done.5 = f32[3,2,128,64]{2,3,0,1:T(8,128)S(1)} collective-permute-done((f32[3,2,128,64]{2,3,0,1:T(8,128)S(1)}, f32[3,2,128,64]{2,3,0,1:T(8,128)S(1)}, u32[]{:S(2)}, u32[]{:S(2)}) %collective-permute-start.5) | collective-permute-done | bytes 196640 | tf_op jit(solution)/shard_map/ppermute | solution.py:166
  46.8 4.7 %collective-permute-done.6 = f32[3,2,128,64]{2,3,0,1:T(8,128)S(1)} collective-permute-done((f32[3,2,128,64]{2,3,0,1:T(8,128)S(1)}, f32[3,2,128,64]{2,3,0,1:T(8,128)S(1)}, u32[]{:S(2)}, u32[]{:S(2)}) %collective-permute-start.6) | collective-permute-done | bytes 196640 | tf_op jit(solution)/shard_map/ppermute | solution.py:166
  51.5 2.5 collective-permute-start.7
  54.1 5.6 %fusion.8 = f32[3,256,2048]{2,1,0:T(8,128)} fusion(bf16[1024,2048]{1,0:T(8,128)(2,1)S(1)} %copy-done.7, f32[1024]{0:T(1024)S(1)} %convert_element_type.258, f32[3,256]{1,0:T(4,128)S(1)} %add_rsqrt_fusion, bf16[3,128,1024]{2,1,0:T(8,128)(2,1)S(1)} %get-tuple-element.22, bf16[3,128,1024]{2,1,0:T(8,128)(2,1)S(1)} %get-tuple-element.21), kind=kOutput, calls=%fused_computation.11 | convolution fusion | flops 3226730496 | bytes 12065792 | tf_op jit(solution)/shard_map/tnd,de->tne/dot_general | solution.py:307
  72.3 2.5 pad_maximum_fusion
  75.8 2.8 %collective-permute-start.20 = (bf16[2,1,32,2560]{3,2,1,0:T(8,128)(2,1)S(1)}, bf16[2,1,32,2560]{3,2,1,0:T(8,128)(2,1)S(1)}, u32[]{:S(2)}, u32[]{:S(2)}) collective-permute-start(bf16[2,1,32,2560]{3,2,1,0:T(8,128)(2,1)S(1)} %pad_maximum_fusion.12), channel_id=1, source_target_pairs={{0,12},{4,8},{8,4},{12,0},{16,28},{20,24},{24,20},{28,16},{1,13},{... | collective-permute-start | bytes 983048 | tf_op jit(solution)/shard_map/ppermute | solution.py:111
  79.6 2.8 %collective-permute-start.16 = (bf16[2,1,32,2560]{3,2,1,0:T(8,128)(2,1)S(1)}, bf16[2,1,32,2560]{3,2,1,0:T(8,128)(2,1)S(1)}, u32[]{:S(2)}, u32[]{:S(2)}) collective-permute-start(bf16[2,1,32,2560]{3,2,1,0:T(8,128)(2,1)S(1)} %pad_maximum_fusion.9), channel_id=1, source_target_pairs={{0,12},{4,8},{8,4},{12,0},{16,28},{20,24},{24,20},{28,16},{1,13},{... | collective-permute-start | bytes 983048 | tf_op jit(solution)/shard_map/ppermute | solution.py:111
  83.1 4.3 %collective-permute-done.20 = bf16[2,1,32,2560]{3,2,1,0:T(8,128)(2,1)S(1)} collective-permute-done((bf16[2,1,32,2560]{3,2,1,0:T(8,128)(2,1)S(1)}, bf16[2,1,32,2560]{3,2,1,0:T(8,128)(2,1)S(1)}, u32[]{:S(2)}, u32[]{:S(2)}) %collective-permute-start.20) | collective-permute-done | bytes 327712 | tf_op jit(solution)/shard_map/ppermute | solution.py:111
  89.0 5.5 %collective-permute-done.19 = bf16[2,1,32,2560]{3,2,1,0:T(8,128)(2,1)S(1)} collective-permute-done((bf16[2,1,32,2560]{3,2,1,0:T(8,128)(2,1)S(1)}, bf16[2,1,32,2560]{3,2,1,0:T(8,128)(2,1)S(1)}, u32[]{:S(2)}, u32[]{:S(2)}) %collective-permute-start.19) | collective-permute-done | bytes 327712 | tf_op jit(solution)/shard_map/ppermute | solution.py:111
  96.7 4.8 %collective-permute-done.16 = bf16[2,1,32,2560]{3,2,1,0:T(8,128)(2,1)S(1)} collective-permute-done((bf16[2,1,32,2560]{3,2,1,0:T(8,128)(2,1)S(1)}, bf16[2,1,32,2560]{3,2,1,0:T(8,128)(2,1)S(1)}, u32[]{:S(2)}, u32[]{:S(2)}) %collective-permute-start.16) | collective-permute-done | bytes 327712 | tf_op jit(solution)/shard_map/ppermute | solution.py:111
  103.0 5.5 %collective-permute-done.15 = bf16[2,1,32,2560]{3,2,1,0:T(8,128)(2,1)S(1)} collective-permute-done((bf16[2,1,32,2560]{3,2,1,0:T(8,128)(2,1)S(1)}, bf16[2,1,32,2560]{3,2,1,0:T(8,128)(2,1)S(1)}, u32[]{:S(2)}, u32[]{:S(2)}) %collective-permute-start.15) | collective-permute-done | bytes 327712 | tf_op jit(solution)/shard_map/ppermute | solution.py:111
  111.7 10.9 %collective-permute-done.12 = bf16[2,1,32,2560]{3,2,1,0:T(8,128)(2,1)S(1)} collective-permute-done((bf16[2,1,32,2560]{3,2,1,0:T(8,128)(2,1)S(1)}, bf16[2,1,32,2560]{3,2,1,0:T(8,128)(2,1)S(1)}, u32[]{:S(2)}, u32[]{:S(2)}) %collective-permute-start.12) | collective-permute-done | bytes 327712 | tf_op jit(solution)/shard_map/ppermute | solution.py:111
  122.7 5.7 %collective-permute-done.11 = bf16[2,1,32,2560]{3,2,1,0:T(8,128)(2,1)S(1)} collective-permute-done((bf16[2,1,32,2560]{3,2,1,0:T(8,128)(2,1)S(1)}, bf16[2,1,32,2560]{3,2,1,0:T(8,128)(2,1)S(1)}, u32[]{:S(2)}, u32[]{:S(2)}) %collective-permute-start.11) | collective-permute-done | bytes 327712 | tf_op jit(solution)/shard_map/ppermute | solution.py:111
  130.3 7.7 %collective-permute-done.13 = bf16[1,32,2560]{2,1,0:T(8,128)(2,1)S(1)} collective-permute-done((bf16[1,32,2560]{2,1,0:T(8,128)(2,1)S(1)}, bf16[1,32,2560]{2,1,0:T(8,128)(2,1)S(1)}, u32[]{:S(2)}, u32[]{:S(2)}) %collective-permute-start.13) | collective-permute-done | bytes 163872 | tf_op jit(solution)/shard_map/ppermute | solution.py:116
  138.9 3.7 %all-to-all-start = ((bf16[3,4,8,1,2560]{4,2,3,0,1:T(8,128)(2,1)}), bf16[3,4,8,1,2560]{4,2,3,0,1:T(8,128)(2,1)S(1)}, u32[]{:S(2)}, u32[]{:S(2)}) async-start(bf16[3,4,8,1,2560]{4,2,3,0,1:T(8,128)(2,1)} %copy.84), calls=%async_computation | async-start | bytes 983040 | tf_op jit(solution)/shard_map/all_to_all | solution.py:317
  142.9 8.0 %all-to-all-done = bf16[3,4,8,1,2560]{4,2,3,0,1:T(8,128)(2,1)S(1)} async-done(((bf16[3,4,8,1,2560]{4,2,3,0,1:T(8,128)(2,1)}), bf16[3,4,8,1,2560]{4,2,3,0,1:T(8,128)(2,1)S(1)}, u32[]{:S(2)}, u32[]{:S(2)}) %all-to-all-start) | async-done | bytes 491552 | tf_op jit(solution)/shard_map/all_to_all | solution.py:317
  152.6 4.6 %fusion.108 = (f32[8,8,24]{2,1,0:T(8,128)S(1)}, f32[8,8,24,256]{3,2,1,0:T(8,128)S(1)}) fusion(pred[8,256]{1,0:T(8,128)(4,1)S(1)} %iota_compare_fusion, bf16[8,256,1024]{2,1,0:T(8,128)(2,1)} %param.27, bf16[3,8,8,8,64]{4,3,2,1,0:T(8,128)(2,1)S(1)} %bitcast.237, bf16[3,8,8,8,64]{4,3,2,1,0:T(8,128)(2,1)S(1)} %bitcast.235), kind=kOutput, calls=%fused_computation.219 | convolution fusion | flops 102627840 | bytes 6168576 | tf_op jit(solution)/shard_map/rhqd,rchd->rhqc/dot_general | solution.py:216
  161.6 3.5 %all-to-all-start.1 = ((bf16[3,1,8,4,2048]{4,2,0,1,3:T(8,128)(2,1)}), bf16[3,1,8,4,2048]{4,2,0,1,3:T(8,128)(2,1)S(1)}, u32[]{:S(2)}, u32[]{:S(2)}) async-start(bf16[3,1,8,4,2048]{4,2,0,1,3:T(8,128)(2,1)} %copy.95), calls=%async_computation.1 | async-start | bytes 786432 | tf_op jit(solution)/shard_map/all_to_all | solution.py:343
  166.9 5.6 %all-to-all-done.1 = bf16[3,1,8,4,2048]{4,2,0,1,3:T(8,128)(2,1)S(1)} async-done(((bf16[3,1,8,4,2048]{4,2,0,1,3:T(8,128)(2,1)}), bf16[3,1,8,4,2048]{4,2,0,1,3:T(8,128)(2,1)S(1)}, u32[]{:S(2)}, u32[]{:S(2)}) %all-to-all-start.1) | async-done | bytes 393248 | tf_op jit(solution)/shard_map/all_to_all | solution.py:343
  175.4 7.9 %collective-permute-done.22 = bf16[3,32,2048]{2,1,0:T(8,128)(2,1)S(1)} collective-permute-done((bf16[3,32,2048]{2,1,0:T(8,128)(2,1)S(1)}, bf16[3,32,2048]{2,1,0:T(8,128)(2,1)S(1)}, u32[]{:S(2)}, u32[]{:S(2)}) %collective-permute-start.22) | collective-permute-done | bytes 393248 | tf_op jit(solution)/shard_map/ppermute | solution.py:82
  186.1 6.9 %collective-permute-done.23 = bf16[3,32,2048]{2,1,0:T(8,128)(2,1)S(1)} collective-permute-done((bf16[3,32,2048]{2,1,0:T(8,128)(2,1)S(1)}, bf16[3,32,2048]{2,1,0:T(8,128)(2,1)S(1)}, u32[]{:S(2)}, u32[]{:S(2)}) %collective-permute-start.23) | collective-permute-done | bytes 393248 | tf_op jit(solution)/shard_map/ppermute | solution.py:82
  195.8 7.3 %collective-permute-done.27 = bf16[3,32,2048]{2,1,0:T(8,128)(2,1)S(1)} collective-permute-done((bf16[3,32,2048]{2,1,0:T(8,128)(2,1)S(1)}, bf16[3,32,2048]{2,1,0:T(8,128)(2,1)S(1)}, u32[]{:S(2)}, u32[]{:S(2)}) %collective-permute-start.27) | collective-permute-done | bytes 393248 | tf_op jit(solution)/shard_map/ppermute | solution.py:79
  205.1 5.8 %collective-permute-done.28 = bf16[3,32,2048]{2,1,0:T(8,128)(2,1)S(1)} collective-permute-done((bf16[3,32,2048]{2,1,0:T(8,128)(2,1)S(1)}, bf16[3,32,2048]{2,1,0:T(8,128)(2,1)S(1)}, u32[]{:S(2)}, u32[]{:S(2)}) %collective-permute-start.28) | collective-permute-done | bytes 393248 | tf_op jit(solution)/shard_map/ppermute | solution.py:79
  214.0 2.6 %gather_fusion = bf16[8,3,32,2048]{3,2,1,0:T(8,128)(2,1)S(1)} fusion(bf16[8,3,32,2048]{3,2,1,0:T(8,128)(2,1)} %bitcast_dynamic-update-slice_fusion.1, s32[1024]{0:T(1024)S(1)} %pad_clamp_fusion), kind=kCustom, calls=%fused_computation | custom fusion | bytes 6291488 | tf_op jit(solution)/shard_map/jit(_take)/gather | solution.py:88
  221.9 5.8 %collective-permute-done.30 = f32[3,2,128,64]{2,3,0,1:T(8,128)S(1)} collective-permute-done((f32[3,2,128,64]{2,3,0,1:T(8,128)S(1)}, f32[3,2,128,64]{2,3,0,1:T(8,128)S(1)}, u32[]{:S(2)}, u32[]{:S(2)}) %collective-permute-start.30) | collective-permute-done | bytes 196640 | tf_op jit(solution)/shard_map/ppermute | solution.py:166
  228.6 3.8 %collective-permute-done.31 = bf16[3,2,128,64]{2,3,0,1:T(8,128)(2,1)S(1)} collective-permute-done((bf16[3,2,128,64]{2,3,0,1:T(8,128)(2,1)S(1)}, bf16[3,2,128,64]{2,3,0,1:T(8,128)(2,1)S(1)}, u32[]{:S(2)}, u32[]{:S(2)}) %collective-permute-start.31) | collective-permute-done | bytes 98336 | tf_op jit(solution)/shard_map/ppermute | solution.py:166
  238.6 5.2 %fusion.6 = f32[3,256,1024]{2,1,0:T(8,128)S(1)} fusion(bf16[3,256,2048]{2,1,0:T(8,128)(2,1)S(1)} %bitcast.232, bf16[2048,1024]{1,0:T(8,128)(2,1)} %param.20), kind=kOutput, calls=%fused_computation.9 | convolution fusion | flops 3221225472 | bytes 10485760 | tf_op jit(solution)/shard_map/tnq,qe->tne/dot_general | solution.py:358
  254.8 2.5 collective-permute-done.39
  257.4 2.8 %collective-permute-done.37 = bf16[1,1,64,1024]{3,2,1,0:T(8,128)(2,1)S(1)} collective-permute-done((bf16[1,1,64,1024]{3,2,1,0:T(8,128)(2,1)S(1)}, bf16[1,1,64,1024]{3,2,1,0:T(8,128)(2,1)S(1)}, u32[]{:S(2)}, u32[]{:S(2)}) %collective-permute-start.37) | collective-permute-done | bytes 131104 | tf_op jit(solution)/shard_map/ppermute | solution.py:190
  (203 shorter events, 95.1 us)
Async XLA Ops:
  3.2 20.9 %collective-permute-start.1 = (bf16[3,128,1024]{2,1,0:T(8,128)(2,1)S(1)}, bf16[3,128,1024]{2,1,0:T(8,128)(2,1)}, u32[]{:S(2)}, u32[]{:S(2)}) collective-permute-start(bf16[3,128,1024]{2,1,0:T(8,128)(2,1)S(1)} %pad_maximum_fusion.1), channel_id=1, source_target_pairs={{0,2},{1,3},{2,0},{3,1},{4,6},{5,7},{6,4},{7,5},{8,10},{9,11},{10,... | collective-permute-start | bytes 2359304 | tf_op jit(solution)/shard_map/ppermute | solution.py:129
  38.5 5.7 %collective-permute-start.5 = (f32[3,2,128,64]{2,3,0,1:T(8,128)S(1)}, f32[3,2,128,64]{2,3,0,1:T(8,128)S(1)}, u32[]{:S(2)}, u32[]{:S(2)}) collective-permute-start(f32[3,2,128,64]{2,3,0,1:T(8,128)S(1)} %fusion.23), channel_id=1, source_target_pairs={{0,4},{4,0},{8,12},{12,8},{16,20},{20,16},{24,28},{28,24},{1,5},{5... | collective-permute-start | bytes 589832 | tf_op jit(solution)/shard_map/ppermute | solution.py:166
  44.3 7.2 %collective-permute-start.6 = (f32[3,2,128,64]{2,3,0,1:T(8,128)S(1)}, f32[3,2,128,64]{2,3,0,1:T(8,128)S(1)}, u32[]{:S(2)}, u32[]{:S(2)}) collective-permute-start(f32[3,2,128,64]{2,3,0,1:T(8,128)S(1)} %add.490), channel_id=1, source_target_pairs={{0,8},{4,12},{8,0},{12,4},{16,24},{20,28},{24,16},{28,20},{1,9},{5... | collective-permute-start | bytes 589832 | tf_op jit(solution)/shard_map/ppermute | solution.py:166
  51.5 8.7 %collective-permute-start.7 = (f32[3,2,128,64]{2,3,0,1:T(8,128)S(1)}, f32[3,2,128,64]{2,3,0,1:T(8,128)S(1)}, u32[]{:S(2)}, u32[]{:S(2)}) collective-permute-start(f32[3,2,128,64]{2,3,0,1:T(8,128)S(1)} %add.491), channel_id=1, source_target_pairs={{0,16},{4,20},{8,24},{12,28},{16,0},{20,4},{24,8},{28,12},{1,17},{... | collective-permute-start | bytes 589832 | tf_op jit(solution)/shard_map/ppermute | solution.py:166
  61.9 5.3 %collective-permute-start.9 = (bf16[3,2,128,64]{2,3,0,1:T(8,128)(2,1)S(1)}, bf16[3,2,128,64]{2,3,0,1:T(8,128)(2,1)S(1)}, u32[]{:S(2)}, u32[]{:S(2)}) collective-permute-start(bf16[3,2,128,64]{2,3,0,1:T(8,128)(2,1)S(1)} %add.493), channel_id=1, source_target_pairs={{0,2},{1,3},{2,0},{3,1},{4,6},{5,7},{6,4},{7,5},{8,10},{9,11},{10,... | collective-permute-start | bytes 294920 | tf_op jit(solution)/shard_map/ppermute | solution.py:166
  75.8 11.6 %collective-permute-start.20 = (bf16[2,1,32,2560]{3,2,1,0:T(8,128)(2,1)S(1)}, bf16[2,1,32,2560]{3,2,1,0:T(8,128)(2,1)S(1)}, u32[]{:S(2)}, u32[]{:S(2)}) collective-permute-start(bf16[2,1,32,2560]{3,2,1,0:T(8,128)(2,1)S(1)} %pad_maximum_fusion.12), channel_id=1, source_target_pairs={{0,12},{4,8},{8,4},{12,0},{16,28},{20,24},{24,20},{28,16},{1,13},{... | collective-permute-start | bytes 983048 | tf_op jit(solution)/shard_map/ppermute | solution.py:111
  78.6 15.8 %collective-permute-start.19 = (bf16[2,1,32,2560]{3,2,1,0:T(8,128)(2,1)S(1)}, bf16[2,1,32,2560]{3,2,1,0:T(8,128)(2,1)S(1)}, u32[]{:S(2)}, u32[]{:S(2)}) collective-permute-start(bf16[2,1,32,2560]{3,2,1,0:T(8,128)(2,1)S(1)} %pad_maximum_fusion.11), channel_id=1, source_target_pairs={{0,8},{4,12},{8,0},{12,4},{16,24},{20,28},{24,16},{28,20},{1,9},{5... | collective-permute-start | bytes 983048 | tf_op jit(solution)/shard_map/ppermute | solution.py:111
  78.9 17.4 %collective-permute-start.18 = (bf16[2,1,32,2560]{3,2,1,0:T(8,128)(2,1)S(1)}, bf16[2,1,32,2560]{3,2,1,0:T(8,128)(2,1)S(1)}, u32[]{:S(2)}, u32[]{:S(2)}) collective-permute-start(bf16[2,1,32,2560]{3,2,1,0:T(8,128)(2,1)S(1)} %pad_maximum_fusion.10), channel_id=1, source_target_pairs={{0,4},{4,0},{8,12},{12,8},{16,20},{20,16},{24,28},{28,24},{1,5},{5... | collective-permute-start | bytes 983048 | tf_op jit(solution)/shard_map/ppermute | solution.py:111
  79.6 21.9 %collective-permute-start.16 = (bf16[2,1,32,2560]{3,2,1,0:T(8,128)(2,1)S(1)}, bf16[2,1,32,2560]{3,2,1,0:T(8,128)(2,1)S(1)}, u32[]{:S(2)}, u32[]{:S(2)}) collective-permute-start(bf16[2,1,32,2560]{3,2,1,0:T(8,128)(2,1)S(1)} %pad_maximum_fusion.9), channel_id=1, source_target_pairs={{0,12},{4,8},{8,4},{12,0},{16,28},{20,24},{24,20},{28,16},{1,13},{... | collective-permute-start | bytes 983048 | tf_op jit(solution)/shard_map/ppermute | solution.py:111
  82.4 26.1 %collective-permute-start.15 = (bf16[2,1,32,2560]{3,2,1,0:T(8,128)(2,1)S(1)}, bf16[2,1,32,2560]{3,2,1,0:T(8,128)(2,1)S(1)}, u32[]{:S(2)}, u32[]{:S(2)}) collective-permute-start(bf16[2,1,32,2560]{3,2,1,0:T(8,128)(2,1)S(1)} %pad_maximum_fusion.8), channel_id=1, source_target_pairs={{0,8},{4,12},{8,0},{12,4},{16,24},{20,28},{24,16},{28,20},{1,9},{5... | collective-permute-start | bytes 983048 | tf_op jit(solution)/shard_map/ppermute | solution.py:111
  87.4 22.7 %collective-permute-start.14 = (bf16[2,1,32,2560]{3,2,1,0:T(8,128)(2,1)S(1)}, bf16[2,1,32,2560]{3,2,1,0:T(8,128)(2,1)S(1)}, u32[]{:S(2)}, u32[]{:S(2)}) collective-permute-start(bf16[2,1,32,2560]{3,2,1,0:T(8,128)(2,1)S(1)} %pad_maximum_fusion.7), channel_id=1, source_target_pairs={{0,4},{4,0},{8,12},{12,8},{16,20},{20,16},{24,28},{28,24},{1,5},{5... | collective-permute-start | bytes 983048 | tf_op jit(solution)/shard_map/ppermute | solution.py:111
  94.5 28.2 %collective-permute-start.12 = (bf16[2,1,32,2560]{3,2,1,0:T(8,128)(2,1)S(1)}, bf16[2,1,32,2560]{3,2,1,0:T(8,128)(2,1)S(1)}, u32[]{:S(2)}, u32[]{:S(2)}) collective-permute-start(bf16[2,1,32,2560]{3,2,1,0:T(8,128)(2,1)S(1)} %pad_maximum_fusion.6), channel_id=1, source_target_pairs={{0,12},{4,8},{8,4},{12,0},{16,28},{20,24},{24,20},{28,16},{1,13},{... | collective-permute-start | bytes 983048 | tf_op jit(solution)/shard_map/ppermute | solution.py:111
  96.3 32.1 %collective-permute-start.11 = (bf16[2,1,32,2560]{3,2,1,0:T(8,128)(2,1)S(1)}, bf16[2,1,32,2560]{3,2,1,0:T(8,128)(2,1)S(1)}, u32[]{:S(2)}, u32[]{:S(2)}) collective-permute-start(bf16[2,1,32,2560]{3,2,1,0:T(8,128)(2,1)S(1)} %pad_maximum_fusion.5), channel_id=1, source_target_pairs={{0,8},{4,12},{8,0},{12,4},{16,24},{20,28},{24,16},{28,20},{1,9},{5... | collective-permute-start | bytes 983048 | tf_op jit(solution)/shard_map/ppermute | solution.py:111
  101.5 26.9 %collective-permute-start.10 = (bf16[2,1,32,2560]{3,2,1,0:T(8,128)(2,1)S(1)}, bf16[2,1,32,2560]{3,2,1,0:T(8,128)(2,1)S(1)}, u32[]{:S(2)}, u32[]{:S(2)}) collective-permute-start(bf16[2,1,32,2560]{3,2,1,0:T(8,128)(2,1)S(1)} %pad_maximum_fusion.4), channel_id=1, source_target_pairs={{0,4},{4,0},{8,12},{12,8},{16,20},{20,16},{24,28},{28,24},{1,5},{5... | collective-permute-start | bytes 983048 | tf_op jit(solution)/shard_map/ppermute | solution.py:111
  108.6 21.5 %collective-permute-start.21 = (bf16[1,32,2560]{2,1,0:T(8,128)(2,1)S(1)}, bf16[1,32,2560]{2,1,0:T(8,128)(2,1)S(1)}, u32[]{:S(2)}, u32[]{:S(2)}) collective-permute-start(bf16[1,32,2560]{2,1,0:T(8,128)(2,1)S(1)} %fusion.79), channel_id=1, source_target_pairs={{0,16},{4,20},{8,24},{12,28},{16,0},{20,4},{24,8},{28,12},{1,17},{... | collective-permute-start | bytes 491528 | tf_op jit(solution)/shard_map/ppermute | solution.py:116
  110.2 20.0 %collective-permute-start.17 = (bf16[1,32,2560]{2,1,0:T(8,128)(2,1)S(1)}, bf16[1,32,2560]{2,1,0:T(8,128)(2,1)S(1)}, u32[]{:S(2)}, u32[]{:S(2)}) collective-permute-start(bf16[1,32,2560]{2,1,0:T(8,128)(2,1)S(1)} %fusion.77), channel_id=1, source_target_pairs={{0,16},{4,20},{8,24},{12,28},{16,0},{20,4},{24,8},{28,12},{1,17},{... | collective-permute-start | bytes 491528 | tf_op jit(solution)/shard_map/ppermute | solution.py:116
  128.6 9.4 %collective-permute-start.13 = (bf16[1,32,2560]{2,1,0:T(8,128)(2,1)S(1)}, bf16[1,32,2560]{2,1,0:T(8,128)(2,1)S(1)}, u32[]{:S(2)}, u32[]{:S(2)}) collective-permute-start(bf16[1,32,2560]{2,1,0:T(8,128)(2,1)S(1)} %fusion.75), channel_id=1, source_target_pairs={{0,16},{4,20},{8,24},{12,28},{16,0},{20,4},{24,8},{28,12},{1,17},{... | collective-permute-start | bytes 491528 | tf_op jit(solution)/shard_map/ppermute | solution.py:116
  138.9 11.9 %all-to-all-start = ((bf16[3,4,8,1,2560]{4,2,3,0,1:T(8,128)(2,1)}), bf16[3,4,8,1,2560]{4,2,3,0,1:T(8,128)(2,1)S(1)}, u32[]{:S(2)}, u32[]{:S(2)}) async-start(bf16[3,4,8,1,2560]{4,2,3,0,1:T(8,128)(2,1)} %copy.84), calls=%async_computation | async-start | bytes 983040 | tf_op jit(solution)/shard_map/all_to_all | solution.py:317
  161.6 10.9 %all-to-all-start.1 = ((bf16[3,1,8,4,2048]{4,2,0,1,3:T(8,128)(2,1)}), bf16[3,1,8,4,2048]{4,2,0,1,3:T(8,128)(2,1)S(1)}, u32[]{:S(2)}, u32[]{:S(2)}) async-start(bf16[3,1,8,4,2048]{4,2,0,1,3:T(8,128)(2,1)} %copy.95), calls=%async_computation.1 | async-start | bytes 786432 | tf_op jit(solution)/shard_map/all_to_all | solution.py:343
  172.5 10.7 %collective-permute-start.22 = (bf16[3,32,2048]{2,1,0:T(8,128)(2,1)S(1)}, bf16[3,32,2048]{2,1,0:T(8,128)(2,1)S(1)}, u32[]{:S(2)}, u32[]{:S(2)}) collective-permute-start(bf16[3,32,2048]{2,1,0:T(8,128)(2,1)S(1)} %bitcast.240), channel_id=1, source_target_pairs={{0,4},{8,0},{16,8},{24,16},{28,24},{20,28},{12,20},{4,12},{1,5},{9... | collective-permute-start | bytes 1179656 | tf_op jit(solution)/shard_map/ppermute | solution.py:82
  173.4 10.7 %collective-permute-start.25 = (bf16[3,32,2048]{2,1,0:T(8,128)(2,1)S(1)}, bf16[3,32,2048]{2,1,0:T(8,128)(2,1)S(1)}, u32[]{:S(2)}, u32[]{:S(2)}) collective-permute-start(bf16[3,32,2048]{2,1,0:T(8,128)(2,1)S(1)} %bitcast.241), channel_id=1, source_target_pairs={{0,8},{8,16},{16,24},{24,28},{28,20},{20,12},{12,4},{4,0},{1,9},{9... | collective-permute-start | bytes 1179656 | tf_op jit(solution)/shard_map/ppermute | solution.py:79
  183.2 9.8 %collective-permute-start.23 = (bf16[3,32,2048]{2,1,0:T(8,128)(2,1)S(1)}, bf16[3,32,2048]{2,1,0:T(8,128)(2,1)S(1)}, u32[]{:S(2)}, u32[]{:S(2)}) collective-permute-start(bf16[3,32,2048]{2,1,0:T(8,128)(2,1)S(1)} %collective-permute-done.22), channel_id=1, source_target_pairs={{0,4},{8,0},{16,8},{24,16},{28,24},{20,28},{12,20},{4,12},{1,5},{9... | collective-permute-start | bytes 1179656 | tf_op jit(solution)/shard_map/ppermute | solution.py:82
  184.1 9.8 %collective-permute-start.26 = (bf16[3,32,2048]{2,1,0:T(8,128)(2,1)S(1)}, bf16[3,32,2048]{2,1,0:T(8,128)(2,1)S(1)}, u32[]{:S(2)}, u32[]{:S(2)}) collective-permute-start(bf16[3,32,2048]{2,1,0:T(8,128)(2,1)S(1)} %collective-permute-done.25), channel_id=1, source_target_pairs={{0,8},{8,16},{16,24},{24,28},{28,20},{20,12},{12,4},{4,0},{1,9},{9... | collective-permute-start | bytes 1179656 | tf_op jit(solution)/shard_map/ppermute | solution.py:79
  193.0 11.3 %collective-permute-start.24 = (bf16[3,32,2048]{2,1,0:T(8,128)(2,1)S(1)}, bf16[3,32,2048]{2,1,0:T(8,128)(2,1)S(1)}, u32[]{:S(2)}, u32[]{:S(2)}) collective-permute-start(bf16[3,32,2048]{2,1,0:T(8,128)(2,1)S(1)} %collective-permute-done.23), channel_id=1, source_target_pairs={{0,4},{8,0},{16,8},{24,16},{28,24},{20,28},{12,20},{4,12},{1,5},{9... | collective-permute-start | bytes 1179656 | tf_op jit(solution)/shard_map/ppermute | solution.py:82
  193.8 9.3 %collective-permute-start.27 = (bf16[3,32,2048]{2,1,0:T(8,128)(2,1)S(1)}, bf16[3,32,2048]{2,1,0:T(8,128)(2,1)S(1)}, u32[]{:S(2)}, u32[]{:S(2)}) collective-permute-start(bf16[3,32,2048]{2,1,0:T(8,128)(2,1)S(1)} %collective-permute-done.26), channel_id=1, source_target_pairs={{0,8},{8,16},{16,24},{24,28},{28,20},{20,12},{12,4},{4,0},{1,9},{9... | collective-permute-start | bytes 1179656 | tf_op jit(solution)/shard_map/ppermute | solution.py:79
  203.1 7.8 %collective-permute-start.28 = (bf16[3,32,2048]{2,1,0:T(8,128)(2,1)S(1)}, bf16[3,32,2048]{2,1,0:T(8,128)(2,1)S(1)}, u32[]{:S(2)}, u32[]{:S(2)}) collective-permute-start(bf16[3,32,2048]{2,1,0:T(8,128)(2,1)S(1)} %collective-permute-done.27), channel_id=1, source_target_pairs={{0,8},{8,16},{16,24},{24,28},{28,20},{20,12},{12,4},{4,0},{1,9},{9... | collective-permute-start | bytes 1179656 | tf_op jit(solution)/shard_map/ppermute | solution.py:79
  220.6 7.0 %collective-permute-start.30 = (f32[3,2,128,64]{2,3,0,1:T(8,128)S(1)}, f32[3,2,128,64]{2,3,0,1:T(8,128)S(1)}, u32[]{:S(2)}, u32[]{:S(2)}) collective-permute-start(f32[3,2,128,64]{2,3,0,1:T(8,128)S(1)} %add.534), channel_id=1, source_target_pairs={{0,2},{1,3},{2,0},{3,1},{4,6},{5,7},{6,4},{7,5},{8,10},{9,11},{10,... | collective-permute-start | bytes 589832 | tf_op jit(solution)/shard_map/ppermute | solution.py:166
  232.4 4.7 %collective-permute-start.32 = (bf16[3,2,128,64]{2,3,0,1:T(8,128)(2,1)S(1)}, bf16[3,2,128,64]{2,3,0,1:T(8,128)(2,1)S(1)}, u32[]{:S(2)}, u32[]{:S(2)}) collective-permute-start(bf16[3,2,128,64]{2,3,0,1:T(8,128)(2,1)S(1)} %add.536), channel_id=1, source_target_pairs={{0,8},{4,12},{8,0},{12,4},{16,24},{20,28},{24,16},{28,20},{1,9},{5... | collective-permute-start | bytes 294920 | tf_op jit(solution)/shard_map/ppermute | solution.py:166
  237.1 6.8 %collective-permute-start.33 = (bf16[3,2,128,64]{2,3,0,1:T(8,128)(2,1)S(1)}, bf16[3,2,128,64]{2,3,0,1:T(8,128)(2,1)S(1)}, u32[]{:S(2)}, u32[]{:S(2)}) collective-permute-start(bf16[3,2,128,64]{2,3,0,1:T(8,128)(2,1)S(1)} %add.537), channel_id=1, source_target_pairs={{0,16},{4,20},{8,24},{12,28},{16,0},{20,4},{24,8},{28,12},{1,17},{... | collective-permute-start | bytes 294920 | tf_op jit(solution)/shard_map/ppermute | solution.py:166
  250.9 6.4 %collective-permute-start.39 = (bf16[1,1,64,1024]{3,2,1,0:T(8,128)(2,1)S(1)}, bf16[1,1,64,1024]{3,2,1,0:T(8,128)(2,1)S(1)}, u32[]{:S(2)}, u32[]{:S(2)}) collective-permute-start(bf16[1,1,64,1024]{3,2,1,0:T(8,128)(2,1)S(1)} %dynamic-slice_convert_fusion), channel_id=1, source_target_pairs={{0,2},{1,3},{2,0},{3,1},{4,6},{5,7},{6,4},{7,5},{8,10},{9,11},{10,... | collective-permute-start | bytes 393224 | tf_op jit(solution)/shard_map/ppermute | solution.py:190
  252.5 7.6 %collective-permute-start.37 = (bf16[1,1,64,1024]{3,2,1,0:T(8,128)(2,1)S(1)}, bf16[1,1,64,1024]{3,2,1,0:T(8,128)(2,1)S(1)}, u32[]{:S(2)}, u32[]{:S(2)}) collective-permute-start(bf16[1,1,64,1024]{3,2,1,0:T(8,128)(2,1)S(1)} %dynamic-slice_convert_fusion.1), channel_id=1, source_target_pairs={{0,2},{1,3},{2,0},{3,1},{4,6},{5,7},{6,4},{7,5},{8,10},{9,11},{10,... | collective-permute-start | bytes 393224 | tf_op jit(solution)/shard_map/ppermute | solution.py:190
  253.3 8.8 %collective-permute-start.35 = (bf16[1,1,64,1024]{3,2,1,0:T(8,128)(2,1)S(1)}, bf16[1,1,64,1024]{3,2,1,0:T(8,128)(2,1)S(1)}, u32[]{:S(2)}, u32[]{:S(2)}) collective-permute-start(bf16[1,1,64,1024]{3,2,1,0:T(8,128)(2,1)S(1)} %dynamic-slice_convert_fusion.2), channel_id=1, source_target_pairs={{0,2},{1,3},{2,0},{3,1},{4,6},{5,7},{6,4},{7,5},{8,10},{9,11},{10,... | collective-permute-start | bytes 393224 | tf_op jit(solution)/shard_map/ppermute | solution.py:190
  (22 other events, 191.0 us)
